TPU v7x, 32 devices: a whole 2x2x4 slice. The times are simulated.
32 devices in a mesh: groups: 2 (over y), gz: 4 (over z), sec: 2 (over x), ch: 2 (over core).
Axes of the slice: x: 2, y: 2, z: 4, core: 2. Of those that a mesh axis runs over, the one named last changes fastest.
Arguments:
- coarse: bfloat16 [64, 32, 4, 256], P('ch', ('groups', 'gz', 'sec')), parts along dimension 1, may hold values from -6 to 6
- saved_pre: bfloat16 [32, 64, 8, 512], P('ch', ('groups', 'gz', 'sec')), parts along dimension 1, may hold values from -6 to 6
- out_grad: bfloat16 [32, 64, 8, 512], P('ch', ('groups', 'gz', 'sec')), parts along dimension 1, may hold values from -6 to 6
- up_weight: bfloat16 [27, 32, 64], replicated, may hold values from -0.21875 to 0.21875
- refine_weight: bfloat16 [27, 32, 32], replicated, may hold values from -0.21875 to 0.21875
Outputs:
- grad_coarse: bfloat16 [64, 32, 4, 256], P('ch', ('groups', 'gz', 'sec')), parts along dimension 1
- grad_up: float32 [54, 32, 64], P('groups', 'ch'), parts along dimension 0
- grad_refine: float32 [54, 32, 32], P('groups', None, 'ch'), parts along dimension 0
There are 2 independent parts, one for each index of `groups`. A program takes and returns all parts, laid end to end along the dimension named above; an argument that names none is the same for every part. Nothing has to cross between parts.
All inputs are finite; a program needn't handle non-finite values.
Results may differ from a plain program's by a relative error of at most 0.0049.
Values may be sent and summed in bfloat16 or wider, within the bound.
No kernel may reach another device: no remote copies, remote signals or barrier semaphores. Data moves between devices by JAX's collectives and lax.ppermute only.
A program may use at most 128 MiB of HBM per device.

v0:
```python
import jax
import jax.numpy as jnp
from jax import lax
from jax.sharding import PartitionSpec as P

leak_slope = 0.2


def padded(block, sides, width):
    for axis, dim in sides:
        count = lax.axis_size(axis)
        forward = [(i, i + 1) for i in range(count - 1)]
        forward.append((count - 1, 0))
        backward = [(target, source) for source, target in forward]
        low = lax.ppermute(
            lax.slice_in_dim(block, block.shape[dim] - width, None, axis=dim), axis, forward
        )
        high = lax.ppermute(lax.slice_in_dim(block, 0, width, axis=dim), axis, backward)
        block = jnp.concatenate([low, block, high], axis=dim)
    return block


def passed_along(block, axis, distance):
    devices = range(lax.axis_size(axis))
    route = [((i - distance) % len(devices), i) for i in devices]
    return lax.ppermute(block, axis, route)


def kernel_offsets():
    return [
        (along_z, along_x, along_y)
        for along_z in range(3)
        for along_x in range(3)
        for along_y in range(3)
    ]


def take_taps(source, along_z, along_x, along_y, coarse_z, coarse_x):
    selected = source[
        :, along_z : along_z + 2 * coarse_z : 2, along_x : along_x + 2 * coarse_x : 2, :
    ]
    return jnp.roll(selected, 1 - along_y, axis=3)[:, :, :, ::2]


def local(coarse, saved_pre, out_grad, up_weight, refine_weight):
    part_ch = saved_pre.shape[0]
    planes_z = saved_pre.shape[1]
    planes_x = saved_pre.shape[2]
    cells_y = saved_pre.shape[3]
    coarse_z = planes_z // 2
    coarse_x = planes_x // 2
    channel_start = lax.axis_index("ch") * part_ch
    pre_act = saved_pre.astype(jnp.float32)
    slopes = jnp.where(pre_act > 0, 1.0, leak_slope).astype(jnp.float32)
    hidden = (pre_act * slopes).astype(jnp.bfloat16)
    every_channel = lax.all_gather(out_grad, "ch", axis=0, tiled=True)
    rimmed_z = padded(every_channel, ((("gz", "sec"), 1),), 2)
    rimmed = jnp.pad(rimmed_z, ((0, 0), (0, 0), (2, 2), (0, 0)))
    refine_cols = lax.dynamic_slice_in_dim(refine_weight, channel_start, part_ch, 2)
    grad_hidden = jnp.zeros(pre_act.shape, jnp.float32)
    refine_terms = []
    for tap_number, (along_z, along_x, along_y) in enumerate(kernel_offsets()):
        shifted = rimmed[
            :,
            4 - 2 * along_z : 4 - 2 * along_z + planes_z,
            4 - 2 * along_x : 4 - 2 * along_x + planes_x,
            :,
        ]
        shifted = jnp.roll(shifted, 2 * (along_y - 1), axis=3)
        grad_hidden = grad_hidden + jnp.einsum(
            "oc,ozxy->czxy", refine_cols[tap_number], shifted, preferred_element_type=jnp.float32
        )
        refine_terms.append(
            jnp.einsum("ozxy,czxy->oc", shifted, hidden, preferred_element_type=jnp.float32)
        )
    grad_pre = (grad_hidden * slopes).astype(jnp.bfloat16)
    below_z = passed_along(grad_pre[:, planes_z - 1 :, :, :], ("gz", "sec"), 1)
    raised_z = jnp.concatenate([below_z, grad_pre], axis=1)
    extended = jnp.pad(raised_z, ((0, 0), (0, 0), (1, 0), (0, 0)))
    selections = [
        take_taps(extended, along_z, along_x, along_y, coarse_z, coarse_x)
        for along_z, along_x, along_y in kernel_offsets()
    ]
    all_coarse = lax.all_gather(coarse, "ch", axis=0, tiled=True)
    up_terms = [
        jnp.einsum("czxy,fzxy->fc", all_coarse, selected, preferred_element_type=jnp.float32)
        for selected in selections
    ]
    up_rows = lax.dynamic_slice_in_dim(up_weight, channel_start, part_ch, 1)
    running = jnp.zeros((coarse.shape[0] * lax.axis_size("ch"),) + coarse.shape[1:], jnp.float32)
    for tap_number, selected in enumerate(selections):
        weight_block = up_rows[tap_number]
        running = running + jnp.einsum(
            "fc,fzxy->czxy", weight_block, selected, preferred_element_type=jnp.float32
        )
    coarse_summed = lax.psum_scatter(running, "ch", scatter_dimension=0, tiled=True)
    grad_coarse = coarse_summed.astype(jnp.bfloat16)
    up_summed, refine_summed = lax.psum(
        (jnp.stack(up_terms), jnp.stack(refine_terms)), ("gz", "sec")
    )
    fine_total = planes_z * lax.axis_size("gz") * lax.axis_size("sec") * planes_x * cells_y
    coarse_total = fine_total // 8
    grad_up = up_summed * float(coarse_total) ** (-0.5)
    grad_refine = refine_summed * float(fine_total) ** (-0.5)
    return (grad_coarse, grad_up, grad_refine)


def solution(mesh):
    placed = (
        P("ch", ("groups", "gz", "sec"), None, None),
        P("ch", ("groups", "gz", "sec"), None, None),
        P("ch", ("groups", "gz", "sec"), None, None),
        P(),
        P(),
    )
    return jax.shard_map(
        local,
        mesh=mesh,
        in_specs=placed,
        out_specs=(
            P("ch", ("groups", "gz", "sec"), None, None),
            P("groups", "ch", None),
            P("groups", None, "ch"),
        ),
        check_vma=False,
    )
```

profile of v0, /device:TPU:0, one launch (start us, length us, event | category | flops | bytes accessed | tf_op | source)
XLA Modules:
  0.0 348.0 jit_solution(7144376566447000384)
XLA Ops:
  7.2 2.2 copy.9
  10.4 2.1 all_gather.7
  12.5 8.8 %all-gather.2.cloned.1.call-done = bf16[32,4,8,512]{3,0,2,1:T(8,128)(2,1)} async-done(((bf16[16,4,8,512]{3,0,2,1:T(8,128)(2,1)}), bf16[32,4,8,512]{3,0,2,1:T(8,128)(2,1)}) %all-gather.2.cloned.1.call-update) | async-done | bytes 1048592 | tf_op jit(solution)/shard_map/all_gather | solution.py:56
  22.7 1.8 collective-permute-start
  24.5 3.0 collective-permute-start.1
  29.0 18.3 %collective-permute-done = bf16[32,2,8,512]{3,0,2,1:T(8,128)(2,1)S(1)} collective-permute-done((bf16[32,2,8,512]{3,0,2,1:T(8,128)(2,1)S(1)}, bf16[32,2,8,512]{3,0,2,1:T(8,128)(2,1)S(1)}, u32[]{:S(2)}, u32[]{:S(2)}) %collective-permute-start) | collective-permute-done | bytes 524320 | tf_op jit(solution)/shard_map/ppermute | solution.py:15
  47.4 2.2 collective-permute-done.1
  50.0 4.6 %fusion.280 = (bf16[32,4,8,510]{3,0,2,1:T(8,128)(2,1)S(1)}, bf16[32,4,8,510]{3,0,2,1:T(8,128)(2,1)S(1)}, bf16[32,4,8,510]{3,0,2,1:T(8,128)(2,1)S(1)}, bf16[32,4,...) fusion(bf16[32,8,12,512]{3,0,2,1:T(8,128)(2,1)S(1)} %fusion.5), kind=kLoop, calls=%fused_computation.425 | loop fusion | bytes 25067520 | tf_op jit(solution)/shard_map/jit(_roll_static)/slice | solution.py:69
  56.2 1.8 fusion.279
  100.3 6.5 %collective-permute-done.2 = bf16[16,1,8,512]{3,0,2,1:T(8,128)(2,1)S(1)} collective-permute-done((bf16[16,1,8,512]{3,0,2,1:T(8,128)(2,1)S(1)}, bf16[16,1,8,512]{3,0,2,1:T(8,128)(2,1)S(1)}, u32[]{:S(2)}, u32[]{:S(2)}) %collective-permute-start.2) | collective-permute-done | bytes 131104 | tf_op jit(solution)/shard_map/ppermute | solution.py:26
  109.2 3.9 %slice.685 = bf16[16,2,4,256]{3,0,2,1:T(8,128)(2,1)} slice(bf16[16,2,4,512]{3,0,2,1:T(8,128)(2,1)} %copy-done.2), slice={[0:16:1], [0:2:1], [0:4:1], [0:512:2]} | slice | bytes 131072 | tf_op jit(solution)/shard_map/slice | solution.py:42
  113.1 1.7 fusion.304
  116.3 3.8 %slice.696 = bf16[16,2,4,256]{3,0,2,1:T(8,128)(2,1)} slice(bf16[16,2,4,512]{3,0,2,1:T(8,128)(2,1)} %get-tuple-element.59), slice={[0:16:1], [0:2:1], [0:4:1], [0:512:2]} | slice | bytes 131072 | tf_op jit(solution)/shard_map/slice | solution.py:42
  121.5 2.9 slice.707
  125.2 2.4 slice.718
  129.0 2.3 slice.729
  132.8 2.3 slice.740
  136.6 2.3 slice.751
  140.4 2.3 slice.762
  143.6 2.4 slice.773
  147.0 2.9 slice.683
  150.9 2.4 slice.689
  154.3 2.9 slice.694
  157.3 1.7 pad_maximum_fusion.21
  158.9 3.4 slice.700
  162.3 1.7 pad_maximum_fusion.22
  164.0 3.8 %slice.705 = bf16[16,2,4,256]{3,0,2,1:T(8,128)(2,1)} slice(bf16[16,2,4,512]{3,0,2,1:T(8,128)(2,1)} %pad_maximum_fusion.22), slice={[0:16:1], [0:2:1], [0:4:1], [0:512:2]} | slice | bytes 131072 | tf_op jit(solution)/shard_map/slice | solution.py:42
  169.4 3.2 slice.711
  172.5 1.7 pad_maximum_fusion.24
  174.2 3.8 %slice.716 = bf16[16,2,4,256]{3,0,2,1:T(8,128)(2,1)} slice(bf16[16,2,4,512]{3,0,2,1:T(8,128)(2,1)} %pad_maximum_fusion.24), slice={[0:16:1], [0:2:1], [0:4:1], [0:512:2]} | slice | bytes 131072 | tf_op jit(solution)/shard_map/slice | solution.py:42
  179.6 3.2 slice.722
  184.4 3.8 %slice.727 = bf16[16,2,4,256]{3,0,2,1:T(8,128)(2,1)} slice(bf16[16,2,4,512]{3,0,2,1:T(8,128)(2,1)} %pad_maximum_fusion.26), slice={[0:16:1], [0:2:1], [0:4:1], [0:512:2]} | slice | bytes 131072 | tf_op jit(solution)/shard_map/slice | solution.py:42
  188.2 1.7 pad_maximum_fusion.27
  189.9 3.8 %slice.733 = bf16[16,2,4,256]{3,0,2,1:T(8,128)(2,1)} slice(bf16[16,2,4,512]{3,0,2,1:T(8,128)(2,1)} %pad_maximum_fusion.27), slice={[0:16:1], [0:2:1], [0:4:1], [0:512:2]} | slice | bytes 131072 | tf_op jit(solution)/shard_map/slice | solution.py:42
  195.3 3.8 %slice.738 = bf16[16,2,4,256]{3,0,2,1:T(8,128)(2,1)} slice(bf16[16,2,4,512]{3,0,2,1:T(8,128)(2,1)} %pad_maximum_fusion.28), slice={[0:16:1], [0:2:1], [0:4:1], [0:512:2]} | slice | bytes 131072 | tf_op jit(solution)/shard_map/slice | solution.py:42
  200.7 3.8 %slice.744 = bf16[16,2,4,256]{3,0,2,1:T(8,128)(2,1)} slice(bf16[16,2,4,512]{3,0,2,1:T(8,128)(2,1)} %pad_maximum_fusion.29), slice={[0:16:1], [0:2:1], [0:4:1], [0:512:2]} | slice | bytes 131072 | tf_op jit(solution)/shard_map/slice | solution.py:42
  206.2 3.8 %slice.749 = bf16[16,2,4,256]{3,0,2,1:T(8,128)(2,1)} slice(bf16[16,2,4,512]{3,0,2,1:T(8,128)(2,1)} %pad_maximum_fusion.30), slice={[0:16:1], [0:2:1], [0:4:1], [0:512:2]} | slice | bytes 131072 | tf_op jit(solution)/shard_map/slice | solution.py:42
  211.6 3.8 %slice.755 = bf16[16,2,4,256]{3,0,2,1:T(8,128)(2,1)} slice(bf16[16,2,4,512]{3,0,2,1:T(8,128)(2,1)} %pad_maximum_fusion.31), slice={[0:16:1], [0:2:1], [0:4:1], [0:512:2]} | slice | bytes 131072 | tf_op jit(solution)/shard_map/slice | solution.py:42
  215.4 1.7 pad_maximum_fusion.32
  217.0 3.8 %slice.760 = bf16[16,2,4,256]{3,0,2,1:T(8,128)(2,1)} slice(bf16[16,2,4,512]{3,0,2,1:T(8,128)(2,1)} %pad_maximum_fusion.32), slice={[0:16:1], [0:2:1], [0:4:1], [0:512:2]} | slice | bytes 131072 | tf_op jit(solution)/shard_map/slice | solution.py:42
  222.4 4.0 %slice.766 = bf16[16,2,4,256]{3,0,2,1:T(8,128)(2,1)} slice(bf16[16,2,4,512]{3,0,2,1:T(8,128)(2,1)} %pad_maximum_fusion.33), slice={[0:16:1], [0:2:1], [0:4:1], [0:512:2]} | slice | bytes 131072 | tf_op jit(solution)/shard_map/slice | solution.py:42
  228.1 3.8 %slice.771 = bf16[16,2,4,256]{3,0,2,1:T(8,128)(2,1)} slice(bf16[16,2,4,512]{3,0,2,1:T(8,128)(2,1)} %pad_maximum_fusion.34), slice={[0:16:1], [0:2:1], [0:4:1], [0:512:2]} | slice | bytes 131072 | tf_op jit(solution)/shard_map/slice | solution.py:42
  233.5 3.2 slice.777
  286.2 1.7 convolution_add_fusion.18
  288.0 1.9 fusion.18
  289.8 2.0 fusion.17
  292.7 36.2 %psum.15 = f32[27,32,16]{1,2,0:T(8,128)S(1)} all-reduce(f32[27,32,16]{1,2,0:T(8,128)S(1)} %fusion.16), channel_id=1, replica_groups=mesh['groups'=2,'gz'=4,'sec'=2,'ch'=2] {'gz','sec'}, use_global_device_ids=true, to_apply=%region_2.3 | all-reduce | flops 13824 | bytes 110592 | tf_op jit(solution)/shard_map/psum | solution.py:98
  331.3 8.0 %reduce-scatter.2.cloned.1.call-done = f32[32,2,4,256]{3,0,2,1:T(8,128)} async-done(((f32[64,2,4,256]{3,0,2,1:T(8,128)}), f32[32,2,4,256]{3,0,2,1:T(8,128)}) %reduce-scatter.2.cloned.1.call-update) | async-done | bytes 262160 | tf_op jit(solution)/shard_map/reduce_scatter | solution.py:96
  (255 shorter events, 134.2 us)
Async XLA Ops:
  7.2 79.4 %copy-start = (bf16[27,32,32]{2,1,0:T(8,128)(2,1)S(1)}, bf16[27,32,32]{2,1,0:T(8,128)(2,1)}, u32[]{:S(2)}) copy-start(bf16[27,32,32]{2,1,0:T(8,128)(2,1)} %param.9) | copy-start | bytes 165892
  7.2 14.1 %all-gather.2.cloned.1.call-start = ((), (), s32[]{:S(2)}) async-start(), calls=%async_computation.1 | async-start | bytes 1572864 | tf_op jit(solution)/shard_map/all_gather | solution.py:56
  9.4 320.2 %all-reduce.4.cloned.1.call-start = ((), (), s32[]{:S(2)}) async-start(), calls=%async_computation.3 | async-start | bytes 442368 | tf_op jit(solution)/shard_map/psum | solution.py:98
  21.3 6.1 %copy-start.1 = (bf16[32,4,8,512]{3,0,2,1:T(8,128)(2,1)S(1)}, bf16[32,4,8,512]{3,0,2,1:T(8,128)(2,1)}, u32[]{:S(2)}) copy-start(bf16[32,4,8,512]{3,0,2,1:T(8,128)(2,1)} %all-gather.2.cloned.1.call-done) | copy-start | bytes 3145732
  22.7 24.7 %collective-permute-start = (bf16[32,2,8,512]{3,0,2,1:T(8,128)(2,1)S(1)}, bf16[32,2,8,512]{3,0,2,1:T(8,128)(2,1)S(1)}, u32[]{:S(2)}, u32[]{:S(2)}) collective-permute-start(bf16[32,2,8,512]{3,0,2,1:T(8,128)(2,1)S(1)} %get-tuple-element.50), channel_id=1, source_target_pairs={{0,2},{2,4},{4,6},{6,8},{8,10},{10,12},{12,14},{14,0},{1,3},{3,5},... | collective-permute-start | bytes 1572872 | tf_op jit(solution)/shard_map/ppermute | solution.py:15
  24.5 25.1 %collective-permute-start.1 = (bf16[32,2,8,512]{3,0,2,1:T(8,128)(2,1)S(1)}, bf16[32,2,8,512]{3,0,2,1:T(8,128)(2,1)S(1)}, u32[]{:S(2)}, u32[]{:S(2)}) collective-permute-start(bf16[32,2,8,512]{3,0,2,1:T(8,128)(2,1)S(1)} %get-tuple-element.51), channel_id=1, source_target_pairs={{2,0},{4,2},{6,4},{8,6},{10,8},{12,10},{14,12},{0,14},{3,1},{5,3},... | collective-permute-start | bytes 1572872 | tf_op jit(solution)/shard_map/ppermute | solution.py:18
  59.1 1.0 copy-start.3
  60.1 1.0 copy-start.30
  72.8 1.0 copy-start.5
  74.7 1.0 copy-start.4
  83.5 1.1 copy-start.31
  99.1 7.7 %collective-permute-start.2 = (bf16[16,1,8,512]{3,0,2,1:T(8,128)(2,1)S(1)}, bf16[16,1,8,512]{3,0,2,1:T(8,128)(2,1)S(1)}, u32[]{:S(2)}, u32[]{:S(2)}) collective-permute-start(bf16[16,1,8,512]{3,0,2,1:T(8,128)(2,1)S(1)} %slice.824), channel_id=1, source_target_pairs={{14,0},{0,2},{2,4},{4,6},{6,8},{8,10},{10,12},{12,14},{15,1},{1,3}... | collective-permute-start | bytes 393224 | tf_op jit(solution)/shard_map/ppermute | solution.py:26
  100.3 8.1 %copy-start.33 = (f32[27,32,16]{1,2,0:T(8,128)}, f32[27,32,16]{1,2,0:T(8,128)S(1)}, u32[]{:S(2)}) copy-start(f32[27,32,16]{1,2,0:T(8,128)S(1)} %fusion.19) | copy-start | bytes 165892
  107.7 0.8 copy-start.2
  127.6 22.3 %copy-start.41 = (bf16[16,2,4,1]{3,0,2,1:T(8,128)(2,1)S(1)}, bf16[16,2,4,1]{3,0,2,1:T(8,128)(2,1)}, u32[]{:S(2)}) copy-start(bf16[16,2,4,1]{3,0,2,1:T(8,128)(2,1)} %get-tuple-element.95) | copy-start | bytes 772
  135.9 31.8 %copy-start.40 = (bf16[16,2,4,1]{3,0,2,1:T(8,128)(2,1)S(1)}, bf16[16,2,4,1]{3,0,2,1:T(8,128)(2,1)}, u32[]{:S(2)}) copy-start(bf16[16,2,4,1]{3,0,2,1:T(8,128)(2,1)} %get-tuple-element.87) | copy-start | bytes 772
  142.7 40.0 %copy-start.39 = (bf16[16,2,4,1]{3,0,2,1:T(8,128)(2,1)S(1)}, bf16[16,2,4,1]{3,0,2,1:T(8,128)(2,1)}, u32[]{:S(2)}) copy-start(bf16[16,2,4,1]{3,0,2,1:T(8,128)(2,1)} %get-tuple-element.80) | copy-start | bytes 772
  143.5 44.7 %copy-start.37 = (bf16[16,2,4,1]{3,0,2,1:T(8,128)(2,1)S(1)}, bf16[16,2,4,1]{3,0,2,1:T(8,128)(2,1)}, u32[]{:S(2)}) copy-start(bf16[16,2,4,1]{3,0,2,1:T(8,128)(2,1)} %get-tuple-element.79) | copy-start | bytes 772
  145.9 47.7 %copy-start.38 = (bf16[16,2,4,1]{3,0,2,1:T(8,128)(2,1)S(1)}, bf16[16,2,4,1]{3,0,2,1:T(8,128)(2,1)}, u32[]{:S(2)}) copy-start(bf16[16,2,4,1]{3,0,2,1:T(8,128)(2,1)} %get-tuple-element.76) | copy-start | bytes 772
  149.9 49.1 %copy-start.36 = (bf16[16,2,4,1]{3,0,2,1:T(8,128)(2,1)S(1)}, bf16[16,2,4,1]{3,0,2,1:T(8,128)(2,1)}, u32[]{:S(2)}) copy-start(bf16[16,2,4,1]{3,0,2,1:T(8,128)(2,1)} %get-tuple-element.75) | copy-start | bytes 772
  157.3 52.7 %copy-start.35 = (bf16[16,2,4,1]{3,0,2,1:T(8,128)(2,1)S(1)}, bf16[16,2,4,1]{3,0,2,1:T(8,128)(2,1)}, u32[]{:S(2)}) copy-start(bf16[16,2,4,1]{3,0,2,1:T(8,128)(2,1)} %get-tuple-element.71) | copy-start | bytes 772
  188.2 50.1 %copy-start.8 = (bf16[16,2,4,256]{3,0,2,1:T(8,128)(2,1)S(1)}, bf16[16,2,4,256]{3,0,2,1:T(8,128)(2,1)}, u32[]{:S(2)}) copy-start(bf16[16,2,4,256]{3,0,2,1:T(8,128)(2,1)} %slice.685) | copy-start | bytes 196612
  200.7 40.8 %copy-start.7 = (bf16[16,2,4,256]{3,0,2,1:T(8,128)(2,1)S(1)}, bf16[16,2,4,256]{3,0,2,1:T(8,128)(2,1)}, u32[]{:S(2)}) copy-start(bf16[16,2,4,256]{3,0,2,1:T(8,128)(2,1)} %slice.696) | copy-start | bytes 196612
  211.6 33.2 %copy-start.6 = (bf16[16,2,4,256]{3,0,2,1:T(8,128)(2,1)S(1)}, bf16[16,2,4,256]{3,0,2,1:T(8,128)(2,1)}, u32[]{:S(2)}) copy-start(bf16[16,2,4,256]{3,0,2,1:T(8,128)(2,1)} %slice.707) | copy-start | bytes 196612
  236.6 9.7 %copy-start.18 = (bf16[16,2,4,256]{3,0,2,1:T(8,128)(2,1)S(1)}, bf16[16,2,4,256]{3,0,2,1:T(8,128)(2,1)}, u32[]{:S(2)}) copy-start(bf16[16,2,4,256]{3,0,2,1:T(8,128)(2,1)} %slice.716) | copy-start | bytes 196612
  236.6 12.1 %copy-start.20 = (bf16[16,2,4,256]{3,0,2,1:T(8,128)(2,1)S(1)}, bf16[16,2,4,256]{3,0,2,1:T(8,128)(2,1)}, u32[]{:S(2)}) copy-start(bf16[16,2,4,256]{3,0,2,1:T(8,128)(2,1)} %slice.727) | copy-start | bytes 196612
  239.1 11.2 %copy-start.9 = (bf16[16,2,4,256]{3,0,2,1:T(8,128)(2,1)S(1)}, bf16[16,2,4,256]{3,0,2,1:T(8,128)(2,1)}, u32[]{:S(2)}) copy-start(bf16[16,2,4,256]{3,0,2,1:T(8,128)(2,1)} %slice.733) | copy-start | bytes 196612
  239.9 11.2 %copy-start.22 = (bf16[16,2,4,256]{3,0,2,1:T(8,128)(2,1)S(1)}, bf16[16,2,4,256]{3,0,2,1:T(8,128)(2,1)}, u32[]{:S(2)}) copy-start(bf16[16,2,4,256]{3,0,2,1:T(8,128)(2,1)} %slice.738) | copy-start | bytes 196612
  242.3 10.3 %copy-start.11 = (bf16[16,2,4,256]{3,0,2,1:T(8,128)(2,1)S(1)}, bf16[16,2,4,256]{3,0,2,1:T(8,128)(2,1)}, u32[]{:S(2)}) copy-start(bf16[16,2,4,256]{3,0,2,1:T(8,128)(2,1)} %slice.744) | copy-start | bytes 196612
  243.1 10.3 %copy-start.24 = (bf16[16,2,4,256]{3,0,2,1:T(8,128)(2,1)S(1)}, bf16[16,2,4,256]{3,0,2,1:T(8,128)(2,1)}, u32[]{:S(2)}) copy-start(bf16[16,2,4,256]{3,0,2,1:T(8,128)(2,1)} %slice.749) | copy-start | bytes 196612
  245.6 9.4 %copy-start.13 = (bf16[16,2,4,256]{3,0,2,1:T(8,128)(2,1)S(1)}, bf16[16,2,4,256]{3,0,2,1:T(8,128)(2,1)}, u32[]{:S(2)}) copy-start(bf16[16,2,4,256]{3,0,2,1:T(8,128)(2,1)} %slice.755) | copy-start | bytes 196612
  246.3 9.4 %copy-start.26 = (bf16[16,2,4,256]{3,0,2,1:T(8,128)(2,1)S(1)}, bf16[16,2,4,256]{3,0,2,1:T(8,128)(2,1)}, u32[]{:S(2)}) copy-start(bf16[16,2,4,256]{3,0,2,1:T(8,128)(2,1)} %slice.760) | copy-start | bytes 196612
  247.9 9.4 %copy-start.15 = (bf16[16,2,4,256]{3,0,2,1:T(8,128)(2,1)S(1)}, bf16[16,2,4,256]{3,0,2,1:T(8,128)(2,1)}, u32[]{:S(2)}) copy-start(bf16[16,2,4,256]{3,0,2,1:T(8,128)(2,1)} %slice.766) | copy-start | bytes 196612
  248.7 9.4 %copy-start.28 = (bf16[16,2,4,256]{3,0,2,1:T(8,128)(2,1)S(1)}, bf16[16,2,4,256]{3,0,2,1:T(8,128)(2,1)}, u32[]{:S(2)}) copy-start(bf16[16,2,4,256]{3,0,2,1:T(8,128)(2,1)} %slice.771) | copy-start | bytes 196612
  260.5 78.7 %reduce-scatter.2.cloned.1.call-start = ((), (), s32[]{:S(2)}) async-start(), calls=%async_computation.2 | async-start | bytes 786432 | tf_op jit(solution)/shard_map/reduce_scatter | solution.py:96
  262.6 4.0 %copy-start.17 = (bf16[16,2,4,256]{3,0,2,1:T(8,128)(2,1)S(1)}, bf16[16,2,4,256]{3,0,2,1:T(8,128)(2,1)}, u32[]{:S(2)}) copy-start(bf16[16,2,4,256]{3,0,2,1:T(8,128)(2,1)} %slice.705) | copy-start | bytes 196612
  265.7 3.9 %copy-start.19 = (bf16[16,2,4,256]{3,0,2,1:T(8,128)(2,1)S(1)}, bf16[16,2,4,256]{3,0,2,1:T(8,128)(2,1)}, u32[]{:S(2)}) copy-start(bf16[16,2,4,256]{3,0,2,1:T(8,128)(2,1)} %slice.716) | copy-start | bytes 196612
  268.6 3.9 %copy-start.21 = (bf16[16,2,4,256]{3,0,2,1:T(8,128)(2,1)S(1)}, bf16[16,2,4,256]{3,0,2,1:T(8,128)(2,1)}, u32[]{:S(2)}) copy-start(bf16[16,2,4,256]{3,0,2,1:T(8,128)(2,1)} %slice.727) | copy-start | bytes 196612
  270.5 3.9 %copy-start.10 = (bf16[16,2,4,256]{3,0,2,1:T(8,128)(2,1)S(1)}, bf16[16,2,4,256]{3,0,2,1:T(8,128)(2,1)}, u32[]{:S(2)}) copy-start(bf16[16,2,4,256]{3,0,2,1:T(8,128)(2,1)} %slice.733) | copy-start | bytes 196612
  271.5 3.9 %copy-start.23 = (bf16[16,2,4,256]{3,0,2,1:T(8,128)(2,1)S(1)}, bf16[16,2,4,256]{3,0,2,1:T(8,128)(2,1)}, u32[]{:S(2)}) copy-start(bf16[16,2,4,256]{3,0,2,1:T(8,128)(2,1)} %slice.738) | copy-start | bytes 196612
  273.5 3.9 %copy-start.12 = (bf16[16,2,4,256]{3,0,2,1:T(8,128)(2,1)S(1)}, bf16[16,2,4,256]{3,0,2,1:T(8,128)(2,1)}, u32[]{:S(2)}) copy-start(bf16[16,2,4,256]{3,0,2,1:T(8,128)(2,1)} %slice.744) | copy-start | bytes 196612
  274.5 3.9 %copy-start.25 = (bf16[16,2,4,256]{3,0,2,1:T(8,128)(2,1)S(1)}, bf16[16,2,4,256]{3,0,2,1:T(8,128)(2,1)}, u32[]{:S(2)}) copy-start(bf16[16,2,4,256]{3,0,2,1:T(8,128)(2,1)} %slice.749) | copy-start | bytes 196612
  276.4 3.9 %copy-start.14 = (bf16[16,2,4,256]{3,0,2,1:T(8,128)(2,1)S(1)}, bf16[16,2,4,256]{3,0,2,1:T(8,128)(2,1)}, u32[]{:S(2)}) copy-start(bf16[16,2,4,256]{3,0,2,1:T(8,128)(2,1)} %slice.755) | copy-start | bytes 196612
  277.4 3.9 %copy-start.27 = (bf16[16,2,4,256]{3,0,2,1:T(8,128)(2,1)S(1)}, bf16[16,2,4,256]{3,0,2,1:T(8,128)(2,1)}, u32[]{:S(2)}) copy-start(bf16[16,2,4,256]{3,0,2,1:T(8,128)(2,1)} %slice.760) | copy-start | bytes 196612
  279.4 3.9 %copy-start.16 = (bf16[16,2,4,256]{3,0,2,1:T(8,128)(2,1)S(1)}, bf16[16,2,4,256]{3,0,2,1:T(8,128)(2,1)}, u32[]{:S(2)}) copy-start(bf16[16,2,4,256]{3,0,2,1:T(8,128)(2,1)} %slice.766) | copy-start | bytes 196612
  280.3 3.9 %copy-start.29 = (bf16[16,2,4,256]{3,0,2,1:T(8,128)(2,1)S(1)}, bf16[16,2,4,256]{3,0,2,1:T(8,128)(2,1)}, u32[]{:S(2)}) copy-start(bf16[16,2,4,256]{3,0,2,1:T(8,128)(2,1)} %slice.771) | copy-start | bytes 196612
  284.2 3.7 %copy-start.34 = (f32[27,32,16]{1,2,0:T(8,128)S(1)}, f32[27,32,16]{1,2,0:T(8,128)}, u32[]{:S(2)}) copy-start(f32[27,32,16]{1,2,0:T(8,128)} %copy-done.33) | copy-start | bytes 165892
  287.9 1.9 copy-start.32
Sparse Core Ops, SparseCore 0:
  9.6 11.7 all-gather.1
  260.7 68.9 all-reduce.3
  332.0 7.2 reduce-scatter.1
where the time goes:
time: 354 us; the launch traced here: 348 us
  local copies, waits for them, and re-layouts  119 us (34%)
  matrix products  87.4 us (25%)
  waiting for transfers between devices  43.9 us (12%)
  other arithmetic  38.6 us (11%)
  blocking collectives  38.3 us (11%)
  between operations  15.1 us (4%)
  starting transfers between devices  5.26 us (1%)
    slice x45, local copies, waits for them, and re-layouts, take_taps(): return jnp.roll(selected, 1 - along_y, axis=3)[:, :, :, ::2]  101 us
    psum x1, blocking collectives, local(): lax.psum((jnp.stack(up_terms), jnp.stack(refine_terms)), ('gz', 'sec'))  36.2 us
    concatenate x18, other arithmetic, take_taps(): return jnp.roll(selected, 1 - along_y, axis=3)[:, :, :, ::2]  27.9 us
    dot_general x27, matrix products, local(): jnp.einsum('fc,fzxy->czxy', weight_block, selected, preferred_element_typ...  26.9 us
    dot_general x27, matrix products, local(): jnp.einsum('ozxy,czxy->oc', shifted, hidden, preferred_element_type=jnp.f...  25.2 us
    dot_general x27, matrix products, local(): jnp.einsum('czxy,fzxy->fc', all_coarse, selected, preferred_element_type=...  23.8 us
    ppermute x1, waiting for transfers between devices, padded(): lax.ppermute(lax.slice_in_dim(block, block.shape[dim] - width, None, axis...  18.3 us
    dot_general x27, matrix products, local(): jnp.einsum('oc,ozxy->czxy', refine_cols[tap_number], shifted, preferred_e...  11.5 us
  transfers between devices with their start and end apart: 6, of which 6 were waited for; matrix products, arithmetic and copies ran while one was open for 11% of the time, Pallas kernels for 0%

commit v1 on v0

v1 whole, which is shorter than its diff:
```python
import jax
import jax.numpy as jnp
from jax import lax
from jax.sharding import PartitionSpec as P

leak_slope = 0.2
SPATIAL = ("NCDHW", "OIDHW", "NCDHW")


def padded(block, sides, width):
    for axis, dim in sides:
        count = lax.axis_size(axis)
        forward = [(i, i + 1) for i in range(count - 1)]
        forward.append((count - 1, 0))
        backward = [(target, source) for source, target in forward]
        low = lax.ppermute(
            lax.slice_in_dim(block, block.shape[dim] - width, None, axis=dim), axis, forward
        )
        high = lax.ppermute(lax.slice_in_dim(block, 0, width, axis=dim), axis, backward)
        block = jnp.concatenate([low, block, high], axis=dim)
    return block


def passed_along(block, axis, distance):
    devices = range(lax.axis_size(axis))
    route = [((i - distance) % len(devices), i) for i in devices]
    return lax.ppermute(block, axis, route)


def wrap_y(block, low, high):
    size = block.shape[3]
    parts = [block[:, :, :, size - low :], block, block[:, :, :, :high]]
    return jnp.concatenate([p for p in parts if p.shape[3]], axis=3)


def conv(lhs, rhs, strides, dilation):
    return lax.conv_general_dilated(
        lhs,
        rhs,
        window_strides=strides,
        padding="VALID",
        rhs_dilation=dilation,
        dimension_numbers=SPATIAL,
        preferred_element_type=jnp.float32,
    )


def filter_grad(lhs, cotangent, strides, dilation):
    return lax.conv_general_dilated(
        lhs,
        cotangent,
        window_strides=strides,
        padding="VALID",
        rhs_dilation=dilation,
        dimension_numbers=("CNDHW", "IODHW", "CNDHW"),
        preferred_element_type=jnp.float32,
    )


def local(coarse, saved_pre, out_grad, up_weight, refine_weight):
    part_ch = saved_pre.shape[0]
    planes_z = saved_pre.shape[1]
    planes_x = saved_pre.shape[2]
    cells_y = saved_pre.shape[3]
    channel_start = lax.axis_index("ch") * part_ch
    pre_act = saved_pre.astype(jnp.float32)
    slopes = jnp.where(pre_act > 0, 1.0, leak_slope).astype(jnp.float32)
    hidden = (pre_act * slopes).astype(jnp.bfloat16)

    rimmed_local = padded(out_grad, ((("gz", "sec"), 1),), 2)
    every_channel = lax.all_gather(rimmed_local, "ch", axis=0, tiled=True)
    rimmed = jnp.pad(every_channel, ((0, 0), (0, 0), (2, 2), (0, 0)))
    rimmed = wrap_y(rimmed, 2, 2)[None]

    refine_cols = lax.dynamic_slice_in_dim(refine_weight, channel_start, part_ch, 2)
    refine_k = refine_cols.reshape(3, 3, 3, refine_cols.shape[1], part_ch)[::-1, ::-1, ::-1]
    refine_k = jnp.transpose(refine_k, (4, 3, 0, 1, 2))

    grad_hidden = conv(rimmed, refine_k, (1, 1, 1), (2, 2, 2))[0]
    refine_grad_k = filter_grad(rimmed, hidden[None], (2, 2, 2), (1, 1, 1))
    refine_terms = jnp.transpose(refine_grad_k[:, :, ::-1, ::-1, ::-1], (2, 3, 4, 1, 0))
    refine_terms = refine_terms.reshape(27, refine_cols.shape[1], part_ch)

    grad_pre = (grad_hidden * slopes).astype(jnp.bfloat16)
    below_z = passed_along(grad_pre[:, planes_z - 1 :, :, :], ("gz", "sec"), 1)
    raised_z = jnp.concatenate([below_z, grad_pre], axis=1)
    extended = jnp.pad(raised_z, ((0, 0), (0, 0), (1, 0), (0, 0)))
    extended = wrap_y(extended, 1, 0)[None]

    all_coarse = lax.all_gather(coarse, "ch", axis=0, tiled=True)
    up_rows = lax.dynamic_slice_in_dim(up_weight, channel_start, part_ch, 1)
    up_k = jnp.transpose(up_rows.reshape(3, 3, 3, part_ch, up_rows.shape[2]), (4, 3, 0, 1, 2))

    running = conv(extended, up_k, (2, 2, 2), (1, 1, 1))
    up_grad_k = filter_grad(extended, all_coarse[None], (1, 1, 1), (2, 2, 2))
    up_terms = jnp.transpose(up_grad_k, (2, 3, 4, 1, 0)).reshape(27, part_ch, up_rows.shape[2])

    coarse_summed = lax.psum_scatter(running[0], "ch", scatter_dimension=0, tiled=True)
    grad_coarse = coarse_summed.astype(jnp.bfloat16)
    flat = jnp.concatenate([up_terms.reshape(-1), refine_terms.reshape(-1)])
    flat = lax.psum(flat, ("gz", "sec"))
    up_summed = flat[: up_terms.size].reshape(up_terms.shape)
    refine_summed = flat[up_terms.size :].reshape(refine_terms.shape)
    fine_total = planes_z * lax.axis_size("gz") * lax.axis_size("sec") * planes_x * cells_y
    coarse_total = fine_total // 8
    grad_up = up_summed * float(coarse_total) ** (-0.5)
    grad_refine = refine_summed * float(fine_total) ** (-0.5)
    return (grad_coarse, grad_up, grad_refine)


def solution(mesh):
    placed = (
        P("ch", ("groups", "gz", "sec"), None, None),
        P("ch", ("groups", "gz", "sec"), None, None),
        P("ch", ("groups", "gz", "sec"), None, None),
        P(),
        P(),
    )
    return jax.shard_map(
        local,
        mesh=mesh,
        in_specs=placed,
        out_specs=(
            P("ch", ("groups", "gz", "sec"), None, None),
            P("groups", "ch", None),
            P("groups", None, "ch"),
        ),
        check_vma=False,
    )
```

time: 354 us -> 504 us (1.42)
  matrix products: 87.4 us -> 234 us
  waiting for transfers between devices: 43.9 us -> 77.7 us
  blocking collectives: 38.3 us -> 6.82 us
  other arithmetic: 38.6 us -> 11.8 us
  local copies, waits for them, and re-layouts: 119 us -> 142 us
    conv_general_dilated x0 -> x3, matrix products: none -> 207 us  [the longest x1 173 us: filter_grad(): lax.conv_general_dilated(lhs, cotangent, window_strides=strides, padding=...]
    slice x55 -> x2, local copies, waits for them, and re-layouts: 113 us -> 0.44 us  [wrap_y(): parts = [block[:, :, :, size - low:], block, block[:, :, :, :high]]]
    dot_general x108 -> x0, matrix products: 87.4 us -> none  [the longest x27 26.9 us: local(): jnp.einsum('fc,fzxy->czxy', weight_block, selected, preferred_element_typ...]
    broadcast_in_dim x0 -> x6, local copies, waits for them, and re-layouts: none -> 83.7 us  [the longest x2 46.2 us: local(): rimmed = wrap_y(rimmed, 2, 2)[None]]
    psum x1, waiting for transfers between devices: 0.06 us -> 64 us  [local(): flat = lax.psum(flat, ('gz', 'sec'))]
    conv_general_dilated x0 -> x9, local copies, waits for them, and re-layouts: none -> 45.2 us  [conv(): lax.conv_general_dilated(lhs, rhs, window_strides=strides, padding='VALID...]
    psum x1 -> x0, blocking collectives: 36.2 us -> none  [local(): lax.psum((jnp.stack(up_terms), jnp.stack(refine_terms)), ('gz', 'sec'))]
    concatenate x26 -> x1, other arithmetic: 34.8 us -> 0.68 us  [local(): flat = jnp.concatenate([up_terms.reshape(-1), refine_terms.reshape(-1)])]
  transfers between devices with their start and end apart: 6 -> 5, of which waited for: 6 -> 4; matrix products, arithmetic and copies ran while one was open for 11% -> 48% of each run, Pallas kernels for 0% -> 0%
where the time goes in v1:
time: 504 us; the launch traced here: 495 us
  matrix products  234 us (46%)
  local copies, waits for them, and re-layouts  142 us (28%)
  waiting for transfers between devices  77.7 us (15%)
  between operations  15.1 us (3%)
  other arithmetic  11.8 us (2%)
  starting transfers between devices  7.84 us (2%)
  blocking collectives  6.82 us (1%)
    conv_general_dilated x1, matrix products, filter_grad(): lax.conv_general_dilated(lhs, cotangent, window_strides=strides, padding=...  173 us
    psum x1, waiting for transfers between devices, local(): flat = lax.psum(flat, ('gz', 'sec'))  64 us
    broadcast_in_dim x2, local copies, waits for them, and re-layouts, local(): rimmed = wrap_y(rimmed, 2, 2)[None]  46.2 us
    conv_general_dilated x9, local copies, waits for them, and re-layouts, conv(): lax.conv_general_dilated(lhs, rhs, window_strides=strides, padding='VALID...  45.2 us
    conv_general_dilated x2, matrix products, conv(): lax.conv_general_dilated(lhs, rhs, window_strides=strides, padding='VALID...  34.2 us
    transpose x1, matrix products, local(): jnp.transpose(up_grad_k, (2, 3, 4, 1, 0))  26.9 us
    broadcast_in_dim x2, local copies, waits for them, and re-layouts, local(): extended = wrap_y(extended, 1, 0)[None]  21.2 us
    broadcast_in_dim x1, local copies, waits for them, and re-layouts, local(): refine_grad_k = filter_grad(rimmed, hidden[None], (2, 2, 2), (1, 1, 1))  14.3 us
  transfers between devices with their start and end apart: 5, of which 4 were waited for; matrix products, arithmetic and copies ran while one was open for 48% of the time, Pallas kernels for 0%

profile of v1, /device:TPU:0, one launch (start us, length us, event | category | flops | bytes accessed | tf_op | source)
XLA Modules:
  0.0 495.2 jit_solution(4544733990261625754)
XLA Ops:
  7.2 1.2 fusion.36
  8.4 6.0 %collective-permute-start.1 = (bf16[16,2,8,512]{3,2,1,0:T(8,128)(2,1)S(1)}, bf16[16,2,8,512]{3,2,1,0:T(8,128)(2,1)S(1)}, u32[]{:S(2)}, u32[]{:S(2)}) collective-permute-start(bf16[16,2,8,512]{3,2,1,0:T(8,128)(2,1)S(1)} %get-tuple-element.21), channel_id=1, source_target_pairs={{2,0},{4,2},{6,4},{8,6},{10,8},{12,10},{14,12},{0,14},{3,1},{5,3},... | collective-permute-start | bytes 786440 | tf_op jit(solution)/shard_map/ppermute | solution.py:19
  14.4 5.6 %collective-permute-done.1 = bf16[16,2,8,512]{3,2,1,0:T(8,128)(2,1)S(1)} collective-permute-done((bf16[16,2,8,512]{3,2,1,0:T(8,128)(2,1)S(1)}, bf16[16,2,8,512]{3,2,1,0:T(8,128)(2,1)S(1)}, u32[]{:S(2)}, u32[]{:S(2)}) %collective-permute-start.1) | collective-permute-done | bytes 262176 | tf_op jit(solution)/shard_map/ppermute | solution.py:19
  20.0 4.9 collective-permute-done
  24.9 2.1 pad_maximum_fusion.1
  27.1 1.2 dynamic-slice
  29.0 0.9 copy.63
  29.9 2.0 all_gather.7
  31.9 2.0 copy.65
  33.9 0.7 constant_dynamic-slice_fusion
  34.7 3.3 all-gather.2.cloned.1.call-done
  38.0 2.5 copy.53
  40.5 0.3 pad_slice_fusion.1
  40.8 0.4 pad.8
  41.2 4.0 fusion.23
  45.2 2.3 pad.10
  47.5 10.9 %reshape.30 = bf16[32,8,12,1,8,65]{5,4,1,2,0,3:T(8,128)(2,1)} reshape(bf16[32,8,12,1,520]{4,1,2,0,3:T(8,128)(2,1)} %pad.10) | data formatting | bytes 6389760 | tf_op jit(solution)/shard_map/conv_general_dilated | solution.py:37
  58.4 17.4 %copy.55 = bf16[32,8,12,1,8,65]{0,4,5,2,1,3:T(8,128)(2,1)} copy(bf16[32,8,12,1,8,65]{5,4,1,2,0,3:T(8,128)(2,1)} %reshape.30) | data formatting | bytes 6389760 | tf_op jit(solution)/shard_map/conv_general_dilated | solution.py:37
  75.8 1.4 slice.44
  77.2 26.0 %broadcast_select_fusion = f32[4,8,8,65,16]{4,2,3,1,0:T(8,128)} fusion(pred[8,65]{0,1:T(8,128)(4,1)S(1)} %copy-done.8, bf16[3,3,3,32,16]{4,3,2,1,0:T(8,128)(2,1)S(1)} %bitcast.62, bf16[32,8,12,1,7,4]{0,4,5,2,1,3:T(8,128)(2,1)S(1)} %slice.44, bf16[32,8,12,1,8,65]{0,4,5,2,1,3:T(8,128)(2,1)} %copy.55), kind=kOutput, calls=%fused_computation.14 | convolution fusion | flops 470503424 | bytes 4460040 | tf_op jit(solution)/shard_map/conv_general_dilated | solution.py:37
  103.2 5.6 %copy.57 = f32[4,8,8,65,16]{3,2,4,1,0:T(8,128)S(1)} copy(f32[4,8,8,65,16]{4,2,3,1,0:T(8,128)} %broadcast_select_fusion) | data formatting | bytes 2129920 | tf_op jit(solution)/shard_map/conv_general_dilated | solution.py:37
  108.8 1.8 reshape.34
  110.6 1.7 fusion.29
  112.4 0.8 copy-done.2
  113.2 0.7 slice.46
  113.8 1.7 collective-permute-start.2
  115.6 43.9 %copy.66 = bf16[1,32,8,12,516]{1,0,4,3,2:T(2,128)(2,1)} copy(bf16[1,32,8,12,516]{4,2,3,1,0:T(8,128)(2,1)} %get-tuple-element.12) | data formatting | bytes 6340608 | tf_op jit(solution)/shard_map/broadcast_in_dim | solution.py:73
  159.4 14.3 %copy.67 = bf16[1,16,4,8,512]{1,0,4,3,2:T(2,128)(2,1)} copy(bf16[1,16,4,8,512]{4,1,3,2,0:T(8,128)(2,1)S(1)} %get-tuple-element.18) | data formatting | bytes 1048576 | tf_op jit(solution)/shard_map/broadcast_in_dim | solution.py:80
  173.7 172.9 %fusion.38 = f32[16,32,3,3,3]{1,0,4,3,2:T(8,128)S(1)} fusion(bf16[1,32,8,12,516]{1,0,4,3,2:T(2,128)(2,1)} %copy.66, bf16[1,16,4,8,512]{1,0,4,3,2:T(2,128)(2,1)} %copy.67), kind=kOutput, calls=%fused_computation.52 | convolution fusion | flops 452984832 | bytes 3749888 | tf_op jit(solution)/shard_map/conv_general_dilated | solution.py:49
  346.9 0.8 reshape_reshape.7
  347.7 1.0 fusion.26
  348.8 0.5 fusion.28
  349.4 1.5 reshape.37
  350.9 5.3 %copy.60 = bf16[16,5,9,1,8,66]{0,4,5,2,1,3:T(8,128)(2,1)} copy(bf16[16,5,9,1,8,66]{5,4,0,2,1,3:T(8,128)(2,1)S(1)} %reshape.37) | data formatting | bytes 1520640 | tf_op jit(solution)/shard_map/conv_general_dilated | solution.py:37
  356.3 1.0 slice.48
  357.3 8.2 %fusion.19 = f32[2,4,8,33,64]{4,2,3,1,0:T(8,128)S(1)} fusion(bf16[3,3,3,16,64]{4,3,2,1,0:T(8,128)(2,1)} %bitcast.63, bf16[16,5,9,1,7,2]{0,4,5,2,1,3:T(8,128)(2,1)S(1)} %slice.48, bf16[16,5,9,1,8,66]{0,4,5,2,1,3:T(8,128)(2,1)} %copy.60, pred[8,33]{0,1:T(8,128)(4,1)S(1)} %copy-done.9), kind=kOutput, calls=%fused_computation.22 | convolution fusion | flops 119270400 | bytes 1376712 | tf_op jit(solution)/shard_map/conv_general_dilated | solution.py:37
  365.4 0.3 copy.61
  365.8 0.4 copy.62
  366.2 21.1 %copy.64 = bf16[1,16,5,9,513]{1,0,4,3,2:T(2,128)(2,1)} copy(bf16[1,16,5,9,513]{4,1,3,2,0:T(8,128)(2,1)S(1)} %get-tuple-element.16) | data formatting | bytes 1477440 | tf_op jit(solution)/shard_map/broadcast_in_dim | solution.py:88
  387.4 26.9 %fusion.37 = f32[3,3,3,16,64]{4,3,2,1,0:T(8,128)S(1)} fusion(bf16[1,16,5,9,513]{1,0,4,3,2:T(2,128)(2,1)} %copy.64, bf16[1,64,2,4,256]{1,0,4,3,2:T(2,128)(2,1)S(1)} %copy-done.4), kind=kOutput, calls=%fused_computation.51 | convolution fusion | flops 113246208 | bytes 1111456 | tf_op jit(solution)/shard_map/transpose | solution.py:96
  414.4 0.7 pad_maximum_fusion.3
  415.1 4.8 all-reduce.7
  420.0 0.7 dynamic-slice_convert_fusion
  420.7 64.0 %all-reduce.6.cloned.1.call-done = f32[41472]{0:T(1024)} async-done(((f32[41472]{0:T(1024)}), f32[41472]{0:T(1024)}) %all-reduce.6.cloned.1.call-update) | async-done | bytes 165904 | tf_op jit(solution)/shard_map/psum | solution.py:101
  484.6 0.9 slice_multiply_fusion
  485.5 0.8 mul.32
  486.3 0.8 slice_multiply_fusion.1
  487.3 0.9 copy.69
  (33 shorter events, 1.0 us)
Async XLA Ops:
  7.2 26.7 %copy-start = (bf16[27,32,64]{2,1,0:T(8,128)(2,1)S(1)}, bf16[27,32,64]{2,1,0:T(8,128)(2,1)}, u32[]{:S(2)}) copy-start(bf16[27,32,64]{2,1,0:T(8,128)(2,1)} %param.8) | copy-start | bytes 331780
  7.2 27.4 %copy-start.7 = (bf16[27,32,32]{2,1,0:T(8,128)(2,1)S(1)}, bf16[27,32,32]{2,1,0:T(8,128)(2,1)}, u32[]{:S(2)}) copy-start(bf16[27,32,32]{2,1,0:T(8,128)(2,1)} %param.9) | copy-start | bytes 165892
  7.2 30.8 %all-gather.2.cloned.1.call-start = ((), (), s32[]{:S(2)}) async-start(), calls=%async_computation | async-start | bytes 3145728 | tf_op jit(solution)/shard_map/all_gather | solution.py:71
  8.4 11.6 %collective-permute-start.1 = (bf16[16,2,8,512]{3,2,1,0:T(8,128)(2,1)S(1)}, bf16[16,2,8,512]{3,2,1,0:T(8,128)(2,1)S(1)}, u32[]{:S(2)}, u32[]{:S(2)}) collective-permute-start(bf16[16,2,8,512]{3,2,1,0:T(8,128)(2,1)S(1)} %get-tuple-element.21), channel_id=1, source_target_pairs={{2,0},{4,2},{6,4},{8,6},{10,8},{12,10},{14,12},{0,14},{3,1},{5,3},... | collective-permute-start | bytes 786440 | tf_op jit(solution)/shard_map/ppermute | solution.py:19
  14.4 10.5 %collective-permute-start = (bf16[16,2,8,512]{3,2,1,0:T(8,128)(2,1)S(1)}, bf16[16,2,8,512]{3,2,1,0:T(8,128)(2,1)S(1)}, u32[]{:S(2)}, u32[]{:S(2)}) collective-permute-start(bf16[16,2,8,512]{3,2,1,0:T(8,128)(2,1)S(1)} %get-tuple-element.20), channel_id=1, source_target_pairs={{0,2},{2,4},{4,6},{6,8},{8,10},{10,12},{12,14},{14,0},{1,3},{3,5},... | collective-permute-start | bytes 786440 | tf_op jit(solution)/shard_map/ppermute | solution.py:16
  27.1 457.6 %all-reduce.6.cloned.1.call-start = ((), (), s32[]{:S(2)}) async-start(), calls=%async_computation.1 | async-start | bytes 335872 | tf_op jit(solution)/shard_map/psum | solution.py:101
  58.4 18.8 %copy-start.8 = (pred[8,65]{0,1:T(8,128)(4,1)S(1)}, pred[8,65]{0,1:T(8,128)(4,1)}, u32[]{:S(2)}) copy-start(pred[8,65]{0,1:T(8,128)(4,1)} %constant.38) | copy-start | bytes 1564
  103.2 7.4 %copy-start.5 = (bf16[16,4,8,512]{3,2,1,0:T(8,128)(2,1)S(1)}, bf16[16,4,8,512]{3,2,1,0:T(8,128)(2,1)}, u32[]{:S(2)}) copy-start(bf16[16,4,8,512]{3,2,1,0:T(8,128)(2,1)} %param.6) | copy-start | bytes 1572868
  112.3 0.8 copy-start.2
  113.8 233.9 %collective-permute-start.2 = (bf16[16,1,8,512]{3,0,2,1:T(8,128)(2,1)}, bf16[16,1,8,512]{3,0,2,1:T(8,128)(2,1)}, u32[]{:S(2)}, u32[]{:S(2)}) collective-permute-start(bf16[16,1,8,512]{3,0,2,1:T(8,128)(2,1)} %slice.46), channel_id=1, source_target_pairs={{14,0},{0,2},{2,4},{4,6},{6,8},{8,10},{10,12},{12,14},{15,1},{1,3}... | collective-permute-start | bytes 393224 | tf_op jit(solution)/shard_map/ppermute | solution.py:27
  173.7 174.0 %copy-start.3 = (bf16[16,4,8,512]{3,0,2,1:T(8,128)(2,1)S(1)}, bf16[16,4,8,512]{3,0,2,1:T(8,128)(2,1)}, u32[]{:S(2)}) copy-start(bf16[16,4,8,512]{3,0,2,1:T(8,128)(2,1)} %copy-done.2) | copy-start | bytes 1572868
  349.3 7.9 %copy-start.9 = (pred[8,33]{0,1:T(8,128)(4,1)S(1)}, pred[8,33]{0,1:T(8,128)(4,1)}, u32[]{:S(2)}) copy-start(pred[8,33]{0,1:T(8,128)(4,1)} %constant.37) | copy-start | bytes 796
  366.2 21.1 %copy-start.4 = (bf16[1,64,2,4,256]{1,0,4,3,2:T(2,128)(2,1)S(1)}, bf16[1,64,2,4,256]{1,0,4,3,2:T(2,128)(2,1)}, u32[]{:S(2)}) copy-start(bf16[1,64,2,4,256]{1,0,4,3,2:T(2,128)(2,1)} %copy.65) | copy-start | bytes 786436
  387.4 27.1 %copy-start.6 = (f32[13824]{0:T(1024)S(1)}, f32[13824]{0:T(1024)}, u32[]{:S(2)}) copy-start(f32[13824]{0:T(1024)} %reshape_reshape.7) | copy-start | bytes 165892
  387.4 100.8 %copy-start.1 = (bf16[27,32,64]{2,1,0:T(8,128)(2,1)S(1)}, bf16[27,32,64]{2,1,0:T(8,128)(2,1)}, u32[]{:S(2)}) copy-start(bf16[27,32,64]{2,1,0:T(8,128)(2,1)} %param.8) | copy-start | bytes 331780
Sparse Core Ops, SparseCore 0:
  27.2 10.7 all-gather.1
  415.3 69.3 all-reduce.5

commit v2 on v1

v2 whole, which is shorter than its diff:
```python
import functools

import jax
import jax.numpy as jnp
from jax import lax
from jax.experimental import pallas as pl
from jax.experimental.pallas import tpu as pltpu
from jax.sharding import PartitionSpec as P

leak_slope = 0.2


def padded(block, sides, width):
    for axis, dim in sides:
        count = lax.axis_size(axis)
        forward = [(i, i + 1) for i in range(count - 1)]
        forward.append((count - 1, 0))
        backward = [(target, source) for source, target in forward]
        low = lax.ppermute(
            lax.slice_in_dim(block, block.shape[dim] - width, None, axis=dim), axis, forward
        )
        high = lax.ppermute(lax.slice_in_dim(block, 0, width, axis=dim), axis, backward)
        block = jnp.concatenate([low, block, high], axis=dim)
    return block


def passed_along(block, axis, distance):
    devices = range(lax.axis_size(axis))
    route = [((i - distance) % len(devices), i) for i in devices]
    return lax.ppermute(block, axis, route)


def vmem_specs(count):
    return [pl.BlockSpec(memory_space=pltpu.VMEM)] * count


def fine_kernel(g_ref, sp_ref, w_ref, gp_ref, r_ref):
    planes_z, planes_x, part_ch, cells_y = sp_ref.shape
    wide = g_ref.shape[4]
    r_ref[...] = jnp.zeros(r_ref.shape, r_ref.dtype)

    def body(step, carry):
        z = step // planes_x
        x = step % planes_x
        pre_act = sp_ref[z, x].astype(jnp.float32)
        slopes = jnp.where(pre_act > 0, 1.0, leak_slope).astype(jnp.float32)
        hidden = (pre_act * slopes).astype(jnp.bfloat16).astype(jnp.float32)
        rolled = jnp.concatenate(
            [pltpu.roll(hidden, 2, 1), hidden, pltpu.roll(hidden, cells_y - 2, 1)], axis=0
        ).astype(jnp.bfloat16)
        total = jnp.zeros((3 * part_ch, cells_y), jnp.float32)
        for dz in range(3):
            block = g_ref[z % 2, z // 2 + 2 - dz, x % 2, pl.ds(x // 2, 3)]
            block = block.reshape(3 * wide, cells_y)
            total = total + jnp.dot(w_ref[dz], block, preferred_element_type=jnp.float32)
            r_ref[dz] += lax.dot_general(
                block, rolled, (((1,), (1,)), ((), ())), preferred_element_type=jnp.float32
            )
        grad_hidden = (
            pltpu.roll(total[:part_ch], cells_y - 2, 1)
            + total[part_ch : 2 * part_ch]
            + pltpu.roll(total[2 * part_ch :], 2, 1)
        )
        gp_ref[z, x] = (grad_hidden * slopes).astype(gp_ref.dtype)
        return carry

    lax.fori_loop(0, planes_z * planes_x, body, 0)


def coarse_kernel(gp_ref, below_ref, c_ref, u_ref, gc_ref, gu_ref, y_ref):
    planes_z = gp_ref.shape[0]
    cells_y = gp_ref.shape[2]
    rows_x = y_ref.shape[1] - 1
    part_ch = y_ref.shape[3]
    half_y = y_ref.shape[4]
    coarse_z, coarse_x = c_ref.shape[0], c_ref.shape[1]
    at_y = lax.broadcasted_iota(jnp.int32, (cells_y, 3 * half_y), 0)
    col = lax.broadcasted_iota(jnp.int32, (cells_y, 3 * half_y), 1)
    target = 2 * (col % half_y) + col // half_y - 1
    target = jnp.where(target < 0, target + cells_y, target)
    pick = (at_y == target).astype(jnp.bfloat16)
    y_ref[:, 0] = jnp.zeros(y_ref[:, 0].shape, y_ref.dtype)
    for zg in range(planes_z + 1):
        source = below_ref[0] if zg == 0 else gp_ref[zg - 1]
        picked = jnp.dot(source, pick, preferred_element_type=jnp.float32).astype(y_ref.dtype)
        for dy in range(3):
            part = picked[:, dy * half_y : (dy + 1) * half_y]
            y_ref[zg, 1:, dy] = part.reshape(rows_x, part_ch, half_y)
    gu_ref[...] = jnp.zeros(gu_ref.shape, gu_ref.dtype)

    def body(step, carry):
        iz = step // coarse_x
        ix = step % coarse_x
        crow = c_ref[iz, ix]
        total = jnp.zeros(gc_ref.shape[2:], jnp.float32)
        for dz in range(3):
            block = y_ref[2 * iz + dz, pl.ds(2 * ix, 3)]
            block = block.reshape(9 * part_ch, half_y)
            total = total + jnp.dot(u_ref[dz], block, preferred_element_type=jnp.float32)
            gu_ref[dz] += lax.dot_general(
                block, crow, (((1,), (1,)), ((), ())), preferred_element_type=jnp.float32
            )
        gc_ref[iz, ix] = total
        return carry

    lax.fori_loop(0, coarse_z * coarse_x, body, 0)


def local(coarse, saved_pre, out_grad, up_weight, refine_weight):
    part_ch = saved_pre.shape[0]
    planes_z = saved_pre.shape[1]
    planes_x = saved_pre.shape[2]
    cells_y = saved_pre.shape[3]
    all_ch = part_ch * lax.axis_size("ch")
    channel_start = lax.axis_index("ch") * part_ch

    rimmed_local = padded(out_grad, ((("gz", "sec"), 1),), 2)
    every_channel = lax.all_gather(rimmed_local, "ch", axis=0, tiled=True)
    rimmed = jnp.pad(every_channel, ((0, 0), (0, 0), (2, 2), (0, 0)))
    halo_z, halo_x = rimmed.shape[1], rimmed.shape[2]
    rimmed = rimmed.reshape(all_ch, halo_z // 2, 2, halo_x // 2, 2, cells_y)
    rimmed = jnp.transpose(rimmed, (2, 1, 4, 3, 0, 5))
    pre_rows = jnp.transpose(saved_pre, (1, 2, 0, 3))

    refine_cols = lax.dynamic_slice_in_dim(refine_weight, channel_start, part_ch, 2)
    refine_w = refine_cols.reshape(3, 3, 3, all_ch, part_ch)[:, ::-1]
    refine_w = jnp.transpose(refine_w, (0, 2, 4, 1, 3)).reshape(3, 3 * part_ch, 3 * all_ch)

    grad_pre, refine_acc = pl.pallas_call(
        fine_kernel,
        out_shape=(
            jax.ShapeDtypeStruct((planes_z, planes_x, part_ch, cells_y), jnp.bfloat16),
            jax.ShapeDtypeStruct((3, 3 * all_ch, 3 * part_ch), jnp.float32),
        ),
        in_specs=vmem_specs(3),
        out_specs=tuple(vmem_specs(2)),
    )(rimmed, pre_rows, refine_w)
    refine_terms = refine_acc.reshape(3, 3, all_ch, 3, part_ch)[:, ::-1]
    refine_terms = jnp.transpose(refine_terms, (0, 1, 3, 2, 4)).reshape(27, all_ch, part_ch)

    grad_rows = grad_pre.reshape(planes_z, planes_x * part_ch, cells_y)
    below_z = passed_along(grad_rows[planes_z - 1 :], ("gz", "sec"), 1)

    all_coarse = lax.all_gather(coarse, "ch", axis=0, tiled=True)
    coarse_in = all_coarse.shape[0]
    coarse_z, coarse_x, cells_yc = coarse.shape[1], coarse.shape[2], coarse.shape[3]
    coarse_rows = jnp.transpose(all_coarse, (1, 2, 0, 3))
    up_rows = lax.dynamic_slice_in_dim(up_weight, channel_start, part_ch, 1)
    up_w = jnp.transpose(up_rows.reshape(3, 9, part_ch, coarse_in), (0, 3, 1, 2))
    up_w = up_w.reshape(3, coarse_in, 9 * part_ch)

    coarse_acc, up_acc = pl.pallas_call(
        coarse_kernel,
        out_shape=(
            jax.ShapeDtypeStruct((coarse_z, coarse_x, coarse_in, cells_yc), jnp.float32),
            jax.ShapeDtypeStruct((3, 9 * part_ch, coarse_in), jnp.float32),
        ),
        in_specs=vmem_specs(4),
        out_specs=tuple(vmem_specs(2)),
        scratch_shapes=[
            pltpu.VMEM((planes_z + 1, planes_x + 1, 3, part_ch, cells_yc), jnp.bfloat16)
        ],
    )(grad_rows, below_z, coarse_rows, up_w)
    up_terms = up_acc.reshape(27, part_ch, coarse_in)
    running = jnp.transpose(coarse_acc, (2, 0, 1, 3))

    coarse_summed = lax.psum_scatter(running, "ch", scatter_dimension=0, tiled=True)
    grad_coarse = coarse_summed.astype(jnp.bfloat16)
    flat = jnp.concatenate([up_terms.reshape(-1), refine_terms.reshape(-1)])
    flat = lax.psum(flat, ("gz", "sec"))
    up_summed = flat[: up_terms.size].reshape(up_terms.shape)
    refine_summed = flat[up_terms.size :].reshape(refine_terms.shape)
    fine_total = planes_z * lax.axis_size("gz") * lax.axis_size("sec") * planes_x * cells_y
    coarse_total = fine_total // 8
    grad_up = up_summed * float(coarse_total) ** (-0.5)
    grad_refine = refine_summed * float(fine_total) ** (-0.5)
    return (grad_coarse, grad_up, grad_refine)


def solution(mesh):
    placed = (
        P("ch", ("groups", "gz", "sec"), None, None),
        P("ch", ("groups", "gz", "sec"), None, None),
        P("ch", ("groups", "gz", "sec"), None, None),
        P(),
        P(),
    )
    return jax.shard_map(
        local,
        mesh=mesh,
        in_specs=placed,
        out_specs=(
            P("ch", ("groups", "gz", "sec"), None, None),
            P("groups", "ch", None),
            P("groups", None, "ch"),
        ),
        check_vma=False,
    )
```

time: 504 us -> 160 us (0.32); the launches traced: 495 us -> 160 us
  matrix products: 234 us -> 0 us
  local copies, waits for them, and re-layouts: 142 us -> 16 us
  Pallas kernels: 0 us -> 20.3 us
  waiting for transfers between devices: 77.7 us -> 95.1 us
  other arithmetic: 11.8 us -> 4.46 us
    conv_general_dilated x3 -> x0, matrix products: 207 us -> none  [the longest x1 173 us: filter_grad(): lax.conv_general_dilated(lhs, cotangent, window_strides=strides, padding=...]
    broadcast_in_dim x6 -> x0, local copies, waits for them, and re-layouts: 83.7 us -> none  [the longest x2 46.2 us: local(): rimmed = wrap_y(rimmed, 2, 2)[None]]
    conv_general_dilated x9 -> x0, local copies, waits for them, and re-layouts: 45.2 us -> none  [conv(): lax.conv_general_dilated(lhs, rhs, window_strides=strides, padding='VALID...]
    transpose x1 -> x0, matrix products: 26.9 us -> none  [local(): jnp.transpose(up_grad_k, (2, 3, 4, 1, 0))]
    pallas_call x0 -> x2, Pallas kernels: none -> 20.3 us  [the longest x1 15.5 us: local(): pl.pallas_call(fine_kernel, out_shape=(jax.ShapeDtypeStruct((planes_z, pl...]
    reduce_scatter x0 -> x1, waiting for transfers between devices: none -> 6.5 us  [local(): lax.psum_scatter(running, 'ch', scatter_dimension=0, tiled=True)]
    broadcast_in_dim x3 -> x0, other arithmetic: 6.23 us -> none  [the longest x1 4.02 us: local(): rimmed = wrap_y(rimmed, 2, 2)[None]]
    all_gather x1, waiting for transfers between devices: 3.28 us -> 8.61 us  [local(): every_channel = lax.all_gather(rimmed_local, 'ch', axis=0, tiled=True)]
  transfers between devices with their start and end apart: 5 -> 6, of which waited for: 4 -> 6; matrix products, arithmetic and copies ran while one was open for 48% -> 6% of each run, Pallas kernels for 0% -> 0%
where the time goes in v2:
time: 160 us
  waiting for transfers between devices  95.1 us (59%)
  Pallas kernels  20.3 us (13%)
  local copies, waits for them, and re-layouts  16 us (10%)
  between operations  13.9 us (9%)
  starting transfers between devices  7.93 us (5%)
  other arithmetic  4.46 us (3%)
  blocking collectives  2.11 us (1%)
    psum x1, waiting for transfers between devices, local(): flat = lax.psum(flat, ('gz', 'sec'))  67.3 us
    pallas_call x1, Pallas kernels, local(): pl.pallas_call(fine_kernel, out_shape=(jax.ShapeDtypeStruct((planes_z, pl...  15.5 us
    all_gather x1, waiting for transfers between devices, local(): every_channel = lax.all_gather(rimmed_local, 'ch', axis=0, tiled=True)  8.61 us
    reduce_scatter x1, waiting for transfers between devices, local(): lax.psum_scatter(running, 'ch', scatter_dimension=0, tiled=True)  6.5 us
    ppermute x1, starting transfers between devices, padded(): lax.ppermute(lax.slice_in_dim(block, 0, width, axis=dim), axis, backward)  6.03 us
    ppermute x1, waiting for transfers between devices, padded(): lax.ppermute(lax.slice_in_dim(block, 0, width, axis=dim), axis, backward)  5.56 us
    unnamed x16, local copies, waits for them, and re-layouts  4.98 us
    ppermute x1, waiting for transfers between devices, padded(): lax.ppermute(lax.slice_in_dim(block, block.shape[dim] - width, None, axis...  4.9 us
  transfers between devices with their start and end apart: 6, of which 6 were waited for; matrix products, arithmetic and copies ran while one was open for 6% of the time, Pallas kernels for 0%

profile of v2, /device:TPU:0, one launch (start us, length us, event | category | flops | bytes accessed | tf_op | source)
XLA Modules:
  0.0 159.8 jit_solution(2906405717842538877)
XLA Ops:
  7.2 0.0 copy-start
  7.2 0.0 copy-start.1
  7.2 0.0 copy-start.2
  7.2 0.0 all-gather.2.cloned.1.call-start
  7.2 1.4 copy.11
  8.7 0.0 copy-start.3
  8.7 6.0 %collective-permute-start.1 = (bf16[16,2,8,512]{3,0,2,1:T(8,128)(2,1)S(1)}, bf16[16,2,8,512]{3,0,2,1:T(8,128)(2,1)S(1)}, u32[]{:S(2)}, u32[]{:S(2)}) collective-permute-start(bf16[16,2,8,512]{3,0,2,1:T(8,128)(2,1)S(1)} %get-tuple-element.18), channel_id=1, source_target_pairs={{2,0},{4,2},{6,4},{8,6},{10,8},{12,10},{14,12},{0,14},{3,1},{5,3},... | collective-permute-start | bytes 786440 | tf_op jit(solution)/shard_map/ppermute | solution.py:22
  14.7 0.0 collective-permute-start
  14.7 5.6 %collective-permute-done.1 = bf16[16,2,8,512]{3,0,2,1:T(8,128)(2,1)S(1)} collective-permute-done((bf16[16,2,8,512]{3,0,2,1:T(8,128)(2,1)S(1)}, bf16[16,2,8,512]{3,0,2,1:T(8,128)(2,1)S(1)}, u32[]{:S(2)}, u32[]{:S(2)}) %collective-permute-start.1) | collective-permute-done | bytes 262176 | tf_op jit(solution)/shard_map/ppermute | solution.py:22
  20.3 4.9 %collective-permute-done = bf16[16,2,8,512]{3,0,2,1:T(8,128)(2,1)S(1)} collective-permute-done((bf16[16,2,8,512]{3,0,2,1:T(8,128)(2,1)S(1)}, bf16[16,2,8,512]{3,0,2,1:T(8,128)(2,1)S(1)}, u32[]{:S(2)}, u32[]{:S(2)}) %collective-permute-start) | collective-permute-done | bytes 262176 | tf_op jit(solution)/shard_map/ppermute | solution.py:19
  25.2 1.1 pad_maximum_fusion
  26.3 0.0 all-gather.2.cloned.1.call-update
  26.3 0.0 all-reduce.3.cloned.1.call-start
  26.4 1.1 copy.28
  27.5 0.1 constant_dynamic-slice_fusion.1
  27.6 0.1 copy.24
  27.8 0.1 copy.17
  27.8 0.7 reshape.44.w_ref
  28.6 8.6 %all-gather.2.cloned.1.call-done = bf16[32,8,8,512]{3,0,2,1:T(8,128)(2,1)} async-done(((bf16[16,8,8,512]{3,0,2,1:T(8,128)(2,1)}), bf16[32,8,8,512]{3,0,2,1:T(8,128)(2,1)}) %all-gather.2.cloned.1.call-update) | async-done | bytes 2097168 | tf_op jit(solution)/shard_map/all_gather | solution.py:118
  37.2 2.0 %pad.4 = bf16[32,8,12,512]{3,0,2,1:T(8,128)(2,1)S(1)} pad(bf16[32,8,8,512]{3,0,2,1:T(8,128)(2,1)} %all-gather.2.cloned.1.call-done, bf16[]{:T(256)} %constant.2.clone.1), padding=0_0x0_0x2_2x0_0 | pad | bytes 5242882 | tf_op jit(solution)/shard_map/jit(_pad)/pad | solution.py:119
  39.3 2.1 %copy.27 = bf16[32,4,2,6,2,512]{5,0,3,4,1,2:T(8,128)(2,1)} copy(bf16[32,4,2,6,2,512]{5,0,4,3,2,1:T(8,128)(2,1)S(1)} %bitcast.25) | data formatting | bytes 6291456 | tf_op jit(solution)/shard_map/reshape | solution.py:121
  41.3 15.5 %shard_map.76 = (bf16[4,8,16,512]{3,2,1,0:T(8,128)(2,1)}, f32[3,96,48]{2,1,0:T(8,128)}) custom-call(bf16[2,4,2,6,32,512]{5,4,3,2,1,0:T(8,128)(2,1)} %bitcast.24, bf16[4,8,16,512]{3,2,1,0:T(8,128)(2,1)} %bitcast.26, bf16[3,48,96]{2,1,0:T(8,128)(2,1)} %reshape.44.w_ref), custom_call_target="tpu_custom_call" | custom-call | tf_op jit(solution)/shard_map/pallas_call | solution.py:129
  56.8 0.9 slice.28
  57.7 1.8 %collective-permute-start.2 = (bf16[1,128,512]{2,1,0:T(8,128)(2,1)S(1)}, bf16[1,128,512]{2,1,0:T(8,128)(2,1)S(1)}, u32[]{:S(2)}, u32[]{:S(2)}) collective-permute-start(bf16[1,128,512]{2,1,0:T(8,128)(2,1)S(1)} %bitcast.33), channel_id=1, source_target_pairs={{14,0},{0,2},{2,4},{4,6},{6,8},{8,10},{10,12},{12,14},{15,1},{1,3}... | collective-permute-start | bytes 393224 | tf_op jit(solution)/shard_map/ppermute | solution.py:30
  59.5 0.8 copy.19.u_ref
  60.3 2.1 %all_gather.7 = bf16[64,2,4,256]{3,0,2,1:T(8,128)(2,1)} all-gather(bf16[32,2,4,256]{3,0,2,1:T(8,128)(2,1)S(1)} %copy.18), channel_id=1, replica_groups=mesh['groups'=2,'gz'=4,'sec'=2,'ch'=2] {'ch'}, dimensions={0}, use_global_device_ids=true | all-gather | bytes 393216 | tf_op jit(solution)/shard_map/all_gather | solution.py:144
  62.4 1.0 copy.20
  63.4 0.2 reshape.48
  63.6 0.7 rev.7
  64.3 0.2 copy.21
  64.5 0.2 reshape_reshape.7
  64.7 1.5 collective-permute-done.2.below_ref
  66.2 0.7 copy-done.4
  66.9 4.8 %shard_map.77 = (f32[2,4,64,256]{3,2,1,0:T(8,128)}, f32[3,144,64]{2,1,0:T(8,128)}) custom-call(bf16[4,128,512]{2,1,0:T(8,128)(2,1)} %bitcast.29, bf16[1,128,512]{2,1,0:T(8,128)(2,1)} %copy-done.4, bf16[2,4,64,256]{3,2,1,0:T(8,128)(2,1)} %bitcast.28, bf16[3,64,144]{2,1,0:T(8,128)(2,1)} %copy.19.u_ref), custom_call_target="tpu_custom_call" | custom-call | tf_op jit(solution)/shard_map/pallas_call | solution.py:152
  71.7 1.0 reshape_reshape.6
  72.7 0.7 pad_maximum_fusion.1
  73.4 0.0 all-reduce.3.cloned.1.call-update
  73.4 0.0 reduce-scatter.2.cloned.1.call-start
  73.5 0.7 reduce-scatter.2.cloned.1.call-update
  74.2 67.3 %all-reduce.3.cloned.1.call-done = f32[41472]{0:T(1024)} async-done(((f32[41472]{0:T(1024)}), f32[41472]{0:T(1024)}) %all-reduce.3.cloned.1.call-update) | async-done | bytes 165904 | tf_op jit(solution)/shard_map/psum | solution.py:170
  141.4 0.9 slice_multiply_fusion
  142.3 0.8 mul.24
  143.1 0.8 slice_multiply_fusion.1
  144.0 0.2 mul.27
  144.1 0.9 copy.23
  145.0 6.5 %reduce-scatter.2.cloned.1.call-done = f32[32,2,4,256]{3,0,2,1:T(8,128)} async-done(((f32[64,2,4,256]{3,0,2,1:T(8,128)}), f32[32,2,4,256]{3,0,2,1:T(8,128)}) %reduce-scatter.2.cloned.1.call-update) | async-done | bytes 262160 | tf_op jit(solution)/shard_map/reduce_scatter | solution.py:167
  151.5 1.0 convert_element_type.5
  152.5 0.8 copy.22
  (9 shorter events, 0.1 us)
Async XLA Ops:
  7.2 52.3 %copy-start = (bf16[27,32,64]{2,1,0:T(8,128)(2,1)S(1)}, bf16[27,32,64]{2,1,0:T(8,128)(2,1)}, u32[]{:S(2)}) copy-start(bf16[27,32,64]{2,1,0:T(8,128)(2,1)} %param.8) | copy-start | bytes 331780
  7.2 19.2 %copy-start.1 = (bf16[16,4,8,512]{3,2,1,0:T(8,128)(2,1)S(1)}, bf16[16,4,8,512]{3,2,1,0:T(8,128)(2,1)}, u32[]{:S(2)}) copy-start(bf16[16,4,8,512]{3,2,1,0:T(8,128)(2,1)} %param.6) | copy-start | bytes 1572868
  7.2 20.3 %copy-start.2 = (bf16[27,32,32]{2,1,0:T(8,128)(2,1)S(1)}, bf16[27,32,32]{2,1,0:T(8,128)(2,1)}, u32[]{:S(2)}) copy-start(bf16[27,32,32]{2,1,0:T(8,128)(2,1)} %param.9) | copy-start | bytes 165892
  7.2 30.0 %all-gather.2.cloned.1.call-start = ((), (), s32[]{:S(2)}) async-start(), calls=%async_computation.1 | async-start | bytes 3145728 | tf_op jit(solution)/shard_map/all_gather | solution.py:118
  8.7 19.9 %copy-start.3 = (bf16[32,2,4,256]{3,2,1,0:T(4,128)(2,1)S(1)}, bf16[32,2,4,256]{3,2,1,0:T(4,128)(2,1)}, u32[]{:S(2)}) copy-start(bf16[32,2,4,256]{3,2,1,0:T(4,128)(2,1)} %param.5) | copy-start | bytes 393220
  8.7 11.6 %collective-permute-start.1 = (bf16[16,2,8,512]{3,0,2,1:T(8,128)(2,1)S(1)}, bf16[16,2,8,512]{3,0,2,1:T(8,128)(2,1)S(1)}, u32[]{:S(2)}, u32[]{:S(2)}) collective-permute-start(bf16[16,2,8,512]{3,0,2,1:T(8,128)(2,1)S(1)} %get-tuple-element.18), channel_id=1, source_target_pairs={{2,0},{4,2},{6,4},{8,6},{10,8},{12,10},{14,12},{0,14},{3,1},{5,3},... | collective-permute-start | bytes 786440 | tf_op jit(solution)/shard_map/ppermute | solution.py:22
  14.7 10.5 %collective-permute-start = (bf16[16,2,8,512]{3,0,2,1:T(8,128)(2,1)S(1)}, bf16[16,2,8,512]{3,0,2,1:T(8,128)(2,1)S(1)}, u32[]{:S(2)}, u32[]{:S(2)}) collective-permute-start(bf16[16,2,8,512]{3,0,2,1:T(8,128)(2,1)S(1)} %get-tuple-element.17), channel_id=1, source_target_pairs={{0,2},{2,4},{4,6},{6,8},{8,10},{10,12},{12,14},{14,0},{1,3},{3,5},... | collective-permute-start | bytes 786440 | tf_op jit(solution)/shard_map/ppermute | solution.py:19
  26.3 115.1 %all-reduce.3.cloned.1.call-start = ((), (), s32[]{:S(2)}) async-start(), calls=%async_computation.3 | async-start | bytes 335872 | tf_op jit(solution)/shard_map/psum | solution.py:170
  57.7 8.5 %collective-permute-start.2 = (bf16[1,128,512]{2,1,0:T(8,128)(2,1)S(1)}, bf16[1,128,512]{2,1,0:T(8,128)(2,1)S(1)}, u32[]{:S(2)}, u32[]{:S(2)}) collective-permute-start(bf16[1,128,512]{2,1,0:T(8,128)(2,1)S(1)} %bitcast.33), channel_id=1, source_target_pairs={{14,0},{0,2},{2,4},{4,6},{6,8},{8,10},{10,12},{12,14},{15,1},{1,3}... | collective-permute-start | bytes 393224 | tf_op jit(solution)/shard_map/ppermute | solution.py:30
  66.2 0.7 copy-start.4
  73.4 78.1 %reduce-scatter.2.cloned.1.call-start = ((), (), s32[]{:S(2)}) async-start(), calls=%async_computation.2 | async-start | bytes 786432 | tf_op jit(solution)/shard_map/reduce_scatter | solution.py:167
Sparse Core Ops, SparseCore 0:
  26.4 10.7 all-gather.1
  73.5 67.8 all-reduce.2
  143.8 7.6 reduce-scatter.1

commit v3 on v2

--- a/solution.py
+++ b/solution.py
@@ -28,6 +28,18 @@
     devices = range(lax.axis_size(axis))
     route = [((i - distance) % len(devices), i) for i in devices]
     return lax.ppermute(block, axis, route)
+
+
+def summed_over_slabs(block, axis):
+    count = lax.axis_size(axis)
+    if count & (count - 1):
+        return lax.psum(block, axis)
+    step = 1
+    while step < count:
+        route = [(i, i ^ step) for i in range(count)]
+        block = block + lax.ppermute(block, axis, route)
+        step *= 2
+    return block
 
 
 def vmem_specs(count):
@@ -137,6 +149,7 @@
     )(rimmed, pre_rows, refine_w)
     refine_terms = refine_acc.reshape(3, 3, all_ch, 3, part_ch)[:, ::-1]
     refine_terms = jnp.transpose(refine_terms, (0, 1, 3, 2, 4)).reshape(27, all_ch, part_ch)
+    refine_summed = summed_over_slabs(refine_terms, ("gz", "sec"))
 
     grad_rows = grad_pre.reshape(planes_z, planes_x * part_ch, cells_y)
     below_z = passed_along(grad_rows[planes_z - 1 :], ("gz", "sec"), 1)
@@ -166,10 +179,7 @@
 
     coarse_summed = lax.psum_scatter(running, "ch", scatter_dimension=0, tiled=True)
     grad_coarse = coarse_summed.astype(jnp.bfloat16)
-    flat = jnp.concatenate([up_terms.reshape(-1), refine_terms.reshape(-1)])
-    flat = lax.psum(flat, ("gz", "sec"))
-    up_summed = flat[: up_terms.size].reshape(up_terms.shape)
-    refine_summed = flat[up_terms.size :].reshape(refine_terms.shape)
+    up_summed = summed_over_slabs(up_terms, ("gz", "sec"))
     fine_total = planes_z * lax.axis_size("gz") * lax.axis_size("sec") * planes_x * cells_y
     coarse_total = fine_total // 8
     grad_up = up_summed * float(coarse_total) ** (-0.5)

time: 160 us -> 127 us (0.79)
  waiting for transfers between devices: 95.1 us -> 57.6 us
  starting transfers between devices: 7.93 us -> 15.1 us
  local copies, waits for them, and re-layouts: 16 us -> 12.8 us
    psum x1 -> x0, waiting for transfers between devices: 67.3 us -> none  [local(): flat = lax.psum(flat, ('gz', 'sec'))]
    ppermute x0 -> x6, waiting for transfers between devices: none -> 34.7 us  [summed_over_slabs(): block = block + lax.ppermute(block, axis, route)]
    ppermute x0 -> x6, starting transfers between devices: none -> 7.22 us  [summed_over_slabs(): block = block + lax.ppermute(block, axis, route)]
    reduce_scatter x1, waiting for transfers between devices: 6.5 us -> 0.01 us  [local(): lax.psum_scatter(running, 'ch', scatter_dimension=0, tiled=True)]
    ppermute x1, waiting for transfers between devices: 1.53 us -> 3.83 us  [passed_along(): return lax.ppermute(block, axis, route)]
    unnamed x16 -> x15, local copies, waits for them, and re-layouts: 4.98 us -> 4.1 us
  transfers between devices with their start and end apart: 6 -> 11, of which waited for: 6 -> 9; matrix products, arithmetic and copies ran while one was open for 6% -> 6% of each run, Pallas kernels for 0% -> 0%
where the time goes in v3:
time: 127 us
  waiting for transfers between devices  57.6 us (45%)
  Pallas kernels  20.3 us (16%)
  starting transfers between devices  15.1 us (12%)
  between operations  14.2 us (11%)
  local copies, waits for them, and re-layouts  12.8 us (10%)
  other arithmetic  4.55 us (4%)
  blocking collectives  2.11 us (2%)
    ppermute x6, waiting for transfers between devices, summed_over_slabs(): block = block + lax.ppermute(block, axis, route)  34.7 us
    pallas_call x1, Pallas kernels, local(): pl.pallas_call(fine_kernel, out_shape=(jax.ShapeDtypeStruct((planes_z, pl...  15.5 us
    all_gather x1, waiting for transfers between devices, local(): every_channel = lax.all_gather(rimmed_local, 'ch', axis=0, tiled=True)  8.63 us
    ppermute x6, starting transfers between devices, summed_over_slabs(): block = block + lax.ppermute(block, axis, route)  7.22 us
    ppermute x1, starting transfers between devices, padded(): lax.ppermute(lax.slice_in_dim(block, 0, width, axis=dim), axis, backward)  6.03 us
    ppermute x1, waiting for transfers between devices, padded(): lax.ppermute(lax.slice_in_dim(block, 0, width, axis=dim), axis, backward)  5.56 us
    ppermute x1, waiting for transfers between devices, padded(): lax.ppermute(lax.slice_in_dim(block, block.shape[dim] - width, None, axis...  4.9 us
    pallas_call x1, Pallas kernels, local(): pl.pallas_call(coarse_kernel, out_shape=(jax.ShapeDtypeStruct((coarse_z,...  4.8 us
  transfers between devices with their start and end apart: 11, of which 9 were waited for; matrix products, arithmetic and copies ran while one was open for 6% of the time, Pallas kernels for 0%

profile of v3, /device:TPU:0, one launch (start us, length us, event | category | flops | bytes accessed | tf_op | source)
XLA Modules:
  0.0 126.7 jit_solution(15192403732237275010)
XLA Ops:
  7.2 0.0 copy-start
  7.2 0.0 all-gather.2.cloned.1.call-start
  7.2 1.4 %copy.23 = bf16[16,4,8,512]{3,0,2,1:T(8,128)(2,1)S(1)} copy(bf16[16,4,8,512]{3,2,1,0:T(8,128)(2,1)} %param.7) | data formatting | bytes 1048576 | tf_op args[2]
  8.7 0.0 copy-start.3
  8.7 6.0 %collective-permute-start.1 = (bf16[16,2,8,512]{3,0,2,1:T(8,128)(2,1)S(1)}, bf16[16,2,8,512]{3,0,2,1:T(8,128)(2,1)S(1)}, u32[]{:S(2)}, u32[]{:S(2)}) collective-permute-start(bf16[16,2,8,512]{3,0,2,1:T(8,128)(2,1)S(1)} %get-tuple-element.21), channel_id=1, source_target_pairs={{2,0},{4,2},{6,4},{8,6},{10,8},{12,10},{14,12},{0,14},{3,1},{5,3},... | collective-permute-start | bytes 786440 | tf_op jit(solution)/shard_map/ppermute | solution.py:22
  14.7 0.0 collective-permute-start
  14.7 5.6 %collective-permute-done.1 = bf16[16,2,8,512]{3,0,2,1:T(8,128)(2,1)S(1)} collective-permute-done((bf16[16,2,8,512]{3,0,2,1:T(8,128)(2,1)S(1)}, bf16[16,2,8,512]{3,0,2,1:T(8,128)(2,1)S(1)}, u32[]{:S(2)}, u32[]{:S(2)}) %collective-permute-start.1) | collective-permute-done | bytes 262176 | tf_op jit(solution)/shard_map/ppermute | solution.py:22
  20.3 4.9 %collective-permute-done = bf16[16,2,8,512]{3,0,2,1:T(8,128)(2,1)S(1)} collective-permute-done((bf16[16,2,8,512]{3,0,2,1:T(8,128)(2,1)S(1)}, bf16[16,2,8,512]{3,0,2,1:T(8,128)(2,1)S(1)}, u32[]{:S(2)}, u32[]{:S(2)}) %collective-permute-start) | collective-permute-done | bytes 262176 | tf_op jit(solution)/shard_map/ppermute | solution.py:19
  25.2 1.1 pad_maximum_fusion
  26.3 0.0 all-gather.2.cloned.1.call-update
  26.3 0.0 reduce-scatter.2.cloned.1.call-start
  26.4 1.1 copy.39
  27.5 0.1 constant_dynamic-slice_fusion.1
  27.6 0.2 copy.35
  27.8 0.1 copy.29
  27.8 0.7 reshape.36.w_ref
  28.6 8.6 %all-gather.2.cloned.1.call-done = bf16[32,8,8,512]{3,0,2,1:T(8,128)(2,1)} async-done(((bf16[16,8,8,512]{3,0,2,1:T(8,128)(2,1)}), bf16[32,8,8,512]{3,0,2,1:T(8,128)(2,1)}) %all-gather.2.cloned.1.call-update) | async-done | bytes 2097168 | tf_op jit(solution)/shard_map/all_gather | solution.py:130
  37.2 2.0 %pad.4 = bf16[32,8,12,512]{3,0,2,1:T(8,128)(2,1)S(1)} pad(bf16[32,8,8,512]{3,0,2,1:T(8,128)(2,1)} %all-gather.2.cloned.1.call-done, bf16[]{:T(256)} %constant.2.clone.1), padding=0_0x0_0x2_2x0_0 | pad | bytes 5242882 | tf_op jit(solution)/shard_map/jit(_pad)/pad | solution.py:131
  39.3 2.1 %copy.38 = bf16[32,4,2,6,2,512]{5,0,3,4,1,2:T(8,128)(2,1)} copy(bf16[32,4,2,6,2,512]{5,0,4,3,2,1:T(8,128)(2,1)S(1)} %bitcast.26) | data formatting | bytes 6291456 | tf_op jit(solution)/shard_map/reshape | solution.py:133
  41.4 15.5 %shard_map.76 = (bf16[4,8,16,512]{3,2,1,0:T(8,128)(2,1)}, f32[3,96,48]{2,1,0:T(8,128)}) custom-call(bf16[2,4,2,6,32,512]{5,4,3,2,1,0:T(8,128)(2,1)} %bitcast.25, bf16[4,8,16,512]{3,2,1,0:T(8,128)(2,1)} %bitcast.27, bf16[3,48,96]{2,1,0:T(8,128)(2,1)} %reshape.36.w_ref), custom_call_target="tpu_custom_call" | custom-call | tf_op jit(solution)/shard_map/pallas_call | solution.py:141
  56.9 0.9 slice.14
  57.8 1.8 %collective-permute-start.2 = (bf16[1,128,512]{2,1,0:T(8,128)(2,1)S(1)}, bf16[1,128,512]{2,1,0:T(8,128)(2,1)S(1)}, u32[]{:S(2)}, u32[]{:S(2)}) collective-permute-start(bf16[1,128,512]{2,1,0:T(8,128)(2,1)S(1)} %bitcast.37), channel_id=1, source_target_pairs={{14,0},{0,2},{2,4},{4,6},{6,8},{8,10},{10,12},{12,14},{15,1},{1,3}... | collective-permute-start | bytes 393224 | tf_op jit(solution)/shard_map/ppermute | solution.py:30
  59.6 0.8 copy.31.u_ref
  60.3 2.1 %all_gather.7 = bf16[64,2,4,256]{3,0,2,1:T(8,128)(2,1)} all-gather(bf16[32,2,4,256]{3,0,2,1:T(8,128)(2,1)S(1)} %copy.30), channel_id=1, replica_groups=mesh['groups'=2,'gz'=4,'sec'=2,'ch'=2] {'ch'}, dimensions={0}, use_global_device_ids=true | all-gather | bytes 393216 | tf_op jit(solution)/shard_map/all_gather | solution.py:157
  62.4 3.8 %collective-permute-done.2.below_ref = bf16[1,128,512]{2,1,0:T(8,128)(2,1)S(1)} collective-permute-done((bf16[1,128,512]{2,1,0:T(8,128)(2,1)S(1)}, bf16[1,128,512]{2,1,0:T(8,128)(2,1)S(1)}, u32[]{:S(2)}, u32[]{:S(2)}) %collective-permute-start.2) | collective-permute-done | bytes 131104 | tf_op jit(solution)/shard_map/ppermute | solution.py:30
  66.3 0.7 copy-done.4
  66.9 4.8 %shard_map.77 = (f32[2,4,64,256]{3,2,1,0:T(8,128)}, f32[3,144,64]{2,1,0:T(8,128)}) custom-call(bf16[4,128,512]{2,1,0:T(8,128)(2,1)} %bitcast.31, bf16[1,128,512]{2,1,0:T(8,128)(2,1)} %copy-done.4, bf16[2,4,64,256]{3,2,1,0:T(8,128)(2,1)} %bitcast.29, bf16[3,64,144]{2,1,0:T(8,128)(2,1)} %copy.31.u_ref), custom_call_target="tpu_custom_call" | custom-call | tf_op jit(solution)/shard_map/pallas_call | solution.py:165
  71.7 0.0 reduce-scatter.2.cloned.1.call-update
  71.8 1.0 copy.32
  72.8 0.2 reshape.41
  72.9 0.7 rev.7
  73.7 0.1 collective-permute-start.6
  73.8 2.0 %collective-permute-start.3 = (f32[27,16,64]{2,1,0:T(8,128)}, f32[27,16,64]{2,1,0:T(8,128)S(1)}, u32[]{:S(2)}, u32[]{:S(2)}) collective-permute-start(f32[27,16,64]{2,1,0:T(8,128)} %bitcast.35), channel_id=1, source_target_pairs={{0,2},{2,0},{4,6},{6,4},{8,10},{10,8},{12,14},{14,12},{1,3},{3,1},... | collective-permute-start | bytes 331784 | tf_op jit(solution)/shard_map/ppermute | solution.py:40
  75.8 6.3 %collective-permute-done.6 = f32[27,32,16]{1,2,0:T(8,128)S(1)} collective-permute-done((f32[27,32,16]{1,2,0:T(8,128)S(1)}, f32[27,32,16]{1,2,0:T(8,128)S(1)}, u32[]{:S(2)}, u32[]{:S(2)}) %collective-permute-start.6) | collective-permute-done | bytes 55328 | tf_op jit(solution)/shard_map/ppermute | solution.py:40
  82.1 3.2 %collective-permute-done.3 = f32[27,16,64]{2,1,0:T(8,128)S(1)} collective-permute-done((f32[27,16,64]{2,1,0:T(8,128)}, f32[27,16,64]{2,1,0:T(8,128)S(1)}, u32[]{:S(2)}, u32[]{:S(2)}) %collective-permute-start.3) | collective-permute-done | bytes 110624 | tf_op jit(solution)/shard_map/ppermute | solution.py:40
  85.4 1.0 add.27
  86.3 0.1 collective-permute-start.4
  86.4 2.0 %collective-permute-start.7 = (f32[27,32,16]{1,2,0:T(8,128)S(1)}, f32[27,32,16]{1,2,0:T(8,128)S(1)}, u32[]{:S(2)}, u32[]{:S(2)}) collective-permute-start(f32[27,32,16]{1,2,0:T(8,128)S(1)} %bitcast_add_fusion), channel_id=1, source_target_pairs={{0,4},{2,6},{4,0},{6,2},{8,12},{10,14},{12,8},{14,10},{1,5},{3,7},... | collective-permute-start | bytes 165896 | tf_op jit(solution)/shard_map/ppermute | solution.py:40
  88.4 8.7 %collective-permute-done.7 = f32[27,32,16]{1,2,0:T(8,128)S(1)} collective-permute-done((f32[27,32,16]{1,2,0:T(8,128)S(1)}, f32[27,32,16]{1,2,0:T(8,128)S(1)}, u32[]{:S(2)}, u32[]{:S(2)}) %collective-permute-start.7) | collective-permute-done | bytes 55328 | tf_op jit(solution)/shard_map/ppermute | solution.py:40
  97.2 0.7 collective-permute-start.8
  97.9 0.0 collective-permute-done.4
  97.9 2.3 %collective-permute-start.5 = (f32[27,16,64]{2,1,0:T(8,128)S(1)}, f32[27,16,64]{2,1,0:T(8,128)S(1)}, u32[]{:S(2)}, u32[]{:S(2)}) collective-permute-start(f32[27,16,64]{2,1,0:T(8,128)S(1)} %add.28), channel_id=1, source_target_pairs={{0,8},{2,10},{4,12},{6,14},{8,0},{10,2},{12,4},{14,6},{1,9},{3,11}... | collective-permute-start | bytes 331784 | tf_op jit(solution)/shard_map/ppermute | solution.py:40
  100.2 12.5 %collective-permute-done.8 = f32[27,32,16]{1,2,0:T(8,128)S(1)} collective-permute-done((f32[27,32,16]{1,2,0:T(8,128)S(1)}, f32[27,32,16]{1,2,0:T(8,128)S(1)}, u32[]{:S(2)}, u32[]{:S(2)}) %collective-permute-start.8) | collective-permute-done | bytes 55328 | tf_op jit(solution)/shard_map/ppermute | solution.py:40
  112.8 0.7 add_multiply_fusion
  113.5 3.9 %collective-permute-done.5 = f32[27,16,64]{2,1,0:T(8,128)S(1)} collective-permute-done((f32[27,16,64]{2,1,0:T(8,128)S(1)}, f32[27,16,64]{2,1,0:T(8,128)S(1)}, u32[]{:S(2)}, u32[]{:S(2)}) %collective-permute-start.5) | collective-permute-done | bytes 110624 | tf_op jit(solution)/shard_map/ppermute | solution.py:40
  117.4 0.7 add_multiply_fusion.1
  118.1 1.0 convert_element_type.5
  119.1 0.8 copy.34
  (16 shorter events, 0.2 us)
Async XLA Ops:
  7.2 52.4 %copy-start = (bf16[27,32,64]{2,1,0:T(8,128)(2,1)S(1)}, bf16[27,32,64]{2,1,0:T(8,128)(2,1)}, u32[]{:S(2)}) copy-start(bf16[27,32,64]{2,1,0:T(8,128)(2,1)} %param.8) | copy-start | bytes 331780
  7.2 19.2 %copy-start.1 = (bf16[16,4,8,512]{3,2,1,0:T(8,128)(2,1)S(1)}, bf16[16,4,8,512]{3,2,1,0:T(8,128)(2,1)}, u32[]{:S(2)}) copy-start(bf16[16,4,8,512]{3,2,1,0:T(8,128)(2,1)} %param.6) | copy-start | bytes 1572868
  7.2 20.3 %copy-start.2 = (bf16[27,32,32]{2,1,0:T(8,128)(2,1)S(1)}, bf16[27,32,32]{2,1,0:T(8,128)(2,1)}, u32[]{:S(2)}) copy-start(bf16[27,32,32]{2,1,0:T(8,128)(2,1)} %param.9) | copy-start | bytes 165892
  7.2 30.0 %all-gather.2.cloned.1.call-start = ((), (), s32[]{:S(2)}) async-start(), calls=%async_computation.1 | async-start | bytes 3145728 | tf_op jit(solution)/shard_map/all_gather | solution.py:130
  8.7 19.9 %copy-start.3 = (bf16[32,2,4,256]{3,2,1,0:T(4,128)(2,1)S(1)}, bf16[32,2,4,256]{3,2,1,0:T(4,128)(2,1)}, u32[]{:S(2)}) copy-start(bf16[32,2,4,256]{3,2,1,0:T(4,128)(2,1)} %param.5) | copy-start | bytes 393220
  8.7 11.6 %collective-permute-start.1 = (bf16[16,2,8,512]{3,0,2,1:T(8,128)(2,1)S(1)}, bf16[16,2,8,512]{3,0,2,1:T(8,128)(2,1)S(1)}, u32[]{:S(2)}, u32[]{:S(2)}) collective-permute-start(bf16[16,2,8,512]{3,0,2,1:T(8,128)(2,1)S(1)} %get-tuple-element.21), channel_id=1, source_target_pairs={{2,0},{4,2},{6,4},{8,6},{10,8},{12,10},{14,12},{0,14},{3,1},{5,3},... | collective-permute-start | bytes 786440 | tf_op jit(solution)/shard_map/ppermute | solution.py:22
  14.7 10.5 %collective-permute-start = (bf16[16,2,8,512]{3,0,2,1:T(8,128)(2,1)S(1)}, bf16[16,2,8,512]{3,0,2,1:T(8,128)(2,1)S(1)}, u32[]{:S(2)}, u32[]{:S(2)}) collective-permute-start(bf16[16,2,8,512]{3,0,2,1:T(8,128)(2,1)S(1)} %get-tuple-element.20), channel_id=1, source_target_pairs={{0,2},{2,4},{4,6},{6,8},{8,10},{10,12},{12,14},{14,0},{1,3},{3,5},... | collective-permute-start | bytes 786440 | tf_op jit(solution)/shard_map/ppermute | solution.py:19
  26.3 91.8 %reduce-scatter.2.cloned.1.call-start = ((), (), s32[]{:S(2)}) async-start(), calls=%async_computation.2 | async-start | bytes 786432 | tf_op jit(solution)/shard_map/reduce_scatter | solution.py:180
  57.8 8.5 %collective-permute-start.2 = (bf16[1,128,512]{2,1,0:T(8,128)(2,1)S(1)}, bf16[1,128,512]{2,1,0:T(8,128)(2,1)S(1)}, u32[]{:S(2)}, u32[]{:S(2)}) collective-permute-start(bf16[1,128,512]{2,1,0:T(8,128)(2,1)S(1)} %bitcast.37), channel_id=1, source_target_pairs={{14,0},{0,2},{2,4},{4,6},{6,8},{8,10},{10,12},{12,14},{15,1},{1,3}... | collective-permute-start | bytes 393224 | tf_op jit(solution)/shard_map/ppermute | solution.py:30
  66.3 0.7 copy-start.4
  73.7 8.4 %collective-permute-start.6 = (f32[27,32,16]{1,2,0:T(8,128)S(1)}, f32[27,32,16]{1,2,0:T(8,128)S(1)}, u32[]{:S(2)}, u32[]{:S(2)}) collective-permute-start(f32[27,32,16]{1,2,0:T(8,128)S(1)} %bitcast.30), channel_id=1, source_target_pairs={{0,2},{2,0},{4,6},{6,4},{8,10},{10,8},{12,14},{14,12},{1,3},{3,1},... | collective-permute-start | bytes 165896 | tf_op jit(solution)/shard_map/ppermute | solution.py:40
  73.8 11.6 %collective-permute-start.3 = (f32[27,16,64]{2,1,0:T(8,128)}, f32[27,16,64]{2,1,0:T(8,128)S(1)}, u32[]{:S(2)}, u32[]{:S(2)}) collective-permute-start(f32[27,16,64]{2,1,0:T(8,128)} %bitcast.35), channel_id=1, source_target_pairs={{0,2},{2,0},{4,6},{6,4},{8,10},{10,8},{12,14},{14,12},{1,3},{3,1},... | collective-permute-start | bytes 331784 | tf_op jit(solution)/shard_map/ppermute | solution.py:40
  86.3 11.6 %collective-permute-start.4 = (f32[27,16,64]{2,1,0:T(8,128)S(1)}, f32[27,16,64]{2,1,0:T(8,128)S(1)}, u32[]{:S(2)}, u32[]{:S(2)}) collective-permute-start(f32[27,16,64]{2,1,0:T(8,128)S(1)} %add.27), channel_id=1, source_target_pairs={{0,4},{2,6},{4,0},{6,2},{8,12},{10,14},{12,8},{14,10},{1,5},{3,7},... | collective-permute-start | bytes 331784 | tf_op jit(solution)/shard_map/ppermute | solution.py:40
  86.4 10.7 %collective-permute-start.7 = (f32[27,32,16]{1,2,0:T(8,128)S(1)}, f32[27,32,16]{1,2,0:T(8,128)S(1)}, u32[]{:S(2)}, u32[]{:S(2)}) collective-permute-start(f32[27,32,16]{1,2,0:T(8,128)S(1)} %bitcast_add_fusion), channel_id=1, source_target_pairs={{0,4},{2,6},{4,0},{6,2},{8,12},{10,14},{12,8},{14,10},{1,5},{3,7},... | collective-permute-start | bytes 165896 | tf_op jit(solution)/shard_map/ppermute | solution.py:40
  97.2 15.6 %collective-permute-start.8 = (f32[27,32,16]{1,2,0:T(8,128)S(1)}, f32[27,32,16]{1,2,0:T(8,128)S(1)}, u32[]{:S(2)}, u32[]{:S(2)}) collective-permute-start(f32[27,32,16]{1,2,0:T(8,128)S(1)} %add.31), channel_id=1, source_target_pairs={{0,8},{2,10},{4,12},{6,14},{8,0},{10,2},{12,4},{14,6},{1,9},{3,11}... | collective-permute-start | bytes 165896 | tf_op jit(solution)/shard_map/ppermute | solution.py:40
  97.9 19.5 %collective-permute-start.5 = (f32[27,16,64]{2,1,0:T(8,128)S(1)}, f32[27,16,64]{2,1,0:T(8,128)S(1)}, u32[]{:S(2)}, u32[]{:S(2)}) collective-permute-start(f32[27,16,64]{2,1,0:T(8,128)S(1)} %add.28), channel_id=1, source_target_pairs={{0,8},{2,10},{4,12},{6,14},{8,0},{10,2},{12,4},{14,6},{1,9},{3,11}... | collective-permute-start | bytes 331784 | tf_op jit(solution)/shard_map/ppermute | solution.py:40
Sparse Core Ops, SparseCore 0:
  26.5 10.7 all-gather.1
  71.9 6.3 reduce-scatter.1

commit v4 on v3

--- a/solution.py
+++ b/solution.py
@@ -149,7 +149,6 @@
     )(rimmed, pre_rows, refine_w)
     refine_terms = refine_acc.reshape(3, 3, all_ch, 3, part_ch)[:, ::-1]
     refine_terms = jnp.transpose(refine_terms, (0, 1, 3, 2, 4)).reshape(27, all_ch, part_ch)
-    refine_summed = summed_over_slabs(refine_terms, ("gz", "sec"))
 
     grad_rows = grad_pre.reshape(planes_z, planes_x * part_ch, cells_y)
     below_z = passed_along(grad_rows[planes_z - 1 :], ("gz", "sec"), 1)
@@ -179,7 +178,10 @@
 
     coarse_summed = lax.psum_scatter(running, "ch", scatter_dimension=0, tiled=True)
     grad_coarse = coarse_summed.astype(jnp.bfloat16)
-    up_summed = summed_over_slabs(up_terms, ("gz", "sec"))
+    flat = jnp.concatenate([up_terms.reshape(-1), refine_terms.reshape(-1)])
+    flat = summed_over_slabs(flat, ("gz", "sec"))
+    up_summed = flat[: up_terms.size].reshape(up_terms.shape)
+    refine_summed = flat[up_terms.size :].reshape(refine_terms.shape)
     fine_total = planes_z * lax.axis_size("gz") * lax.axis_size("sec") * planes_x * cells_y
     coarse_total = fine_total // 8
     grad_up = up_summed * float(coarse_total) ** (-0.5)

time: 127 us -> 103 us (0.81)
  waiting for transfers between devices: 57.6 us -> 37.7 us
  starting transfers between devices: 15.1 us -> 10.3 us
  local copies, waits for them, and re-layouts: 12.8 us -> 16 us
  other arithmetic: 4.55 us -> 2.13 us
    ppermute x6 -> x3, waiting for transfers between devices: 34.7 us -> 17 us  [summed_over_slabs(): block = block + lax.ppermute(block, axis, route)]
    ppermute x6 -> x3, starting transfers between devices: 7.22 us -> 2.41 us  [summed_over_slabs(): block = block + lax.ppermute(block, axis, route)]
    ppermute x1, waiting for transfers between devices: 3.83 us -> 1.53 us  [passed_along(): return lax.ppermute(block, axis, route)]
    unnamed x15 -> x17, local copies, waits for them, and re-layouts: 4.1 us -> 4.97 us
  transfers between devices with their start and end apart: 11 -> 8, of which waited for: 9 -> 7; matrix products, arithmetic and copies ran while one was open for 6% -> 7% of each run, Pallas kernels for 0% -> 0%
where the time goes in v4:
time: 103 us
  waiting for transfers between devices  37.7 us (37%)
  Pallas kernels  20.3 us (20%)
  local copies, waits for them, and re-layouts  16 us (16%)
  between operations  14.2 us (14%)
  starting transfers between devices  10.3 us (10%)
  other arithmetic  2.13 us (2%)
  blocking collectives  2.11 us (2%)
    ppermute x3, waiting for transfers between devices, summed_over_slabs(): block = block + lax.ppermute(block, axis, route)  17 us
    pallas_call x1, Pallas kernels, local(): pl.pallas_call(fine_kernel, out_shape=(jax.ShapeDtypeStruct((planes_z, pl...  15.5 us
    all_gather x1, waiting for transfers between devices, local(): every_channel = lax.all_gather(rimmed_local, 'ch', axis=0, tiled=True)  8.63 us
    ppermute x1, starting transfers between devices, padded(): lax.ppermute(lax.slice_in_dim(block, 0, width, axis=dim), axis, backward)  6.03 us
    ppermute x1, waiting for transfers between devices, padded(): lax.ppermute(lax.slice_in_dim(block, 0, width, axis=dim), axis, backward)  5.56 us
    unnamed x17, local copies, waits for them, and re-layouts  4.97 us
    ppermute x1, waiting for transfers between devices, padded(): lax.ppermute(lax.slice_in_dim(block, block.shape[dim] - width, None, axis...  4.9 us
    pallas_call x1, Pallas kernels, local(): pl.pallas_call(coarse_kernel, out_shape=(jax.ShapeDtypeStruct((coarse_z,...  4.8 us
  transfers between devices with their start and end apart: 8, of which 7 were waited for; matrix products, arithmetic and copies ran while one was open for 7% of the time, Pallas kernels for 0%

profile of v4, /device:TPU:0, one launch (start us, length us, event | category | flops | bytes accessed | tf_op | source)
XLA Modules:
  0.0 102.8 jit_solution(7963306142922804853)
XLA Ops:
  7.2 0.0 copy-start
  7.2 0.0 copy-start.1
  7.2 0.0 copy-start.2
  7.2 0.0 all-gather.2.cloned.1.call-start
  7.2 1.4 %copy.11 = bf16[16,4,8,512]{3,0,2,1:T(8,128)(2,1)S(1)} copy(bf16[16,4,8,512]{3,2,1,0:T(8,128)(2,1)} %param.7) | data formatting | bytes 1048576 | tf_op args[2]
  8.7 0.0 copy-start.3
  8.7 6.0 %collective-permute-start.1 = (bf16[16,2,8,512]{3,0,2,1:T(8,128)(2,1)S(1)}, bf16[16,2,8,512]{3,0,2,1:T(8,128)(2,1)S(1)}, u32[]{:S(2)}, u32[]{:S(2)}) collective-permute-start(bf16[16,2,8,512]{3,0,2,1:T(8,128)(2,1)S(1)} %get-tuple-element.18), channel_id=1, source_target_pairs={{2,0},{4,2},{6,4},{8,6},{10,8},{12,10},{14,12},{0,14},{3,1},{5,3},... | collective-permute-start | bytes 786440 | tf_op jit(solution)/shard_map/ppermute | solution.py:22
  14.7 0.0 collective-permute-start
  14.7 5.6 %collective-permute-done.1 = bf16[16,2,8,512]{3,0,2,1:T(8,128)(2,1)S(1)} collective-permute-done((bf16[16,2,8,512]{3,0,2,1:T(8,128)(2,1)S(1)}, bf16[16,2,8,512]{3,0,2,1:T(8,128)(2,1)S(1)}, u32[]{:S(2)}, u32[]{:S(2)}) %collective-permute-start.1) | collective-permute-done | bytes 262176 | tf_op jit(solution)/shard_map/ppermute | solution.py:22
  20.3 4.9 %collective-permute-done = bf16[16,2,8,512]{3,0,2,1:T(8,128)(2,1)S(1)} collective-permute-done((bf16[16,2,8,512]{3,0,2,1:T(8,128)(2,1)S(1)}, bf16[16,2,8,512]{3,0,2,1:T(8,128)(2,1)S(1)}, u32[]{:S(2)}, u32[]{:S(2)}) %collective-permute-start) | collective-permute-done | bytes 262176 | tf_op jit(solution)/shard_map/ppermute | solution.py:19
  25.2 1.1 %pad_maximum_fusion = bf16[16,8,8,512]{3,0,2,1:T(8,128)(2,1)} fusion(bf16[16,2,8,512]{3,0,2,1:T(8,128)(2,1)S(1)} %collective-permute-done.1, bf16[16,4,8,512]{3,0,2,1:T(8,128)(2,1)S(1)} %copy.11, bf16[16,2,8,512]{3,0,2,1:T(8,128)(2,1)S(1)} %collective-permute-done), kind=kLoop, calls=%fused_computation.1 | loop fusion | flops 1048576 | bytes 2097152 | tf_op jit(solution)/shard_map/concatenate | solution.py:23
  26.3 0.0 all-gather.2.cloned.1.call-update
  26.3 0.0 reduce-scatter.2.cloned.1.call-start
  26.4 0.0 copy-done.1
  26.4 1.1 %copy.28 = bf16[16,4,8,512]{3,0,2,1:T(8,128)(2,1)} copy(bf16[16,4,8,512]{3,2,1,0:T(8,128)(2,1)S(1)} %copy-done.1) | data formatting | bytes 1048576 | tf_op args[1]
  27.5 0.1 constant_dynamic-slice_fusion.1
  27.6 0.1 copy.24
  27.8 0.1 copy.17
  27.8 0.7 reshape.44.w_ref
  28.6 8.6 %all-gather.2.cloned.1.call-done = bf16[32,8,8,512]{3,0,2,1:T(8,128)(2,1)} async-done(((bf16[16,8,8,512]{3,0,2,1:T(8,128)(2,1)}), bf16[32,8,8,512]{3,0,2,1:T(8,128)(2,1)}) %all-gather.2.cloned.1.call-update) | async-done | bytes 2097168 | tf_op jit(solution)/shard_map/all_gather | solution.py:130
  37.2 2.0 %pad.4 = bf16[32,8,12,512]{3,0,2,1:T(8,128)(2,1)S(1)} pad(bf16[32,8,8,512]{3,0,2,1:T(8,128)(2,1)} %all-gather.2.cloned.1.call-done, bf16[]{:T(256)} %constant.2.clone.1), padding=0_0x0_0x2_2x0_0 | pad | bytes 5242882 | tf_op jit(solution)/shard_map/jit(_pad)/pad | solution.py:131
  39.3 2.1 %copy.27 = bf16[32,4,2,6,2,512]{5,0,3,4,1,2:T(8,128)(2,1)} copy(bf16[32,4,2,6,2,512]{5,0,4,3,2,1:T(8,128)(2,1)S(1)} %bitcast.25) | data formatting | bytes 6291456 | tf_op jit(solution)/shard_map/reshape | solution.py:133
  41.4 15.5 %shard_map.76 = (bf16[4,8,16,512]{3,2,1,0:T(8,128)(2,1)}, f32[3,96,48]{2,1,0:T(8,128)}) custom-call(bf16[2,4,2,6,32,512]{5,4,3,2,1,0:T(8,128)(2,1)} %bitcast.24, bf16[4,8,16,512]{3,2,1,0:T(8,128)(2,1)} %bitcast.26, bf16[3,48,96]{2,1,0:T(8,128)(2,1)} %reshape.44.w_ref), custom_call_target="tpu_custom_call" | custom-call | tf_op jit(solution)/shard_map/pallas_call | solution.py:141
  56.8 0.9 slice.28
  57.8 1.8 %collective-permute-start.2 = (bf16[1,128,512]{2,1,0:T(8,128)(2,1)S(1)}, bf16[1,128,512]{2,1,0:T(8,128)(2,1)S(1)}, u32[]{:S(2)}, u32[]{:S(2)}) collective-permute-start(bf16[1,128,512]{2,1,0:T(8,128)(2,1)S(1)} %bitcast.33), channel_id=1, source_target_pairs={{14,0},{0,2},{2,4},{4,6},{6,8},{8,10},{10,12},{12,14},{15,1},{1,3}... | collective-permute-start | bytes 393224 | tf_op jit(solution)/shard_map/ppermute | solution.py:30
  59.6 0.8 copy.19.u_ref
  60.3 2.1 %all_gather.7 = bf16[64,2,4,256]{3,0,2,1:T(8,128)(2,1)} all-gather(bf16[32,2,4,256]{3,0,2,1:T(8,128)(2,1)S(1)} %copy.18), channel_id=1, replica_groups=mesh['groups'=2,'gz'=4,'sec'=2,'ch'=2] {'ch'}, dimensions={0}, use_global_device_ids=true | all-gather | bytes 393216 | tf_op jit(solution)/shard_map/all_gather | solution.py:156
  62.4 1.0 copy.20
  63.4 0.2 reshape.48
  63.6 0.7 rev.7
  64.3 0.2 copy.21
  64.6 0.2 reshape_reshape.7
  64.7 1.5 %collective-permute-done.2.below_ref = bf16[1,128,512]{2,1,0:T(8,128)(2,1)S(1)} collective-permute-done((bf16[1,128,512]{2,1,0:T(8,128)(2,1)S(1)}, bf16[1,128,512]{2,1,0:T(8,128)(2,1)S(1)}, u32[]{:S(2)}, u32[]{:S(2)}) %collective-permute-start.2) | collective-permute-done | bytes 131104 | tf_op jit(solution)/shard_map/ppermute | solution.py:30
  66.3 0.7 copy-done.4
  66.9 4.8 %shard_map.77 = (f32[2,4,64,256]{3,2,1,0:T(8,128)}, f32[3,144,64]{2,1,0:T(8,128)}) custom-call(bf16[4,128,512]{2,1,0:T(8,128)(2,1)} %bitcast.29, bf16[1,128,512]{2,1,0:T(8,128)(2,1)} %copy-done.4, bf16[2,4,64,256]{3,2,1,0:T(8,128)(2,1)} %bitcast.28, bf16[3,64,144]{2,1,0:T(8,128)(2,1)} %copy.19.u_ref), custom_call_target="tpu_custom_call" | custom-call | tf_op jit(solution)/shard_map/pallas_call | solution.py:164
  71.7 1.0 reshape_reshape.6
  72.8 0.1 collective-permute-start.3
  72.9 5.7 %collective-permute-done.3 = f32[41472]{0:T(1024)S(1)} collective-permute-done((f32[41472]{0:T(1024)S(1)}, f32[41472]{0:T(1024)S(1)}, u32[]{:S(2)}, u32[]{:S(2)}) %collective-permute-start.3) | collective-permute-done | bytes 165920 | tf_op jit(solution)/shard_map/ppermute | solution.py:40
  78.6 0.6 collective-permute-start.4
  79.3 4.8 %collective-permute-done.4 = f32[41472]{0:T(1024)S(1)} collective-permute-done((f32[41472]{0:T(1024)S(1)}, f32[41472]{0:T(1024)S(1)}, u32[]{:S(2)}, u32[]{:S(2)}) %collective-permute-start.4) | collective-permute-done | bytes 165920 | tf_op jit(solution)/shard_map/ppermute | solution.py:40
  84.1 1.7 %collective-permute-start.5 = (f32[41472]{0:T(1024)S(1)}, f32[41472]{0:T(1024)S(1)}, u32[]{:S(2)}, u32[]{:S(2)}) collective-permute-start(f32[41472]{0:T(1024)S(1)} %add.19), channel_id=1, source_target_pairs={{0,8},{2,10},{4,12},{6,14},{8,0},{10,2},{12,4},{14,6},{1,9},{3,11}... | collective-permute-start | bytes 497672 | tf_op jit(solution)/shard_map/ppermute | solution.py:40
  85.8 0.0 reduce-scatter.2.cloned.1.call-update
  85.8 6.5 %collective-permute-done.5 = f32[41472]{0:T(1024)S(1)} collective-permute-done((f32[41472]{0:T(1024)S(1)}, f32[41472]{0:T(1024)S(1)}, u32[]{:S(2)}, u32[]{:S(2)}) %collective-permute-start.5) | collective-permute-done | bytes 165920 | tf_op jit(solution)/shard_map/ppermute | solution.py:40
  92.4 0.8 mul.24
  93.2 0.2 mul.27
  93.3 0.9 copy.23
  94.2 1.0 convert_element_type.5
  95.2 0.8 copy.22
  (16 shorter events, 0.2 us)
Async XLA Ops:
  7.2 52.4 %copy-start = (bf16[27,32,64]{2,1,0:T(8,128)(2,1)S(1)}, bf16[27,32,64]{2,1,0:T(8,128)(2,1)}, u32[]{:S(2)}) copy-start(bf16[27,32,64]{2,1,0:T(8,128)(2,1)} %param.8) | copy-start | bytes 331780
  7.2 19.2 %copy-start.1 = (bf16[16,4,8,512]{3,2,1,0:T(8,128)(2,1)S(1)}, bf16[16,4,8,512]{3,2,1,0:T(8,128)(2,1)}, u32[]{:S(2)}) copy-start(bf16[16,4,8,512]{3,2,1,0:T(8,128)(2,1)} %param.6) | copy-start | bytes 1572868
  7.2 20.3 %copy-start.2 = (bf16[27,32,32]{2,1,0:T(8,128)(2,1)S(1)}, bf16[27,32,32]{2,1,0:T(8,128)(2,1)}, u32[]{:S(2)}) copy-start(bf16[27,32,32]{2,1,0:T(8,128)(2,1)} %param.9) | copy-start | bytes 165892
  7.2 30.0 %all-gather.2.cloned.1.call-start = ((), (), s32[]{:S(2)}) async-start(), calls=%async_computation.1 | async-start | bytes 3145728 | tf_op jit(solution)/shard_map/all_gather | solution.py:130
  8.7 19.9 %copy-start.3 = (bf16[32,2,4,256]{3,2,1,0:T(4,128)(2,1)S(1)}, bf16[32,2,4,256]{3,2,1,0:T(4,128)(2,1)}, u32[]{:S(2)}) copy-start(bf16[32,2,4,256]{3,2,1,0:T(4,128)(2,1)} %param.5) | copy-start | bytes 393220
  8.7 11.6 %collective-permute-start.1 = (bf16[16,2,8,512]{3,0,2,1:T(8,128)(2,1)S(1)}, bf16[16,2,8,512]{3,0,2,1:T(8,128)(2,1)S(1)}, u32[]{:S(2)}, u32[]{:S(2)}) collective-permute-start(bf16[16,2,8,512]{3,0,2,1:T(8,128)(2,1)S(1)} %get-tuple-element.18), channel_id=1, source_target_pairs={{2,0},{4,2},{6,4},{8,6},{10,8},{12,10},{14,12},{0,14},{3,1},{5,3},... | collective-permute-start | bytes 786440 | tf_op jit(solution)/shard_map/ppermute | solution.py:22
  14.7 10.5 %collective-permute-start = (bf16[16,2,8,512]{3,0,2,1:T(8,128)(2,1)S(1)}, bf16[16,2,8,512]{3,0,2,1:T(8,128)(2,1)S(1)}, u32[]{:S(2)}, u32[]{:S(2)}) collective-permute-start(bf16[16,2,8,512]{3,0,2,1:T(8,128)(2,1)S(1)} %get-tuple-element.17), channel_id=1, source_target_pairs={{0,2},{2,4},{4,6},{6,8},{8,10},{10,12},{12,14},{14,0},{1,3},{3,5},... | collective-permute-start | bytes 786440 | tf_op jit(solution)/shard_map/ppermute | solution.py:19
  26.3 67.9 %reduce-scatter.2.cloned.1.call-start = ((), (), s32[]{:S(2)}) async-start(), calls=%async_computation.2 | async-start | bytes 786432 | tf_op jit(solution)/shard_map/reduce_scatter | solution.py:179
  57.8 8.5 %collective-permute-start.2 = (bf16[1,128,512]{2,1,0:T(8,128)(2,1)S(1)}, bf16[1,128,512]{2,1,0:T(8,128)(2,1)S(1)}, u32[]{:S(2)}, u32[]{:S(2)}) collective-permute-start(bf16[1,128,512]{2,1,0:T(8,128)(2,1)S(1)} %bitcast.33), channel_id=1, source_target_pairs={{14,0},{0,2},{2,4},{4,6},{6,8},{8,10},{10,12},{12,14},{15,1},{1,3}... | collective-permute-start | bytes 393224 | tf_op jit(solution)/shard_map/ppermute | solution.py:30
  66.3 0.7 copy-start.4
  72.8 5.8 %collective-permute-start.3 = (f32[41472]{0:T(1024)S(1)}, f32[41472]{0:T(1024)S(1)}, u32[]{:S(2)}, u32[]{:S(2)}) collective-permute-start(f32[41472]{0:T(1024)S(1)} %constant_dynamic-update-slice_fusion), channel_id=1, source_target_pairs={{0,2},{2,0},{4,6},{6,4},{8,10},{10,8},{12,14},{14,12},{1,3},{3,1},... | collective-permute-start | bytes 497672 | tf_op jit(solution)/shard_map/ppermute | solution.py:40
  78.6 5.4 %collective-permute-start.4 = (f32[41472]{0:T(1024)S(1)}, f32[41472]{0:T(1024)S(1)}, u32[]{:S(2)}, u32[]{:S(2)}) collective-permute-start(f32[41472]{0:T(1024)S(1)} %add.18), channel_id=1, source_target_pairs={{0,4},{2,6},{4,0},{6,2},{8,12},{10,14},{12,8},{14,10},{1,5},{3,7},... | collective-permute-start | bytes 497672 | tf_op jit(solution)/shard_map/ppermute | solution.py:40
  84.1 8.2 %collective-permute-start.5 = (f32[41472]{0:T(1024)S(1)}, f32[41472]{0:T(1024)S(1)}, u32[]{:S(2)}, u32[]{:S(2)}) collective-permute-start(f32[41472]{0:T(1024)S(1)} %add.19), channel_id=1, source_target_pairs={{0,8},{2,10},{4,12},{6,14},{8,0},{10,2},{12,4},{14,6},{1,9},{3,11}... | collective-permute-start | bytes 497672 | tf_op jit(solution)/shard_map/ppermute | solution.py:40
Sparse Core Ops, SparseCore 0:
  26.4 10.7 all-gather.1
  85.9 6.9 reduce-scatter.1

commit v5 on v4

--- a/solution.py
+++ b/solution.py
@@ -126,15 +126,27 @@
     all_ch = part_ch * lax.axis_size("ch")
     channel_start = lax.axis_index("ch") * part_ch
 
-    rimmed_local = padded(out_grad, ((("gz", "sec"), 1),), 2)
-    every_channel = lax.all_gather(rimmed_local, "ch", axis=0, tiled=True)
-    rimmed = jnp.pad(every_channel, ((0, 0), (0, 0), (2, 2), (0, 0)))
-    halo_z, halo_x = rimmed.shape[1], rimmed.shape[2]
-    rimmed = rimmed.reshape(all_ch, halo_z // 2, 2, halo_x // 2, 2, cells_y)
-    rimmed = jnp.transpose(rimmed, (2, 1, 4, 3, 0, 5))
+    rows = jnp.transpose(out_grad, (1, 2, 0, 3))
+    count = lax.axis_size(("gz", "sec"))
+    forward = [(i, (i + 1) % count) for i in range(count)]
+    backward = [(target, source) for source, target in forward]
+    swap = [(i, i ^ 1) for i in range(lax.axis_size("ch"))]
+    low = lax.ppermute(rows[planes_z - 2 :], ("gz", "sec"), forward)
+    high = lax.ppermute(rows[:2], ("gz", "sec"), backward)
+    rows_other = lax.ppermute(rows, "ch", swap)
+    low_other = lax.ppermute(low, "ch", swap)
+    high_other = lax.ppermute(high, "ch", swap)
+    mine = jnp.concatenate([low, rows, high], axis=0)
+    other = jnp.concatenate([low_other, rows_other, high_other], axis=0)
+    rimmed = jnp.concatenate([mine, other], axis=2)
+    rimmed = jnp.pad(rimmed, ((0, 0), (2, 2), (0, 0), (0, 0)))
+    halo_z, halo_x = rimmed.shape[0], rimmed.shape[1]
+    rimmed = rimmed.reshape(halo_z // 2, 2, halo_x // 2, 2, all_ch, cells_y)
+    rimmed = jnp.transpose(rimmed, (1, 0, 3, 2, 4, 5))
     pre_rows = jnp.transpose(saved_pre, (1, 2, 0, 3))
 
     refine_cols = lax.dynamic_slice_in_dim(refine_weight, channel_start, part_ch, 2)
+    refine_cols = jnp.roll(refine_cols, -channel_start, axis=1)
     refine_w = refine_cols.reshape(3, 3, 3, all_ch, part_ch)[:, ::-1]
     refine_w = jnp.transpose(refine_w, (0, 2, 4, 1, 3)).reshape(3, 3 * part_ch, 3 * all_ch)
 
@@ -149,6 +161,7 @@
     )(rimmed, pre_rows, refine_w)
     refine_terms = refine_acc.reshape(3, 3, all_ch, 3, part_ch)[:, ::-1]
     refine_terms = jnp.transpose(refine_terms, (0, 1, 3, 2, 4)).reshape(27, all_ch, part_ch)
+    refine_terms = jnp.roll(refine_terms, channel_start, axis=1)
 
     grad_rows = grad_pre.reshape(planes_z, planes_x * part_ch, cells_y)
     below_z = passed_along(grad_rows[planes_z - 1 :], ("gz", "sec"), 1)

time: 103 us -> 94.8 us (0.920)
  waiting for transfers between devices: 37.7 us -> 30.2 us
  other arithmetic: 2.13 us -> 4.79 us
  starting transfers between devices: 10.3 us -> 7.95 us
  local copies, waits for them, and re-layouts: 16 us -> 14.9 us
    all_gather x1 -> x0, waiting for transfers between devices: 8.63 us -> none  [local(): every_channel = lax.all_gather(rimmed_local, 'ch', axis=0, tiled=True)]
    concatenate x1 -> x3, other arithmetic: 1.08 us -> 3.75 us  [the longest x1 3.39 us: local(): rimmed = jnp.concatenate([mine, other], axis=2)]
    pad x1 -> x0, local copies, waits for them, and re-layouts: 2.05 us -> none  [local(): rimmed = jnp.pad(every_channel, ((0, 0), (0, 0), (2, 2), (0, 0)))]
    ppermute x3, waiting for transfers between devices: 17 us -> 18.8 us  [summed_over_slabs(): block = block + lax.ppermute(block, axis, route)]
    ppermute x3, starting transfers between devices: 2.41 us -> 0.75 us  [summed_over_slabs(): block = block + lax.ppermute(block, axis, route)]
    ppermute x2 -> x5, waiting for transfers between devices: 10.5 us -> 9.24 us  [the longest x1 4.89 us: local(): low = lax.ppermute(rows[planes_z - 2:], ('gz', 'sec'), forward)]
    reshape x1 -> x2, local copies, waits for them, and re-layouts: 2.08 us -> 2.25 us  [the longest x1 2.07 us: local(): rimmed = rimmed.reshape(halo_z // 2, 2, halo_x // 2, 2, all_ch, cells_y)]
    ppermute x2 -> x5, starting transfers between devices: 6.03 us -> 6.04 us  [the longest x1 6.03 us: local(): high = lax.ppermute(rows[:2], ('gz', 'sec'), backward)]
  transfers between devices with their start and end apart: 8 -> 10, of which waited for: 7 -> 6; matrix products, arithmetic and copies ran while one was open for 7% -> 9% of each run, Pallas kernels for 0% -> 0%
where the time goes in v5:
time: 94.8 us; the launch traced here: 94.5 us
  waiting for transfers between devices  30.2 us (32%)
  Pallas kernels  20.3 us (21%)
  local copies, waits for them, and re-layouts  14.9 us (16%)
  between operations  14.3 us (15%)
  starting transfers between devices  7.95 us (8%)
  other arithmetic  4.79 us (5%)
  blocking collectives  2.11 us (2%)
    ppermute x3, waiting for transfers between devices, summed_over_slabs(): block = block + lax.ppermute(block, axis, route)  18.8 us
    pallas_call x1, Pallas kernels, local(): pl.pallas_call(fine_kernel, out_shape=(jax.ShapeDtypeStruct((planes_z, pl...  15.5 us
    ppermute x1, starting transfers between devices, local(): high = lax.ppermute(rows[:2], ('gz', 'sec'), backward)  6.03 us
    unnamed x15, local copies, waits for them, and re-layouts  4.98 us
    ppermute x1, waiting for transfers between devices, local(): low = lax.ppermute(rows[planes_z - 2:], ('gz', 'sec'), forward)  4.89 us
    pallas_call x1, Pallas kernels, local(): pl.pallas_call(coarse_kernel, out_shape=(jax.ShapeDtypeStruct((coarse_z,...  4.8 us
    ppermute x1, waiting for transfers between devices, local(): high = lax.ppermute(rows[:2], ('gz', 'sec'), backward)  4.34 us
    concatenate x1, other arithmetic, local(): rimmed = jnp.concatenate([mine, other], axis=2)  3.39 us
  transfers between devices with their start and end apart: 10, of which 6 were waited for; matrix products, arithmetic and copies ran while one was open for 9% of the time, Pallas kernels for 0%

profile of v5, /device:TPU:0, one launch (start us, length us, event | category | flops | bytes accessed | tf_op | source)
XLA Modules:
  0.0 94.5 jit_solution(12114052163138461513)
XLA Ops:
  7.2 0.0 copy-start
  7.2 0.0 reduce-scatter.2.cloned.1.call-start
  7.2 1.4 %copy.29 = bf16[16,4,8,512]{3,0,2,1:T(8,128)(2,1)S(1)} copy(bf16[16,4,8,512]{3,2,1,0:T(8,128)(2,1)} %param.7) | data formatting | bytes 1048576 | tf_op args[2]
  8.7 6.0 %collective-permute-start.1 = (bf16[2,8,16,512]{3,2,1,0:T(8,128)(2,1)S(1)}, bf16[2,8,16,512]{3,2,1,0:T(8,128)(2,1)S(1)}, u32[]{:S(2)}, u32[]{:S(2)}) collective-permute-start(bf16[2,8,16,512]{3,2,1,0:T(8,128)(2,1)S(1)} %get-tuple-element.18), channel_id=1, source_target_pairs={{2,0},{4,2},{6,4},{8,6},{10,8},{12,10},{14,12},{0,14},{3,1},{5,3},... | collective-permute-start | bytes 786440 | tf_op jit(solution)/shard_map/ppermute | solution.py:135
  14.7 0.0 collective-permute-start
  14.7 0.0 collective-permute-start.3
  14.7 1.1 %constant_dynamic-slice_fusion.1 = bf16[27,32,16]{2,1,0:T(8,128)(2,1)S(1)} fusion(bf16[27,32,32]{2,1,0:T(8,128)(2,1)} %param.9, s32[]{:T(128)S(6)} %select_n.27), kind=kLoop, calls=%fused_computation.21 | loop fusion | bytes 55300 | tf_op jit(solution)/shard_map/dynamic_slice | solution.py:148
  15.8 0.1 copy.23
  15.9 4.3 %collective-permute-done.1 = bf16[2,8,16,512]{3,2,1,0:T(8,128)(2,1)S(1)} collective-permute-done((bf16[2,8,16,512]{3,2,1,0:T(8,128)(2,1)S(1)}, bf16[2,8,16,512]{3,2,1,0:T(8,128)(2,1)S(1)}, u32[]{:S(2)}, u32[]{:S(2)}) %collective-permute-start.1) | collective-permute-done | bytes 262176 | tf_op jit(solution)/shard_map/ppermute | solution.py:135
  20.3 0.0 collective-permute-start.4
  20.3 4.9 %collective-permute-done = bf16[2,8,16,512]{3,2,1,0:T(8,128)(2,1)S(1)} collective-permute-done((bf16[2,8,16,512]{3,2,1,0:T(8,128)(2,1)S(1)}, bf16[2,8,16,512]{3,2,1,0:T(8,128)(2,1)S(1)}, u32[]{:S(2)}, u32[]{:S(2)}) %collective-permute-start) | collective-permute-done | bytes 262176 | tf_op jit(solution)/shard_map/ppermute | solution.py:134
  25.2 0.0 collective-permute-start.2
  25.2 0.2 dynamic-slice_maximum_fusion.1
  25.4 1.1 %copy.28 = bf16[16,4,8,512]{3,0,2,1:T(8,128)(2,1)} copy(bf16[16,4,8,512]{3,2,1,0:T(8,128)(2,1)S(1)} %copy-done.1) | data formatting | bytes 1048576 | tf_op args[1]
  26.5 0.1 copy.15
  26.5 0.7 reshape.50.w_ref
  27.4 0.0 collective-permute-done.4
  27.4 0.0 collective-permute-done.3
  27.4 0.0 collective-permute-done.2
  27.4 3.4 %fusion.1 = bf16[8,12,32,512]{3,2,1,0:T(8,128)(2,1)S(1)} fusion(bf16[2,8,16,512]{3,2,1,0:T(8,128)(2,1)S(1)} %collective-permute-done.4, bf16[2,8,16,512]{3,2,1,0:T(8,128)(2,1)S(1)} %collective-permute-done.1, bf16[4,8,16,512]{3,2,1,0:T(8,128)(2,1)S(1)} %collective-permute-done.3, bf16[2,8,16,512]{3,2,1,0:T(8,128)(2,1)S(1)} %collective-permute-done.2, ...), kind=kLoop, calls=%fused_computation.4 | loop fusion | flops 33030144 | bytes 5242880 | tf_op jit(solution)/shard_map/concatenate | solution.py:141
  30.8 2.1 %copy.27 = bf16[4,2,6,2,32,512]{5,4,2,3,0,1:T(8,128)(2,1)} copy(bf16[4,2,6,2,32,512]{5,4,3,2,1,0:T(8,128)(2,1)S(1)} %bitcast.26) | data formatting | bytes 6291456 | tf_op jit(solution)/shard_map/reshape | solution.py:144
  32.9 15.5 %shard_map.76 = (bf16[4,8,16,512]{3,2,1,0:T(8,128)(2,1)}, f32[3,96,48]{2,1,0:T(8,128)}) custom-call(bf16[2,4,2,6,32,512]{5,4,3,2,1,0:T(8,128)(2,1)} %bitcast.27, bf16[4,8,16,512]{3,2,1,0:T(8,128)(2,1)} %bitcast.31, bf16[3,48,96]{2,1,0:T(8,128)(2,1)} %reshape.50.w_ref), custom_call_target="tpu_custom_call" | custom-call | tf_op jit(solution)/shard_map/pallas_call | solution.py:153
  48.3 0.9 slice.28
  49.3 1.1 %collective-permute-start.5 = (bf16[1,128,512]{2,1,0:T(8,128)(2,1)S(1)}, bf16[1,128,512]{2,1,0:T(8,128)(2,1)S(1)}, u32[]{:S(2)}, u32[]{:S(2)}) collective-permute-start(bf16[1,128,512]{2,1,0:T(8,128)(2,1)S(1)} %bitcast.39), channel_id=1, source_target_pairs={{14,0},{0,2},{2,4},{4,6},{6,8},{8,10},{10,12},{12,14},{15,1},{1,3}... | collective-permute-start | bytes 393224 | tf_op jit(solution)/shard_map/ppermute | solution.py:30
  50.4 2.1 %all_gather.3 = bf16[64,2,4,256]{3,0,2,1:T(8,128)(2,1)} all-gather(bf16[32,2,4,256]{3,0,2,1:T(8,128)(2,1)S(1)} %copy.16), channel_id=1, replica_groups=mesh['groups'=2,'gz'=4,'sec'=2,'ch'=2] {'ch'}, dimensions={0}, use_global_device_ids=true | all-gather | bytes 393216 | tf_op jit(solution)/shard_map/all_gather | solution.py:169
  52.5 0.8 copy.17.u_ref
  53.3 1.0 %copy.18 = f32[3,96,48]{1,2,0:T(8,128)S(1)} copy(f32[3,96,48]{2,1,0:T(8,128)} %get-tuple-element.10) | data formatting | bytes 110592 | tf_op jit(solution)/shard_map/pallas_call | solution.py:153
  54.3 0.2 reshape.54
  54.4 0.7 rev.7
  55.2 0.2 dynamic-slice_maximum_fusion
  55.4 0.2 copy.20
  55.6 0.2 reshape.56
  55.8 2.1 %collective-permute-done.5.below_ref = bf16[1,128,512]{2,1,0:T(8,128)(2,1)S(1)} collective-permute-done((bf16[1,128,512]{2,1,0:T(8,128)(2,1)S(1)}, bf16[1,128,512]{2,1,0:T(8,128)(2,1)S(1)}, u32[]{:S(2)}, u32[]{:S(2)}) %collective-permute-start.5) | collective-permute-done | bytes 131104 | tf_op jit(solution)/shard_map/ppermute | solution.py:30
  57.9 0.7 copy-done.3
  58.6 4.8 %shard_map.77 = (f32[2,4,64,256]{3,2,1,0:T(8,128)}, f32[3,144,64]{2,1,0:T(8,128)}) custom-call(bf16[4,128,512]{2,1,0:T(8,128)(2,1)} %bitcast.35, bf16[1,128,512]{2,1,0:T(8,128)(2,1)} %copy-done.3, bf16[2,4,64,256]{3,2,1,0:T(8,128)(2,1)} %bitcast.33, bf16[3,64,144]{2,1,0:T(8,128)(2,1)} %copy.17.u_ref), custom_call_target="tpu_custom_call" | custom-call | tf_op jit(solution)/shard_map/pallas_call | solution.py:177
  63.4 1.0 %reshape_reshape.3 = f32[27648]{0:T(1024)S(1)} reshape(f32[3,144,64]{2,1,0:T(8,128)} %get-tuple-element.9) | data formatting | bytes 221184 | tf_op jit(solution)/shard_map/reshape;reshape | solution.py:194
  64.4 0.1 collective-permute-start.6
  64.5 5.9 %collective-permute-done.6 = f32[41472]{0:T(1024)S(1)} collective-permute-done((f32[41472]{0:T(1024)S(1)}, f32[41472]{0:T(1024)S(1)}, u32[]{:S(2)}, u32[]{:S(2)}) %collective-permute-start.6) | collective-permute-done | bytes 165920 | tf_op jit(solution)/shard_map/ppermute | solution.py:40
  70.4 0.1 collective-permute-start.7
  70.5 5.3 %collective-permute-done.7 = f32[41472]{0:T(1024)S(1)} collective-permute-done((f32[41472]{0:T(1024)S(1)}, f32[41472]{0:T(1024)S(1)}, u32[]{:S(2)}, u32[]{:S(2)}) %collective-permute-start.7) | collective-permute-done | bytes 165920 | tf_op jit(solution)/shard_map/ppermute | solution.py:40
  75.9 0.6 collective-permute-start.8
  76.5 0.0 reduce-scatter.2.cloned.1.call-update
  76.5 7.5 %collective-permute-done.8 = f32[41472]{0:T(1024)S(1)} collective-permute-done((f32[41472]{0:T(1024)S(1)}, f32[41472]{0:T(1024)S(1)}, u32[]{:S(2)}, u32[]{:S(2)}) %collective-permute-start.8) | collective-permute-done | bytes 165920 | tf_op jit(solution)/shard_map/ppermute | solution.py:40
  84.1 0.8 mul.24
  84.9 0.2 mul.27
  85.1 0.9 copy.22
  85.9 1.0 %convert_element_type.5 = bf16[32,2,4,256]{3,0,2,1:T(8,128)(2,1)S(1)} convert(f32[32,2,4,256]{3,0,2,1:T(8,128)} %reduce-scatter.2.cloned.1.call-done) | non-fusion elementwise | flops 65536 | bytes 393216 | tf_op jit(solution)/shard_map/convert_element_type | solution.py:193
  86.9 0.8 copy.21
  (19 shorter events, 0.2 us)
Async XLA Ops:
  7.2 20.2 %copy-start = (bf16[27,32,64]{2,1,0:T(8,128)(2,1)S(1)}, bf16[27,32,64]{2,1,0:T(8,128)(2,1)}, u32[]{:S(2)}) copy-start(bf16[27,32,64]{2,1,0:T(8,128)(2,1)} %param.8) | copy-start | bytes 331780
  7.2 18.2 %copy-start.1 = (bf16[16,4,8,512]{3,2,1,0:T(8,128)(2,1)S(1)}, bf16[16,4,8,512]{3,2,1,0:T(8,128)(2,1)}, u32[]{:S(2)}) copy-start(bf16[16,4,8,512]{3,2,1,0:T(8,128)(2,1)} %param.6) | copy-start | bytes 1572868
  7.2 20.1 %copy-start.2 = (bf16[32,2,4,256]{3,2,1,0:T(4,128)(2,1)S(1)}, bf16[32,2,4,256]{3,2,1,0:T(4,128)(2,1)}, u32[]{:S(2)}) copy-start(bf16[32,2,4,256]{3,2,1,0:T(4,128)(2,1)} %param.5) | copy-start | bytes 393220
  7.2 78.7 %reduce-scatter.2.cloned.1.call-start = ((), (), s32[]{:S(2)}) async-start(), calls=%async_computation.1 | async-start | bytes 786432 | tf_op jit(solution)/shard_map/reduce_scatter | solution.py:192
  8.7 11.6 %collective-permute-start.1 = (bf16[2,8,16,512]{3,2,1,0:T(8,128)(2,1)S(1)}, bf16[2,8,16,512]{3,2,1,0:T(8,128)(2,1)S(1)}, u32[]{:S(2)}, u32[]{:S(2)}) collective-permute-start(bf16[2,8,16,512]{3,2,1,0:T(8,128)(2,1)S(1)} %get-tuple-element.18), channel_id=1, source_target_pairs={{2,0},{4,2},{6,4},{8,6},{10,8},{12,10},{14,12},{0,14},{3,1},{5,3},... | collective-permute-start | bytes 786440 | tf_op jit(solution)/shard_map/ppermute | solution.py:135
  14.7 10.5 %collective-permute-start = (bf16[2,8,16,512]{3,2,1,0:T(8,128)(2,1)S(1)}, bf16[2,8,16,512]{3,2,1,0:T(8,128)(2,1)S(1)}, u32[]{:S(2)}, u32[]{:S(2)}) collective-permute-start(bf16[2,8,16,512]{3,2,1,0:T(8,128)(2,1)S(1)} %get-tuple-element.17), channel_id=1, source_target_pairs={{0,2},{2,4},{4,6},{6,8},{8,10},{10,12},{12,14},{14,0},{1,3},{3,5},... | collective-permute-start | bytes 786440 | tf_op jit(solution)/shard_map/ppermute | solution.py:134
  14.7 12.6 %collective-permute-start.3 = (bf16[4,8,16,512]{3,2,1,0:T(8,128)(2,1)S(1)}, bf16[4,8,16,512]{3,2,1,0:T(8,128)(2,1)S(1)}, u32[]{:S(2)}, u32[]{:S(2)}) collective-permute-start(bf16[4,8,16,512]{3,2,1,0:T(8,128)(2,1)S(1)} %bitcast.29), channel_id=1, source_target_pairs={{0,1},{1,0},{2,3},{3,2},{4,5},{5,4},{6,7},{7,6},{8,9},{9,8},{10,11... | collective-permute-start | bytes 1572872 | tf_op jit(solution)/shard_map/ppermute | solution.py:136
  20.3 7.1 %collective-permute-start.4 = (bf16[2,8,16,512]{3,2,1,0:T(8,128)(2,1)S(1)}, bf16[2,8,16,512]{3,2,1,0:T(8,128)(2,1)S(1)}, u32[]{:S(2)}, u32[]{:S(2)}) collective-permute-start(bf16[2,8,16,512]{3,2,1,0:T(8,128)(2,1)S(1)} %collective-permute-done.1), channel_id=1, source_target_pairs={{0,1},{1,0},{2,3},{3,2},{4,5},{5,4},{6,7},{7,6},{8,9},{9,8},{10,11... | collective-permute-start | bytes 786440 | tf_op jit(solution)/shard_map/ppermute | solution.py:138
  25.2 2.2 %collective-permute-start.2 = (bf16[2,8,16,512]{3,2,1,0:T(8,128)(2,1)S(1)}, bf16[2,8,16,512]{3,2,1,0:T(8,128)(2,1)S(1)}, u32[]{:S(2)}, u32[]{:S(2)}) collective-permute-start(bf16[2,8,16,512]{3,2,1,0:T(8,128)(2,1)S(1)} %collective-permute-done), channel_id=1, source_target_pairs={{0,1},{1,0},{2,3},{3,2},{4,5},{5,4},{6,7},{7,6},{8,9},{9,8},{10,11... | collective-permute-start | bytes 786440 | tf_op jit(solution)/shard_map/ppermute | solution.py:137
  49.3 8.7 %collective-permute-start.5 = (bf16[1,128,512]{2,1,0:T(8,128)(2,1)S(1)}, bf16[1,128,512]{2,1,0:T(8,128)(2,1)S(1)}, u32[]{:S(2)}, u32[]{:S(2)}) collective-permute-start(bf16[1,128,512]{2,1,0:T(8,128)(2,1)S(1)} %bitcast.39), channel_id=1, source_target_pairs={{14,0},{0,2},{2,4},{4,6},{6,8},{8,10},{10,12},{12,14},{15,1},{1,3}... | collective-permute-start | bytes 393224 | tf_op jit(solution)/shard_map/ppermute | solution.py:30
  57.9 0.7 copy-start.3
  64.4 6.0 %collective-permute-start.6 = (f32[41472]{0:T(1024)S(1)}, f32[41472]{0:T(1024)S(1)}, u32[]{:S(2)}, u32[]{:S(2)}) collective-permute-start(f32[41472]{0:T(1024)S(1)} %constant_dynamic-update-slice_fusion), channel_id=1, source_target_pairs={{0,2},{2,0},{4,6},{6,4},{8,10},{10,8},{12,14},{14,12},{1,3},{3,1},... | collective-permute-start | bytes 497672 | tf_op jit(solution)/shard_map/ppermute | solution.py:40
  70.4 5.4 %collective-permute-start.7 = (f32[41472]{0:T(1024)S(1)}, f32[41472]{0:T(1024)S(1)}, u32[]{:S(2)}, u32[]{:S(2)}) collective-permute-start(f32[41472]{0:T(1024)S(1)} %add.41), channel_id=1, source_target_pairs={{0,4},{2,6},{4,0},{6,2},{8,12},{10,14},{12,8},{14,10},{1,5},{3,7},... | collective-permute-start | bytes 497672 | tf_op jit(solution)/shard_map/ppermute | solution.py:40
  75.9 8.2 %collective-permute-start.8 = (f32[41472]{0:T(1024)S(1)}, f32[41472]{0:T(1024)S(1)}, u32[]{:S(2)}, u32[]{:S(2)}) collective-permute-start(f32[41472]{0:T(1024)S(1)} %add.42), channel_id=1, source_target_pairs={{0,8},{2,10},{4,12},{6,14},{8,0},{10,2},{12,4},{14,6},{1,9},{3,11}... | collective-permute-start | bytes 497672 | tf_op jit(solution)/shard_map/ppermute | solution.py:40
Sparse Core Ops, SparseCore 0:
  76.6 7.0 reduce-scatter.1

commit v6 on v5

--- a/solution.py
+++ b/solution.py
@@ -166,11 +166,13 @@
     grad_rows = grad_pre.reshape(planes_z, planes_x * part_ch, cells_y)
     below_z = passed_along(grad_rows[planes_z - 1 :], ("gz", "sec"), 1)
 
-    all_coarse = lax.all_gather(coarse, "ch", axis=0, tiled=True)
-    coarse_in = all_coarse.shape[0]
+    coarse_own = jnp.transpose(coarse, (1, 2, 0, 3))
+    coarse_rows = jnp.concatenate([coarse_own, lax.ppermute(coarse_own, "ch", swap)], axis=2)
+    coarse_in = coarse_rows.shape[2]
+    coarse_start = lax.axis_index("ch") * coarse.shape[0]
     coarse_z, coarse_x, cells_yc = coarse.shape[1], coarse.shape[2], coarse.shape[3]
-    coarse_rows = jnp.transpose(all_coarse, (1, 2, 0, 3))
     up_rows = lax.dynamic_slice_in_dim(up_weight, channel_start, part_ch, 1)
+    up_rows = jnp.roll(up_rows, -coarse_start, axis=2)
     up_w = jnp.transpose(up_rows.reshape(3, 9, part_ch, coarse_in), (0, 3, 1, 2))
     up_w = up_w.reshape(3, coarse_in, 9 * part_ch)
 
@@ -186,11 +188,11 @@
             pltpu.VMEM((planes_z + 1, planes_x + 1, 3, part_ch, cells_yc), jnp.bfloat16)
         ],
     )(grad_rows, below_z, coarse_rows, up_w)
-    up_terms = up_acc.reshape(27, part_ch, coarse_in)
-    running = jnp.transpose(coarse_acc, (2, 0, 1, 3))
-
-    coarse_summed = lax.psum_scatter(running, "ch", scatter_dimension=0, tiled=True)
-    grad_coarse = coarse_summed.astype(jnp.bfloat16)
+    up_terms = jnp.roll(up_acc.reshape(27, part_ch, coarse_in), coarse_start, axis=2)
+    own_k = coarse.shape[0]
+    received = lax.ppermute(coarse_acc[:, :, own_k:], "ch", swap)
+    coarse_summed = coarse_acc[:, :, :own_k] + received
+    grad_coarse = jnp.transpose(coarse_summed, (2, 0, 1, 3)).astype(jnp.bfloat16)
     flat = jnp.concatenate([up_terms.reshape(-1), refine_terms.reshape(-1)])
     flat = summed_over_slabs(flat, ("gz", "sec"))
     up_summed = flat[: up_terms.size].reshape(up_terms.shape)

time: 94.8 us -> 80.7 us (0.85)
  between operations: 14.3 us -> 0.91 us
  other arithmetic: 4.79 us -> 6.95 us
  blocking collectives: 2.11 us -> 0 us
  waiting for transfers between devices: 30.2 us -> 28.4 us
    ppermute x3, waiting for transfers between devices: 18.8 us -> 16.5 us  [summed_over_slabs(): block = block + lax.ppermute(block, axis, route)]
    ppermute x1, waiting for transfers between devices: 2.14 us -> 4.3 us  [passed_along(): return lax.ppermute(block, axis, route)]
    concatenate x0 -> x3, other arithmetic: none -> 2.12 us  [the longest x1 1.22 us: local(): jnp.roll(up_acc.reshape(27, part_ch, coarse_in), coarse_start, axis=2)]
    all_gather x1 -> x0, blocking collectives: 2.11 us -> none  [local(): all_coarse = lax.all_gather(coarse, 'ch', axis=0, tiled=True)]
    ppermute x1, waiting for transfers between devices: 4.34 us -> 2.67 us  [local(): high = lax.ppermute(rows[:2], ('gz', 'sec'), backward)]
    another operation x1 -> x0, local copies, waits for them, and re-layouts: 1.02 us -> none  [local(): flat = jnp.concatenate([up_terms.reshape(-1), refine_terms.reshape(-1)])]
    slice x0 -> x1, local copies, waits for them, and re-layouts: none -> 0.97 us  [local(): received = lax.ppermute(coarse_acc[:, :, own_k:], 'ch', swap)]
    unnamed x15 -> x13, local copies, waits for them, and re-layouts: 4.98 us -> 5.88 us
  transfers between devices with their start and end apart: 10 -> 11, of which waited for: 6 -> 6; matrix products, arithmetic and copies ran while one was open for 9% -> 22% of each run, Pallas kernels for 0% -> 19%
where the time goes in v6:
time: 80.7 us; the launch traced here: 80.4 us
  waiting for transfers between devices  28.4 us (35%)
  Pallas kernels  20.3 us (25%)
  local copies, waits for them, and re-layouts  15.8 us (20%)
  starting transfers between devices  8.02 us (10%)
  other arithmetic  6.95 us (9%)
  between operations  0.91 us (1%)
    ppermute x3, waiting for transfers between devices, summed_over_slabs(): block = block + lax.ppermute(block, axis, route)  16.5 us
    pallas_call x1, Pallas kernels, local(): pl.pallas_call(fine_kernel, out_shape=(jax.ShapeDtypeStruct((planes_z, pl...  15.5 us
    ppermute x1, starting transfers between devices, local(): high = lax.ppermute(rows[:2], ('gz', 'sec'), backward)  6.03 us
    unnamed x13, local copies, waits for them, and re-layouts  5.88 us
    ppermute x1, waiting for transfers between devices, local(): low = lax.ppermute(rows[planes_z - 2:], ('gz', 'sec'), forward)  4.89 us
    pallas_call x1, Pallas kernels, local(): pl.pallas_call(coarse_kernel, out_shape=(jax.ShapeDtypeStruct((coarse_z,...  4.8 us
    ppermute x1, waiting for transfers between devices, passed_along(): return lax.ppermute(block, axis, route)  4.3 us
    concatenate x1, other arithmetic, local(): rimmed = jnp.concatenate([mine, other], axis=2)  3.39 us
  transfers between devices with their start and end apart: 11, of which 6 were waited for; matrix products, arithmetic and copies ran while one was open for 22% of the time, Pallas kernels for 19%

profile of v6, /device:TPU:0, one launch (start us, length us, event | category | flops | bytes accessed | tf_op | source)
XLA Modules:
  0.0 80.4 jit_solution(971194219546316585)
XLA Ops:
  0.6 0.0 copy-start
  0.7 1.4 %copy.30 = bf16[16,4,8,512]{3,0,2,1:T(8,128)(2,1)S(1)} copy(bf16[16,4,8,512]{3,2,1,0:T(8,128)(2,1)} %param.7) | data formatting | bytes 1048576 | tf_op args[2]
  2.1 6.0 %collective-permute-start.1 = (bf16[2,8,16,512]{3,2,1,0:T(8,128)(2,1)S(1)}, bf16[2,8,16,512]{3,2,1,0:T(8,128)(2,1)S(1)}, u32[]{:S(2)}, u32[]{:S(2)}) collective-permute-start(bf16[2,8,16,512]{3,2,1,0:T(8,128)(2,1)S(1)} %get-tuple-element.18), channel_id=1, source_target_pairs={{2,0},{4,2},{6,4},{8,6},{10,8},{12,10},{14,12},{0,14},{3,1},{5,3},... | collective-permute-start | bytes 786440 | tf_op jit(solution)/shard_map/ppermute | solution.py:135
  8.1 0.0 collective-permute-start
  8.1 0.0 collective-permute-start.3
  8.1 0.9 %copy.31 = bf16[32,2,4,256]{3,0,2,1:T(8,128)(2,1)S(1)} copy(bf16[32,2,4,256]{3,2,1,0:T(4,128)(2,1)} %param.5) | data formatting | bytes 262144 | tf_op args[0]
  9.1 0.6 collective-permute-start.6
  9.6 1.1 %constant_dynamic-slice_fusion.1 = bf16[27,32,16]{2,1,0:T(8,128)(2,1)S(1)} fusion(bf16[27,32,32]{2,1,0:T(8,128)(2,1)} %param.9, s32[]{:T(128)S(6)} %select_n.47), kind=kLoop, calls=%fused_computation.27 | loop fusion | bytes 55300 | tf_op jit(solution)/shard_map/dynamic_slice | solution.py:148
  10.7 0.1 copy.23
  10.9 0.2 dynamic-slice_maximum_fusion.3
  11.0 2.7 %collective-permute-done.1 = bf16[2,8,16,512]{3,2,1,0:T(8,128)(2,1)S(1)} collective-permute-done((bf16[2,8,16,512]{3,2,1,0:T(8,128)(2,1)S(1)}, bf16[2,8,16,512]{3,2,1,0:T(8,128)(2,1)S(1)}, u32[]{:S(2)}, u32[]{:S(2)}) %collective-permute-start.1) | collective-permute-done | bytes 262176 | tf_op jit(solution)/shard_map/ppermute | solution.py:135
  13.7 0.0 collective-permute-start.4
  13.7 4.9 %collective-permute-done = bf16[2,8,16,512]{3,2,1,0:T(8,128)(2,1)S(1)} collective-permute-done((bf16[2,8,16,512]{3,2,1,0:T(8,128)(2,1)S(1)}, bf16[2,8,16,512]{3,2,1,0:T(8,128)(2,1)S(1)}, u32[]{:S(2)}, u32[]{:S(2)}) %collective-permute-start) | collective-permute-done | bytes 262176 | tf_op jit(solution)/shard_map/ppermute | solution.py:134
  18.7 1.1 %copy.29 = bf16[16,4,8,512]{3,0,2,1:T(8,128)(2,1)} copy(bf16[16,4,8,512]{3,2,1,0:T(8,128)(2,1)S(1)} %copy-done.1) | data formatting | bytes 1048576 | tf_op args[1]
  19.8 0.1 copy.15
  19.8 0.7 reshape.56.w_ref
  20.6 0.2 dynamic-slice_maximum_fusion.2
  20.8 0.8 copy.17.u_ref
  21.5 3.4 %fusion.1 = bf16[8,12,32,512]{3,2,1,0:T(8,128)(2,1)S(1)} fusion(bf16[2,8,16,512]{3,2,1,0:T(8,128)(2,1)S(1)} %collective-permute-done.4, bf16[2,8,16,512]{3,2,1,0:T(8,128)(2,1)S(1)} %collective-permute-done.1, bf16[4,8,16,512]{3,2,1,0:T(8,128)(2,1)S(1)} %collective-permute-done.3, bf16[2,8,16,512]{3,2,1,0:T(8,128)(2,1)S(1)} %collective-permute-done.2, ...), kind=kLoop, calls=%fused_computation.4 | loop fusion | flops 33030144 | bytes 5242880 | tf_op jit(solution)/shard_map/concatenate | solution.py:141
  24.9 2.1 %copy.28 = bf16[4,2,6,2,32,512]{5,4,2,3,0,1:T(8,128)(2,1)} copy(bf16[4,2,6,2,32,512]{5,4,3,2,1,0:T(8,128)(2,1)S(1)} %bitcast.30) | data formatting | bytes 6291456 | tf_op jit(solution)/shard_map/reshape | solution.py:144
  27.0 15.5 %shard_map.76 = (bf16[4,8,16,512]{3,2,1,0:T(8,128)(2,1)}, f32[3,96,48]{2,1,0:T(8,128)}) custom-call(bf16[2,4,2,6,32,512]{5,4,3,2,1,0:T(8,128)(2,1)} %bitcast.31, bf16[4,8,16,512]{3,2,1,0:T(8,128)(2,1)} %bitcast.35, bf16[3,48,96]{2,1,0:T(8,128)(2,1)} %reshape.56.w_ref), custom_call_target="tpu_custom_call" | custom-call | tf_op jit(solution)/shard_map/pallas_call | solution.py:153
  42.5 0.9 %slice.34 = bf16[1,8,16,512]{3,2,1,0:T(8,128)(2,1)S(1)} slice(bf16[4,8,16,512]{3,2,1,0:T(8,128)(2,1)} %get-tuple-element.7), slice={[3:4], [0:8], [0:16], [0:512]} | slice | bytes 262144 | tf_op jit(solution)/shard_map/slice | solution.py:167
  43.4 1.1 %collective-permute-start.5 = (bf16[1,128,512]{2,1,0:T(8,128)(2,1)S(1)}, bf16[1,128,512]{2,1,0:T(8,128)(2,1)S(1)}, u32[]{:S(2)}, u32[]{:S(2)}) collective-permute-start(bf16[1,128,512]{2,1,0:T(8,128)(2,1)S(1)} %bitcast.44), channel_id=1, source_target_pairs={{14,0},{0,2},{2,4},{4,6},{6,8},{8,10},{10,12},{12,14},{15,1},{1,3}... | collective-permute-start | bytes 393224 | tf_op jit(solution)/shard_map/ppermute | solution.py:30
  44.5 0.7 pad_maximum_fusion.c_ref
  45.3 1.0 %copy.18 = f32[3,96,48]{1,2,0:T(8,128)S(1)} copy(f32[3,96,48]{2,1,0:T(8,128)} %get-tuple-element.10) | data formatting | bytes 110592 | tf_op jit(solution)/shard_map/pallas_call | solution.py:153
  46.3 0.2 reshape.62
  46.4 0.7 rev.7
  47.2 0.2 dynamic-slice_maximum_fusion
  47.4 0.2 copy.20
  47.6 0.2 reshape.64
  47.8 4.3 %collective-permute-done.5.below_ref = bf16[1,128,512]{2,1,0:T(8,128)(2,1)S(1)} collective-permute-done((bf16[1,128,512]{2,1,0:T(8,128)(2,1)S(1)}, bf16[1,128,512]{2,1,0:T(8,128)(2,1)S(1)}, u32[]{:S(2)}, u32[]{:S(2)}) %collective-permute-start.5) | collective-permute-done | bytes 131104 | tf_op jit(solution)/shard_map/ppermute | solution.py:30
  52.1 0.7 copy-done.2
  52.7 4.8 %shard_map.77 = (f32[2,4,64,256]{3,2,1,0:T(8,128)}, f32[3,144,64]{2,1,0:T(8,128)}) custom-call(bf16[4,128,512]{2,1,0:T(8,128)(2,1)} %bitcast.38, bf16[1,128,512]{2,1,0:T(8,128)(2,1)} %copy-done.2, bf16[2,4,64,256]{3,2,1,0:T(8,128)(2,1)} %pad_maximum_fusion.c_ref, bf16[3,64,144]{2,1,0:T(8,128)(2,1)} %copy.17.u_ref), custom_call_target="tpu_custom_call" | custom-call | tf_op jit(solution)/shard_map/pallas_call | solution.py:179
  57.5 1.2 %dynamic-slice_maximum_fusion.1 = f32[27,16,64]{2,1,0:T(8,128)S(1)} fusion(s32[]{:T(128)S(6)} %select_n.53, f32[27,16,64]{2,1,0:T(8,128)} %bitcast.43), kind=kLoop, calls=%fused_computation.16 | loop fusion | flops 27648 | bytes 221188 | tf_op jit(solution)/shard_map/jit(_roll_dynamic)/concatenate | solution.py:191
  58.7 0.1 reshape.61
  58.9 0.1 collective-permute-start.8
  58.9 1.0 %slice.37 = f32[2,4,32,256]{3,2,1,0:T(8,128)S(1)} slice(f32[2,4,64,256]{3,2,1,0:T(8,128)} %get-tuple-element.8), slice={[0:2], [0:4], [32:64], [0:256]} | slice | bytes 524288 | tf_op jit(solution)/shard_map/slice | solution.py:193
  59.9 0.1 collective-permute-start.7
  60.0 4.8 %collective-permute-done.8 = f32[41472]{0:T(1024)S(1)} collective-permute-done((f32[41472]{0:T(1024)S(1)}, f32[41472]{0:T(1024)S(1)}, u32[]{:S(2)}, u32[]{:S(2)}) %collective-permute-start.8) | collective-permute-done | bytes 165920 | tf_op jit(solution)/shard_map/ppermute | solution.py:40
  64.9 0.1 collective-permute-start.9
  65.0 5.3 %collective-permute-done.9 = f32[41472]{0:T(1024)S(1)} collective-permute-done((f32[41472]{0:T(1024)S(1)}, f32[41472]{0:T(1024)S(1)}, u32[]{:S(2)}, u32[]{:S(2)}) %collective-permute-start.9) | collective-permute-done | bytes 165920 | tf_op jit(solution)/shard_map/ppermute | solution.py:40
  70.3 0.1 collective-permute-start.10
  70.4 1.0 %fusion.5 = bf16[32,2,4,256]{3,0,2,1:T(8,128)(2,1)S(1)} fusion(f32[2,4,32,256]{3,2,1,0:T(8,128)S(1)} %collective-permute-done.7, f32[2,4,64,256]{3,2,1,0:T(8,128)} %get-tuple-element.8), kind=kLoop, calls=%fused_computation.17 | loop fusion | flops 131072 | bytes 655360 | tf_op jit(solution)/shard_map/convert_element_type | solution.py:195
  71.4 0.8 copy.21
  72.2 6.3 %collective-permute-done.10 = f32[41472]{0:T(1024)S(1)} collective-permute-done((f32[41472]{0:T(1024)S(1)}, f32[41472]{0:T(1024)S(1)}, u32[]{:S(2)}, u32[]{:S(2)}) %collective-permute-start.10) | collective-permute-done | bytes 165920 | tf_op jit(solution)/shard_map/ppermute | solution.py:40
  78.6 0.8 mul.28
  79.3 0.2 mul.31
  79.5 0.9 %copy.22 = f32[27,32,16]{1,2,0:T(8,128)} copy(f32[27,32,16]{2,1,0:T(8,128)S(1)} %mul.31) | data formatting | bytes 110592
  (21 shorter events, 0.2 us)
Async XLA Ops:
  0.6 19.9 %copy-start = (bf16[27,32,64]{2,1,0:T(8,128)(2,1)S(1)}, bf16[27,32,64]{2,1,0:T(8,128)(2,1)}, u32[]{:S(2)}) copy-start(bf16[27,32,64]{2,1,0:T(8,128)(2,1)} %param.8) | copy-start | bytes 331780
  0.6 18.0 %copy-start.1 = (bf16[16,4,8,512]{3,2,1,0:T(8,128)(2,1)S(1)}, bf16[16,4,8,512]{3,2,1,0:T(8,128)(2,1)}, u32[]{:S(2)}) copy-start(bf16[16,4,8,512]{3,2,1,0:T(8,128)(2,1)} %param.6) | copy-start | bytes 1572868
  2.1 11.6 %collective-permute-start.1 = (bf16[2,8,16,512]{3,2,1,0:T(8,128)(2,1)S(1)}, bf16[2,8,16,512]{3,2,1,0:T(8,128)(2,1)S(1)}, u32[]{:S(2)}, u32[]{:S(2)}) collective-permute-start(bf16[2,8,16,512]{3,2,1,0:T(8,128)(2,1)S(1)} %get-tuple-element.18), channel_id=1, source_target_pairs={{2,0},{4,2},{6,4},{8,6},{10,8},{12,10},{14,12},{0,14},{3,1},{5,3},... | collective-permute-start | bytes 786440 | tf_op jit(solution)/shard_map/ppermute | solution.py:135
  8.1 10.5 %collective-permute-start = (bf16[2,8,16,512]{3,2,1,0:T(8,128)(2,1)S(1)}, bf16[2,8,16,512]{3,2,1,0:T(8,128)(2,1)S(1)}, u32[]{:S(2)}, u32[]{:S(2)}) collective-permute-start(bf16[2,8,16,512]{3,2,1,0:T(8,128)(2,1)S(1)} %get-tuple-element.17), channel_id=1, source_target_pairs={{0,2},{2,4},{4,6},{6,8},{8,10},{10,12},{12,14},{14,0},{1,3},{3,5},... | collective-permute-start | bytes 786440 | tf_op jit(solution)/shard_map/ppermute | solution.py:134
  8.1 13.4 %collective-permute-start.3 = (bf16[4,8,16,512]{3,2,1,0:T(8,128)(2,1)S(1)}, bf16[4,8,16,512]{3,2,1,0:T(8,128)(2,1)S(1)}, u32[]{:S(2)}, u32[]{:S(2)}) collective-permute-start(bf16[4,8,16,512]{3,2,1,0:T(8,128)(2,1)S(1)} %bitcast.33), channel_id=1, source_target_pairs={{0,1},{1,0},{2,3},{3,2},{4,5},{5,4},{6,7},{7,6},{8,9},{9,8},{10,11... | collective-permute-start | bytes 1572872 | tf_op jit(solution)/shard_map/ppermute | solution.py:136
  9.1 35.5 %collective-permute-start.6 = (bf16[2,4,32,256]{3,2,1,0:T(8,128)(2,1)S(1)}, bf16[2,4,32,256]{3,2,1,0:T(8,128)(2,1)S(1)}, u32[]{:S(2)}, u32[]{:S(2)}) collective-permute-start(bf16[2,4,32,256]{3,2,1,0:T(8,128)(2,1)S(1)} %bitcast.39), channel_id=1, source_target_pairs={{0,1},{1,0},{2,3},{3,2},{4,5},{5,4},{6,7},{7,6},{8,9},{9,8},{10,11... | collective-permute-start | bytes 393224 | tf_op jit(solution)/shard_map/ppermute | solution.py:170
  13.7 7.8 %collective-permute-start.4 = (bf16[2,8,16,512]{3,2,1,0:T(8,128)(2,1)S(1)}, bf16[2,8,16,512]{3,2,1,0:T(8,128)(2,1)S(1)}, u32[]{:S(2)}, u32[]{:S(2)}) collective-permute-start(bf16[2,8,16,512]{3,2,1,0:T(8,128)(2,1)S(1)} %collective-permute-done.1), channel_id=1, source_target_pairs={{0,1},{1,0},{2,3},{3,2},{4,5},{5,4},{6,7},{7,6},{8,9},{9,8},{10,11... | collective-permute-start | bytes 786440 | tf_op jit(solution)/shard_map/ppermute | solution.py:138
  18.6 2.9 %collective-permute-start.2 = (bf16[2,8,16,512]{3,2,1,0:T(8,128)(2,1)S(1)}, bf16[2,8,16,512]{3,2,1,0:T(8,128)(2,1)S(1)}, u32[]{:S(2)}, u32[]{:S(2)}) collective-permute-start(bf16[2,8,16,512]{3,2,1,0:T(8,128)(2,1)S(1)} %collective-permute-done), channel_id=1, source_target_pairs={{0,1},{1,0},{2,3},{3,2},{4,5},{5,4},{6,7},{7,6},{8,9},{9,8},{10,11... | collective-permute-start | bytes 786440 | tf_op jit(solution)/shard_map/ppermute | solution.py:137
  43.4 8.7 %collective-permute-start.5 = (bf16[1,128,512]{2,1,0:T(8,128)(2,1)S(1)}, bf16[1,128,512]{2,1,0:T(8,128)(2,1)S(1)}, u32[]{:S(2)}, u32[]{:S(2)}) collective-permute-start(bf16[1,128,512]{2,1,0:T(8,128)(2,1)S(1)} %bitcast.44), channel_id=1, source_target_pairs={{14,0},{0,2},{2,4},{4,6},{6,8},{8,10},{10,12},{12,14},{15,1},{1,3}... | collective-permute-start | bytes 393224 | tf_op jit(solution)/shard_map/ppermute | solution.py:30
  52.1 0.7 copy-start.2
  58.9 6.0 %collective-permute-start.8 = (f32[41472]{0:T(1024)S(1)}, f32[41472]{0:T(1024)S(1)}, u32[]{:S(2)}, u32[]{:S(2)}) collective-permute-start(f32[41472]{0:T(1024)S(1)} %constant_dynamic-update-slice_fusion), channel_id=1, source_target_pairs={{0,2},{2,0},{4,6},{6,4},{8,10},{10,8},{12,14},{14,12},{1,3},{3,1},... | collective-permute-start | bytes 497672 | tf_op jit(solution)/shard_map/ppermute | solution.py:40
  59.9 10.5 %collective-permute-start.7 = (f32[2,4,32,256]{3,2,1,0:T(8,128)S(1)}, f32[2,4,32,256]{3,2,1,0:T(8,128)S(1)}, u32[]{:S(2)}, u32[]{:S(2)}) collective-permute-start(f32[2,4,32,256]{3,2,1,0:T(8,128)S(1)} %slice.37), channel_id=1, source_target_pairs={{0,1},{1,0},{2,3},{3,2},{4,5},{5,4},{6,7},{7,6},{8,9},{9,8},{10,11... | collective-permute-start | bytes 786440 | tf_op jit(solution)/shard_map/ppermute | solution.py:193
  64.9 5.4 %collective-permute-start.9 = (f32[41472]{0:T(1024)S(1)}, f32[41472]{0:T(1024)S(1)}, u32[]{:S(2)}, u32[]{:S(2)}) collective-permute-start(f32[41472]{0:T(1024)S(1)} %add.65), channel_id=1, source_target_pairs={{0,4},{2,6},{4,0},{6,2},{8,12},{10,14},{12,8},{14,10},{1,5},{3,7},... | collective-permute-start | bytes 497672 | tf_op jit(solution)/shard_map/ppermute | solution.py:40
  70.3 8.2 %collective-permute-start.10 = (f32[41472]{0:T(1024)S(1)}, f32[41472]{0:T(1024)S(1)}, u32[]{:S(2)}, u32[]{:S(2)}) collective-permute-start(f32[41472]{0:T(1024)S(1)} %add.66), channel_id=1, source_target_pairs={{0,8},{2,10},{4,12},{6,14},{8,0},{10,2},{12,4},{14,6},{1,9},{3,11}... | collective-permute-start | bytes 497672 | tf_op jit(solution)/shard_map/ppermute | solution.py:40

commit v7 on v6

--- a/solution.py
+++ b/solution.py
@@ -46,13 +46,13 @@
     return [pl.BlockSpec(memory_space=pltpu.VMEM)] * count
 
 
-def fine_kernel(g_ref, sp_ref, w_ref, gp_ref, r_ref):
+def fine_kernel(z_lo, z_hi, g_ref, sp_ref, w_ref, gp_ref, r_ref):
     planes_z, planes_x, part_ch, cells_y = sp_ref.shape
     wide = g_ref.shape[4]
     r_ref[...] = jnp.zeros(r_ref.shape, r_ref.dtype)
 
     def body(step, carry):
-        z = step // planes_x
+        z = z_lo + step // planes_x
         x = step % planes_x
         pre_act = sp_ref[z, x].astype(jnp.float32)
         slopes = jnp.where(pre_act > 0, 1.0, leak_slope).astype(jnp.float32)
@@ -73,14 +73,14 @@
             + total[part_ch : 2 * part_ch]
             + pltpu.roll(total[2 * part_ch :], 2, 1)
         )
-        gp_ref[z, x] = (grad_hidden * slopes).astype(gp_ref.dtype)
+        gp_ref[z - z_lo, x] = (grad_hidden * slopes).astype(gp_ref.dtype)
         return carry
 
-    lax.fori_loop(0, planes_z * planes_x, body, 0)
-
-
-def coarse_kernel(gp_ref, below_ref, c_ref, u_ref, gc_ref, gu_ref, y_ref):
-    planes_z = gp_ref.shape[0]
+    lax.fori_loop(0, (z_hi - z_lo) * planes_x, body, 0)
+
+
+def coarse_kernel(gp_ref, last_ref, below_ref, c_ref, u_ref, gc_ref, gu_ref, y_ref):
+    planes_z = gp_ref.shape[0] + 1
     cells_y = gp_ref.shape[2]
     rows_x = y_ref.shape[1] - 1
     part_ch = y_ref.shape[3]
@@ -93,7 +93,12 @@
     pick = (at_y == target).astype(jnp.bfloat16)
     y_ref[:, 0] = jnp.zeros(y_ref[:, 0].shape, y_ref.dtype)
     for zg in range(planes_z + 1):
-        source = below_ref[0] if zg == 0 else gp_ref[zg - 1]
+        if zg == 0:
+            source = below_ref[0]
+        elif zg == planes_z:
+            source = last_ref[0]
+        else:
+            source = gp_ref[zg - 1]
         picked = jnp.dot(source, pick, preferred_element_type=jnp.float32).astype(y_ref.dtype)
         for dy in range(3):
             part = picked[:, dy * half_y : (dy + 1) * half_y]
@@ -150,21 +155,27 @@
     refine_w = refine_cols.reshape(3, 3, 3, all_ch, part_ch)[:, ::-1]
     refine_w = jnp.transpose(refine_w, (0, 2, 4, 1, 3)).reshape(3, 3 * part_ch, 3 * all_ch)
 
-    grad_pre, refine_acc = pl.pallas_call(
-        fine_kernel,
-        out_shape=(
-            jax.ShapeDtypeStruct((planes_z, planes_x, part_ch, cells_y), jnp.bfloat16),
-            jax.ShapeDtypeStruct((3, 3 * all_ch, 3 * part_ch), jnp.float32),
-        ),
-        in_specs=vmem_specs(3),
-        out_specs=tuple(vmem_specs(2)),
-    )(rimmed, pre_rows, refine_w)
+    def fine_rows(z_lo, z_hi):
+        return pl.pallas_call(
+            functools.partial(fine_kernel, z_lo, z_hi),
+            out_shape=(
+                jax.ShapeDtypeStruct((z_hi - z_lo, planes_x, part_ch, cells_y), jnp.bfloat16),
+                jax.ShapeDtypeStruct((3, 3 * all_ch, 3 * part_ch), jnp.float32),
+            ),
+            in_specs=vmem_specs(3),
+            out_specs=tuple(vmem_specs(2)),
+        )(rimmed, pre_rows, refine_w)
+
+    grad_last, refine_last = fine_rows(planes_z - 1, planes_z)
+    last_rows = grad_last.reshape(1, planes_x * part_ch, cells_y)
+    below_z = passed_along(last_rows, ("gz", "sec"), 1)
+    grad_main, refine_main = fine_rows(0, planes_z - 1)
+    grad_rows = grad_main.reshape(planes_z - 1, planes_x * part_ch, cells_y)
+    refine_acc = refine_main + refine_last
     refine_terms = refine_acc.reshape(3, 3, all_ch, 3, part_ch)[:, ::-1]
     refine_terms = jnp.transpose(refine_terms, (0, 1, 3, 2, 4)).reshape(27, all_ch, part_ch)
     refine_terms = jnp.roll(refine_terms, channel_start, axis=1)
 
-    grad_rows = grad_pre.reshape(planes_z, planes_x * part_ch, cells_y)
-    below_z = passed_along(grad_rows[planes_z - 1 :], ("gz", "sec"), 1)
 
     coarse_own = jnp.transpose(coarse, (1, 2, 0, 3))
     coarse_rows = jnp.concatenate([coarse_own, lax.ppermute(coarse_own, "ch", swap)], axis=2)
@@ -182,12 +193,12 @@
             jax.ShapeDtypeStruct((coarse_z, coarse_x, coarse_in, cells_yc), jnp.float32),
             jax.ShapeDtypeStruct((3, 9 * part_ch, coarse_in), jnp.float32),
         ),
-        in_specs=vmem_specs(4),
+        in_specs=vmem_specs(5),
         out_specs=tuple(vmem_specs(2)),
         scratch_shapes=[
             pltpu.VMEM((planes_z + 1, planes_x + 1, 3, part_ch, cells_yc), jnp.bfloat16)
         ],
-    )(grad_rows, below_z, coarse_rows, up_w)
+    )(grad_rows, last_rows, below_z, coarse_rows, up_w)
     up_terms = jnp.roll(up_acc.reshape(27, part_ch, coarse_in), coarse_start, axis=2)
     own_k = coarse.shape[0]
     received = lax.ppermute(coarse_acc[:, :, own_k:], "ch", swap)

time: 80.7 us -> 79.9 us (0.990)
  waiting for transfers between devices: 28.4 us -> 21.9 us
  starting transfers between devices: 8.02 us -> 12 us
  Pallas kernels: 20.3 us -> 23 us
  local copies, waits for them, and re-layouts: 15.8 us -> 14 us
  other arithmetic: 6.95 us -> 7.87 us
    ppermute x1, waiting for transfers between devices: 4.3 us -> 0.01 us  [passed_along(): return lax.ppermute(block, axis, route)]
    ppermute x3, starting transfers between devices: 0.21 us -> 4.21 us  [summed_over_slabs(): block = block + lax.ppermute(block, axis, route)]
    pallas_call x1 -> x2, Pallas kernels: 15.5 us -> 18.2 us  [fine_rows(): pl.pallas_call(functools.partial(fine_kernel, z_lo, z_hi), out_shape=(jax...]
    ppermute x3, waiting for transfers between devices: 16.5 us -> 14.3 us  [summed_over_slabs(): block = block + lax.ppermute(block, axis, route)]
    pallas_call x1 -> x0, local copies, waits for them, and re-layouts: 0.99 us -> none  [local(): pl.pallas_call(fine_kernel, out_shape=(jax.ShapeDtypeStruct((planes_z, pl...]
    add x0 -> x1, other arithmetic: none -> 0.93 us  [local(): refine_acc = refine_main + refine_last]
    slice x1 -> x0, local copies, waits for them, and re-layouts: 0.91 us -> none  [local(): below_z = passed_along(grad_rows[planes_z - 1:], ('gz', 'sec'), 1)]
    unnamed x13 -> x15, local copies, waits for them, and re-layouts: 5.88 us -> 5.86 us
  transfers between devices with their start and end apart: 11 -> 11, of which waited for: 6 -> 5; matrix products, arithmetic and copies ran while one was open for 22% -> 21% of each run, Pallas kernels for 19% -> 23%
where the time goes in v7:
time: 79.9 us; the launch traced here: 79.6 us
  Pallas kernels  23 us (29%)
  waiting for transfers between devices  21.9 us (27%)
  local copies, waits for them, and re-layouts  14 us (18%)
  starting transfers between devices  12 us (15%)
  other arithmetic  7.87 us (10%)
  between operations  0.9 us (1%)
    pallas_call x2, Pallas kernels, fine_rows(): pl.pallas_call(functools.partial(fine_kernel, z_lo, z_hi), out_shape=(jax...  18.2 us
    ppermute x3, waiting for transfers between devices, summed_over_slabs(): block = block + lax.ppermute(block, axis, route)  14.3 us
    ppermute x1, starting transfers between devices, local(): high = lax.ppermute(rows[:2], ('gz', 'sec'), backward)  6.03 us
    unnamed x15, local copies, waits for them, and re-layouts  5.86 us
    ppermute x1, waiting for transfers between devices, local(): low = lax.ppermute(rows[planes_z - 2:], ('gz', 'sec'), forward)  4.89 us
    pallas_call x1, Pallas kernels, local(): pl.pallas_call(coarse_kernel, out_shape=(jax.ShapeDtypeStruct((coarse_z,...  4.8 us
    ppermute x3, starting transfers between devices, summed_over_slabs(): block = block + lax.ppermute(block, axis, route)  4.21 us
    concatenate x1, other arithmetic, local(): rimmed = jnp.concatenate([mine, other], axis=2)  3.39 us
  transfers between devices with their start and end apart: 11, of which 5 were waited for; matrix products, arithmetic and copies ran while one was open for 21% of the time, Pallas kernels for 23%

profile of v7, /device:TPU:0, one launch (start us, length us, event | category | flops | bytes accessed | tf_op | source)
XLA Modules:
  0.0 79.6 jit_solution(8407449997384633531)
XLA Ops:
  0.6 0.0 copy-start
  0.7 1.4 %copy.30 = bf16[16,4,8,512]{3,0,2,1:T(8,128)(2,1)S(1)} copy(bf16[16,4,8,512]{3,2,1,0:T(8,128)(2,1)} %param.7) | data formatting | bytes 1048576 | tf_op args[2]
  2.1 6.0 %collective-permute-start.1 = (bf16[2,8,16,512]{3,2,1,0:T(8,128)(2,1)S(1)}, bf16[2,8,16,512]{3,2,1,0:T(8,128)(2,1)S(1)}, u32[]{:S(2)}, u32[]{:S(2)}) collective-permute-start(bf16[2,8,16,512]{3,2,1,0:T(8,128)(2,1)S(1)} %get-tuple-element.22), channel_id=1, source_target_pairs={{2,0},{4,2},{6,4},{8,6},{10,8},{12,10},{14,12},{0,14},{3,1},{5,3},... | collective-permute-start | bytes 786440 | tf_op jit(solution)/shard_map/ppermute | solution.py:140
  8.1 0.9 %copy.31 = bf16[32,2,4,256]{3,0,2,1:T(8,128)(2,1)S(1)} copy(bf16[32,2,4,256]{3,2,1,0:T(4,128)(2,1)} %param.5) | data formatting | bytes 262144 | tf_op args[0]
  9.1 0.6 collective-permute-start.6
  9.6 1.1 %constant_dynamic-slice_fusion.1 = bf16[27,32,16]{2,1,0:T(8,128)(2,1)S(1)} fusion(bf16[27,32,32]{2,1,0:T(8,128)(2,1)} %param.9, s32[]{:T(128)S(6)} %select_n.47), kind=kLoop, calls=%fused_computation.27 | loop fusion | bytes 55300 | tf_op jit(solution)/shard_map/dynamic_slice | solution.py:153
  10.7 0.1 copy.23
  10.9 0.2 dynamic-slice_maximum_fusion.3
  11.0 2.7 %collective-permute-done.1 = bf16[2,8,16,512]{3,2,1,0:T(8,128)(2,1)S(1)} collective-permute-done((bf16[2,8,16,512]{3,2,1,0:T(8,128)(2,1)S(1)}, bf16[2,8,16,512]{3,2,1,0:T(8,128)(2,1)S(1)}, u32[]{:S(2)}, u32[]{:S(2)}) %collective-permute-start.1) | collective-permute-done | bytes 262176 | tf_op jit(solution)/shard_map/ppermute | solution.py:140
  13.7 4.9 %collective-permute-done = bf16[2,8,16,512]{3,2,1,0:T(8,128)(2,1)S(1)} collective-permute-done((bf16[2,8,16,512]{3,2,1,0:T(8,128)(2,1)S(1)}, bf16[2,8,16,512]{3,2,1,0:T(8,128)(2,1)S(1)}, u32[]{:S(2)}, u32[]{:S(2)}) %collective-permute-start) | collective-permute-done | bytes 262176 | tf_op jit(solution)/shard_map/ppermute | solution.py:139
  18.7 1.1 %copy.29 = bf16[16,4,8,512]{3,0,2,1:T(8,128)(2,1)} copy(bf16[16,4,8,512]{3,2,1,0:T(8,128)(2,1)S(1)} %copy-done.1) | data formatting | bytes 1048576 | tf_op args[1]
  19.8 0.1 copy.15
  19.8 0.7 reshape.58.w_ref
  20.6 0.2 dynamic-slice_maximum_fusion.2
  20.7 0.8 copy.17.u_ref
  21.5 0.0 collective-permute-done.2
  21.5 3.4 %fusion.1 = bf16[8,12,32,512]{3,2,1,0:T(8,128)(2,1)S(1)} fusion(bf16[2,8,16,512]{3,2,1,0:T(8,128)(2,1)S(1)} %collective-permute-done.4, bf16[2,8,16,512]{3,2,1,0:T(8,128)(2,1)S(1)} %collective-permute-done.1, bf16[4,8,16,512]{3,2,1,0:T(8,128)(2,1)S(1)} %collective-permute-done.3, bf16[2,8,16,512]{3,2,1,0:T(8,128)(2,1)S(1)} %collective-permute-done.2, ...), kind=kLoop, calls=%fused_computation.4 | loop fusion | flops 33030144 | bytes 5242880 | tf_op jit(solution)/shard_map/concatenate | solution.py:146
  24.9 2.1 %copy.28 = bf16[4,2,6,2,32,512]{5,4,2,3,0,1:T(8,128)(2,1)} copy(bf16[4,2,6,2,32,512]{5,4,3,2,1,0:T(8,128)(2,1)S(1)} %bitcast.32) | data formatting | bytes 6291456 | tf_op jit(solution)/shard_map/reshape | solution.py:149
  27.0 5.9 %shard_map.77 = (bf16[1,8,16,512]{3,2,1,0:T(8,128)(2,1)}, f32[3,96,48]{2,1,0:T(8,128)}) custom-call(bf16[2,4,2,6,32,512]{5,4,3,2,1,0:T(8,128)(2,1)} %bitcast.30, bf16[4,8,16,512]{3,2,1,0:T(8,128)(2,1)} %bitcast.36, bf16[3,48,96]{2,1,0:T(8,128)(2,1)} %reshape.58.w_ref), custom_call_target="tpu_custom_call" | custom-call | tf_op jit(solution)/shard_map/pallas_call | solution.py:159
  32.9 1.1 %collective-permute-start.5 = (bf16[1,128,512]{2,1,0:T(8,128)(2,1)}, bf16[1,128,512]{2,1,0:T(8,128)(2,1)S(1)}, u32[]{:S(2)}, u32[]{:S(2)}) collective-permute-start(bf16[1,128,512]{2,1,0:T(8,128)(2,1)} %bitcast.46), channel_id=1, source_target_pairs={{14,0},{0,2},{2,4},{4,6},{6,8},{8,10},{10,12},{12,14},{15,1},{1,3}... | collective-permute-start | bytes 393224 | tf_op jit(solution)/shard_map/ppermute | solution.py:30
  34.0 0.7 pad_maximum_fusion.c_ref
  34.7 12.3 %shard_map.76 = (bf16[3,8,16,512]{3,2,1,0:T(8,128)(2,1)}, f32[3,96,48]{2,1,0:T(8,128)}) custom-call(bf16[2,4,2,6,32,512]{5,4,3,2,1,0:T(8,128)(2,1)} %bitcast.31, bf16[4,8,16,512]{3,2,1,0:T(8,128)(2,1)} %bitcast.37, bf16[3,48,96]{2,1,0:T(8,128)(2,1)} %reshape.58.w_ref), custom_call_target="tpu_custom_call" | custom-call | tf_op jit(solution)/shard_map/pallas_call | solution.py:159
  46.9 0.9 %add.66 = f32[3,96,48]{2,1,0:T(8,128)S(1)} add(f32[3,96,48]{2,1,0:T(8,128)} %get-tuple-element.13, f32[3,96,48]{2,1,0:T(8,128)S(1)} %copy-done.2) | non-fusion elementwise | flops 13824 | bytes 165888 | tf_op jit(solution)/shard_map/add | solution.py:174
  47.9 0.1 copy.18
  48.0 0.2 reshape.65
  48.1 0.7 rev.7
  48.9 0.2 dynamic-slice_maximum_fusion
  49.1 0.2 copy.20
  49.3 0.2 reshape.67
  49.5 0.0 collective-permute-done.5.below_ref
  49.5 0.0 copy-start.3
  49.5 0.6 copy-done.3
  50.1 4.8 %shard_map.78 = (f32[2,4,64,256]{3,2,1,0:T(8,128)}, f32[3,144,64]{2,1,0:T(8,128)}) custom-call(bf16[3,128,512]{2,1,0:T(8,128)(2,1)} %bitcast.44, bf16[1,128,512]{2,1,0:T(8,128)(2,1)} %bitcast.47, bf16[1,128,512]{2,1,0:T(8,128)(2,1)} %copy-done.3, bf16[2,4,64,256]{3,2,1,0:T(8,128)(2,1)} %pad_maximum_fusion.c_ref, bf16[3,64,144]{2,1,0:T(8,128)(2,1)} %copy.17.u_ref), custom_call_target="tpu_custom_call" | custom-call | tf_op jit(solution)/shard_map/pallas_call | solution.py:190
  54.9 1.2 %dynamic-slice_maximum_fusion.1 = f32[27,16,64]{2,1,0:T(8,128)S(1)} fusion(s32[]{:T(128)S(6)} %select_n.53, f32[27,16,64]{2,1,0:T(8,128)} %bitcast.45), kind=kLoop, calls=%fused_computation.16 | loop fusion | flops 27648 | bytes 221188 | tf_op jit(solution)/shard_map/jit(_roll_dynamic)/concatenate | solution.py:202
  56.2 0.1 reshape.64
  56.3 1.2 %collective-permute-start.8 = (f32[41472]{0:T(1024)S(1)}, f32[41472]{0:T(1024)S(1)}, u32[]{:S(2)}, u32[]{:S(2)}) collective-permute-start(f32[41472]{0:T(1024)S(1)} %constant_dynamic-update-slice_fusion), channel_id=1, source_target_pairs={{0,2},{2,0},{4,6},{6,4},{8,10},{10,8},{12,14},{14,12},{1,3},{3,1},... | collective-permute-start | bytes 497672 | tf_op jit(solution)/shard_map/ppermute | solution.py:40
  57.5 1.0 %slice.29 = f32[2,4,32,256]{3,2,1,0:T(8,128)S(1)} slice(f32[2,4,64,256]{3,2,1,0:T(8,128)} %get-tuple-element.11), slice={[0:2], [0:4], [32:64], [0:256]} | slice | bytes 524288 | tf_op jit(solution)/shard_map/slice | solution.py:204
  58.5 0.1 collective-permute-start.7
  58.6 4.2 %collective-permute-done.8 = f32[41472]{0:T(1024)S(1)} collective-permute-done((f32[41472]{0:T(1024)S(1)}, f32[41472]{0:T(1024)S(1)}, u32[]{:S(2)}, u32[]{:S(2)}) %collective-permute-start.8) | collective-permute-done | bytes 165920 | tf_op jit(solution)/shard_map/ppermute | solution.py:40
  62.8 1.0 %collective-permute-start.9 = (f32[41472]{0:T(1024)S(1)}, f32[41472]{0:T(1024)S(1)}, u32[]{:S(2)}, u32[]{:S(2)}) collective-permute-start(f32[41472]{0:T(1024)S(1)} %add.69), channel_id=1, source_target_pairs={{0,4},{2,6},{4,0},{6,2},{8,12},{10,14},{12,8},{14,10},{1,5},{3,7},... | collective-permute-start | bytes 497672 | tf_op jit(solution)/shard_map/ppermute | solution.py:40
  63.8 4.7 %collective-permute-done.9 = f32[41472]{0:T(1024)S(1)} collective-permute-done((f32[41472]{0:T(1024)S(1)}, f32[41472]{0:T(1024)S(1)}, u32[]{:S(2)}, u32[]{:S(2)}) %collective-permute-start.9) | collective-permute-done | bytes 165920 | tf_op jit(solution)/shard_map/ppermute | solution.py:40
  68.5 2.0 %collective-permute-start.10 = (f32[41472]{0:T(1024)S(1)}, f32[41472]{0:T(1024)S(1)}, u32[]{:S(2)}, u32[]{:S(2)}) collective-permute-start(f32[41472]{0:T(1024)S(1)} %add.70), channel_id=1, source_target_pairs={{0,8},{2,10},{4,12},{6,14},{8,0},{10,2},{12,4},{14,6},{1,9},{3,11}... | collective-permute-start | bytes 497672 | tf_op jit(solution)/shard_map/ppermute | solution.py:40
  70.5 1.0 %fusion.5 = bf16[32,2,4,256]{3,0,2,1:T(8,128)(2,1)S(1)} fusion(f32[2,4,32,256]{3,2,1,0:T(8,128)S(1)} %collective-permute-done.7, f32[2,4,64,256]{3,2,1,0:T(8,128)} %get-tuple-element.11), kind=kLoop, calls=%fused_computation.17 | loop fusion | flops 131072 | bytes 655360 | tf_op jit(solution)/shard_map/convert_element_type | solution.py:206
  71.5 0.8 copy.21
  72.2 5.5 %collective-permute-done.10 = f32[41472]{0:T(1024)S(1)} collective-permute-done((f32[41472]{0:T(1024)S(1)}, f32[41472]{0:T(1024)S(1)}, u32[]{:S(2)}, u32[]{:S(2)}) %collective-permute-start.10) | collective-permute-done | bytes 165920 | tf_op jit(solution)/shard_map/ppermute | solution.py:40
  77.8 0.8 mul.28
  78.5 0.2 mul.31
  78.7 0.9 %copy.22 = f32[27,32,16]{1,2,0:T(8,128)} copy(f32[27,32,16]{2,1,0:T(8,128)S(1)} %mul.31) | data formatting | bytes 110592
  (24 shorter events, 0.2 us)
Async XLA Ops:
  0.6 19.9 %copy-start = (bf16[27,32,64]{2,1,0:T(8,128)(2,1)S(1)}, bf16[27,32,64]{2,1,0:T(8,128)(2,1)}, u32[]{:S(2)}) copy-start(bf16[27,32,64]{2,1,0:T(8,128)(2,1)} %param.8) | copy-start | bytes 331780
  0.6 18.0 %copy-start.1 = (bf16[16,4,8,512]{3,2,1,0:T(8,128)(2,1)S(1)}, bf16[16,4,8,512]{3,2,1,0:T(8,128)(2,1)}, u32[]{:S(2)}) copy-start(bf16[16,4,8,512]{3,2,1,0:T(8,128)(2,1)} %param.6) | copy-start | bytes 1572868
  2.1 11.6 %collective-permute-start.1 = (bf16[2,8,16,512]{3,2,1,0:T(8,128)(2,1)S(1)}, bf16[2,8,16,512]{3,2,1,0:T(8,128)(2,1)S(1)}, u32[]{:S(2)}, u32[]{:S(2)}) collective-permute-start(bf16[2,8,16,512]{3,2,1,0:T(8,128)(2,1)S(1)} %get-tuple-element.22), channel_id=1, source_target_pairs={{2,0},{4,2},{6,4},{8,6},{10,8},{12,10},{14,12},{0,14},{3,1},{5,3},... | collective-permute-start | bytes 786440 | tf_op jit(solution)/shard_map/ppermute | solution.py:140
  8.1 10.5 %collective-permute-start = (bf16[2,8,16,512]{3,2,1,0:T(8,128)(2,1)S(1)}, bf16[2,8,16,512]{3,2,1,0:T(8,128)(2,1)S(1)}, u32[]{:S(2)}, u32[]{:S(2)}) collective-permute-start(bf16[2,8,16,512]{3,2,1,0:T(8,128)(2,1)S(1)} %get-tuple-element.21), channel_id=1, source_target_pairs={{0,2},{2,4},{4,6},{6,8},{8,10},{10,12},{12,14},{14,0},{1,3},{3,5},... | collective-permute-start | bytes 786440 | tf_op jit(solution)/shard_map/ppermute | solution.py:139
  8.1 13.4 %collective-permute-start.3 = (bf16[4,8,16,512]{3,2,1,0:T(8,128)(2,1)S(1)}, bf16[4,8,16,512]{3,2,1,0:T(8,128)(2,1)S(1)}, u32[]{:S(2)}, u32[]{:S(2)}) collective-permute-start(bf16[4,8,16,512]{3,2,1,0:T(8,128)(2,1)S(1)} %bitcast.34), channel_id=1, source_target_pairs={{0,1},{1,0},{2,3},{3,2},{4,5},{5,4},{6,7},{7,6},{8,9},{9,8},{10,11... | collective-permute-start | bytes 1572872 | tf_op jit(solution)/shard_map/ppermute | solution.py:141
  9.1 24.9 %collective-permute-start.6 = (bf16[2,4,32,256]{3,2,1,0:T(8,128)(2,1)S(1)}, bf16[2,4,32,256]{3,2,1,0:T(8,128)(2,1)S(1)}, u32[]{:S(2)}, u32[]{:S(2)}) collective-permute-start(bf16[2,4,32,256]{3,2,1,0:T(8,128)(2,1)S(1)} %bitcast.40), channel_id=1, source_target_pairs={{0,1},{1,0},{2,3},{3,2},{4,5},{5,4},{6,7},{7,6},{8,9},{9,8},{10,11... | collective-permute-start | bytes 393224 | tf_op jit(solution)/shard_map/ppermute | solution.py:181
  13.7 7.8 %collective-permute-start.4 = (bf16[2,8,16,512]{3,2,1,0:T(8,128)(2,1)S(1)}, bf16[2,8,16,512]{3,2,1,0:T(8,128)(2,1)S(1)}, u32[]{:S(2)}, u32[]{:S(2)}) collective-permute-start(bf16[2,8,16,512]{3,2,1,0:T(8,128)(2,1)S(1)} %collective-permute-done.1), channel_id=1, source_target_pairs={{0,1},{1,0},{2,3},{3,2},{4,5},{5,4},{6,7},{7,6},{8,9},{9,8},{10,11... | collective-permute-start | bytes 786440 | tf_op jit(solution)/shard_map/ppermute | solution.py:143
  18.6 2.9 %collective-permute-start.2 = (bf16[2,8,16,512]{3,2,1,0:T(8,128)(2,1)S(1)}, bf16[2,8,16,512]{3,2,1,0:T(8,128)(2,1)S(1)}, u32[]{:S(2)}, u32[]{:S(2)}) collective-permute-start(bf16[2,8,16,512]{3,2,1,0:T(8,128)(2,1)S(1)} %collective-permute-done), channel_id=1, source_target_pairs={{0,1},{1,0},{2,3},{3,2},{4,5},{5,4},{6,7},{7,6},{8,9},{9,8},{10,11... | collective-permute-start | bytes 786440 | tf_op jit(solution)/shard_map/ppermute | solution.py:142
  32.9 14.1 %copy-start.2 = (f32[3,96,48]{2,1,0:T(8,128)S(1)}, f32[3,96,48]{2,1,0:T(8,128)}, u32[]{:S(2)}) copy-start(f32[3,96,48]{2,1,0:T(8,128)} %get-tuple-element.14) | copy-start | bytes 165892
  32.9 16.6 %collective-permute-start.5 = (bf16[1,128,512]{2,1,0:T(8,128)(2,1)}, bf16[1,128,512]{2,1,0:T(8,128)(2,1)S(1)}, u32[]{:S(2)}, u32[]{:S(2)}) collective-permute-start(bf16[1,128,512]{2,1,0:T(8,128)(2,1)} %bitcast.46), channel_id=1, source_target_pairs={{14,0},{0,2},{2,4},{4,6},{6,8},{8,10},{10,12},{12,14},{15,1},{1,3}... | collective-permute-start | bytes 393224 | tf_op jit(solution)/shard_map/ppermute | solution.py:30
  49.5 0.7 copy-start.3
  56.3 6.5 %collective-permute-start.8 = (f32[41472]{0:T(1024)S(1)}, f32[41472]{0:T(1024)S(1)}, u32[]{:S(2)}, u32[]{:S(2)}) collective-permute-start(f32[41472]{0:T(1024)S(1)} %constant_dynamic-update-slice_fusion), channel_id=1, source_target_pairs={{0,2},{2,0},{4,6},{6,4},{8,10},{10,8},{12,14},{14,12},{1,3},{3,1},... | collective-permute-start | bytes 497672 | tf_op jit(solution)/shard_map/ppermute | solution.py:40
  58.5 12.0 %collective-permute-start.7 = (f32[2,4,32,256]{3,2,1,0:T(8,128)S(1)}, f32[2,4,32,256]{3,2,1,0:T(8,128)S(1)}, u32[]{:S(2)}, u32[]{:S(2)}) collective-permute-start(f32[2,4,32,256]{3,2,1,0:T(8,128)S(1)} %slice.29), channel_id=1, source_target_pairs={{0,1},{1,0},{2,3},{3,2},{4,5},{5,4},{6,7},{7,6},{8,9},{9,8},{10,11... | collective-permute-start | bytes 786440 | tf_op jit(solution)/shard_map/ppermute | solution.py:204
  62.8 5.6 %collective-permute-start.9 = (f32[41472]{0:T(1024)S(1)}, f32[41472]{0:T(1024)S(1)}, u32[]{:S(2)}, u32[]{:S(2)}) collective-permute-start(f32[41472]{0:T(1024)S(1)} %add.69), channel_id=1, source_target_pairs={{0,4},{2,6},{4,0},{6,2},{8,12},{10,14},{12,8},{14,10},{1,5},{3,7},... | collective-permute-start | bytes 497672 | tf_op jit(solution)/shard_map/ppermute | solution.py:40
  68.5 9.2 %collective-permute-start.10 = (f32[41472]{0:T(1024)S(1)}, f32[41472]{0:T(1024)S(1)}, u32[]{:S(2)}, u32[]{:S(2)}) collective-permute-start(f32[41472]{0:T(1024)S(1)} %add.70), channel_id=1, source_target_pairs={{0,8},{2,10},{4,12},{6,14},{8,0},{10,2},{12,4},{14,6},{1,9},{3,11}... | collective-permute-start | bytes 497672 | tf_op jit(solution)/shard_map/ppermute | solution.py:40

commit v8 on v7

--- a/solution.py
+++ b/solution.py
@@ -46,10 +46,35 @@
     return [pl.BlockSpec(memory_space=pltpu.VMEM)] * count
 
 
-def fine_kernel(z_lo, z_hi, g_ref, sp_ref, w_ref, gp_ref, r_ref):
+def fine_kernel(z_lo, z_hi, *refs):
+    pieces = refs[:6]
+    sp_ref, w_ref, gp_ref, r_ref, g_ref, sems = refs[6:]
     planes_z, planes_x, part_ch, cells_y = sp_ref.shape
-    wide = g_ref.shape[4]
+    wide = g_ref.shape[3]
+    low_count = pieces[0].shape[0]
+    needed = sorted({z + 4 - 2 * dz for z in range(z_lo, z_hi) for dz in range(3)})
+    edge = jnp.zeros(g_ref[:, :, 0:2].shape, g_ref.dtype)
+    g_ref[:, :, 0:2] = edge
+    g_ref[:, :, planes_x + 2 :] = edge
+    copies = []
+    for plane in needed:
+        if plane < low_count:
+            part, at = 0, plane
+        elif plane < low_count + planes_z:
+            part, at = 1, plane - low_count
+        else:
+            part, at = 2, plane - low_count - planes_z
+        for half in range(2):
+            copy = pltpu.make_async_copy(
+                pieces[3 * half + part].at[at],
+                g_ref.at[plane % 2, plane // 2, pl.ds(2, planes_x), pl.ds(half * part_ch, part_ch)],
+                sems.at[len(copies)],
+            )
+            copy.start()
+            copies.append(copy)
     r_ref[...] = jnp.zeros(r_ref.shape, r_ref.dtype)
+    for copy in copies:
+        copy.wait()
 
     def body(step, carry):
         z = z_lo + step // planes_x
@@ -61,11 +86,11 @@
             [pltpu.roll(hidden, 2, 1), hidden, pltpu.roll(hidden, cells_y - 2, 1)], axis=0
         ).astype(jnp.bfloat16)
         total = jnp.zeros((3 * part_ch, cells_y), jnp.float32)
-        for dz in range(3):
-            block = g_ref[z % 2, z // 2 + 2 - dz, x % 2, pl.ds(x // 2, 3)]
+        for dx in range(3):
+            block = g_ref[z % 2, pl.ds(z // 2, 3), x + 4 - 2 * dx]
             block = block.reshape(3 * wide, cells_y)
-            total = total + jnp.dot(w_ref[dz], block, preferred_element_type=jnp.float32)
-            r_ref[dz] += lax.dot_general(
+            total = total + jnp.dot(w_ref[dx], block, preferred_element_type=jnp.float32)
+            r_ref[dx] += lax.dot_general(
                 block, rolled, (((1,), (1,)), ((), ())), preferred_element_type=jnp.float32
             )
         grad_hidden = (
@@ -141,19 +166,13 @@
     rows_other = lax.ppermute(rows, "ch", swap)
     low_other = lax.ppermute(low, "ch", swap)
     high_other = lax.ppermute(high, "ch", swap)
-    mine = jnp.concatenate([low, rows, high], axis=0)
-    other = jnp.concatenate([low_other, rows_other, high_other], axis=0)
-    rimmed = jnp.concatenate([mine, other], axis=2)
-    rimmed = jnp.pad(rimmed, ((0, 0), (2, 2), (0, 0), (0, 0)))
-    halo_z, halo_x = rimmed.shape[0], rimmed.shape[1]
-    rimmed = rimmed.reshape(halo_z // 2, 2, halo_x // 2, 2, all_ch, cells_y)
-    rimmed = jnp.transpose(rimmed, (1, 0, 3, 2, 4, 5))
+    halo_z = low.shape[0] + planes_z + high.shape[0]
     pre_rows = jnp.transpose(saved_pre, (1, 2, 0, 3))
 
     refine_cols = lax.dynamic_slice_in_dim(refine_weight, channel_start, part_ch, 2)
     refine_cols = jnp.roll(refine_cols, -channel_start, axis=1)
-    refine_w = refine_cols.reshape(3, 3, 3, all_ch, part_ch)[:, ::-1]
-    refine_w = jnp.transpose(refine_w, (0, 2, 4, 1, 3)).reshape(3, 3 * part_ch, 3 * all_ch)
+    refine_w = refine_cols.reshape(3, 3, 3, all_ch, part_ch)[::-1]
+    refine_w = jnp.transpose(refine_w, (1, 2, 4, 0, 3)).reshape(3, 3 * part_ch, 3 * all_ch)
 
     def fine_rows(z_lo, z_hi):
         return pl.pallas_call(
@@ -162,9 +181,13 @@
                 jax.ShapeDtypeStruct((z_hi - z_lo, planes_x, part_ch, cells_y), jnp.bfloat16),
                 jax.ShapeDtypeStruct((3, 3 * all_ch, 3 * part_ch), jnp.float32),
             ),
-            in_specs=vmem_specs(3),
+            in_specs=[pl.BlockSpec(memory_space=pl.ANY)] * 6 + vmem_specs(2),
             out_specs=tuple(vmem_specs(2)),
-        )(rimmed, pre_rows, refine_w)
+            scratch_shapes=[
+                pltpu.VMEM((2, halo_z // 2, planes_x + 4, all_ch, cells_y), jnp.bfloat16),
+                pltpu.SemaphoreType.DMA((4 * halo_z,)),
+            ],
+        )(low, rows, high, low_other, rows_other, high_other, pre_rows, refine_w)
 
     grad_last, refine_last = fine_rows(planes_z - 1, planes_z)
     last_rows = grad_last.reshape(1, planes_x * part_ch, cells_y)
@@ -173,7 +196,7 @@
     grad_rows = grad_main.reshape(planes_z - 1, planes_x * part_ch, cells_y)
     refine_acc = refine_main + refine_last
     refine_terms = refine_acc.reshape(3, 3, all_ch, 3, part_ch)[:, ::-1]
-    refine_terms = jnp.transpose(refine_terms, (0, 1, 3, 2, 4)).reshape(27, all_ch, part_ch)
+    refine_terms = jnp.transpose(refine_terms, (1, 0, 3, 2, 4)).reshape(27, all_ch, part_ch)
     refine_terms = jnp.roll(refine_terms, channel_start, axis=1)
 
 

time: 79.9 us -> 77.1 us (0.965)
  other arithmetic: 7.87 us -> 3.57 us
  local copies, waits for them, and re-layouts: 14 us -> 11.3 us
  starting transfers between devices: 12 us -> 14 us
  Pallas kernels: 23 us -> 24.4 us
    concatenate x1 -> x0, other arithmetic: 3.39 us -> none  [local(): rimmed = jnp.concatenate([mine, other], axis=2)]
    ppermute x1, starting transfers between devices: 6.03 us -> 3.04 us  [local(): high = lax.ppermute(rows[:2], ('gz', 'sec'), backward)]
    ppermute x1, starting transfers between devices: 0.01 us -> 2.94 us  [local(): low = lax.ppermute(rows[planes_z - 2:], ('gz', 'sec'), forward)]
    ppermute x3, starting transfers between devices: 4.21 us -> 6.71 us  [summed_over_slabs(): block = block + lax.ppermute(block, axis, route)]
    ppermute x1, waiting for transfers between devices: 4.89 us -> 7.38 us  [local(): low = lax.ppermute(rows[planes_z - 2:], ('gz', 'sec'), forward)]
    reshape x2 -> x1, local copies, waits for them, and re-layouts: 2.8 us -> 0.74 us  [local(): jnp.transpose(refine_w, (1, 2, 4, 0, 3)).reshape(3, 3 * part_ch, 3 * all_ch)]
    pallas_call x2, Pallas kernels: 18.2 us -> 19.6 us  [fine_rows(): pl.pallas_call(functools.partial(fine_kernel, z_lo, z_hi), out_shape=(jax...]
    ppermute x3, waiting for transfers between devices: 14.3 us -> 13.2 us  [summed_over_slabs(): block = block + lax.ppermute(block, axis, route)]
  transfers between devices with their start and end apart: 11 -> 11, of which waited for: 5 -> 5; matrix products, arithmetic and copies ran while one was open for 21% -> 10% of each run, Pallas kernels for 23% -> 26%
where the time goes in v8:
time: 77.1 us; the launch traced here: 76.8 us
  Pallas kernels  24.4 us (32%)
  waiting for transfers between devices  22.5 us (29%)
  starting transfers between devices  14 us (18%)
  local copies, waits for them, and re-layouts  11.3 us (15%)
  other arithmetic  3.57 us (5%)
  between operations  0.98 us (1%)
    pallas_call x2, Pallas kernels, fine_rows(): pl.pallas_call(functools.partial(fine_kernel, z_lo, z_hi), out_shape=(jax...  19.6 us
    ppermute x3, waiting for transfers between devices, summed_over_slabs(): block = block + lax.ppermute(block, axis, route)  13.2 us
    ppermute x1, waiting for transfers between devices, local(): low = lax.ppermute(rows[planes_z - 2:], ('gz', 'sec'), forward)  7.38 us
    ppermute x3, starting transfers between devices, summed_over_slabs(): block = block + lax.ppermute(block, axis, route)  6.71 us
    unnamed x33, local copies, waits for them, and re-layouts  6.47 us
    pallas_call x1, Pallas kernels, local(): pl.pallas_call(coarse_kernel, out_shape=(jax.ShapeDtypeStruct((coarse_z,...  4.8 us
    ppermute x1, starting transfers between devices, local(): high = lax.ppermute(rows[:2], ('gz', 'sec'), backward)  3.04 us
    ppermute x1, starting transfers between devices, local(): low = lax.ppermute(rows[planes_z - 2:], ('gz', 'sec'), forward)  2.94 us
  transfers between devices with their start and end apart: 11, of which 5 were waited for; matrix products, arithmetic and copies ran while one was open for 10% of the time, Pallas kernels for 26%

profile of v8, /device:TPU:0, one launch (start us, length us, event | category | flops | bytes accessed | tf_op | source)
XLA Modules:
  0.0 76.8 jit_solution(5355044733799443303)
XLA Ops:
  0.6 0.0 copy-start
  0.6 1.4 %copy.28 = bf16[16,4,8,512]{3,0,2,1:T(8,128)(2,1)S(1)} copy(bf16[16,4,8,512]{3,2,1,0:T(8,128)(2,1)} %param.7) | data formatting | bytes 1048576 | tf_op args[2]
  2.0 0.0 copy-start.11
  2.0 0.7 fusion.1
  2.8 2.9 %collective-permute-start = (bf16[2,8,16,512]{3,2,1,0:T(8,128)(2,1)}, bf16[2,8,16,512]{3,2,1,0:T(8,128)(2,1)S(1)}, u32[]{:S(2)}, u32[]{:S(2)}) collective-permute-start(bf16[2,8,16,512]{3,2,1,0:T(8,128)(2,1)} %get-tuple-element.22), channel_id=1, source_target_pairs={{0,2},{2,4},{4,6},{6,8},{8,10},{10,12},{12,14},{14,0},{1,3},{3,5},... | collective-permute-start | bytes 786440 | tf_op jit(solution)/shard_map/ppermute | solution.py:164
  5.7 3.0 %collective-permute-start.1 = (bf16[2,8,16,512]{3,2,1,0:T(8,128)(2,1)S(1)}, bf16[2,8,16,512]{3,2,1,0:T(8,128)(2,1)S(1)}, u32[]{:S(2)}, u32[]{:S(2)}) collective-permute-start(bf16[2,8,16,512]{3,2,1,0:T(8,128)(2,1)S(1)} %get-tuple-element.21), channel_id=1, source_target_pairs={{2,0},{4,2},{6,4},{8,6},{10,8},{12,10},{14,12},{0,14},{3,1},{5,3},... | collective-permute-start | bytes 786440 | tf_op jit(solution)/shard_map/ppermute | solution.py:165
  8.8 0.6 collective-permute-start.6
  9.4 0.1 constant_dynamic-slice_fusion.1
  9.5 0.1 copy.23
  9.7 0.2 dynamic-slice_maximum_fusion.3
  9.8 0.0 copy-start.7
  9.8 7.4 %collective-permute-done.refs_0_ = bf16[2,8,16,512]{3,2,1,0:T(8,128)(2,1)S(1)} collective-permute-done((bf16[2,8,16,512]{3,2,1,0:T(8,128)(2,1)}, bf16[2,8,16,512]{3,2,1,0:T(8,128)(2,1)S(1)}, u32[]{:S(2)}, u32[]{:S(2)}) %collective-permute-start) | collective-permute-done | bytes 262176 | tf_op jit(solution)/shard_map/ppermute | solution.py:164
  17.2 1.9 %collective-permute-done.1.refs_2_ = bf16[2,8,16,512]{3,2,1,0:T(8,128)(2,1)S(1)} collective-permute-done((bf16[2,8,16,512]{3,2,1,0:T(8,128)(2,1)S(1)}, bf16[2,8,16,512]{3,2,1,0:T(8,128)(2,1)S(1)}, u32[]{:S(2)}, u32[]{:S(2)}) %collective-permute-start.1) | collective-permute-done | bytes 262176 | tf_op jit(solution)/shard_map/ppermute | solution.py:165
  19.2 0.1 copy.15
  19.3 0.6 copy-done.4
  19.8 0.7 reshape.54.refs_7_
  20.6 1.1 %copy.27 = bf16[16,4,8,512]{3,0,2,1:T(8,128)(2,1)} copy(bf16[16,4,8,512]{3,2,1,0:T(8,128)(2,1)S(1)} %copy-done.7) | data formatting | bytes 1048576 | tf_op args[1]
  21.7 0.2 dynamic-slice_maximum_fusion.2
  21.8 0.8 copy.17.u_ref
  22.6 0.7 copy-done.5
  23.3 0.1 copy-done.6
  23.4 0.2 copy-done.2
  23.6 6.4 %shard_map.77 = (bf16[1,8,16,512]{3,2,1,0:T(8,128)(2,1)}, f32[3,96,48]{2,1,0:T(8,128)}) custom-call(bf16[2,8,16,512]{3,2,1,0:T(8,128)(2,1)} %copy-done.3, bf16[4,8,16,512]{3,2,1,0:T(8,128)(2,1)} %bitcast.28, bf16[2,8,16,512]{3,2,1,0:T(8,128)(2,1)} %copy-done.4, bf16[2,8,16,512]{3,2,1,0:T(8,128)(2,1)} %copy-done.5, bf16[4,8,16,512]{3,2,1,0:T(8,128)(2,1)} %copy-done.2, ...), custom_call_target="tpu_custom_call" | custom-call | tf_op jit(solution)/shard_map/pallas_call | solution.py:178
  30.0 0.6 collective-permute-start.5
  30.6 0.7 pad_maximum_fusion.c_ref
  31.4 13.2 %shard_map.76 = (bf16[3,8,16,512]{3,2,1,0:T(8,128)(2,1)}, f32[3,96,48]{2,1,0:T(8,128)}) custom-call(bf16[2,8,16,512]{3,2,1,0:T(8,128)(2,1)} %copy-done.3, bf16[4,8,16,512]{3,2,1,0:T(8,128)(2,1)} %bitcast.29, bf16[2,8,16,512]{3,2,1,0:T(8,128)(2,1)} %copy-done.4, bf16[2,8,16,512]{3,2,1,0:T(8,128)(2,1)} %copy-done.5, bf16[4,8,16,512]{3,2,1,0:T(8,128)(2,1)} %copy-done.2, ...), custom_call_target="tpu_custom_call" | custom-call | tf_op jit(solution)/shard_map/pallas_call | solution.py:178
  44.6 0.9 %add.64 = f32[3,96,48]{2,1,0:T(8,128)S(1)} add(f32[3,96,48]{2,1,0:T(8,128)} %get-tuple-element.13, f32[3,96,48]{2,1,0:T(8,128)S(1)} %copy-done.10) | non-fusion elementwise | flops 13824 | bytes 165888 | tf_op jit(solution)/shard_map/add | solution.py:197
  45.5 0.1 copy.18
  45.6 0.2 reshape.61
  45.8 0.7 rev.7
  46.5 0.2 dynamic-slice_maximum_fusion
  46.7 0.2 copy.20
  46.9 0.2 reshape.63
  47.1 0.6 copy-done.12
  47.8 4.8 %shard_map.78 = (f32[2,4,64,256]{3,2,1,0:T(8,128)}, f32[3,144,64]{2,1,0:T(8,128)}) custom-call(bf16[3,128,512]{2,1,0:T(8,128)(2,1)} %bitcast.38, bf16[1,128,512]{2,1,0:T(8,128)(2,1)} %bitcast.41, bf16[1,128,512]{2,1,0:T(8,128)(2,1)} %copy-done.12, bf16[2,4,64,256]{3,2,1,0:T(8,128)(2,1)} %pad_maximum_fusion.c_ref, bf16[3,64,144]{2,1,0:T(8,128)(2,1)} %copy.17.u_ref), custom_call_target="tpu_custom_call" | custom-call | tf_op jit(solution)/shard_map/pallas_call | solution.py:213
  52.6 1.3 %dynamic-slice_maximum_fusion.1 = f32[27,16,64]{2,1,0:T(8,128)S(1)} fusion(s32[]{:T(128)S(6)} %select_n.53, f32[27,16,64]{2,1,0:T(8,128)} %bitcast.39), kind=kLoop, calls=%fused_computation.5 | loop fusion | flops 27648 | bytes 221188 | tf_op jit(solution)/shard_map/jit(_roll_dynamic)/concatenate | solution.py:225
  53.9 0.1 reshape.60
  54.0 2.4 %collective-permute-start.8 = (f32[41472]{0:T(1024)S(1)}, f32[41472]{0:T(1024)S(1)}, u32[]{:S(2)}, u32[]{:S(2)}) collective-permute-start(f32[41472]{0:T(1024)S(1)} %constant_dynamic-update-slice_fusion), channel_id=1, source_target_pairs={{0,2},{2,0},{4,6},{6,4},{8,10},{10,8},{12,14},{14,12},{1,3},{3,1},... | collective-permute-start | bytes 497672 | tf_op jit(solution)/shard_map/ppermute | solution.py:40
  56.5 0.1 collective-permute-start.7
  56.5 4.1 %collective-permute-done.8 = f32[41472]{0:T(1024)S(1)} collective-permute-done((f32[41472]{0:T(1024)S(1)}, f32[41472]{0:T(1024)S(1)}, u32[]{:S(2)}, u32[]{:S(2)}) %collective-permute-start.8) | collective-permute-done | bytes 165920 | tf_op jit(solution)/shard_map/ppermute | solution.py:40
  60.7 1.6 %collective-permute-start.9 = (f32[41472]{0:T(1024)S(1)}, f32[41472]{0:T(1024)S(1)}, u32[]{:S(2)}, u32[]{:S(2)}) collective-permute-start(f32[41472]{0:T(1024)S(1)} %add.67), channel_id=1, source_target_pairs={{0,4},{2,6},{4,0},{6,2},{8,12},{10,14},{12,8},{14,10},{1,5},{3,7},... | collective-permute-start | bytes 497672 | tf_op jit(solution)/shard_map/ppermute | solution.py:40
  62.3 3.8 %collective-permute-done.9 = f32[41472]{0:T(1024)S(1)} collective-permute-done((f32[41472]{0:T(1024)S(1)}, f32[41472]{0:T(1024)S(1)}, u32[]{:S(2)}, u32[]{:S(2)}) %collective-permute-start.9) | collective-permute-done | bytes 165920 | tf_op jit(solution)/shard_map/ppermute | solution.py:40
  66.1 2.6 %collective-permute-start.10 = (f32[41472]{0:T(1024)S(1)}, f32[41472]{0:T(1024)S(1)}, u32[]{:S(2)}, u32[]{:S(2)}) collective-permute-start(f32[41472]{0:T(1024)S(1)} %add.68), channel_id=1, source_target_pairs={{0,8},{2,10},{4,12},{6,14},{8,0},{10,2},{12,4},{14,6},{1,9},{3,11}... | collective-permute-start | bytes 497672 | tf_op jit(solution)/shard_map/ppermute | solution.py:40
  68.8 0.8 copy.21
  69.6 5.3 %collective-permute-done.10 = f32[41472]{0:T(1024)S(1)} collective-permute-done((f32[41472]{0:T(1024)S(1)}, f32[41472]{0:T(1024)S(1)}, u32[]{:S(2)}, u32[]{:S(2)}) %collective-permute-start.10) | collective-permute-done | bytes 165920 | tf_op jit(solution)/shard_map/ppermute | solution.py:40
  74.9 0.2 mul.31
  75.1 0.9 %copy.22 = f32[27,32,16]{1,2,0:T(8,128)} copy(f32[27,32,16]{2,1,0:T(8,128)S(1)} %mul.31) | data formatting | bytes 110592
  76.0 0.8 %mul.28 = f32[27,16,64]{2,1,0:T(8,128)} reshape(f32[27648]{0:T(1024)S(1)} %slice_multiply_fusion) | data formatting | bytes 221184 | tf_op jit(solution)/shard_map/mul | solution.py:236
  (40 shorter events, 0.3 us)
Async XLA Ops:
  0.6 18.5 %copy-start = (bf16[27,32,64]{2,1,0:T(8,128)(2,1)S(1)}, bf16[27,32,64]{2,1,0:T(8,128)(2,1)}, u32[]{:S(2)}) copy-start(bf16[27,32,64]{2,1,0:T(8,128)(2,1)} %param.8) | copy-start | bytes 331780
  2.0 6.8 %copy-start.1 = (bf16[16,4,8,512]{3,0,2,1:T(8,128)(2,1)}, bf16[16,4,8,512]{3,0,2,1:T(8,128)(2,1)S(1)}, u32[]{:S(2)}) copy-start(bf16[16,4,8,512]{3,0,2,1:T(8,128)(2,1)S(1)} %copy.28) | copy-start | bytes 1572868
  2.0 6.7 %copy-start.11 = (bf16[32,2,4,256]{3,2,1,0:T(4,128)(2,1)S(1)}, bf16[32,2,4,256]{3,2,1,0:T(4,128)(2,1)}, u32[]{:S(2)}) copy-start(bf16[32,2,4,256]{3,2,1,0:T(4,128)(2,1)} %param.5) | copy-start | bytes 393220
  2.8 6.6 %copy-start.9 = (bf16[27,32,32]{2,1,0:T(8,128)(2,1)S(1)}, bf16[27,32,32]{2,1,0:T(8,128)(2,1)}, u32[]{:S(2)}) copy-start(bf16[27,32,32]{2,1,0:T(8,128)(2,1)} %param.9) | copy-start | bytes 165892
  2.8 14.4 %collective-permute-start = (bf16[2,8,16,512]{3,2,1,0:T(8,128)(2,1)}, bf16[2,8,16,512]{3,2,1,0:T(8,128)(2,1)S(1)}, u32[]{:S(2)}, u32[]{:S(2)}) collective-permute-start(bf16[2,8,16,512]{3,2,1,0:T(8,128)(2,1)} %get-tuple-element.22), channel_id=1, source_target_pairs={{0,2},{2,4},{4,6},{6,8},{8,10},{10,12},{12,14},{14,0},{1,3},{3,5},... | collective-permute-start | bytes 786440 | tf_op jit(solution)/shard_map/ppermute | solution.py:164
  5.7 13.4 %collective-permute-start.1 = (bf16[2,8,16,512]{3,2,1,0:T(8,128)(2,1)S(1)}, bf16[2,8,16,512]{3,2,1,0:T(8,128)(2,1)S(1)}, u32[]{:S(2)}, u32[]{:S(2)}) collective-permute-start(bf16[2,8,16,512]{3,2,1,0:T(8,128)(2,1)S(1)} %get-tuple-element.21), channel_id=1, source_target_pairs={{2,0},{4,2},{6,4},{8,6},{10,8},{12,10},{14,12},{0,14},{3,1},{5,3},... | collective-permute-start | bytes 786440 | tf_op jit(solution)/shard_map/ppermute | solution.py:165
  8.8 13.8 %collective-permute-start.3 = (bf16[4,8,16,512]{3,2,1,0:T(8,128)(2,1)S(1)}, bf16[4,8,16,512]{3,2,1,0:T(8,128)(2,1)S(1)}, u32[]{:S(2)}, u32[]{:S(2)}) collective-permute-start(bf16[4,8,16,512]{3,2,1,0:T(8,128)(2,1)S(1)} %bitcast.27), channel_id=1, source_target_pairs={{0,1},{1,0},{2,3},{3,2},{4,5},{5,4},{6,7},{7,6},{8,9},{9,8},{10,11... | collective-permute-start | bytes 1572872 | tf_op jit(solution)/shard_map/ppermute | solution.py:166
  8.8 21.8 %collective-permute-start.6 = (bf16[2,4,32,256]{3,2,1,0:T(8,128)(2,1)S(1)}, bf16[2,4,32,256]{3,2,1,0:T(8,128)(2,1)S(1)}, u32[]{:S(2)}, u32[]{:S(2)}) collective-permute-start(bf16[2,4,32,256]{3,2,1,0:T(8,128)(2,1)S(1)} %bitcast.34), channel_id=1, source_target_pairs={{0,1},{1,0},{2,3},{3,2},{4,5},{5,4},{6,7},{7,6},{8,9},{9,8},{10,11... | collective-permute-start | bytes 393224 | tf_op jit(solution)/shard_map/ppermute | solution.py:204
  9.8 10.7 %copy-start.7 = (bf16[16,4,8,512]{3,2,1,0:T(8,128)(2,1)S(1)}, bf16[16,4,8,512]{3,2,1,0:T(8,128)(2,1)}, u32[]{:S(2)}) copy-start(bf16[16,4,8,512]{3,2,1,0:T(8,128)(2,1)} %param.6) | copy-start | bytes 1572868
  17.2 2.0 %copy-start.3 = (bf16[2,8,16,512]{3,2,1,0:T(8,128)(2,1)}, bf16[2,8,16,512]{3,2,1,0:T(8,128)(2,1)S(1)}, u32[]{:S(2)}) copy-start(bf16[2,8,16,512]{3,2,1,0:T(8,128)(2,1)S(1)} %collective-permute-done.refs_0_) | copy-start | bytes 786436
  17.2 5.4 %collective-permute-start.2 = (bf16[2,8,16,512]{3,2,1,0:T(8,128)(2,1)S(1)}, bf16[2,8,16,512]{3,2,1,0:T(8,128)(2,1)S(1)}, u32[]{:S(2)}, u32[]{:S(2)}) collective-permute-start(bf16[2,8,16,512]{3,2,1,0:T(8,128)(2,1)S(1)} %collective-permute-done.refs_0_), channel_id=1, source_target_pairs={{0,1},{1,0},{2,3},{3,2},{4,5},{5,4},{6,7},{7,6},{8,9},{9,8},{10,11... | collective-permute-start | bytes 786440 | tf_op jit(solution)/shard_map/ppermute | solution.py:167
  19.1 0.7 copy-start.4
  19.1 3.5 %collective-permute-start.4 = (bf16[2,8,16,512]{3,2,1,0:T(8,128)(2,1)S(1)}, bf16[2,8,16,512]{3,2,1,0:T(8,128)(2,1)S(1)}, u32[]{:S(2)}, u32[]{:S(2)}) collective-permute-start(bf16[2,8,16,512]{3,2,1,0:T(8,128)(2,1)S(1)} %collective-permute-done.1.refs_2_), channel_id=1, source_target_pairs={{0,1},{1,0},{2,3},{3,2},{4,5},{5,4},{6,7},{7,6},{8,9},{9,8},{10,11... | collective-permute-start | bytes 786440 | tf_op jit(solution)/shard_map/ppermute | solution.py:168
  22.6 0.7 copy-start.5
  22.6 0.8 %copy-start.6 = (bf16[2,8,16,512]{3,2,1,0:T(8,128)(2,1)}, bf16[2,8,16,512]{3,2,1,0:T(8,128)(2,1)S(1)}, u32[]{:S(2)}) copy-start(bf16[2,8,16,512]{3,2,1,0:T(8,128)(2,1)S(1)} %collective-permute-done.4.refs_5_) | copy-start | bytes 786436
  22.6 1.0 %copy-start.2 = (bf16[4,8,16,512]{3,2,1,0:T(8,128)(2,1)}, bf16[4,8,16,512]{3,2,1,0:T(8,128)(2,1)S(1)}, u32[]{:S(2)}) copy-start(bf16[4,8,16,512]{3,2,1,0:T(8,128)(2,1)S(1)} %collective-permute-done.3.refs_4_) | copy-start | bytes 1572868
  30.0 17.1 %collective-permute-start.5 = (bf16[1,128,512]{2,1,0:T(8,128)(2,1)}, bf16[1,128,512]{2,1,0:T(8,128)(2,1)S(1)}, u32[]{:S(2)}, u32[]{:S(2)}) collective-permute-start(bf16[1,128,512]{2,1,0:T(8,128)(2,1)} %bitcast.40), channel_id=1, source_target_pairs={{14,0},{0,2},{2,4},{4,6},{6,8},{8,10},{10,12},{12,14},{15,1},{1,3}... | collective-permute-start | bytes 393224 | tf_op jit(solution)/shard_map/ppermute | solution.py:30
  31.4 13.2 %copy-start.10 = (f32[3,96,48]{2,1,0:T(8,128)S(1)}, f32[3,96,48]{2,1,0:T(8,128)}, u32[]{:S(2)}) copy-start(f32[3,96,48]{2,1,0:T(8,128)} %get-tuple-element.14) | copy-start | bytes 165892
  47.1 0.7 copy-start.12
  52.6 3.8 %copy-start.8 = (f32[2,4,64,256]{3,2,1,0:T(8,128)S(1)}, f32[2,4,64,256]{3,2,1,0:T(8,128)}, u32[]{:S(2)}) copy-start(f32[2,4,64,256]{3,2,1,0:T(8,128)} %get-tuple-element.11) | copy-start | bytes 1572868
  54.0 6.6 %collective-permute-start.8 = (f32[41472]{0:T(1024)S(1)}, f32[41472]{0:T(1024)S(1)}, u32[]{:S(2)}, u32[]{:S(2)}) collective-permute-start(f32[41472]{0:T(1024)S(1)} %constant_dynamic-update-slice_fusion), channel_id=1, source_target_pairs={{0,2},{2,0},{4,6},{6,4},{8,10},{10,8},{12,14},{14,12},{1,3},{3,1},... | collective-permute-start | bytes 497672 | tf_op jit(solution)/shard_map/ppermute | solution.py:40
  56.5 12.3 %collective-permute-start.7 = (f32[2,4,32,256]{3,2,1,0:T(8,128)S(1)}, f32[2,4,32,256]{3,2,1,0:T(8,128)S(1)}, u32[]{:S(2)}, u32[]{:S(2)}) collective-permute-start(f32[2,4,32,256]{3,2,1,0:T(8,128)S(1)} %slice.29), channel_id=1, source_target_pairs={{0,1},{1,0},{2,3},{3,2},{4,5},{5,4},{6,7},{7,6},{8,9},{9,8},{10,11... | collective-permute-start | bytes 786440 | tf_op jit(solution)/shard_map/ppermute | solution.py:227
  60.7 5.4 %collective-permute-start.9 = (f32[41472]{0:T(1024)S(1)}, f32[41472]{0:T(1024)S(1)}, u32[]{:S(2)}, u32[]{:S(2)}) collective-permute-start(f32[41472]{0:T(1024)S(1)} %add.67), channel_id=1, source_target_pairs={{0,4},{2,6},{4,0},{6,2},{8,12},{10,14},{12,8},{14,10},{1,5},{3,7},... | collective-permute-start | bytes 497672 | tf_op jit(solution)/shard_map/ppermute | solution.py:40
  66.1 8.8 %collective-permute-start.10 = (f32[41472]{0:T(1024)S(1)}, f32[41472]{0:T(1024)S(1)}, u32[]{:S(2)}, u32[]{:S(2)}) collective-permute-start(f32[41472]{0:T(1024)S(1)} %add.68), channel_id=1, source_target_pairs={{0,8},{2,10},{4,12},{6,14},{8,0},{10,2},{12,4},{14,6},{1,9},{3,11}... | collective-permute-start | bytes 497672 | tf_op jit(solution)/shard_map/ppermute | solution.py:40

commit v9 on v8

--- a/solution.py
+++ b/solution.py
@@ -50,12 +50,12 @@
     pieces = refs[:6]
     sp_ref, w_ref, gp_ref, r_ref, g_ref, sems = refs[6:]
     planes_z, planes_x, part_ch, cells_y = sp_ref.shape
-    wide = g_ref.shape[3]
+    wide = g_ref.shape[4]
     low_count = pieces[0].shape[0]
     needed = sorted({z + 4 - 2 * dz for z in range(z_lo, z_hi) for dz in range(3)})
-    edge = jnp.zeros(g_ref[:, :, 0:2].shape, g_ref.dtype)
-    g_ref[:, :, 0:2] = edge
-    g_ref[:, :, planes_x + 2 :] = edge
+    edge = jnp.zeros(g_ref[:, :, :, 0].shape, g_ref.dtype)
+    g_ref[:, :, :, 0] = edge
+    g_ref[:, :, :, planes_x // 2 + 1] = edge
     copies = []
     for plane in needed:
         if plane < low_count:
@@ -65,13 +65,20 @@
         else:
             part, at = 2, plane - low_count - planes_z
         for half in range(2):
-            copy = pltpu.make_async_copy(
-                pieces[3 * half + part].at[at],
-                g_ref.at[plane % 2, plane // 2, pl.ds(2, planes_x), pl.ds(half * part_ch, part_ch)],
-                sems.at[len(copies)],
-            )
-            copy.start()
-            copies.append(copy)
+            for parity in range(2):
+                copy = pltpu.make_async_copy(
+                    pieces[3 * half + part].at[at, parity],
+                    g_ref.at[
+                        plane % 2,
+                        plane // 2,
+                        parity,
+                        pl.ds(1, planes_x // 2),
+                        pl.ds(half * part_ch, part_ch),
+                    ],
+                    sems.at[len(copies)],
+                )
+                copy.start()
+                copies.append(copy)
     r_ref[...] = jnp.zeros(r_ref.shape, r_ref.dtype)
     for copy in copies:
         copy.wait()
@@ -85,14 +92,12 @@
         rolled = jnp.concatenate(
             [pltpu.roll(hidden, 2, 1), hidden, pltpu.roll(hidden, cells_y - 2, 1)], axis=0
         ).astype(jnp.bfloat16)
-        total = jnp.zeros((3 * part_ch, cells_y), jnp.float32)
-        for dx in range(3):
-            block = g_ref[z % 2, pl.ds(z // 2, 3), x + 4 - 2 * dx]
-            block = block.reshape(3 * wide, cells_y)
-            total = total + jnp.dot(w_ref[dx], block, preferred_element_type=jnp.float32)
-            r_ref[dx] += lax.dot_general(
-                block, rolled, (((1,), (1,)), ((), ())), preferred_element_type=jnp.float32
-            )
+        block = g_ref[z % 2, pl.ds(z // 2, 3), x % 2, pl.ds(x // 2, 3)]
+        block = block.reshape(9 * wide, cells_y)
+        total = jnp.dot(w_ref[...], block, preferred_element_type=jnp.float32)
+        r_ref[...] += lax.dot_general(
+            block, rolled, (((1,), (1,)), ((), ())), preferred_element_type=jnp.float32
+        )
         grad_hidden = (
             pltpu.roll(total[:part_ch], cells_y - 2, 1)
             + total[part_ch : 2 * part_ch]
@@ -156,7 +161,8 @@
     all_ch = part_ch * lax.axis_size("ch")
     channel_start = lax.axis_index("ch") * part_ch
 
-    rows = jnp.transpose(out_grad, (1, 2, 0, 3))
+    rows = out_grad.reshape(part_ch, planes_z, planes_x // 2, 2, cells_y)
+    rows = jnp.transpose(rows, (1, 3, 2, 0, 4))
     count = lax.axis_size(("gz", "sec"))
     forward = [(i, (i + 1) % count) for i in range(count)]
     backward = [(target, source) for source, target in forward]
@@ -171,20 +177,22 @@
 
     refine_cols = lax.dynamic_slice_in_dim(refine_weight, channel_start, part_ch, 2)
     refine_cols = jnp.roll(refine_cols, -channel_start, axis=1)
-    refine_w = refine_cols.reshape(3, 3, 3, all_ch, part_ch)[::-1]
-    refine_w = jnp.transpose(refine_w, (1, 2, 4, 0, 3)).reshape(3, 3 * part_ch, 3 * all_ch)
+    refine_w = refine_cols.reshape(3, 3, 3, all_ch, part_ch)[::-1, ::-1]
+    refine_w = jnp.transpose(refine_w, (2, 4, 0, 1, 3)).reshape(3 * part_ch, 9 * all_ch)
 
     def fine_rows(z_lo, z_hi):
         return pl.pallas_call(
             functools.partial(fine_kernel, z_lo, z_hi),
             out_shape=(
                 jax.ShapeDtypeStruct((z_hi - z_lo, planes_x, part_ch, cells_y), jnp.bfloat16),
-                jax.ShapeDtypeStruct((3, 3 * all_ch, 3 * part_ch), jnp.float32),
+                jax.ShapeDtypeStruct((9 * all_ch, 3 * part_ch), jnp.float32),
             ),
             in_specs=[pl.BlockSpec(memory_space=pl.ANY)] * 6 + vmem_specs(2),
             out_specs=tuple(vmem_specs(2)),
             scratch_shapes=[
-                pltpu.VMEM((2, halo_z // 2, planes_x + 4, all_ch, cells_y), jnp.bfloat16),
+                pltpu.VMEM(
+                    (2, halo_z // 2, 2, planes_x // 2 + 2, all_ch, cells_y), jnp.bfloat16
+                ),
                 pltpu.SemaphoreType.DMA((4 * halo_z,)),
             ],
         )(low, rows, high, low_other, rows_other, high_other, pre_rows, refine_w)
@@ -195,8 +203,8 @@
     grad_main, refine_main = fine_rows(0, planes_z - 1)
     grad_rows = grad_main.reshape(planes_z - 1, planes_x * part_ch, cells_y)
     refine_acc = refine_main + refine_last
-    refine_terms = refine_acc.reshape(3, 3, all_ch, 3, part_ch)[:, ::-1]
-    refine_terms = jnp.transpose(refine_terms, (1, 0, 3, 2, 4)).reshape(27, all_ch, part_ch)
+    refine_terms = refine_acc.reshape(3, 3, all_ch, 3, part_ch)[::-1, ::-1]
+    refine_terms = jnp.transpose(refine_terms, (0, 1, 3, 2, 4)).reshape(27, all_ch, part_ch)
     refine_terms = jnp.roll(refine_terms, channel_start, axis=1)
 
 

time: 77.1 us -> 74 us (0.960)
  Pallas kernels: 24.4 us -> 21.4 us
    pallas_call x2, Pallas kernels: 19.6 us -> 16.6 us  [fine_rows(): pl.pallas_call(functools.partial(fine_kernel, z_lo, z_hi), out_shape=(jax...]
  transfers between devices with their start and end apart: 11 -> 11, of which waited for: 5 -> 5; matrix products, arithmetic and copies ran while one was open for 10% -> 10% of each run, Pallas kernels for 26% -> 23%
where the time goes in v9:
time: 74 us; the launch traced here: 73.7 us
  waiting for transfers between devices  22.5 us (30%)
  Pallas kernels  21.4 us (29%)
  starting transfers between devices  14 us (19%)
  local copies, waits for them, and re-layouts  11.3 us (15%)
  other arithmetic  3.57 us (5%)
  between operations  0.98 us (1%)
    pallas_call x2, Pallas kernels, fine_rows(): pl.pallas_call(functools.partial(fine_kernel, z_lo, z_hi), out_shape=(jax...  16.6 us
    ppermute x3, waiting for transfers between devices, summed_over_slabs(): block = block + lax.ppermute(block, axis, route)  13.2 us
    ppermute x1, waiting for transfers between devices, local(): low = lax.ppermute(rows[planes_z - 2:], ('gz', 'sec'), forward)  7.38 us
    ppermute x3, starting transfers between devices, summed_over_slabs(): block = block + lax.ppermute(block, axis, route)  6.71 us
    unnamed x33, local copies, waits for them, and re-layouts  6.47 us
    pallas_call x1, Pallas kernels, local(): pl.pallas_call(coarse_kernel, out_shape=(jax.ShapeDtypeStruct((coarse_z,...  4.8 us
    ppermute x1, starting transfers between devices, local(): high = lax.ppermute(rows[:2], ('gz', 'sec'), backward)  3.04 us
    ppermute x1, starting transfers between devices, local(): low = lax.ppermute(rows[planes_z - 2:], ('gz', 'sec'), forward)  2.94 us
  transfers between devices with their start and end apart: 11, of which 5 were waited for; matrix products, arithmetic and copies ran while one was open for 10% of the time, Pallas kernels for 23%

profile of v9, /device:TPU:0, one launch (start us, length us, event | category | flops | bytes accessed | tf_op | source)
XLA Modules:
  0.0 73.7 jit_solution(11495105797348432377)
XLA Ops:
  0.6 0.0 copy-start
  0.6 1.4 %copy.11 = bf16[16,4,8,512]{3,0,2,1:T(8,128)(2,1)S(1)} copy(bf16[16,4,8,512]{3,2,1,0:T(8,128)(2,1)} %param.7) | data formatting | bytes 1048576 | tf_op args[2]
  2.1 0.8 %fusion.1 = (bf16[2,2,4,16,512]{4,3,2,1,0:T(8,128)(2,1)S(1)}, bf16[2,2,4,16,512]{4,3,2,1,0:T(8,128)(2,1)}) fusion(bf16[4,2,4,16,512]{4,3,2,1,0:T(8,128)(2,1)S(1)} %bitcast.27), kind=kLoop, calls=%fused_computation.17 | loop fusion | bytes 1048576 | tf_op jit(solution)/shard_map/slice | solution.py:171
  2.8 2.9 %collective-permute-start = (bf16[2,2,4,16,512]{4,3,2,1,0:T(8,128)(2,1)}, bf16[2,2,4,16,512]{4,3,2,1,0:T(8,128)(2,1)S(1)}, u32[]{:S(2)}, u32[]{:S(2)}) collective-permute-start(bf16[2,2,4,16,512]{4,3,2,1,0:T(8,128)(2,1)} %get-tuple-element.22), channel_id=1, source_target_pairs={{0,2},{2,4},{4,6},{6,8},{8,10},{10,12},{12,14},{14,0},{1,3},{3,5},... | collective-permute-start | bytes 786440 | tf_op jit(solution)/shard_map/ppermute | solution.py:170
  5.8 3.0 %collective-permute-start.1 = (bf16[2,2,4,16,512]{4,3,2,1,0:T(8,128)(2,1)S(1)}, bf16[2,2,4,16,512]{4,3,2,1,0:T(8,128)(2,1)S(1)}, u32[]{:S(2)}, u32[]{:S(2)}) collective-permute-start(bf16[2,2,4,16,512]{4,3,2,1,0:T(8,128)(2,1)S(1)} %get-tuple-element.21), channel_id=1, source_target_pairs={{2,0},{4,2},{6,4},{8,6},{10,8},{12,10},{14,12},{0,14},{3,1},{5,3},... | collective-permute-start | bytes 786440 | tf_op jit(solution)/shard_map/ppermute | solution.py:171
  8.9 0.6 collective-permute-start.6
  9.4 0.1 constant_dynamic-slice_fusion.1
  9.6 0.1 copy.23
  9.7 0.2 dynamic-slice_maximum_fusion.3
  9.9 0.0 copy-start.7
  9.9 7.4 %collective-permute-done.refs_0_ = bf16[2,2,4,16,512]{4,3,2,1,0:T(8,128)(2,1)S(1)} collective-permute-done((bf16[2,2,4,16,512]{4,3,2,1,0:T(8,128)(2,1)}, bf16[2,2,4,16,512]{4,3,2,1,0:T(8,128)(2,1)S(1)}, u32[]{:S(2)}, u32[]{:S(2)}) %collective-permute-start) | collective-permute-done | bytes 262176 | tf_op jit(solution)/shard_map/ppermute | solution.py:170
  17.3 1.9 %collective-permute-done.1.refs_2_ = bf16[2,2,4,16,512]{4,3,2,1,0:T(8,128)(2,1)S(1)} collective-permute-done((bf16[2,2,4,16,512]{4,3,2,1,0:T(8,128)(2,1)S(1)}, bf16[2,2,4,16,512]{4,3,2,1,0:T(8,128)(2,1)S(1)}, u32[]{:S(2)}, u32[]{:S(2)}) %collective-permute-start.1) | collective-permute-done | bytes 262176 | tf_op jit(solution)/shard_map/ppermute | solution.py:171
  19.3 0.1 copy.15
  19.3 0.6 copy-done.4
  19.9 0.7 %reshape.58.refs_7_ = bf16[48,288]{1,0:T(8,128)(2,1)} reshape(bf16[3,16,3,3,32]{4,3,2,1,0:T(4,128)(2,1)S(1)} %copy.15) | data formatting | bytes 55296 | tf_op jit(solution)/shard_map/reshape | solution.py:181
  20.6 1.1 %copy.27 = bf16[16,4,8,512]{3,0,2,1:T(8,128)(2,1)} copy(bf16[16,4,8,512]{3,2,1,0:T(8,128)(2,1)S(1)} %copy-done.7) | data formatting | bytes 1048576 | tf_op args[1]
  21.7 0.2 dynamic-slice_maximum_fusion.2
  21.9 0.8 %copy.17.u_ref = bf16[3,64,144]{2,1,0:T(8,128)(2,1)} copy(bf16[3,64,144]{1,2,0:T(8,128)(2,1)S(1)} %bitcast.39) | data formatting | bytes 110592 | tf_op jit(solution)/shard_map/reshape | solution.py:219
  22.7 0.7 copy-done.5
  23.3 0.1 copy-done.6
  23.4 0.2 copy-done.2
  23.6 5.7 %shard_map.77 = (bf16[1,8,16,512]{3,2,1,0:T(8,128)(2,1)}, f32[288,48]{1,0:T(8,128)}) custom-call(bf16[2,2,4,16,512]{4,3,2,1,0:T(8,128)(2,1)} %copy-done.3, bf16[4,2,4,16,512]{4,3,2,1,0:T(8,128)(2,1)} %bitcast.29, bf16[2,2,4,16,512]{4,3,2,1,0:T(8,128)(2,1)} %copy-done.4, bf16[2,2,4,16,512]{4,3,2,1,0:T(8,128)(2,1)} %copy-done.5, ...), custom_call_target="tpu_custom_call" | custom-call | tf_op jit(solution)/shard_map/pallas_call | solution.py:184
  29.3 0.6 collective-permute-start.5
  29.9 0.7 pad_maximum_fusion.c_ref
  30.7 10.9 %shard_map.76 = (bf16[3,8,16,512]{3,2,1,0:T(8,128)(2,1)}, f32[288,48]{1,0:T(8,128)}) custom-call(bf16[2,2,4,16,512]{4,3,2,1,0:T(8,128)(2,1)} %copy-done.3, bf16[4,2,4,16,512]{4,3,2,1,0:T(8,128)(2,1)} %bitcast.30, bf16[2,2,4,16,512]{4,3,2,1,0:T(8,128)(2,1)} %copy-done.4, bf16[2,2,4,16,512]{4,3,2,1,0:T(8,128)(2,1)} %copy-done.5, ...), custom_call_target="tpu_custom_call" | custom-call | tf_op jit(solution)/shard_map/pallas_call | solution.py:184
  41.6 0.9 %add.64 = f32[288,48]{1,0:T(8,128)S(1)} add(f32[288,48]{1,0:T(8,128)} %get-tuple-element.13, f32[288,48]{1,0:T(8,128)S(1)} %copy-done.10) | non-fusion elementwise | flops 13824 | bytes 165888 | tf_op jit(solution)/shard_map/add | solution.py:205
  42.5 0.1 copy.18
  42.7 0.2 reshape.65
  42.8 0.6 rev.7
  43.4 0.2 dynamic-slice_maximum_fusion
  43.6 0.2 copy.20
  43.8 0.2 reshape.67
  44.0 0.0 copy-start.12
  44.0 0.6 copy-done.12
  44.7 4.8 %shard_map.78 = (f32[2,4,64,256]{3,2,1,0:T(8,128)}, f32[3,144,64]{2,1,0:T(8,128)}) custom-call(bf16[3,128,512]{2,1,0:T(8,128)(2,1)} %bitcast.40, bf16[1,128,512]{2,1,0:T(8,128)(2,1)} %bitcast.43, bf16[1,128,512]{2,1,0:T(8,128)(2,1)} %copy-done.12, bf16[2,4,64,256]{3,2,1,0:T(8,128)(2,1)} %pad_maximum_fusion.c_ref, bf16[3,64,144]{2,1,0:T(8,128)(2,1)} %copy.17.u_ref), custom_call_target="tpu_custom_call" | custom-call | tf_op jit(solution)/shard_map/pallas_call | solution.py:221
  49.5 1.3 %dynamic-slice_maximum_fusion.1 = f32[27,16,64]{2,1,0:T(8,128)S(1)} fusion(s32[]{:T(128)S(6)} %select_n.53, f32[27,16,64]{2,1,0:T(8,128)} %bitcast.41), kind=kLoop, calls=%fused_computation.5 | loop fusion | flops 27648 | bytes 221188 | tf_op jit(solution)/shard_map/jit(_roll_dynamic)/concatenate | solution.py:233
  50.8 0.1 reshape.64
  50.9 2.4 %collective-permute-start.8 = (f32[41472]{0:T(1024)S(1)}, f32[41472]{0:T(1024)S(1)}, u32[]{:S(2)}, u32[]{:S(2)}) collective-permute-start(f32[41472]{0:T(1024)S(1)} %constant_dynamic-update-slice_fusion), channel_id=1, source_target_pairs={{0,2},{2,0},{4,6},{6,4},{8,10},{10,8},{12,14},{14,12},{1,3},{3,1},... | collective-permute-start | bytes 497672 | tf_op jit(solution)/shard_map/ppermute | solution.py:40
  53.3 0.1 collective-permute-start.7
  53.4 4.1 %collective-permute-done.8 = f32[41472]{0:T(1024)S(1)} collective-permute-done((f32[41472]{0:T(1024)S(1)}, f32[41472]{0:T(1024)S(1)}, u32[]{:S(2)}, u32[]{:S(2)}) %collective-permute-start.8) | collective-permute-done | bytes 165920 | tf_op jit(solution)/shard_map/ppermute | solution.py:40
  57.5 1.6 %collective-permute-start.9 = (f32[41472]{0:T(1024)S(1)}, f32[41472]{0:T(1024)S(1)}, u32[]{:S(2)}, u32[]{:S(2)}) collective-permute-start(f32[41472]{0:T(1024)S(1)} %add.67), channel_id=1, source_target_pairs={{0,4},{2,6},{4,0},{6,2},{8,12},{10,14},{12,8},{14,10},{1,5},{3,7},... | collective-permute-start | bytes 497672 | tf_op jit(solution)/shard_map/ppermute | solution.py:40
  59.2 3.8 %collective-permute-done.9 = f32[41472]{0:T(1024)S(1)} collective-permute-done((f32[41472]{0:T(1024)S(1)}, f32[41472]{0:T(1024)S(1)}, u32[]{:S(2)}, u32[]{:S(2)}) %collective-permute-start.9) | collective-permute-done | bytes 165920 | tf_op jit(solution)/shard_map/ppermute | solution.py:40
  63.0 2.6 %collective-permute-start.10 = (f32[41472]{0:T(1024)S(1)}, f32[41472]{0:T(1024)S(1)}, u32[]{:S(2)}, u32[]{:S(2)}) collective-permute-start(f32[41472]{0:T(1024)S(1)} %add.68), channel_id=1, source_target_pairs={{0,8},{2,10},{4,12},{6,14},{8,0},{10,2},{12,4},{14,6},{1,9},{3,11}... | collective-permute-start | bytes 497672 | tf_op jit(solution)/shard_map/ppermute | solution.py:40
  65.7 0.8 %copy.21 = bf16[32,2,4,256]{3,2,1,0:T(4,128)(2,1)} copy(bf16[32,2,4,256]{3,0,2,1:T(8,128)(2,1)S(1)} %fusion) | data formatting | bytes 262144
  66.4 5.3 %collective-permute-done.10 = f32[41472]{0:T(1024)S(1)} collective-permute-done((f32[41472]{0:T(1024)S(1)}, f32[41472]{0:T(1024)S(1)}, u32[]{:S(2)}, u32[]{:S(2)}) %collective-permute-start.10) | collective-permute-done | bytes 165920 | tf_op jit(solution)/shard_map/ppermute | solution.py:40
  71.8 0.2 mul.31
  72.0 0.9 %copy.22 = f32[27,32,16]{1,2,0:T(8,128)} copy(f32[27,32,16]{2,1,0:T(8,128)S(1)} %mul.31) | data formatting | bytes 110592
  72.9 0.8 %mul.28 = f32[27,16,64]{2,1,0:T(8,128)} reshape(f32[27648]{0:T(1024)S(1)} %slice_multiply_fusion) | data formatting | bytes 221184 | tf_op jit(solution)/shard_map/mul | solution.py:244
  (41 shorter events, 0.3 us)
Async XLA Ops:
  0.6 18.6 %copy-start = (bf16[27,32,64]{2,1,0:T(8,128)(2,1)S(1)}, bf16[27,32,64]{2,1,0:T(8,128)(2,1)}, u32[]{:S(2)}) copy-start(bf16[27,32,64]{2,1,0:T(8,128)(2,1)} %param.8) | copy-start | bytes 331780
  2.1 6.8 %copy-start.1 = (bf16[16,4,4,2,512]{4,0,2,3,1:T(8,128)(2,1)}, bf16[16,4,4,2,512]{4,0,2,3,1:T(8,128)(2,1)S(1)}, u32[]{:S(2)}) copy-start(bf16[16,4,4,2,512]{4,0,2,3,1:T(8,128)(2,1)S(1)} %copy.28) | copy-start | bytes 1572868
  2.1 6.8 %copy-start.11 = (bf16[32,2,4,256]{3,2,1,0:T(4,128)(2,1)S(1)}, bf16[32,2,4,256]{3,2,1,0:T(4,128)(2,1)}, u32[]{:S(2)}) copy-start(bf16[32,2,4,256]{3,2,1,0:T(4,128)(2,1)} %param.5) | copy-start | bytes 393220
  2.8 6.6 %copy-start.9 = (bf16[27,32,32]{2,1,0:T(8,128)(2,1)S(1)}, bf16[27,32,32]{2,1,0:T(8,128)(2,1)}, u32[]{:S(2)}) copy-start(bf16[27,32,32]{2,1,0:T(8,128)(2,1)} %param.9) | copy-start | bytes 165892
  2.8 14.4 %collective-permute-start = (bf16[2,2,4,16,512]{4,3,2,1,0:T(8,128)(2,1)}, bf16[2,2,4,16,512]{4,3,2,1,0:T(8,128)(2,1)S(1)}, u32[]{:S(2)}, u32[]{:S(2)}) collective-permute-start(bf16[2,2,4,16,512]{4,3,2,1,0:T(8,128)(2,1)} %get-tuple-element.22), channel_id=1, source_target_pairs={{0,2},{2,4},{4,6},{6,8},{8,10},{10,12},{12,14},{14,0},{1,3},{3,5},... | collective-permute-start | bytes 786440 | tf_op jit(solution)/shard_map/ppermute | solution.py:170
  5.8 13.4 %collective-permute-start.1 = (bf16[2,2,4,16,512]{4,3,2,1,0:T(8,128)(2,1)S(1)}, bf16[2,2,4,16,512]{4,3,2,1,0:T(8,128)(2,1)S(1)}, u32[]{:S(2)}, u32[]{:S(2)}) collective-permute-start(bf16[2,2,4,16,512]{4,3,2,1,0:T(8,128)(2,1)S(1)} %get-tuple-element.21), channel_id=1, source_target_pairs={{2,0},{4,2},{6,4},{8,6},{10,8},{12,10},{14,12},{0,14},{3,1},{5,3},... | collective-permute-start | bytes 786440 | tf_op jit(solution)/shard_map/ppermute | solution.py:171
  8.8 13.9 %collective-permute-start.3 = (bf16[4,2,4,16,512]{4,3,2,1,0:T(8,128)(2,1)S(1)}, bf16[4,2,4,16,512]{4,3,2,1,0:T(8,128)(2,1)S(1)}, u32[]{:S(2)}, u32[]{:S(2)}) collective-permute-start(bf16[4,2,4,16,512]{4,3,2,1,0:T(8,128)(2,1)S(1)} %bitcast.28), channel_id=1, source_target_pairs={{0,1},{1,0},{2,3},{3,2},{4,5},{5,4},{6,7},{7,6},{8,9},{9,8},{10,11... | collective-permute-start | bytes 1572872 | tf_op jit(solution)/shard_map/ppermute | solution.py:172
  8.9 21.1 %collective-permute-start.6 = (bf16[2,4,32,256]{3,2,1,0:T(8,128)(2,1)S(1)}, bf16[2,4,32,256]{3,2,1,0:T(8,128)(2,1)S(1)}, u32[]{:S(2)}, u32[]{:S(2)}) collective-permute-start(bf16[2,4,32,256]{3,2,1,0:T(8,128)(2,1)S(1)} %bitcast.36), channel_id=1, source_target_pairs={{0,1},{1,0},{2,3},{3,2},{4,5},{5,4},{6,7},{7,6},{8,9},{9,8},{10,11... | collective-permute-start | bytes 393224 | tf_op jit(solution)/shard_map/ppermute | solution.py:212
  9.9 10.8 %copy-start.7 = (bf16[16,4,8,512]{3,2,1,0:T(8,128)(2,1)S(1)}, bf16[16,4,8,512]{3,2,1,0:T(8,128)(2,1)}, u32[]{:S(2)}) copy-start(bf16[16,4,8,512]{3,2,1,0:T(8,128)(2,1)} %param.6) | copy-start | bytes 1572868
  17.3 2.0 %copy-start.3 = (bf16[2,2,4,16,512]{4,3,2,1,0:T(8,128)(2,1)}, bf16[2,2,4,16,512]{4,3,2,1,0:T(8,128)(2,1)S(1)}, u32[]{:S(2)}) copy-start(bf16[2,2,4,16,512]{4,3,2,1,0:T(8,128)(2,1)S(1)} %collective-permute-done.refs_0_) | copy-start | bytes 786436
  17.3 5.4 %collective-permute-start.2 = (bf16[2,2,4,16,512]{4,3,2,1,0:T(8,128)(2,1)S(1)}, bf16[2,2,4,16,512]{4,3,2,1,0:T(8,128)(2,1)S(1)}, u32[]{:S(2)}, u32[]{:S(2)}) collective-permute-start(bf16[2,2,4,16,512]{4,3,2,1,0:T(8,128)(2,1)S(1)} %collective-permute-done.refs_0_), channel_id=1, source_target_pairs={{0,1},{1,0},{2,3},{3,2},{4,5},{5,4},{6,7},{7,6},{8,9},{9,8},{10,11... | collective-permute-start | bytes 786440 | tf_op jit(solution)/shard_map/ppermute | solution.py:173
  19.2 0.7 copy-start.4
  19.2 3.5 %collective-permute-start.4 = (bf16[2,2,4,16,512]{4,3,2,1,0:T(8,128)(2,1)S(1)}, bf16[2,2,4,16,512]{4,3,2,1,0:T(8,128)(2,1)S(1)}, u32[]{:S(2)}, u32[]{:S(2)}) collective-permute-start(bf16[2,2,4,16,512]{4,3,2,1,0:T(8,128)(2,1)S(1)} %collective-permute-done.1.refs_2_), channel_id=1, source_target_pairs={{0,1},{1,0},{2,3},{3,2},{4,5},{5,4},{6,7},{7,6},{8,9},{9,8},{10,11... | collective-permute-start | bytes 786440 | tf_op jit(solution)/shard_map/ppermute | solution.py:174
  22.7 0.7 copy-start.5
  22.7 0.8 %copy-start.6 = (bf16[2,2,4,16,512]{4,3,2,1,0:T(8,128)(2,1)}, bf16[2,2,4,16,512]{4,3,2,1,0:T(8,128)(2,1)S(1)}, u32[]{:S(2)}) copy-start(bf16[2,2,4,16,512]{4,3,2,1,0:T(8,128)(2,1)S(1)} %collective-permute-done.4.refs_5_) | copy-start | bytes 786436
  22.7 1.0 %copy-start.2 = (bf16[4,2,4,16,512]{4,3,2,1,0:T(8,128)(2,1)}, bf16[4,2,4,16,512]{4,3,2,1,0:T(8,128)(2,1)S(1)}, u32[]{:S(2)}) copy-start(bf16[4,2,4,16,512]{4,3,2,1,0:T(8,128)(2,1)S(1)} %collective-permute-done.3.refs_4_) | copy-start | bytes 1572868
  29.3 14.7 %collective-permute-start.5 = (bf16[1,128,512]{2,1,0:T(8,128)(2,1)}, bf16[1,128,512]{2,1,0:T(8,128)(2,1)S(1)}, u32[]{:S(2)}, u32[]{:S(2)}) collective-permute-start(bf16[1,128,512]{2,1,0:T(8,128)(2,1)} %bitcast.42), channel_id=1, source_target_pairs={{14,0},{0,2},{2,4},{4,6},{6,8},{8,10},{10,12},{12,14},{15,1},{1,3}... | collective-permute-start | bytes 393224 | tf_op jit(solution)/shard_map/ppermute | solution.py:30
  30.7 11.0 %copy-start.10 = (f32[288,48]{1,0:T(8,128)S(1)}, f32[288,48]{1,0:T(8,128)}, u32[]{:S(2)}) copy-start(f32[288,48]{1,0:T(8,128)} %get-tuple-element.14) | copy-start | bytes 165892
  44.0 0.7 copy-start.12
  49.5 3.9 %copy-start.8 = (f32[2,4,64,256]{3,2,1,0:T(8,128)S(1)}, f32[2,4,64,256]{3,2,1,0:T(8,128)}, u32[]{:S(2)}) copy-start(f32[2,4,64,256]{3,2,1,0:T(8,128)} %get-tuple-element.11) | copy-start | bytes 1572868
  50.9 6.6 %collective-permute-start.8 = (f32[41472]{0:T(1024)S(1)}, f32[41472]{0:T(1024)S(1)}, u32[]{:S(2)}, u32[]{:S(2)}) collective-permute-start(f32[41472]{0:T(1024)S(1)} %constant_dynamic-update-slice_fusion), channel_id=1, source_target_pairs={{0,2},{2,0},{4,6},{6,4},{8,10},{10,8},{12,14},{14,12},{1,3},{3,1},... | collective-permute-start | bytes 497672 | tf_op jit(solution)/shard_map/ppermute | solution.py:40
  53.3 12.3 %collective-permute-start.7 = (f32[2,4,32,256]{3,2,1,0:T(8,128)S(1)}, f32[2,4,32,256]{3,2,1,0:T(8,128)S(1)}, u32[]{:S(2)}, u32[]{:S(2)}) collective-permute-start(f32[2,4,32,256]{3,2,1,0:T(8,128)S(1)} %slice.29), channel_id=1, source_target_pairs={{0,1},{1,0},{2,3},{3,2},{4,5},{5,4},{6,7},{7,6},{8,9},{9,8},{10,11... | collective-permute-start | bytes 786440 | tf_op jit(solution)/shard_map/ppermute | solution.py:235
  57.5 5.4 %collective-permute-start.9 = (f32[41472]{0:T(1024)S(1)}, f32[41472]{0:T(1024)S(1)}, u32[]{:S(2)}, u32[]{:S(2)}) collective-permute-start(f32[41472]{0:T(1024)S(1)} %add.67), channel_id=1, source_target_pairs={{0,4},{2,6},{4,0},{6,2},{8,12},{10,14},{12,8},{14,10},{1,5},{3,7},... | collective-permute-start | bytes 497672 | tf_op jit(solution)/shard_map/ppermute | solution.py:40
  63.0 8.8 %collective-permute-start.10 = (f32[41472]{0:T(1024)S(1)}, f32[41472]{0:T(1024)S(1)}, u32[]{:S(2)}, u32[]{:S(2)}) collective-permute-start(f32[41472]{0:T(1024)S(1)} %add.68), channel_id=1, source_target_pairs={{0,8},{2,10},{4,12},{6,14},{8,0},{10,2},{12,4},{14,6},{1,9},{3,11}... | collective-permute-start | bytes 497672 | tf_op jit(solution)/shard_map/ppermute | solution.py:40

commit v10 on v9

--- a/solution.py
+++ b/solution.py
@@ -46,9 +46,13 @@
     return [pl.BlockSpec(memory_space=pltpu.VMEM)] * count
 
 
-def fine_kernel(z_lo, z_hi, *refs):
+def fine_kernel(z_lo, z_hi, scale, *refs):
     pieces = refs[:6]
-    sp_ref, w_ref, gp_ref, r_ref, g_ref, sems = refs[6:]
+    if len(refs) == 13:
+        sp_ref, w_ref, start_ref, gp_ref, r_ref, g_ref, sems = refs[6:]
+    else:
+        sp_ref, w_ref, gp_ref, r_ref, g_ref, sems = refs[6:]
+        start_ref = None
     planes_z, planes_x, part_ch, cells_y = sp_ref.shape
     wide = g_ref.shape[4]
     low_count = pieces[0].shape[0]
@@ -79,7 +83,10 @@
                 )
                 copy.start()
                 copies.append(copy)
-    r_ref[...] = jnp.zeros(r_ref.shape, r_ref.dtype)
+    if start_ref is None:
+        r_ref[...] = jnp.zeros(r_ref.shape, r_ref.dtype)
+    else:
+        r_ref[...] = start_ref[...]
     for copy in copies:
         copy.wait()
 
@@ -107,9 +114,11 @@
         return carry
 
     lax.fori_loop(0, (z_hi - z_lo) * planes_x, body, 0)
-
-
-def coarse_kernel(gp_ref, last_ref, below_ref, c_ref, u_ref, gc_ref, gu_ref, y_ref):
+    if scale != 1.0:
+        r_ref[...] = r_ref[...] * scale
+
+
+def coarse_kernel(scale, gp_ref, last_ref, below_ref, c_ref, u_ref, gc_ref, gu_ref, y_ref):
     planes_z = gp_ref.shape[0] + 1
     cells_y = gp_ref.shape[2]
     rows_x = y_ref.shape[1] - 1
@@ -151,6 +160,7 @@
         return carry
 
     lax.fori_loop(0, coarse_z * coarse_x, body, 0)
+    gu_ref[...] = gu_ref[...] * scale
 
 
 def local(coarse, saved_pre, out_grad, up_weight, refine_weight):
@@ -180,14 +190,18 @@
     refine_w = refine_cols.reshape(3, 3, 3, all_ch, part_ch)[::-1, ::-1]
     refine_w = jnp.transpose(refine_w, (2, 4, 0, 1, 3)).reshape(3 * part_ch, 9 * all_ch)
 
-    def fine_rows(z_lo, z_hi):
+    fine_total = planes_z * lax.axis_size("gz") * lax.axis_size("sec") * planes_x * cells_y
+    coarse_total = fine_total // 8
+
+    def fine_rows(z_lo, z_hi, *start):
+        scale = float(fine_total) ** (-0.5) if start else 1.0
         return pl.pallas_call(
-            functools.partial(fine_kernel, z_lo, z_hi),
+            functools.partial(fine_kernel, z_lo, z_hi, scale),
             out_shape=(
                 jax.ShapeDtypeStruct((z_hi - z_lo, planes_x, part_ch, cells_y), jnp.bfloat16),
                 jax.ShapeDtypeStruct((9 * all_ch, 3 * part_ch), jnp.float32),
             ),
-            in_specs=[pl.BlockSpec(memory_space=pl.ANY)] * 6 + vmem_specs(2),
+            in_specs=[pl.BlockSpec(memory_space=pl.ANY)] * 6 + vmem_specs(2 + len(start)),
             out_specs=tuple(vmem_specs(2)),
             scratch_shapes=[
                 pltpu.VMEM(
@@ -195,31 +209,32 @@
                 ),
                 pltpu.SemaphoreType.DMA((4 * halo_z,)),
             ],
-        )(low, rows, high, low_other, rows_other, high_other, pre_rows, refine_w)
+        )(low, rows, high, low_other, rows_other, high_other, pre_rows, refine_w, *start)
 
     grad_last, refine_last = fine_rows(planes_z - 1, planes_z)
     last_rows = grad_last.reshape(1, planes_x * part_ch, cells_y)
     below_z = passed_along(last_rows, ("gz", "sec"), 1)
-    grad_main, refine_main = fine_rows(0, planes_z - 1)
+    grad_main, refine_acc = fine_rows(0, planes_z - 1, refine_last)
     grad_rows = grad_main.reshape(planes_z - 1, planes_x * part_ch, cells_y)
-    refine_acc = refine_main + refine_last
     refine_terms = refine_acc.reshape(3, 3, all_ch, 3, part_ch)[::-1, ::-1]
     refine_terms = jnp.transpose(refine_terms, (0, 1, 3, 2, 4)).reshape(27, all_ch, part_ch)
     refine_terms = jnp.roll(refine_terms, channel_start, axis=1)
 
 
     coarse_own = jnp.transpose(coarse, (1, 2, 0, 3))
-    coarse_rows = jnp.concatenate([coarse_own, lax.ppermute(coarse_own, "ch", swap)], axis=2)
+    coarse_other = lax.ppermute(coarse_own, "ch", swap)
+    own_k = coarse.shape[0]
+    coarse_start = lax.axis_index("ch") * own_k
+    coarse_rows = jnp.concatenate([coarse_own, coarse_other, coarse_own], axis=2)
+    coarse_rows = lax.dynamic_slice_in_dim(coarse_rows, coarse_start, 2 * own_k, 2)
     coarse_in = coarse_rows.shape[2]
-    coarse_start = lax.axis_index("ch") * coarse.shape[0]
     coarse_z, coarse_x, cells_yc = coarse.shape[1], coarse.shape[2], coarse.shape[3]
     up_rows = lax.dynamic_slice_in_dim(up_weight, channel_start, part_ch, 1)
-    up_rows = jnp.roll(up_rows, -coarse_start, axis=2)
     up_w = jnp.transpose(up_rows.reshape(3, 9, part_ch, coarse_in), (0, 3, 1, 2))
     up_w = up_w.reshape(3, coarse_in, 9 * part_ch)
 
     coarse_acc, up_acc = pl.pallas_call(
-        coarse_kernel,
+        functools.partial(coarse_kernel, float(coarse_total) ** (-0.5)),
         out_shape=(
             jax.ShapeDtypeStruct((coarse_z, coarse_x, coarse_in, cells_yc), jnp.float32),
             jax.ShapeDtypeStruct((3, 9 * part_ch, coarse_in), jnp.float32),
@@ -230,19 +245,15 @@
             pltpu.VMEM((planes_z + 1, planes_x + 1, 3, part_ch, cells_yc), jnp.bfloat16)
         ],
     )(grad_rows, last_rows, below_z, coarse_rows, up_w)
-    up_terms = jnp.roll(up_acc.reshape(27, part_ch, coarse_in), coarse_start, axis=2)
-    own_k = coarse.shape[0]
-    received = lax.ppermute(coarse_acc[:, :, own_k:], "ch", swap)
-    coarse_summed = coarse_acc[:, :, :own_k] + received
+    up_terms = up_acc.reshape(27, part_ch, coarse_in)
+    other_start = own_k - coarse_start
+    received = lax.ppermute(lax.dynamic_slice_in_dim(coarse_acc, other_start, own_k, 2), "ch", swap)
+    coarse_summed = lax.dynamic_slice_in_dim(coarse_acc, coarse_start, own_k, 2) + received
     grad_coarse = jnp.transpose(coarse_summed, (2, 0, 1, 3)).astype(jnp.bfloat16)
     flat = jnp.concatenate([up_terms.reshape(-1), refine_terms.reshape(-1)])
     flat = summed_over_slabs(flat, ("gz", "sec"))
-    up_summed = flat[: up_terms.size].reshape(up_terms.shape)
-    refine_summed = flat[up_terms.size :].reshape(refine_terms.shape)
-    fine_total = planes_z * lax.axis_size("gz") * lax.axis_size("sec") * planes_x * cells_y
-    coarse_total = fine_total // 8
-    grad_up = up_summed * float(coarse_total) ** (-0.5)
-    grad_refine = refine_summed * float(fine_total) ** (-0.5)
+    grad_up = flat[: up_terms.size].reshape(up_terms.shape)
+    grad_refine = flat[up_terms.size :].reshape(refine_terms.shape)
     return (grad_coarse, grad_up, grad_refine)
 
 

time: 74 us -> 74.9 us (1.012)
  local copies, waits for them, and re-layouts: 11.3 us -> 13 us
  other arithmetic: 3.57 us -> 2.2 us
    another operation x0 -> x1, local copies, waits for them, and re-layouts: none -> 1.08 us  [local(): flat = jnp.concatenate([up_terms.reshape(-1), refine_terms.reshape(-1)])]
    pallas_call x0 -> x1, local copies, waits for them, and re-layouts: none -> 1.02 us  [fine_rows(): pl.pallas_call(functools.partial(fine_kernel, z_lo, z_hi, scale), out_sha...]
    mul x2 -> x0, local copies, waits for them, and re-layouts: 0.96 us -> none  [the longest x1 0.79 us: local(): grad_up = up_summed * float(coarse_total) ** (-0.5)]
    add x1 -> x0, other arithmetic: 0.93 us -> none  [local(): refine_acc = refine_main + refine_last]
    reshape x0 -> x1, local copies, waits for them, and re-layouts: none -> 0.79 us  [local(): grad_up = flat[:up_terms.size].reshape(up_terms.shape)]
    concatenate x3 -> x1, other arithmetic: 2.16 us -> 1.74 us  [local(): jnp.concatenate([coarse_own, coarse_other, coarse_own], axis=2)]
  transfers between devices with their start and end apart: 11 -> 11, of which waited for: 5 -> 5; matrix products, arithmetic and copies ran while one was open for 10% -> 11% of each run, Pallas kernels for 23% -> 22%
where the time goes in v10:
time: 74.9 us; the launch traced here: 74.5 us
  waiting for transfers between devices  23 us (31%)
  Pallas kernels  21.4 us (29%)
  starting transfers between devices  13.9 us (19%)
  local copies, waits for them, and re-layouts  13 us (17%)
  other arithmetic  2.2 us (3%)
  between operations  0.96 us (1%)
    pallas_call x2, Pallas kernels, fine_rows(): pl.pallas_call(functools.partial(fine_kernel, z_lo, z_hi, scale), out_sha...  16.6 us
    ppermute x3, waiting for transfers between devices, summed_over_slabs(): block = block + lax.ppermute(block, axis, route)  13.7 us
    ppermute x1, waiting for transfers between devices, local(): low = lax.ppermute(rows[planes_z - 2:], ('gz', 'sec'), forward)  7.17 us
    unnamed x33, local copies, waits for them, and re-layouts  6.98 us
    ppermute x3, starting transfers between devices, summed_over_slabs(): block = block + lax.ppermute(block, axis, route)  6.71 us
    pallas_call x1, Pallas kernels, local(): pl.pallas_call(functools.partial(coarse_kernel, float(coarse_total) ** (-...  4.8 us
    ppermute x1, starting transfers between devices, local(): high = lax.ppermute(rows[:2], ('gz', 'sec'), backward)  3.1 us
    ppermute x1, starting transfers between devices, local(): low = lax.ppermute(rows[planes_z - 2:], ('gz', 'sec'), forward)  2.99 us
  transfers between devices with their start and end apart: 11, of which 5 were waited for; matrix products, arithmetic and copies ran while one was open for 11% of the time, Pallas kernels for 22%

profile of v10, /device:TPU:0, one launch (start us, length us, event | category | flops | bytes accessed | tf_op | source)
XLA Modules:
  0.0 74.5 jit_solution(3520481368986160200)
XLA Ops:
  0.6 0.0 copy-start
  0.6 1.4 %copy.11 = bf16[16,4,8,512]{3,0,2,1:T(8,128)(2,1)S(1)} copy(bf16[16,4,8,512]{3,2,1,0:T(8,128)(2,1)} %param.7) | data formatting | bytes 1048576 | tf_op args[2]
  2.1 0.0 copy-start.11
  2.1 0.0 copy-start.10
  2.1 3.0 %collective-permute-start = (bf16[2,2,4,16,512]{4,3,2,1,0:T(8,128)(2,1)S(1)}, bf16[2,2,4,16,512]{4,3,2,1,0:T(8,128)(2,1)S(1)}, u32[]{:S(2)}, u32[]{:S(2)}) collective-permute-start(bf16[2,2,4,16,512]{4,3,2,1,0:T(8,128)(2,1)S(1)} %get-tuple-element.22), channel_id=1, source_target_pairs={{0,2},{2,4},{4,6},{6,8},{8,10},{10,12},{12,14},{14,0},{1,3},{3,5},... | collective-permute-start | bytes 786440 | tf_op jit(solution)/shard_map/ppermute | solution.py:180
  5.1 3.1 %collective-permute-start.1 = (bf16[2,2,4,16,512]{4,3,2,1,0:T(8,128)(2,1)S(1)}, bf16[2,2,4,16,512]{4,3,2,1,0:T(8,128)(2,1)S(1)}, u32[]{:S(2)}, u32[]{:S(2)}) collective-permute-start(bf16[2,2,4,16,512]{4,3,2,1,0:T(8,128)(2,1)S(1)} %get-tuple-element.21), channel_id=1, source_target_pairs={{2,0},{4,2},{6,4},{8,6},{10,8},{12,10},{14,12},{0,14},{3,1},{5,3},... | collective-permute-start | bytes 786440 | tf_op jit(solution)/shard_map/ppermute | solution.py:181
  8.3 0.6 collective-permute-start.6
  8.9 0.1 constant_dynamic-slice_fusion.2
  9.0 0.1 copy.23
  9.1 0.0 copy-start.9
  9.1 7.2 %collective-permute-done.refs_0_ = bf16[2,2,4,16,512]{4,3,2,1,0:T(8,128)(2,1)S(1)} collective-permute-done((bf16[2,2,4,16,512]{4,3,2,1,0:T(8,128)(2,1)S(1)}, bf16[2,2,4,16,512]{4,3,2,1,0:T(8,128)(2,1)S(1)}, u32[]{:S(2)}, u32[]{:S(2)}) %collective-permute-start) | collective-permute-done | bytes 262176 | tf_op jit(solution)/shard_map/ppermute | solution.py:180
  16.3 2.2 %collective-permute-done.1.refs_2_ = bf16[2,2,4,16,512]{4,3,2,1,0:T(8,128)(2,1)S(1)} collective-permute-done((bf16[2,2,4,16,512]{4,3,2,1,0:T(8,128)(2,1)S(1)}, bf16[2,2,4,16,512]{4,3,2,1,0:T(8,128)(2,1)S(1)}, u32[]{:S(2)}, u32[]{:S(2)}) %collective-permute-start.1) | collective-permute-done | bytes 262176 | tf_op jit(solution)/shard_map/ppermute | solution.py:181
  18.5 0.2 dynamic-slice_maximum_fusion.1
  18.7 0.1 copy.15
  18.8 0.4 copy-done.4
  19.2 0.7 reshape.50.refs_7_
  20.0 1.1 %copy.27 = bf16[16,4,8,512]{3,0,2,1:T(8,128)(2,1)} copy(bf16[16,4,8,512]{3,2,1,0:T(8,128)(2,1)S(1)} %copy-done.9) | data formatting | bytes 1048576 | tf_op args[1]
  21.1 0.8 %copy.17.u_ref = bf16[3,64,144]{2,1,0:T(8,128)(2,1)} copy(bf16[3,64,144]{1,2,0:T(8,128)(2,1)S(1)} %bitcast.38) | data formatting | bytes 110592 | tf_op jit(solution)/shard_map/reshape | solution.py:234
  21.9 0.7 copy-done.5
  22.6 0.1 copy-done.6
  22.7 0.2 copy-done.2
  22.8 5.7 %shard_map.76 = (bf16[1,8,16,512]{3,2,1,0:T(8,128)(2,1)}, f32[288,48]{1,0:T(8,128)}) custom-call(bf16[2,2,4,16,512]{4,3,2,1,0:T(8,128)(2,1)} %copy-done.3, bf16[4,2,4,16,512]{4,3,2,1,0:T(8,128)(2,1)} %bitcast.28, bf16[2,2,4,16,512]{4,3,2,1,0:T(8,128)(2,1)} %copy-done.4, bf16[2,2,4,16,512]{4,3,2,1,0:T(8,128)(2,1)} %copy-done.5, ...), custom_call_target="tpu_custom_call" | custom-call | tf_op jit(solution)/shard_map/pallas_call | solution.py:198
  28.5 0.4 collective-permute-start.5
  28.9 1.7 %fusion.1.c_ref = bf16[2,4,64,256]{3,2,1,0:T(8,128)(2,1)} fusion(s32[]{:T(128)S(6)} %select_n.39, bf16[2,4,32,256]{3,2,1,0:T(8,128)(2,1)S(1)} %bitcast.36, bf16[2,4,32,256]{3,2,1,0:T(8,128)(2,1)} %collective-permute-done.6), kind=kLoop, calls=%fused_computation.6 | loop fusion | flops 786432 | bytes 524292 | tf_op jit(solution)/shard_map/concatenate | solution.py:228
  30.7 11.0 %shard_map.77 = (bf16[3,8,16,512]{3,2,1,0:T(8,128)(2,1)}, f32[288,48]{1,0:T(8,128)}) custom-call(bf16[2,2,4,16,512]{4,3,2,1,0:T(8,128)(2,1)} %copy-done.3, bf16[4,2,4,16,512]{4,3,2,1,0:T(8,128)(2,1)} %bitcast.29, bf16[2,2,4,16,512]{4,3,2,1,0:T(8,128)(2,1)} %copy-done.4, bf16[2,2,4,16,512]{4,3,2,1,0:T(8,128)(2,1)} %copy-done.5, ...), custom_call_target="tpu_custom_call" | custom-call | tf_op jit(solution)/shard_map/pallas_call | solution.py:198
  41.6 1.0 %copy.18 = f32[288,48]{0,1:T(8,128)S(1)} copy(f32[288,48]{1,0:T(8,128)} %get-tuple-element.14) | data formatting | bytes 110592 | tf_op jit(solution)/shard_map/pallas_call | solution.py:198
  42.7 0.2 reshape.55
  42.8 0.6 rev.7
  43.4 0.2 dynamic-slice_maximum_fusion
  43.6 0.2 copy.20
  43.8 0.2 reshape.57
  44.0 0.6 copy-done.12
  44.7 4.8 %shard_map.78 = (f32[2,4,64,256]{3,2,1,0:T(8,128)}, f32[3,144,64]{2,1,0:T(8,128)}) custom-call(bf16[3,128,512]{2,1,0:T(8,128)(2,1)} %bitcast.39, bf16[1,128,512]{2,1,0:T(8,128)(2,1)} %bitcast.41, bf16[1,128,512]{2,1,0:T(8,128)(2,1)} %copy-done.12, bf16[2,4,64,256]{3,2,1,0:T(8,128)(2,1)} %fusion.1.c_ref, bf16[3,64,144]{2,1,0:T(8,128)(2,1)} %copy.17.u_ref), custom_call_target="tpu_custom_call" | custom-call | tf_op jit(solution)/shard_map/pallas_call | solution.py:236
  49.5 1.1 %reshape_reshape.3 = f32[27648]{0:T(1024)S(1)} reshape(f32[3,144,64]{2,1,0:T(8,128)} %get-tuple-element.13) | data formatting | bytes 221184 | tf_op jit(solution)/shard_map/reshape;reshape | solution.py:253
  50.6 2.4 %collective-permute-start.8 = (f32[41472]{0:T(1024)S(1)}, f32[41472]{0:T(1024)S(1)}, u32[]{:S(2)}, u32[]{:S(2)}) collective-permute-start(f32[41472]{0:T(1024)S(1)} %constant_dynamic-update-slice_fusion), channel_id=1, source_target_pairs={{0,2},{2,0},{4,6},{6,4},{8,10},{10,8},{12,14},{14,12},{1,3},{3,1},... | collective-permute-start | bytes 497672 | tf_op jit(solution)/shard_map/ppermute | solution.py:40
  53.0 0.1 collective-permute-start.7
  53.1 4.2 %collective-permute-done.8 = f32[41472]{0:T(1024)S(1)} collective-permute-done((f32[41472]{0:T(1024)S(1)}, f32[41472]{0:T(1024)S(1)}, u32[]{:S(2)}, u32[]{:S(2)}) %collective-permute-start.8) | collective-permute-done | bytes 165920 | tf_op jit(solution)/shard_map/ppermute | solution.py:40
  57.3 1.6 %collective-permute-start.9 = (f32[41472]{0:T(1024)S(1)}, f32[41472]{0:T(1024)S(1)}, u32[]{:S(2)}, u32[]{:S(2)}) collective-permute-start(f32[41472]{0:T(1024)S(1)} %add.54), channel_id=1, source_target_pairs={{0,4},{2,6},{4,0},{6,2},{8,12},{10,14},{12,8},{14,10},{1,5},{3,7},... | collective-permute-start | bytes 497672 | tf_op jit(solution)/shard_map/ppermute | solution.py:40
  58.9 3.9 %collective-permute-done.9 = f32[41472]{0:T(1024)S(1)} collective-permute-done((f32[41472]{0:T(1024)S(1)}, f32[41472]{0:T(1024)S(1)}, u32[]{:S(2)}, u32[]{:S(2)}) %collective-permute-start.9) | collective-permute-done | bytes 165920 | tf_op jit(solution)/shard_map/ppermute | solution.py:40
  62.8 2.6 %collective-permute-start.10 = (f32[41472]{0:T(1024)S(1)}, f32[41472]{0:T(1024)S(1)}, u32[]{:S(2)}, u32[]{:S(2)}) collective-permute-start(f32[41472]{0:T(1024)S(1)} %add.55), channel_id=1, source_target_pairs={{0,8},{2,10},{4,12},{6,14},{8,0},{10,2},{12,4},{14,6},{1,9},{3,11}... | collective-permute-start | bytes 497672 | tf_op jit(solution)/shard_map/ppermute | solution.py:40
  65.5 0.8 %copy.21 = bf16[32,2,4,256]{3,2,1,0:T(4,128)(2,1)} copy(bf16[32,2,4,256]{3,0,2,1:T(8,128)(2,1)S(1)} %fusion.2) | data formatting | bytes 262144
  66.3 5.6 %collective-permute-done.10 = f32[41472]{0:T(1024)S(1)} collective-permute-done((f32[41472]{0:T(1024)S(1)}, f32[41472]{0:T(1024)S(1)}, u32[]{:S(2)}, u32[]{:S(2)}) %collective-permute-start.10) | collective-permute-done | bytes 165920 | tf_op jit(solution)/shard_map/ppermute | solution.py:40
  72.0 0.0 copy-start.7
  72.0 0.6 copy-done.7
  72.6 0.2 slice.26
  72.8 0.9 %copy.22 = f32[27,32,16]{1,2,0:T(8,128)} copy(f32[27,32,16]{2,1,0:T(8,128)S(1)} %slice.26) | data formatting | bytes 110592
  73.7 0.0 slice-done
  73.7 0.8 %reshape.58 = f32[27,16,64]{2,1,0:T(8,128)} reshape(f32[27648]{0:T(1024)S(1)} %slice-done) | data formatting | bytes 221184 | tf_op jit(solution)/shard_map/reshape | solution.py:255
  (39 shorter events, 0.3 us)
Async XLA Ops:
  0.6 20.4 %copy-start = (bf16[27,32,64]{2,1,0:T(8,128)(2,1)S(1)}, bf16[27,32,64]{2,1,0:T(8,128)(2,1)}, u32[]{:S(2)}) copy-start(bf16[27,32,64]{2,1,0:T(8,128)(2,1)} %param.8) | copy-start | bytes 331780
  2.1 6.2 %copy-start.1 = (bf16[16,4,4,2,512]{4,0,2,3,1:T(8,128)(2,1)}, bf16[16,4,4,2,512]{4,0,2,3,1:T(8,128)(2,1)S(1)}, u32[]{:S(2)}) copy-start(bf16[16,4,4,2,512]{4,0,2,3,1:T(8,128)(2,1)S(1)} %copy.28) | copy-start | bytes 1572868
  2.1 6.2 %copy-start.11 = (bf16[32,2,4,256]{3,2,1,0:T(4,128)(2,1)S(1)}, bf16[32,2,4,256]{3,2,1,0:T(4,128)(2,1)}, u32[]{:S(2)}) copy-start(bf16[32,2,4,256]{3,2,1,0:T(4,128)(2,1)} %param.5) | copy-start | bytes 393220
  2.1 6.7 %copy-start.10 = (bf16[27,32,32]{2,1,0:T(8,128)(2,1)S(1)}, bf16[27,32,32]{2,1,0:T(8,128)(2,1)}, u32[]{:S(2)}) copy-start(bf16[27,32,32]{2,1,0:T(8,128)(2,1)} %param.9) | copy-start | bytes 165892
  2.1 14.2 %collective-permute-start = (bf16[2,2,4,16,512]{4,3,2,1,0:T(8,128)(2,1)S(1)}, bf16[2,2,4,16,512]{4,3,2,1,0:T(8,128)(2,1)S(1)}, u32[]{:S(2)}, u32[]{:S(2)}) collective-permute-start(bf16[2,2,4,16,512]{4,3,2,1,0:T(8,128)(2,1)S(1)} %get-tuple-element.22), channel_id=1, source_target_pairs={{0,2},{2,4},{4,6},{6,8},{8,10},{10,12},{12,14},{14,0},{1,3},{3,5},... | collective-permute-start | bytes 786440 | tf_op jit(solution)/shard_map/ppermute | solution.py:180
  5.1 13.4 %collective-permute-start.1 = (bf16[2,2,4,16,512]{4,3,2,1,0:T(8,128)(2,1)S(1)}, bf16[2,2,4,16,512]{4,3,2,1,0:T(8,128)(2,1)S(1)}, u32[]{:S(2)}, u32[]{:S(2)}) collective-permute-start(bf16[2,2,4,16,512]{4,3,2,1,0:T(8,128)(2,1)S(1)} %get-tuple-element.21), channel_id=1, source_target_pairs={{2,0},{4,2},{6,4},{8,6},{10,8},{12,10},{14,12},{0,14},{3,1},{5,3},... | collective-permute-start | bytes 786440 | tf_op jit(solution)/shard_map/ppermute | solution.py:181
  8.2 13.7 %collective-permute-start.3 = (bf16[4,2,4,16,512]{4,3,2,1,0:T(8,128)(2,1)S(1)}, bf16[4,2,4,16,512]{4,3,2,1,0:T(8,128)(2,1)S(1)}, u32[]{:S(2)}, u32[]{:S(2)}) collective-permute-start(bf16[4,2,4,16,512]{4,3,2,1,0:T(8,128)(2,1)S(1)} %bitcast.27), channel_id=1, source_target_pairs={{0,1},{1,0},{2,3},{3,2},{4,5},{5,4},{6,7},{7,6},{8,9},{9,8},{10,11... | collective-permute-start | bytes 1572872 | tf_op jit(solution)/shard_map/ppermute | solution.py:182
  8.3 20.6 %collective-permute-start.6 = (bf16[2,4,32,256]{3,2,1,0:T(8,128)(2,1)S(1)}, bf16[2,4,32,256]{3,2,1,0:T(8,128)(2,1)}, u32[]{:S(2)}, u32[]{:S(2)}) collective-permute-start(bf16[2,4,32,256]{3,2,1,0:T(8,128)(2,1)S(1)} %bitcast.35), channel_id=1, source_target_pairs={{0,1},{1,0},{2,3},{3,2},{4,5},{5,4},{6,7},{7,6},{8,9},{9,8},{10,11... | collective-permute-start | bytes 393224 | tf_op jit(solution)/shard_map/ppermute | solution.py:225
  9.1 10.8 %copy-start.9 = (bf16[16,4,8,512]{3,2,1,0:T(8,128)(2,1)S(1)}, bf16[16,4,8,512]{3,2,1,0:T(8,128)(2,1)}, u32[]{:S(2)}) copy-start(bf16[16,4,8,512]{3,2,1,0:T(8,128)(2,1)} %param.6) | copy-start | bytes 1572868
  16.3 2.5 %copy-start.3 = (bf16[2,2,4,16,512]{4,3,2,1,0:T(8,128)(2,1)}, bf16[2,2,4,16,512]{4,3,2,1,0:T(8,128)(2,1)S(1)}, u32[]{:S(2)}) copy-start(bf16[2,2,4,16,512]{4,3,2,1,0:T(8,128)(2,1)S(1)} %collective-permute-done.refs_0_) | copy-start | bytes 786436
  16.3 5.6 %collective-permute-start.2 = (bf16[2,2,4,16,512]{4,3,2,1,0:T(8,128)(2,1)S(1)}, bf16[2,2,4,16,512]{4,3,2,1,0:T(8,128)(2,1)S(1)}, u32[]{:S(2)}, u32[]{:S(2)}) collective-permute-start(bf16[2,2,4,16,512]{4,3,2,1,0:T(8,128)(2,1)S(1)} %collective-permute-done.refs_0_), channel_id=1, source_target_pairs={{0,1},{1,0},{2,3},{3,2},{4,5},{5,4},{6,7},{7,6},{8,9},{9,8},{10,11... | collective-permute-start | bytes 786440 | tf_op jit(solution)/shard_map/ppermute | solution.py:183
  18.5 0.7 copy-start.4
  18.5 3.4 %collective-permute-start.4 = (bf16[2,2,4,16,512]{4,3,2,1,0:T(8,128)(2,1)S(1)}, bf16[2,2,4,16,512]{4,3,2,1,0:T(8,128)(2,1)S(1)}, u32[]{:S(2)}, u32[]{:S(2)}) collective-permute-start(bf16[2,2,4,16,512]{4,3,2,1,0:T(8,128)(2,1)S(1)} %collective-permute-done.1.refs_2_), channel_id=1, source_target_pairs={{0,1},{1,0},{2,3},{3,2},{4,5},{5,4},{6,7},{7,6},{8,9},{9,8},{10,11... | collective-permute-start | bytes 786440 | tf_op jit(solution)/shard_map/ppermute | solution.py:184
  21.9 0.7 copy-start.5
  21.9 0.8 %copy-start.6 = (bf16[2,2,4,16,512]{4,3,2,1,0:T(8,128)(2,1)}, bf16[2,2,4,16,512]{4,3,2,1,0:T(8,128)(2,1)S(1)}, u32[]{:S(2)}) copy-start(bf16[2,2,4,16,512]{4,3,2,1,0:T(8,128)(2,1)S(1)} %collective-permute-done.4.refs_5_) | copy-start | bytes 786436
  21.9 0.9 %copy-start.2 = (bf16[4,2,4,16,512]{4,3,2,1,0:T(8,128)(2,1)}, bf16[4,2,4,16,512]{4,3,2,1,0:T(8,128)(2,1)S(1)}, u32[]{:S(2)}) copy-start(bf16[4,2,4,16,512]{4,3,2,1,0:T(8,128)(2,1)S(1)} %collective-permute-done.3.refs_4_) | copy-start | bytes 1572868
  28.5 15.5 %collective-permute-start.5 = (bf16[1,128,512]{2,1,0:T(8,128)(2,1)}, bf16[1,128,512]{2,1,0:T(8,128)(2,1)S(1)}, u32[]{:S(2)}, u32[]{:S(2)}) collective-permute-start(bf16[1,128,512]{2,1,0:T(8,128)(2,1)} %bitcast.40), channel_id=1, source_target_pairs={{14,0},{0,2},{2,4},{4,6},{6,8},{8,10},{10,12},{12,14},{15,1},{1,3}... | collective-permute-start | bytes 393224 | tf_op jit(solution)/shard_map/ppermute | solution.py:30
  44.0 0.7 copy-start.12
  49.5 3.5 %copy-start.8 = (f32[2,4,64,256]{3,2,1,0:T(8,128)S(1)}, f32[2,4,64,256]{3,2,1,0:T(8,128)}, u32[]{:S(2)}) copy-start(f32[2,4,64,256]{3,2,1,0:T(8,128)} %get-tuple-element.12) | copy-start | bytes 1572868
  50.6 6.7 %collective-permute-start.8 = (f32[41472]{0:T(1024)S(1)}, f32[41472]{0:T(1024)S(1)}, u32[]{:S(2)}, u32[]{:S(2)}) collective-permute-start(f32[41472]{0:T(1024)S(1)} %constant_dynamic-update-slice_fusion), channel_id=1, source_target_pairs={{0,2},{2,0},{4,6},{6,4},{8,10},{10,8},{12,14},{14,12},{1,3},{3,1},... | collective-permute-start | bytes 497672 | tf_op jit(solution)/shard_map/ppermute | solution.py:40
  53.0 12.4 %collective-permute-start.7 = (f32[2,4,32,256]{3,2,1,0:T(8,128)S(1)}, f32[2,4,32,256]{3,2,1,0:T(8,128)S(1)}, u32[]{:S(2)}, u32[]{:S(2)}) collective-permute-start(f32[2,4,32,256]{3,2,1,0:T(8,128)S(1)} %constant_dynamic-slice_fusion), channel_id=1, source_target_pairs={{0,1},{1,0},{2,3},{3,2},{4,5},{5,4},{6,7},{7,6},{8,9},{9,8},{10,11... | collective-permute-start | bytes 786440 | tf_op jit(solution)/shard_map/ppermute | solution.py:250
  57.3 5.5 %collective-permute-start.9 = (f32[41472]{0:T(1024)S(1)}, f32[41472]{0:T(1024)S(1)}, u32[]{:S(2)}, u32[]{:S(2)}) collective-permute-start(f32[41472]{0:T(1024)S(1)} %add.54), channel_id=1, source_target_pairs={{0,4},{2,6},{4,0},{6,2},{8,12},{10,14},{12,8},{14,10},{1,5},{3,7},... | collective-permute-start | bytes 497672 | tf_op jit(solution)/shard_map/ppermute | solution.py:40
  62.8 9.1 %collective-permute-start.10 = (f32[41472]{0:T(1024)S(1)}, f32[41472]{0:T(1024)S(1)}, u32[]{:S(2)}, u32[]{:S(2)}) collective-permute-start(f32[41472]{0:T(1024)S(1)} %add.55), channel_id=1, source_target_pairs={{0,8},{2,10},{4,12},{6,14},{8,0},{10,2},{12,4},{14,6},{1,9},{3,11}... | collective-permute-start | bytes 497672 | tf_op jit(solution)/shard_map/ppermute | solution.py:40
  72.0 0.7 copy-start.7
  72.8 0.9 %slice-start = ((f32[41472]{0:T(1024)}), f32[27648]{0:T(1024)S(1)}, s32[]{:S(2)}) async-start(f32[41472]{0:T(1024)} %copy-done.7), calls=%async_computation | async-start | bytes 221184 | tf_op jit(solution)/shard_map/slice | solution.py:255

commit v11 on v10

--- a/solution.py
+++ b/solution.py
@@ -203,6 +203,11 @@
             ),
             in_specs=[pl.BlockSpec(memory_space=pl.ANY)] * 6 + vmem_specs(2 + len(start)),
             out_specs=tuple(vmem_specs(2)),
+            cost_estimate=pl.CostEstimate(
+                flops=4 * (z_hi - z_lo) * planes_x * 27 * all_ch * part_ch * cells_y,
+                bytes_accessed=2 * halo_z * planes_x * all_ch * cells_y,
+                transcendentals=0,
+            ),
             scratch_shapes=[
                 pltpu.VMEM(
                     (2, halo_z // 2, 2, planes_x // 2 + 2, all_ch, cells_y), jnp.bfloat16
@@ -219,6 +224,7 @@
     refine_terms = refine_acc.reshape(3, 3, all_ch, 3, part_ch)[::-1, ::-1]
     refine_terms = jnp.transpose(refine_terms, (0, 1, 3, 2, 4)).reshape(27, all_ch, part_ch)
     refine_terms = jnp.roll(refine_terms, channel_start, axis=1)
+    grad_refine = summed_over_slabs(refine_terms, ("gz", "sec"))
 
 
     coarse_own = jnp.transpose(coarse, (1, 2, 0, 3))
@@ -241,6 +247,12 @@
         ),
         in_specs=vmem_specs(5),
         out_specs=tuple(vmem_specs(2)),
+        cost_estimate=pl.CostEstimate(
+            flops=4 * coarse_z * coarse_x * 27 * part_ch * coarse_in * cells_yc
+            + 2 * (planes_z + 1) * planes_x * part_ch * cells_y * 3 * cells_yc,
+            bytes_accessed=2 * (planes_z + 1) * planes_x * part_ch * cells_y,
+            transcendentals=0,
+        ),
         scratch_shapes=[
             pltpu.VMEM((planes_z + 1, planes_x + 1, 3, part_ch, cells_yc), jnp.bfloat16)
         ],
@@ -250,10 +262,7 @@
     received = lax.ppermute(lax.dynamic_slice_in_dim(coarse_acc, other_start, own_k, 2), "ch", swap)
     coarse_summed = lax.dynamic_slice_in_dim(coarse_acc, coarse_start, own_k, 2) + received
     grad_coarse = jnp.transpose(coarse_summed, (2, 0, 1, 3)).astype(jnp.bfloat16)
-    flat = jnp.concatenate([up_terms.reshape(-1), refine_terms.reshape(-1)])
-    flat = summed_over_slabs(flat, ("gz", "sec"))
-    grad_up = flat[: up_terms.size].reshape(up_terms.shape)
-    grad_refine = flat[up_terms.size :].reshape(refine_terms.shape)
+    grad_up = summed_over_slabs(up_terms, ("gz", "sec"))
     return (grad_coarse, grad_up, grad_refine)
 
 

time: 74.9 us -> 85.6 us (1.14)
  waiting for transfers between devices: 23 us -> 33.8 us
  local copies, waits for them, and re-layouts: 13 us -> 10.3 us
  starting transfers between devices: 13.9 us -> 15.9 us
    ppermute x3 -> x6, waiting for transfers between devices: 13.7 us -> 24.5 us  [summed_over_slabs(): block = block + lax.ppermute(block, axis, route)]
    unnamed x33 -> x31, local copies, waits for them, and re-layouts: 6.98 us -> 5.04 us
    add x3 -> x6, other arithmetic: 0.06 us -> 1.71 us  [summed_over_slabs(): block = block + lax.ppermute(block, axis, route)]
    ppermute x3 -> x6, starting transfers between devices: 6.71 us -> 8.19 us  [summed_over_slabs(): block = block + lax.ppermute(block, axis, route)]
    another operation x1 -> x0, local copies, waits for them, and re-layouts: 1.08 us -> none  [local(): flat = jnp.concatenate([up_terms.reshape(-1), refine_terms.reshape(-1)])]
    reshape x2 -> x0, local copies, waits for them, and re-layouts: 0.96 us -> none  [the longest x1 0.79 us: local(): grad_up = flat[:up_terms.size].reshape(up_terms.shape)]
    dynamic_slice x1, local copies, waits for them, and re-layouts: 0.02 us -> 0.97 us  [local(): lax.dynamic_slice_in_dim(coarse_acc, other_start, own_k, 2)]
    concatenate x1, other arithmetic: 1.74 us -> 0.85 us  [local(): jnp.concatenate([coarse_own, coarse_other, coarse_own], axis=2)]
  transfers between devices with their start and end apart: 11 -> 14, of which waited for: 5 -> 5; matrix products, arithmetic and copies ran while one was open for 11% -> 10% of each run, Pallas kernels for 22% -> 18%
where the time goes in v11:
time: 85.6 us; the launch traced here: 85.2 us
  waiting for transfers between devices  33.8 us (39%)
  Pallas kernels  21.4 us (25%)
  starting transfers between devices  15.9 us (19%)
  local copies, waits for them, and re-layouts  10.3 us (12%)
  other arithmetic  2.96 us (3%)
  between operations  0.9 us (1%)
    ppermute x6, waiting for transfers between devices, summed_over_slabs(): block = block + lax.ppermute(block, axis, route)  24.5 us
    pallas_call x2, Pallas kernels, fine_rows(): pl.pallas_call(functools.partial(fine_kernel, z_lo, z_hi, scale), out_sha...  16.6 us
    ppermute x6, starting transfers between devices, summed_over_slabs(): block = block + lax.ppermute(block, axis, route)  8.19 us
    ppermute x1, waiting for transfers between devices, local(): low = lax.ppermute(rows[planes_z - 2:], ('gz', 'sec'), forward)  7.38 us
    unnamed x31, local copies, waits for them, and re-layouts  5.04 us
    pallas_call x1, Pallas kernels, local(): pl.pallas_call(functools.partial(coarse_kernel, float(coarse_total) ** (-...  4.8 us
    ppermute x1, starting transfers between devices, local(): high = lax.ppermute(rows[:2], ('gz', 'sec'), backward)  3.04 us
    ppermute x1, starting transfers between devices, local(): low = lax.ppermute(rows[planes_z - 2:], ('gz', 'sec'), forward)  2.94 us
  transfers between devices with their start and end apart: 14, of which 5 were waited for; matrix products, arithmetic and copies ran while one was open for 10% of the time, Pallas kernels for 18%

profile of v11, /device:TPU:0, one launch (start us, length us, event | category | flops | bytes accessed | tf_op | source)
XLA Modules:
  0.0 85.2 jit_solution(15981370136868458881)
XLA Ops:
  0.6 0.0 copy-start
  0.6 1.4 %copy.21 = bf16[16,4,8,512]{3,0,2,1:T(8,128)(2,1)S(1)} copy(bf16[16,4,8,512]{3,2,1,0:T(8,128)(2,1)} %param.7) | data formatting | bytes 1048576 | tf_op args[2]
  2.1 0.0 copy-start.11
  2.1 0.8 fusion.3
  2.9 2.9 %collective-permute-start = (bf16[2,2,4,16,512]{4,3,2,1,0:T(8,128)(2,1)}, bf16[2,2,4,16,512]{4,3,2,1,0:T(8,128)(2,1)S(1)}, u32[]{:S(2)}, u32[]{:S(2)}) collective-permute-start(bf16[2,2,4,16,512]{4,3,2,1,0:T(8,128)(2,1)} %get-tuple-element.25), channel_id=1, source_target_pairs={{0,2},{2,4},{4,6},{6,8},{8,10},{10,12},{12,14},{14,0},{1,3},{3,5},... | collective-permute-start | bytes 786440 | tf_op jit(solution)/shard_map/ppermute | solution.py:180
  5.8 3.0 %collective-permute-start.1 = (bf16[2,2,4,16,512]{4,3,2,1,0:T(8,128)(2,1)S(1)}, bf16[2,2,4,16,512]{4,3,2,1,0:T(8,128)(2,1)S(1)}, u32[]{:S(2)}, u32[]{:S(2)}) collective-permute-start(bf16[2,2,4,16,512]{4,3,2,1,0:T(8,128)(2,1)S(1)} %get-tuple-element.24), channel_id=1, source_target_pairs={{2,0},{4,2},{6,4},{8,6},{10,8},{12,10},{14,12},{0,14},{3,1},{5,3},... | collective-permute-start | bytes 786440 | tf_op jit(solution)/shard_map/ppermute | solution.py:181
  8.9 0.6 collective-permute-start.6
  9.5 0.1 constant_dynamic-slice_fusion.2
  9.6 0.1 copy.31
  9.7 0.0 copy-start.8
  9.8 0.2 dynamic-slice_maximum_fusion.1
  9.9 7.4 %collective-permute-done.refs_0_ = bf16[2,2,4,16,512]{4,3,2,1,0:T(8,128)(2,1)S(1)} collective-permute-done((bf16[2,2,4,16,512]{4,3,2,1,0:T(8,128)(2,1)}, bf16[2,2,4,16,512]{4,3,2,1,0:T(8,128)(2,1)S(1)}, u32[]{:S(2)}, u32[]{:S(2)}) %collective-permute-start) | collective-permute-done | bytes 262176 | tf_op jit(solution)/shard_map/ppermute | solution.py:180
  17.3 1.9 %collective-permute-done.1.refs_2_ = bf16[2,2,4,16,512]{4,3,2,1,0:T(8,128)(2,1)S(1)} collective-permute-done((bf16[2,2,4,16,512]{4,3,2,1,0:T(8,128)(2,1)S(1)}, bf16[2,2,4,16,512]{4,3,2,1,0:T(8,128)(2,1)S(1)}, u32[]{:S(2)}, u32[]{:S(2)}) %collective-permute-start.1) | collective-permute-done | bytes 262176 | tf_op jit(solution)/shard_map/ppermute | solution.py:181
  19.2 0.0 collective-permute-start.4
  19.2 0.1 copy.25
  19.3 0.7 reshape.38.refs_7_
  20.0 1.1 %copy.35 = bf16[16,4,8,512]{3,0,2,1:T(8,128)(2,1)} copy(bf16[16,4,8,512]{3,2,1,0:T(8,128)(2,1)S(1)} %copy-done.8) | data formatting | bytes 1048576 | tf_op args[1]
  21.1 0.8 copy.27.u_ref
  21.9 0.9 %fusion.1.c_ref = bf16[2,4,64,256]{3,2,1,0:T(8,128)(2,1)} fusion(s32[]{:T(128)S(6)} %select_n.39, bf16[2,4,32,256]{3,2,1,0:T(8,128)(2,1)S(1)} %bitcast.38, bf16[2,4,32,256]{3,2,1,0:T(8,128)(2,1)S(1)} %collective-permute-done.6), kind=kLoop, calls=%fused_computation.6 | loop fusion | flops 786432 | bytes 524292 | tf_op jit(solution)/shard_map/concatenate | solution.py:234
  22.8 0.0 collective-permute-done.3.refs_4_
  22.8 0.7 copy-done.5
  23.5 0.1 copy-done.6
  23.6 0.2 copy-done.2
  23.8 5.7 %shard_map.76 = (bf16[1,8,16,512]{3,2,1,0:T(8,128)(2,1)}, f32[288,48]{1,0:T(8,128)}) custom-call(bf16[2,2,4,16,512]{4,3,2,1,0:T(8,128)(2,1)} %copy-done.3, bf16[4,2,4,16,512]{4,3,2,1,0:T(8,128)(2,1)} %bitcast.29, bf16[2,2,4,16,512]{4,3,2,1,0:T(8,128)(2,1)} %copy-done.4, bf16[2,2,4,16,512]{4,3,2,1,0:T(8,128)(2,1)} %copy-done.5, ...), custom_call_target="tpu_custom_call" | custom-call | flops 226492416 | bytes 2097152 | tf_op jit(solution)/shard_map/pallas_call | solution.py:198
  29.4 1.1 %collective-permute-start.5 = (bf16[1,128,512]{2,1,0:T(8,128)(2,1)}, bf16[1,128,512]{2,1,0:T(8,128)(2,1)S(1)}, u32[]{:S(2)}, u32[]{:S(2)}) collective-permute-start(bf16[1,128,512]{2,1,0:T(8,128)(2,1)} %bitcast.44), channel_id=1, source_target_pairs={{14,0},{0,2},{2,4},{4,6},{6,8},{8,10},{10,12},{12,14},{15,1},{1,3}... | collective-permute-start | bytes 393224 | tf_op jit(solution)/shard_map/ppermute | solution.py:30
  30.5 11.0 %shard_map.77 = (bf16[3,8,16,512]{3,2,1,0:T(8,128)(2,1)}, f32[288,48]{1,0:T(8,128)}) custom-call(bf16[2,2,4,16,512]{4,3,2,1,0:T(8,128)(2,1)} %copy-done.3, bf16[4,2,4,16,512]{4,3,2,1,0:T(8,128)(2,1)} %bitcast.30, bf16[2,2,4,16,512]{4,3,2,1,0:T(8,128)(2,1)} %copy-done.4, bf16[2,2,4,16,512]{4,3,2,1,0:T(8,128)(2,1)} %copy-done.5, ...), custom_call_target="tpu_custom_call" | custom-call | flops 679477248 | bytes 2097152 | tf_op jit(solution)/shard_map/pallas_call | solution.py:198
  41.4 1.0 %copy.28 = f32[288,48]{0,1:T(8,128)S(1)} copy(f32[288,48]{1,0:T(8,128)} %get-tuple-element.14) | data formatting | bytes 110592 | tf_op jit(solution)/shard_map/pallas_call | solution.py:198
  42.5 0.2 reshape.44
  42.6 0.6 rev.7
  43.2 0.2 dynamic-slice_maximum_fusion
  43.4 2.0 %collective-permute-start.11 = (f32[27,32,16]{1,2,0:T(8,128)S(1)}, f32[27,32,16]{1,2,0:T(8,128)S(1)}, u32[]{:S(2)}, u32[]{:S(2)}) collective-permute-start(f32[27,32,16]{1,2,0:T(8,128)S(1)} %dynamic-slice_maximum_fusion), channel_id=1, source_target_pairs={{0,2},{2,0},{4,6},{6,4},{8,10},{10,8},{12,14},{14,12},{1,3},{3,1},... | collective-permute-start | bytes 165896 | tf_op jit(solution)/shard_map/ppermute | solution.py:40
  45.4 0.7 copy-done.12
  46.1 4.8 %shard_map.78 = (f32[2,4,64,256]{3,2,1,0:T(8,128)}, f32[3,144,64]{2,1,0:T(8,128)}) custom-call(bf16[3,128,512]{2,1,0:T(8,128)(2,1)} %bitcast.43, bf16[1,128,512]{2,1,0:T(8,128)(2,1)} %bitcast.45, bf16[1,128,512]{2,1,0:T(8,128)(2,1)} %copy-done.12, bf16[2,4,64,256]{3,2,1,0:T(8,128)(2,1)} %fusion.1.c_ref, bf16[3,64,144]{2,1,0:T(8,128)(2,1)} %copy.27.u_ref), custom_call_target="tpu_custom_call" | custom-call | flops 729808896 | bytes 655360 | tf_op jit(solution)/shard_map/pallas_call | solution.py:242
  50.9 0.1 collective-permute-start.8
  51.0 1.0 %constant_dynamic-slice_fusion = f32[2,4,32,256]{3,2,1,0:T(8,128)S(1)} fusion(f32[2,4,64,256]{3,2,1,0:T(8,128)} %get-tuple-element.12, s32[]{:T(128)S(6)} %select_n.41), kind=kLoop, calls=%fused_computation.13 | loop fusion | bytes 524292 | tf_op jit(solution)/shard_map/dynamic_slice | solution.py:262
  52.0 0.0 copy-start.10
  52.0 0.1 collective-permute-start.7
  52.1 0.2 fusion.4
  52.3 1.6 %collective-permute-start.12 = (f32[27,32,16]{1,2,0:T(8,128)S(1)}, f32[27,32,16]{1,2,0:T(8,128)S(1)}, u32[]{:S(2)}, u32[]{:S(2)}) collective-permute-start(f32[27,32,16]{1,2,0:T(8,128)S(1)} %fusion.4), channel_id=1, source_target_pairs={{0,4},{2,6},{4,0},{6,2},{8,12},{10,14},{12,8},{14,10},{1,5},{3,7},... | collective-permute-start | bytes 165896 | tf_op jit(solution)/shard_map/ppermute | solution.py:40
  53.9 4.5 %collective-permute-done.8 = f32[27,16,64]{2,1,0:T(8,128)S(1)} collective-permute-done((f32[27,16,64]{2,1,0:T(8,128)}, f32[27,16,64]{2,1,0:T(8,128)S(1)}, u32[]{:S(2)}, u32[]{:S(2)}) %collective-permute-start.8) | collective-permute-done | bytes 110624 | tf_op jit(solution)/shard_map/ppermute | solution.py:40
  58.4 1.7 %collective-permute-start.9 = (f32[27,16,64]{2,1,0:T(8,128)S(1)}, f32[27,16,64]{2,1,0:T(8,128)S(1)}, u32[]{:S(2)}, u32[]{:S(2)}) collective-permute-start(f32[27,16,64]{2,1,0:T(8,128)S(1)} %add.61), channel_id=1, source_target_pairs={{0,4},{2,6},{4,0},{6,2},{8,12},{10,14},{12,8},{14,10},{1,5},{3,7},... | collective-permute-start | bytes 331784 | tf_op jit(solution)/shard_map/ppermute | solution.py:40
  60.2 2.6 %collective-permute-start.13 = (f32[27,32,16]{1,2,0:T(8,128)S(1)}, f32[27,32,16]{1,2,0:T(8,128)S(1)}, u32[]{:S(2)}, u32[]{:S(2)}) collective-permute-start(f32[27,32,16]{1,2,0:T(8,128)S(1)} %add.67), channel_id=1, source_target_pairs={{0,8},{2,10},{4,12},{6,14},{8,0},{10,2},{12,4},{14,6},{1,9},{3,11}... | collective-permute-start | bytes 165896 | tf_op jit(solution)/shard_map/ppermute | solution.py:40
  62.8 10.1 %collective-permute-done.13 = f32[27,32,16]{1,2,0:T(8,128)S(1)} collective-permute-done((f32[27,32,16]{1,2,0:T(8,128)S(1)}, f32[27,32,16]{1,2,0:T(8,128)S(1)}, u32[]{:S(2)}, u32[]{:S(2)}) %collective-permute-start.13) | collective-permute-done | bytes 55328 | tf_op jit(solution)/shard_map/ppermute | solution.py:40
  73.0 0.7 add.68
  73.7 0.1 collective-permute-start.10
  73.9 0.8 copy.30
  74.6 9.9 %collective-permute-done.10 = f32[27,16,64]{2,1,0:T(8,128)S(1)} collective-permute-done((f32[27,16,64]{2,1,0:T(8,128)S(1)}, f32[27,16,64]{2,1,0:T(8,128)S(1)}, u32[]{:S(2)}, u32[]{:S(2)}) %collective-permute-start.10) | collective-permute-done | bytes 110624 | tf_op jit(solution)/shard_map/ppermute | solution.py:40
  84.5 0.7 add.63
  (37 shorter events, 0.3 us)
Async XLA Ops:
  0.6 20.5 %copy-start = (bf16[27,32,64]{2,1,0:T(8,128)(2,1)S(1)}, bf16[27,32,64]{2,1,0:T(8,128)(2,1)}, u32[]{:S(2)}) copy-start(bf16[27,32,64]{2,1,0:T(8,128)(2,1)} %param.8) | copy-start | bytes 331780
  2.1 6.8 %copy-start.1 = (bf16[16,4,4,2,512]{4,0,2,3,1:T(8,128)(2,1)}, bf16[16,4,4,2,512]{4,0,2,3,1:T(8,128)(2,1)S(1)}, u32[]{:S(2)}) copy-start(bf16[16,4,4,2,512]{4,0,2,3,1:T(8,128)(2,1)S(1)} %copy.36) | copy-start | bytes 1572868
  2.1 6.8 %copy-start.11 = (bf16[32,2,4,256]{3,2,1,0:T(4,128)(2,1)S(1)}, bf16[32,2,4,256]{3,2,1,0:T(4,128)(2,1)}, u32[]{:S(2)}) copy-start(bf16[32,2,4,256]{3,2,1,0:T(4,128)(2,1)} %param.5) | copy-start | bytes 393220
  2.9 6.6 %copy-start.9 = (bf16[27,32,32]{2,1,0:T(8,128)(2,1)S(1)}, bf16[27,32,32]{2,1,0:T(8,128)(2,1)}, u32[]{:S(2)}) copy-start(bf16[27,32,32]{2,1,0:T(8,128)(2,1)} %param.9) | copy-start | bytes 165892
  2.9 14.4 %collective-permute-start = (bf16[2,2,4,16,512]{4,3,2,1,0:T(8,128)(2,1)}, bf16[2,2,4,16,512]{4,3,2,1,0:T(8,128)(2,1)S(1)}, u32[]{:S(2)}, u32[]{:S(2)}) collective-permute-start(bf16[2,2,4,16,512]{4,3,2,1,0:T(8,128)(2,1)} %get-tuple-element.25), channel_id=1, source_target_pairs={{0,2},{2,4},{4,6},{6,8},{8,10},{10,12},{12,14},{14,0},{1,3},{3,5},... | collective-permute-start | bytes 786440 | tf_op jit(solution)/shard_map/ppermute | solution.py:180
  5.8 13.4 %collective-permute-start.1 = (bf16[2,2,4,16,512]{4,3,2,1,0:T(8,128)(2,1)S(1)}, bf16[2,2,4,16,512]{4,3,2,1,0:T(8,128)(2,1)S(1)}, u32[]{:S(2)}, u32[]{:S(2)}) collective-permute-start(bf16[2,2,4,16,512]{4,3,2,1,0:T(8,128)(2,1)S(1)} %get-tuple-element.24), channel_id=1, source_target_pairs={{2,0},{4,2},{6,4},{8,6},{10,8},{12,10},{14,12},{0,14},{3,1},{5,3},... | collective-permute-start | bytes 786440 | tf_op jit(solution)/shard_map/ppermute | solution.py:181
  8.8 14.0 %collective-permute-start.3 = (bf16[4,2,4,16,512]{4,3,2,1,0:T(8,128)(2,1)S(1)}, bf16[4,2,4,16,512]{4,3,2,1,0:T(8,128)(2,1)S(1)}, u32[]{:S(2)}, u32[]{:S(2)}) collective-permute-start(bf16[4,2,4,16,512]{4,3,2,1,0:T(8,128)(2,1)S(1)} %bitcast.28), channel_id=1, source_target_pairs={{0,1},{1,0},{2,3},{3,2},{4,5},{5,4},{6,7},{7,6},{8,9},{9,8},{10,11... | collective-permute-start | bytes 1572872 | tf_op jit(solution)/shard_map/ppermute | solution.py:182
  8.9 13.0 %collective-permute-start.6 = (bf16[2,4,32,256]{3,2,1,0:T(8,128)(2,1)S(1)}, bf16[2,4,32,256]{3,2,1,0:T(8,128)(2,1)S(1)}, u32[]{:S(2)}, u32[]{:S(2)}) collective-permute-start(bf16[2,4,32,256]{3,2,1,0:T(8,128)(2,1)S(1)} %bitcast.37), channel_id=1, source_target_pairs={{0,1},{1,0},{2,3},{3,2},{4,5},{5,4},{6,7},{7,6},{8,9},{9,8},{10,11... | collective-permute-start | bytes 393224 | tf_op jit(solution)/shard_map/ppermute | solution.py:231
  9.7 10.3 %copy-start.8 = (bf16[16,4,8,512]{3,2,1,0:T(8,128)(2,1)S(1)}, bf16[16,4,8,512]{3,2,1,0:T(8,128)(2,1)}, u32[]{:S(2)}) copy-start(bf16[16,4,8,512]{3,2,1,0:T(8,128)(2,1)} %param.6) | copy-start | bytes 1572868
  17.3 2.7 %copy-start.3 = (bf16[2,2,4,16,512]{4,3,2,1,0:T(8,128)(2,1)}, bf16[2,2,4,16,512]{4,3,2,1,0:T(8,128)(2,1)S(1)}, u32[]{:S(2)}) copy-start(bf16[2,2,4,16,512]{4,3,2,1,0:T(8,128)(2,1)S(1)} %collective-permute-done.refs_0_) | copy-start | bytes 786436
  17.3 5.5 %collective-permute-start.2 = (bf16[2,2,4,16,512]{4,3,2,1,0:T(8,128)(2,1)S(1)}, bf16[2,2,4,16,512]{4,3,2,1,0:T(8,128)(2,1)S(1)}, u32[]{:S(2)}, u32[]{:S(2)}) collective-permute-start(bf16[2,2,4,16,512]{4,3,2,1,0:T(8,128)(2,1)S(1)} %collective-permute-done.refs_0_), channel_id=1, source_target_pairs={{0,1},{1,0},{2,3},{3,2},{4,5},{5,4},{6,7},{7,6},{8,9},{9,8},{10,11... | collective-permute-start | bytes 786440 | tf_op jit(solution)/shard_map/ppermute | solution.py:183
  19.2 0.8 copy-start.4
  19.2 3.6 %collective-permute-start.4 = (bf16[2,2,4,16,512]{4,3,2,1,0:T(8,128)(2,1)S(1)}, bf16[2,2,4,16,512]{4,3,2,1,0:T(8,128)(2,1)S(1)}, u32[]{:S(2)}, u32[]{:S(2)}) collective-permute-start(bf16[2,2,4,16,512]{4,3,2,1,0:T(8,128)(2,1)S(1)} %collective-permute-done.1.refs_2_), channel_id=1, source_target_pairs={{0,1},{1,0},{2,3},{3,2},{4,5},{5,4},{6,7},{7,6},{8,9},{9,8},{10,11... | collective-permute-start | bytes 786440 | tf_op jit(solution)/shard_map/ppermute | solution.py:184
  22.8 0.7 copy-start.5
  22.8 0.8 copy-start.6
  22.8 0.9 %copy-start.2 = (bf16[4,2,4,16,512]{4,3,2,1,0:T(8,128)(2,1)}, bf16[4,2,4,16,512]{4,3,2,1,0:T(8,128)(2,1)S(1)}, u32[]{:S(2)}) copy-start(bf16[4,2,4,16,512]{4,3,2,1,0:T(8,128)(2,1)S(1)} %collective-permute-done.3.refs_4_) | copy-start | bytes 1572868
  29.4 16.0 %collective-permute-start.5 = (bf16[1,128,512]{2,1,0:T(8,128)(2,1)}, bf16[1,128,512]{2,1,0:T(8,128)(2,1)S(1)}, u32[]{:S(2)}, u32[]{:S(2)}) collective-permute-start(bf16[1,128,512]{2,1,0:T(8,128)(2,1)} %bitcast.44), channel_id=1, source_target_pairs={{14,0},{0,2},{2,4},{4,6},{6,8},{8,10},{10,12},{12,14},{15,1},{1,3}... | collective-permute-start | bytes 393224 | tf_op jit(solution)/shard_map/ppermute | solution.py:30
  43.4 8.6 %collective-permute-start.11 = (f32[27,32,16]{1,2,0:T(8,128)S(1)}, f32[27,32,16]{1,2,0:T(8,128)S(1)}, u32[]{:S(2)}, u32[]{:S(2)}) collective-permute-start(f32[27,32,16]{1,2,0:T(8,128)S(1)} %dynamic-slice_maximum_fusion), channel_id=1, source_target_pairs={{0,2},{2,0},{4,6},{6,4},{8,10},{10,8},{12,14},{14,12},{1,3},{3,1},... | collective-permute-start | bytes 165896 | tf_op jit(solution)/shard_map/ppermute | solution.py:40
  45.4 0.7 copy-start.12
  50.9 7.5 %collective-permute-start.8 = (f32[27,16,64]{2,1,0:T(8,128)}, f32[27,16,64]{2,1,0:T(8,128)S(1)}, u32[]{:S(2)}, u32[]{:S(2)}) collective-permute-start(f32[27,16,64]{2,1,0:T(8,128)} %bitcast.41), channel_id=1, source_target_pairs={{0,2},{2,0},{4,6},{6,4},{8,10},{10,8},{12,14},{14,12},{1,3},{3,1},... | collective-permute-start | bytes 331784 | tf_op jit(solution)/shard_map/ppermute | solution.py:40
  52.0 6.4 %copy-start.10 = (f32[3,144,64]{2,1,0:T(8,128)S(1)}, f32[3,144,64]{2,1,0:T(8,128)}, u32[]{:S(2)}) copy-start(f32[3,144,64]{2,1,0:T(8,128)} %get-tuple-element.13) | copy-start | bytes 331780
  52.0 21.8 %collective-permute-start.7 = (f32[2,4,32,256]{3,2,1,0:T(8,128)S(1)}, f32[2,4,32,256]{3,2,1,0:T(8,128)S(1)}, u32[]{:S(2)}, u32[]{:S(2)}) collective-permute-start(f32[2,4,32,256]{3,2,1,0:T(8,128)S(1)} %constant_dynamic-slice_fusion), channel_id=1, source_target_pairs={{0,1},{1,0},{2,3},{3,2},{4,5},{5,4},{6,7},{7,6},{8,9},{9,8},{10,11... | collective-permute-start | bytes 786440 | tf_op jit(solution)/shard_map/ppermute | solution.py:262
  52.3 7.9 %collective-permute-start.12 = (f32[27,32,16]{1,2,0:T(8,128)S(1)}, f32[27,32,16]{1,2,0:T(8,128)S(1)}, u32[]{:S(2)}, u32[]{:S(2)}) collective-permute-start(f32[27,32,16]{1,2,0:T(8,128)S(1)} %fusion.4), channel_id=1, source_target_pairs={{0,4},{2,6},{4,0},{6,2},{8,12},{10,14},{12,8},{14,10},{1,5},{3,7},... | collective-permute-start | bytes 165896 | tf_op jit(solution)/shard_map/ppermute | solution.py:40
  58.4 15.3 %collective-permute-start.9 = (f32[27,16,64]{2,1,0:T(8,128)S(1)}, f32[27,16,64]{2,1,0:T(8,128)S(1)}, u32[]{:S(2)}, u32[]{:S(2)}) collective-permute-start(f32[27,16,64]{2,1,0:T(8,128)S(1)} %add.61), channel_id=1, source_target_pairs={{0,4},{2,6},{4,0},{6,2},{8,12},{10,14},{12,8},{14,10},{1,5},{3,7},... | collective-permute-start | bytes 331784 | tf_op jit(solution)/shard_map/ppermute | solution.py:40
  60.2 12.8 %collective-permute-start.13 = (f32[27,32,16]{1,2,0:T(8,128)S(1)}, f32[27,32,16]{1,2,0:T(8,128)S(1)}, u32[]{:S(2)}, u32[]{:S(2)}) collective-permute-start(f32[27,32,16]{1,2,0:T(8,128)S(1)} %add.67), channel_id=1, source_target_pairs={{0,8},{2,10},{4,12},{6,14},{8,0},{10,2},{12,4},{14,6},{1,9},{3,11}... | collective-permute-start | bytes 165896 | tf_op jit(solution)/shard_map/ppermute | solution.py:40
  62.8 11.0 %copy-start.7 = (f32[2,4,64,256]{3,2,1,0:T(8,128)S(1)}, f32[2,4,64,256]{3,2,1,0:T(8,128)}, u32[]{:S(2)}) copy-start(f32[2,4,64,256]{3,2,1,0:T(8,128)} %get-tuple-element.12) | copy-start | bytes 1572868
  73.7 10.8 %collective-permute-start.10 = (f32[27,16,64]{2,1,0:T(8,128)S(1)}, f32[27,16,64]{2,1,0:T(8,128)S(1)}, u32[]{:S(2)}, u32[]{:S(2)}) collective-permute-start(f32[27,16,64]{2,1,0:T(8,128)S(1)} %add.62), channel_id=1, source_target_pairs={{0,8},{2,10},{4,12},{6,14},{8,0},{10,2},{12,4},{14,6},{1,9},{3,11}... | collective-permute-start | bytes 331784 | tf_op jit(solution)/shard_map/ppermute | solution.py:40

commit v12 on v10

--- a/solution.py
+++ b/solution.py
@@ -118,13 +118,14 @@
         r_ref[...] = r_ref[...] * scale
 
 
-def coarse_kernel(scale, gp_ref, last_ref, below_ref, c_ref, u_ref, gc_ref, gu_ref, y_ref):
+def coarse_kernel(scale, gp_ref, last_ref, below_ref, own_ref, other_ref, u_ref, gc_ref, gu_ref, y_ref):
     planes_z = gp_ref.shape[0] + 1
     cells_y = gp_ref.shape[2]
     rows_x = y_ref.shape[1] - 1
     part_ch = y_ref.shape[3]
     half_y = y_ref.shape[4]
-    coarse_z, coarse_x = c_ref.shape[0], c_ref.shape[1]
+    coarse_z, coarse_x = own_ref.shape[0], own_ref.shape[1]
+    first = lax.axis_index("ch") == 0
     at_y = lax.broadcasted_iota(jnp.int32, (cells_y, 3 * half_y), 0)
     col = lax.broadcasted_iota(jnp.int32, (cells_y, 3 * half_y), 1)
     target = 2 * (col % half_y) + col // half_y - 1
@@ -147,7 +148,11 @@
     def body(step, carry):
         iz = step // coarse_x
         ix = step % coarse_x
-        crow = c_ref[iz, ix]
+        own = own_ref[iz, ix]
+        other = other_ref[iz, ix]
+        crow = jnp.concatenate(
+            [jnp.where(first, own, other), jnp.where(first, other, own)], axis=0
+        )
         total = jnp.zeros(gc_ref.shape[2:], jnp.float32)
         for dz in range(3):
             block = y_ref[2 * iz + dz, pl.ds(2 * ix, 3)]
@@ -225,9 +230,7 @@
     coarse_other = lax.ppermute(coarse_own, "ch", swap)
     own_k = coarse.shape[0]
     coarse_start = lax.axis_index("ch") * own_k
-    coarse_rows = jnp.concatenate([coarse_own, coarse_other, coarse_own], axis=2)
-    coarse_rows = lax.dynamic_slice_in_dim(coarse_rows, coarse_start, 2 * own_k, 2)
-    coarse_in = coarse_rows.shape[2]
+    coarse_in = 2 * own_k
     coarse_z, coarse_x, cells_yc = coarse.shape[1], coarse.shape[2], coarse.shape[3]
     up_rows = lax.dynamic_slice_in_dim(up_weight, channel_start, part_ch, 1)
     up_w = jnp.transpose(up_rows.reshape(3, 9, part_ch, coarse_in), (0, 3, 1, 2))
@@ -239,12 +242,12 @@
             jax.ShapeDtypeStruct((coarse_z, coarse_x, coarse_in, cells_yc), jnp.float32),
             jax.ShapeDtypeStruct((3, 9 * part_ch, coarse_in), jnp.float32),
         ),
-        in_specs=vmem_specs(5),
+        in_specs=vmem_specs(6),
         out_specs=tuple(vmem_specs(2)),
         scratch_shapes=[
             pltpu.VMEM((planes_z + 1, planes_x + 1, 3, part_ch, cells_yc), jnp.bfloat16)
         ],
-    )(grad_rows, last_rows, below_z, coarse_rows, up_w)
+    )(grad_rows, last_rows, below_z, coarse_own, coarse_other, up_w)
     up_terms = up_acc.reshape(27, part_ch, coarse_in)
     other_start = own_k - coarse_start
     received = lax.ppermute(lax.dynamic_slice_in_dim(coarse_acc, other_start, own_k, 2), "ch", swap)

time: 74.9 us -> 73.7 us (0.984)
  other arithmetic: 2.2 us -> 0.45 us
    concatenate x1 -> x0, other arithmetic: 1.74 us -> none  [local(): jnp.concatenate([coarse_own, coarse_other, coarse_own], axis=2)]
    unnamed x33 -> x37, local copies, waits for them, and re-layouts: 6.98 us -> 7.01 us
  transfers between devices with their start and end apart: 11 -> 11, of which waited for: 5 -> 5; matrix products, arithmetic and copies ran while one was open for 11% -> 9% of each run, Pallas kernels for 22% -> 23%
where the time goes in v12:
time: 73.7 us; the launch traced here: 73.3 us
  waiting for transfers between devices  23.5 us (32%)
  Pallas kernels  21.5 us (29%)
  starting transfers between devices  13.8 us (19%)
  local copies, waits for them, and re-layouts  13 us (18%)
  between operations  1 us (1%)
    pallas_call x2, Pallas kernels, fine_rows(): pl.pallas_call(functools.partial(fine_kernel, z_lo, z_hi, scale), out_sha...  16.7 us
    ppermute x3, waiting for transfers between devices, summed_over_slabs(): block = block + lax.ppermute(block, axis, route)  13.8 us
    ppermute x1, waiting for transfers between devices, local(): low = lax.ppermute(rows[planes_z - 2:], ('gz', 'sec'), forward)  7.46 us
    unnamed x37, local copies, waits for them, and re-layouts  7.01 us
    ppermute x3, starting transfers between devices, summed_over_slabs(): block = block + lax.ppermute(block, axis, route)  6.55 us
    pallas_call x1, Pallas kernels, local(): pl.pallas_call(functools.partial(coarse_kernel, float(coarse_total) ** (-...  4.8 us
    ppermute x1, starting transfers between devices, local(): high = lax.ppermute(rows[:2], ('gz', 'sec'), backward)  3.1 us
    ppermute x1, starting transfers between devices, local(): low = lax.ppermute(rows[planes_z - 2:], ('gz', 'sec'), forward)  2.99 us
  transfers between devices with their start and end apart: 11, of which 5 were waited for; matrix products, arithmetic and copies ran while one was open for 9% of the time, Pallas kernels for 23%

profile of v12, /device:TPU:0, one launch (start us, length us, event | category | flops | bytes accessed | tf_op | source)
XLA Modules:
  0.0 73.3 jit_solution(1380023888484499733)
XLA Ops:
  0.6 0.0 copy-start
  0.6 1.4 %copy.11 = bf16[16,4,8,512]{3,0,2,1:T(8,128)(2,1)S(1)} copy(bf16[16,4,8,512]{3,2,1,0:T(8,128)(2,1)} %param.7) | data formatting | bytes 1048576 | tf_op args[2]
  2.1 0.0 copy-start.12
  2.1 3.0 %collective-permute-start = (bf16[2,2,4,16,512]{4,3,2,1,0:T(8,128)(2,1)S(1)}, bf16[2,2,4,16,512]{4,3,2,1,0:T(8,128)(2,1)S(1)}, u32[]{:S(2)}, u32[]{:S(2)}) collective-permute-start(bf16[2,2,4,16,512]{4,3,2,1,0:T(8,128)(2,1)S(1)} %get-tuple-element.22), channel_id=1, source_target_pairs={{0,2},{2,4},{4,6},{6,8},{8,10},{10,12},{12,14},{14,0},{1,3},{3,5},... | collective-permute-start | bytes 786440 | tf_op jit(solution)/shard_map/ppermute | solution.py:185
  5.1 3.1 %collective-permute-start.1 = (bf16[2,2,4,16,512]{4,3,2,1,0:T(8,128)(2,1)S(1)}, bf16[2,2,4,16,512]{4,3,2,1,0:T(8,128)(2,1)S(1)}, u32[]{:S(2)}, u32[]{:S(2)}) collective-permute-start(bf16[2,2,4,16,512]{4,3,2,1,0:T(8,128)(2,1)S(1)} %get-tuple-element.21), channel_id=1, source_target_pairs={{2,0},{4,2},{6,4},{8,6},{10,8},{12,10},{14,12},{0,14},{3,1},{5,3},... | collective-permute-start | bytes 786440 | tf_op jit(solution)/shard_map/ppermute | solution.py:186
  8.3 0.6 collective-permute-start.6
  8.9 7.5 %collective-permute-done.refs_0_ = bf16[2,2,4,16,512]{4,3,2,1,0:T(8,128)(2,1)S(1)} collective-permute-done((bf16[2,2,4,16,512]{4,3,2,1,0:T(8,128)(2,1)S(1)}, bf16[2,2,4,16,512]{4,3,2,1,0:T(8,128)(2,1)S(1)}, u32[]{:S(2)}, u32[]{:S(2)}) %collective-permute-start) | collective-permute-done | bytes 262176 | tf_op jit(solution)/shard_map/ppermute | solution.py:185
  16.3 2.2 %collective-permute-done.1.refs_2_ = bf16[2,2,4,16,512]{4,3,2,1,0:T(8,128)(2,1)S(1)} collective-permute-done((bf16[2,2,4,16,512]{4,3,2,1,0:T(8,128)(2,1)S(1)}, bf16[2,2,4,16,512]{4,3,2,1,0:T(8,128)(2,1)S(1)}, u32[]{:S(2)}, u32[]{:S(2)}) %collective-permute-start.1) | collective-permute-done | bytes 262176 | tf_op jit(solution)/shard_map/ppermute | solution.py:186
  18.5 0.1 constant_dynamic-slice_fusion.2
  18.7 0.1 copy.23
  18.9 0.4 copy-done.4
  19.2 0.2 dynamic-slice_maximum_fusion.1
  19.4 0.1 copy.15
  19.5 0.7 %reshape.50.refs_7_ = bf16[48,288]{1,0:T(8,128)(2,1)} reshape(bf16[3,16,3,3,32]{4,3,2,1,0:T(4,128)(2,1)S(1)} %copy.15) | data formatting | bytes 55296 | tf_op jit(solution)/shard_map/reshape | solution.py:196
  20.2 0.1 copy-done.9
  20.3 1.1 %copy.27 = bf16[16,4,8,512]{3,0,2,1:T(8,128)(2,1)} copy(bf16[16,4,8,512]{3,2,1,0:T(8,128)(2,1)S(1)} %copy-done.9) | data formatting | bytes 1048576 | tf_op args[1]
  21.4 0.7 copy-done.5
  22.1 0.1 copy-done.6
  22.2 0.2 copy-done.2
  22.4 5.7 %shard_map.76 = (bf16[1,8,16,512]{3,2,1,0:T(8,128)(2,1)}, f32[288,48]{1,0:T(8,128)}) custom-call(bf16[2,2,4,16,512]{4,3,2,1,0:T(8,128)(2,1)} %copy-done.3, bf16[4,2,4,16,512]{4,3,2,1,0:T(8,128)(2,1)} %bitcast.28, bf16[2,2,4,16,512]{4,3,2,1,0:T(8,128)(2,1)} %copy-done.4, bf16[2,2,4,16,512]{4,3,2,1,0:T(8,128)(2,1)} %copy-done.5, ...), custom_call_target="tpu_custom_call" | custom-call | tf_op jit(solution)/shard_map/pallas_call | solution.py:203
  28.0 0.5 collective-permute-start.5
  28.5 0.8 %copy.17.u_ref = bf16[3,64,144]{2,1,0:T(8,128)(2,1)} copy(bf16[3,64,144]{1,2,0:T(8,128)(2,1)S(1)} %bitcast.37) | data formatting | bytes 110592 | tf_op jit(solution)/shard_map/reshape | solution.py:237
  29.3 11.1 %shard_map.77 = (bf16[3,8,16,512]{3,2,1,0:T(8,128)(2,1)}, f32[288,48]{1,0:T(8,128)}) custom-call(bf16[2,2,4,16,512]{4,3,2,1,0:T(8,128)(2,1)} %copy-done.3, bf16[4,2,4,16,512]{4,3,2,1,0:T(8,128)(2,1)} %bitcast.29, bf16[2,2,4,16,512]{4,3,2,1,0:T(8,128)(2,1)} %copy-done.4, bf16[2,2,4,16,512]{4,3,2,1,0:T(8,128)(2,1)} %copy-done.5, ...), custom_call_target="tpu_custom_call" | custom-call | tf_op jit(solution)/shard_map/pallas_call | solution.py:203
  40.4 1.0 %copy.18 = f32[288,48]{0,1:T(8,128)S(1)} copy(f32[288,48]{1,0:T(8,128)} %get-tuple-element.14) | data formatting | bytes 110592 | tf_op jit(solution)/shard_map/pallas_call | solution.py:203
  41.4 0.2 reshape.55
  41.6 0.6 rev.7
  42.2 0.2 dynamic-slice_maximum_fusion
  42.4 0.2 copy.20
  42.6 0.2 reshape.57
  42.8 0.6 copy-done.13
  43.4 0.1 copy-done.14
  43.4 4.8 %shard_map.78 = (f32[2,4,64,256]{3,2,1,0:T(8,128)}, f32[3,144,64]{2,1,0:T(8,128)}) custom-call(bf16[3,128,512]{2,1,0:T(8,128)(2,1)} %bitcast.39, bf16[1,128,512]{2,1,0:T(8,128)(2,1)} %bitcast.41, bf16[1,128,512]{2,1,0:T(8,128)(2,1)} %copy-done.14, bf16[2,4,32,256]{3,2,1,0:T(8,128)(2,1)} %bitcast.36, bf16[2,4,32,256]{3,2,1,0:T(8,128)(2,1)} %copy-done.13, ...), custom_call_target="tpu_custom_call" | custom-call | tf_op jit(solution)/shard_map/pallas_call | solution.py:239
  48.2 1.1 %reshape_reshape.3 = f32[27648]{0:T(1024)S(1)} reshape(f32[3,144,64]{2,1,0:T(8,128)} %get-tuple-element.13) | data formatting | bytes 221184 | tf_op jit(solution)/shard_map/reshape;reshape | solution.py:256
  49.4 2.3 %collective-permute-start.8 = (f32[41472]{0:T(1024)S(1)}, f32[41472]{0:T(1024)S(1)}, u32[]{:S(2)}, u32[]{:S(2)}) collective-permute-start(f32[41472]{0:T(1024)S(1)} %constant_dynamic-update-slice_fusion), channel_id=1, source_target_pairs={{0,2},{2,0},{4,6},{6,4},{8,10},{10,8},{12,14},{14,12},{1,3},{3,1},... | collective-permute-start | bytes 497672 | tf_op jit(solution)/shard_map/ppermute | solution.py:40
  51.7 0.1 collective-permute-start.7
  51.7 4.2 %collective-permute-done.8 = f32[41472]{0:T(1024)S(1)} collective-permute-done((f32[41472]{0:T(1024)S(1)}, f32[41472]{0:T(1024)S(1)}, u32[]{:S(2)}, u32[]{:S(2)}) %collective-permute-start.8) | collective-permute-done | bytes 165920 | tf_op jit(solution)/shard_map/ppermute | solution.py:40
  56.0 1.6 %collective-permute-start.9 = (f32[41472]{0:T(1024)S(1)}, f32[41472]{0:T(1024)S(1)}, u32[]{:S(2)}, u32[]{:S(2)}) collective-permute-start(f32[41472]{0:T(1024)S(1)} %add.50), channel_id=1, source_target_pairs={{0,4},{2,6},{4,0},{6,2},{8,12},{10,14},{12,8},{14,10},{1,5},{3,7},... | collective-permute-start | bytes 497672 | tf_op jit(solution)/shard_map/ppermute | solution.py:40
  57.6 3.9 %collective-permute-done.9 = f32[41472]{0:T(1024)S(1)} collective-permute-done((f32[41472]{0:T(1024)S(1)}, f32[41472]{0:T(1024)S(1)}, u32[]{:S(2)}, u32[]{:S(2)}) %collective-permute-start.9) | collective-permute-done | bytes 165920 | tf_op jit(solution)/shard_map/ppermute | solution.py:40
  61.6 2.7 %collective-permute-start.10 = (f32[41472]{0:T(1024)S(1)}, f32[41472]{0:T(1024)S(1)}, u32[]{:S(2)}, u32[]{:S(2)}) collective-permute-start(f32[41472]{0:T(1024)S(1)} %add.51), channel_id=1, source_target_pairs={{0,8},{2,10},{4,12},{6,14},{8,0},{10,2},{12,4},{14,6},{1,9},{3,11}... | collective-permute-start | bytes 497672 | tf_op jit(solution)/shard_map/ppermute | solution.py:40
  64.3 0.8 %copy.21 = bf16[32,2,4,256]{3,2,1,0:T(4,128)(2,1)} copy(bf16[32,2,4,256]{3,0,2,1:T(8,128)(2,1)S(1)} %fusion) | data formatting | bytes 262144
  65.0 5.7 %collective-permute-done.10 = f32[41472]{0:T(1024)S(1)} collective-permute-done((f32[41472]{0:T(1024)S(1)}, f32[41472]{0:T(1024)S(1)}, u32[]{:S(2)}, u32[]{:S(2)}) %collective-permute-start.10) | collective-permute-done | bytes 165920 | tf_op jit(solution)/shard_map/ppermute | solution.py:40
  70.7 0.0 copy-start.7
  70.7 0.6 copy-done.7
  71.4 0.2 slice.26
  71.6 0.0 slice-start
  71.6 0.9 %copy.22 = f32[27,32,16]{1,2,0:T(8,128)} copy(f32[27,32,16]{2,1,0:T(8,128)S(1)} %slice.26) | data formatting | bytes 110592
  72.4 0.0 slice-done
  72.5 0.8 %reshape.58 = f32[27,16,64]{2,1,0:T(8,128)} reshape(f32[27648]{0:T(1024)S(1)} %slice-done) | data formatting | bytes 221184 | tf_op jit(solution)/shard_map/reshape | solution.py:258
  (42 shorter events, 0.3 us)
Async XLA Ops:
  0.6 27.9 %copy-start = (bf16[27,32,64]{2,1,0:T(8,128)(2,1)S(1)}, bf16[27,32,64]{2,1,0:T(8,128)(2,1)}, u32[]{:S(2)}) copy-start(bf16[27,32,64]{2,1,0:T(8,128)(2,1)} %param.8) | copy-start | bytes 331780
  2.1 6.2 %copy-start.1 = (bf16[16,4,4,2,512]{4,0,2,3,1:T(8,128)(2,1)}, bf16[16,4,4,2,512]{4,0,2,3,1:T(8,128)(2,1)S(1)}, u32[]{:S(2)}) copy-start(bf16[16,4,4,2,512]{4,0,2,3,1:T(8,128)(2,1)S(1)} %copy.28) | copy-start | bytes 1572868
  2.1 6.2 %copy-start.12 = (bf16[32,2,4,256]{3,2,1,0:T(4,128)(2,1)S(1)}, bf16[32,2,4,256]{3,2,1,0:T(4,128)(2,1)}, u32[]{:S(2)}) copy-start(bf16[32,2,4,256]{3,2,1,0:T(4,128)(2,1)} %param.5) | copy-start | bytes 393220
  2.1 16.4 %copy-start.11 = (bf16[27,32,32]{2,1,0:T(8,128)(2,1)S(1)}, bf16[27,32,32]{2,1,0:T(8,128)(2,1)}, u32[]{:S(2)}) copy-start(bf16[27,32,32]{2,1,0:T(8,128)(2,1)} %param.9) | copy-start | bytes 165892
  2.1 14.2 %collective-permute-start = (bf16[2,2,4,16,512]{4,3,2,1,0:T(8,128)(2,1)S(1)}, bf16[2,2,4,16,512]{4,3,2,1,0:T(8,128)(2,1)S(1)}, u32[]{:S(2)}, u32[]{:S(2)}) collective-permute-start(bf16[2,2,4,16,512]{4,3,2,1,0:T(8,128)(2,1)S(1)} %get-tuple-element.22), channel_id=1, source_target_pairs={{0,2},{2,4},{4,6},{6,8},{8,10},{10,12},{12,14},{14,0},{1,3},{3,5},... | collective-permute-start | bytes 786440 | tf_op jit(solution)/shard_map/ppermute | solution.py:185
  5.1 13.4 %collective-permute-start.1 = (bf16[2,2,4,16,512]{4,3,2,1,0:T(8,128)(2,1)S(1)}, bf16[2,2,4,16,512]{4,3,2,1,0:T(8,128)(2,1)S(1)}, u32[]{:S(2)}, u32[]{:S(2)}) collective-permute-start(bf16[2,2,4,16,512]{4,3,2,1,0:T(8,128)(2,1)S(1)} %get-tuple-element.21), channel_id=1, source_target_pairs={{2,0},{4,2},{6,4},{8,6},{10,8},{12,10},{14,12},{0,14},{3,1},{5,3},... | collective-permute-start | bytes 786440 | tf_op jit(solution)/shard_map/ppermute | solution.py:186
  8.2 13.2 %collective-permute-start.3 = (bf16[4,2,4,16,512]{4,3,2,1,0:T(8,128)(2,1)S(1)}, bf16[4,2,4,16,512]{4,3,2,1,0:T(8,128)(2,1)S(1)}, u32[]{:S(2)}, u32[]{:S(2)}) collective-permute-start(bf16[4,2,4,16,512]{4,3,2,1,0:T(8,128)(2,1)S(1)} %bitcast.27), channel_id=1, source_target_pairs={{0,1},{1,0},{2,3},{3,2},{4,5},{5,4},{6,7},{7,6},{8,9},{9,8},{10,11... | collective-permute-start | bytes 1572872 | tf_op jit(solution)/shard_map/ppermute | solution.py:187
  8.3 10.4 %copy-start.10 = (bf16[32,2,4,256]{3,0,2,1:T(8,128)(2,1)}, bf16[32,2,4,256]{3,0,2,1:T(8,128)(2,1)S(1)}, u32[]{:S(2)}) copy-start(bf16[32,2,4,256]{3,0,2,1:T(8,128)(2,1)S(1)} %copy.29) | copy-start | bytes 393220
  8.3 34.4 %collective-permute-start.6 = (bf16[2,4,32,256]{3,2,1,0:T(8,128)(2,1)S(1)}, bf16[2,4,32,256]{3,2,1,0:T(8,128)(2,1)S(1)}, u32[]{:S(2)}, u32[]{:S(2)}) collective-permute-start(bf16[2,4,32,256]{3,2,1,0:T(8,128)(2,1)S(1)} %bitcast.35), channel_id=1, source_target_pairs={{0,1},{1,0},{2,3},{3,2},{4,5},{5,4},{6,7},{7,6},{8,9},{9,8},{10,11... | collective-permute-start | bytes 393224 | tf_op jit(solution)/shard_map/ppermute | solution.py:230
  16.3 2.5 %copy-start.3 = (bf16[2,2,4,16,512]{4,3,2,1,0:T(8,128)(2,1)}, bf16[2,2,4,16,512]{4,3,2,1,0:T(8,128)(2,1)S(1)}, u32[]{:S(2)}) copy-start(bf16[2,2,4,16,512]{4,3,2,1,0:T(8,128)(2,1)S(1)} %collective-permute-done.refs_0_) | copy-start | bytes 786436
  16.3 5.1 %collective-permute-start.2 = (bf16[2,2,4,16,512]{4,3,2,1,0:T(8,128)(2,1)S(1)}, bf16[2,2,4,16,512]{4,3,2,1,0:T(8,128)(2,1)S(1)}, u32[]{:S(2)}, u32[]{:S(2)}) collective-permute-start(bf16[2,2,4,16,512]{4,3,2,1,0:T(8,128)(2,1)S(1)} %collective-permute-done.refs_0_), channel_id=1, source_target_pairs={{0,1},{1,0},{2,3},{3,2},{4,5},{5,4},{6,7},{7,6},{8,9},{9,8},{10,11... | collective-permute-start | bytes 786440 | tf_op jit(solution)/shard_map/ppermute | solution.py:188
  18.5 0.7 copy-start.4
  18.5 2.9 %collective-permute-start.4 = (bf16[2,2,4,16,512]{4,3,2,1,0:T(8,128)(2,1)S(1)}, bf16[2,2,4,16,512]{4,3,2,1,0:T(8,128)(2,1)S(1)}, u32[]{:S(2)}, u32[]{:S(2)}) collective-permute-start(bf16[2,2,4,16,512]{4,3,2,1,0:T(8,128)(2,1)S(1)} %collective-permute-done.1.refs_2_), channel_id=1, source_target_pairs={{0,1},{1,0},{2,3},{3,2},{4,5},{5,4},{6,7},{7,6},{8,9},{9,8},{10,11... | collective-permute-start | bytes 786440 | tf_op jit(solution)/shard_map/ppermute | solution.py:189
  19.2 1.0 %copy-start.9 = (bf16[16,4,8,512]{3,2,1,0:T(8,128)(2,1)S(1)}, bf16[16,4,8,512]{3,2,1,0:T(8,128)(2,1)}, u32[]{:S(2)}) copy-start(bf16[16,4,8,512]{3,2,1,0:T(8,128)(2,1)} %param.6) | copy-start | bytes 1572868
  21.4 0.7 copy-start.5
  21.4 0.8 %copy-start.6 = (bf16[2,2,4,16,512]{4,3,2,1,0:T(8,128)(2,1)}, bf16[2,2,4,16,512]{4,3,2,1,0:T(8,128)(2,1)S(1)}, u32[]{:S(2)}) copy-start(bf16[2,2,4,16,512]{4,3,2,1,0:T(8,128)(2,1)S(1)} %collective-permute-done.4.refs_5_) | copy-start | bytes 786436
  21.4 1.0 %copy-start.2 = (bf16[4,2,4,16,512]{4,3,2,1,0:T(8,128)(2,1)}, bf16[4,2,4,16,512]{4,3,2,1,0:T(8,128)(2,1)S(1)}, u32[]{:S(2)}) copy-start(bf16[4,2,4,16,512]{4,3,2,1,0:T(8,128)(2,1)S(1)} %collective-permute-done.3.refs_4_) | copy-start | bytes 1572868
  28.0 14.7 %collective-permute-start.5 = (bf16[1,128,512]{2,1,0:T(8,128)(2,1)}, bf16[1,128,512]{2,1,0:T(8,128)(2,1)S(1)}, u32[]{:S(2)}, u32[]{:S(2)}) collective-permute-start(bf16[1,128,512]{2,1,0:T(8,128)(2,1)} %bitcast.40), channel_id=1, source_target_pairs={{14,0},{0,2},{2,4},{4,6},{6,8},{8,10},{10,12},{12,14},{15,1},{1,3}... | collective-permute-start | bytes 393224 | tf_op jit(solution)/shard_map/ppermute | solution.py:30
  42.7 0.6 copy-start.13
  42.8 0.7 copy-start.14
  48.2 3.4 %copy-start.8 = (f32[2,4,64,256]{3,2,1,0:T(8,128)S(1)}, f32[2,4,64,256]{3,2,1,0:T(8,128)}, u32[]{:S(2)}) copy-start(f32[2,4,64,256]{3,2,1,0:T(8,128)} %get-tuple-element.12) | copy-start | bytes 1572868
  49.4 6.6 %collective-permute-start.8 = (f32[41472]{0:T(1024)S(1)}, f32[41472]{0:T(1024)S(1)}, u32[]{:S(2)}, u32[]{:S(2)}) collective-permute-start(f32[41472]{0:T(1024)S(1)} %constant_dynamic-update-slice_fusion), channel_id=1, source_target_pairs={{0,2},{2,0},{4,6},{6,4},{8,10},{10,8},{12,14},{14,12},{1,3},{3,1},... | collective-permute-start | bytes 497672 | tf_op jit(solution)/shard_map/ppermute | solution.py:40
  51.7 12.6 %collective-permute-start.7 = (f32[2,4,32,256]{3,2,1,0:T(8,128)S(1)}, f32[2,4,32,256]{3,2,1,0:T(8,128)S(1)}, u32[]{:S(2)}, u32[]{:S(2)}) collective-permute-start(f32[2,4,32,256]{3,2,1,0:T(8,128)S(1)} %constant_dynamic-slice_fusion), channel_id=1, source_target_pairs={{0,1},{1,0},{2,3},{3,2},{4,5},{5,4},{6,7},{7,6},{8,9},{9,8},{10,11... | collective-permute-start | bytes 786440 | tf_op jit(solution)/shard_map/ppermute | solution.py:253
  56.0 5.6 %collective-permute-start.9 = (f32[41472]{0:T(1024)S(1)}, f32[41472]{0:T(1024)S(1)}, u32[]{:S(2)}, u32[]{:S(2)}) collective-permute-start(f32[41472]{0:T(1024)S(1)} %add.50), channel_id=1, source_target_pairs={{0,4},{2,6},{4,0},{6,2},{8,12},{10,14},{12,8},{14,10},{1,5},{3,7},... | collective-permute-start | bytes 497672 | tf_op jit(solution)/shard_map/ppermute | solution.py:40
  61.6 9.1 %collective-permute-start.10 = (f32[41472]{0:T(1024)S(1)}, f32[41472]{0:T(1024)S(1)}, u32[]{:S(2)}, u32[]{:S(2)}) collective-permute-start(f32[41472]{0:T(1024)S(1)} %add.51), channel_id=1, source_target_pairs={{0,8},{2,10},{4,12},{6,14},{8,0},{10,2},{12,4},{14,6},{1,9},{3,11}... | collective-permute-start | bytes 497672 | tf_op jit(solution)/shard_map/ppermute | solution.py:40
  70.7 0.7 copy-start.7
  71.6 0.9 %slice-start = ((f32[41472]{0:T(1024)}), f32[27648]{0:T(1024)S(1)}, s32[]{:S(2)}) async-start(f32[41472]{0:T(1024)} %copy-done.7), calls=%async_computation | async-start | bytes 221184 | tf_op jit(solution)/shard_map/slice | solution.py:258

commit v13 on v12

--- a/solution.py
+++ b/solution.py
@@ -185,8 +185,15 @@
     low = lax.ppermute(rows[planes_z - 2 :], ("gz", "sec"), forward)
     high = lax.ppermute(rows[:2], ("gz", "sec"), backward)
     rows_other = lax.ppermute(rows, "ch", swap)
-    low_other = lax.ppermute(low, "ch", swap)
-    high_other = lax.ppermute(high, "ch", swap)
+    cores = lax.axis_size("ch")
+    cross_forward = [
+        (s * cores + c, t * cores + (c ^ 1)) for s, t in forward for c in range(cores)
+    ]
+    cross_backward = [
+        (s * cores + c, t * cores + (c ^ 1)) for s, t in backward for c in range(cores)
+    ]
+    low_other = lax.ppermute(rows[planes_z - 2 :], ("gz", "sec", "ch"), cross_forward)
+    high_other = lax.ppermute(rows[:2], ("gz", "sec", "ch"), cross_backward)
     halo_z = low.shape[0] + planes_z + high.shape[0]
     pre_rows = jnp.transpose(saved_pre, (1, 2, 0, 3))
 

time: 73.7 us -> 83.9 us (1.14)
  waiting for transfers between devices: 23.5 us -> 34.4 us
    ppermute x2, waiting for transfers between devices: 0.01 us -> 4.96 us  [the longest x1 3.06 us: local(): high_other = lax.ppermute(rows[:2], ('gz', 'sec', 'ch'), cross_backward)]
    ppermute x1, waiting for transfers between devices: 7.46 us -> 11.1 us  [local(): low = lax.ppermute(rows[planes_z - 2:], ('gz', 'sec'), forward)]
    ppermute x2, starting transfers between devices: 0.01 us -> 1.39 us  [the longest x1 1.31 us: local(): lax.ppermute(rows[planes_z - 2:], ('gz', 'sec', 'ch'), cross_forward)]
    ppermute x3, starting transfers between devices: 6.55 us -> 5.19 us  [summed_over_slabs(): block = block + lax.ppermute(block, axis, route)]
    ppermute x3, waiting for transfers between devices: 13.8 us -> 15 us  [summed_over_slabs(): block = block + lax.ppermute(block, axis, route)]
    ppermute x1, waiting for transfers between devices: 2.2 us -> 3.25 us  [local(): high = lax.ppermute(rows[:2], ('gz', 'sec'), backward)]
  transfers between devices with their start and end apart: 11 -> 11, of which waited for: 5 -> 7; matrix products, arithmetic and copies ran while one was open for 9% -> 8% of each run, Pallas kernels for 23% -> 20%
where the time goes in v13:
time: 83.9 us; the launch traced here: 83.5 us
  waiting for transfers between devices  34.4 us (41%)
  Pallas kernels  21.4 us (26%)
  local copies, waits for them, and re-layouts  13.3 us (16%)
  starting transfers between devices  13 us (15%)
  between operations  1 us (1%)
    pallas_call x2, Pallas kernels, fine_rows(): pl.pallas_call(functools.partial(fine_kernel, z_lo, z_hi, scale), out_sha...  16.6 us
    ppermute x3, waiting for transfers between devices, summed_over_slabs(): block = block + lax.ppermute(block, axis, route)  15 us
    ppermute x1, waiting for transfers between devices, local(): low = lax.ppermute(rows[planes_z - 2:], ('gz', 'sec'), forward)  11.1 us
    unnamed x37, local copies, waits for them, and re-layouts  6.54 us
    ppermute x3, starting transfers between devices, summed_over_slabs(): block = block + lax.ppermute(block, axis, route)  5.19 us
    pallas_call x1, Pallas kernels, local(): pl.pallas_call(functools.partial(coarse_kernel, float(coarse_total) ** (-...  4.8 us
    ppermute x1, waiting for transfers between devices, local(): high = lax.ppermute(rows[:2], ('gz', 'sec'), backward)  3.25 us
    ppermute x1, starting transfers between devices, local(): high = lax.ppermute(rows[:2], ('gz', 'sec'), backward)  3.17 us
  transfers between devices with their start and end apart: 11, of which 7 were waited for; matrix products, arithmetic and copies ran while one was open for 8% of the time, Pallas kernels for 20%

profile of v13, /device:TPU:0, one launch (start us, length us, event | category | flops | bytes accessed | tf_op | source)
XLA Modules:
  0.0 83.5 jit_solution(13477158061489421867)
XLA Ops:
  0.6 0.0 copy-start
  0.6 1.4 %copy.11 = bf16[16,4,8,512]{3,0,2,1:T(8,128)(2,1)S(1)} copy(bf16[16,4,8,512]{3,2,1,0:T(8,128)(2,1)} %param.7) | data formatting | bytes 1048576 | tf_op args[2]
  2.1 0.5 collective-permute-start.3
  2.6 0.7 fusion.1
  3.3 2.6 %collective-permute-start = (bf16[2,2,4,16,512]{4,3,2,1,0:T(8,128)(2,1)}, bf16[2,2,4,16,512]{4,3,2,1,0:T(8,128)(2,1)S(1)}, u32[]{:S(2)}, u32[]{:S(2)}) collective-permute-start(bf16[2,2,4,16,512]{4,3,2,1,0:T(8,128)(2,1)} %get-tuple-element.22), channel_id=1, source_target_pairs={{0,2},{2,4},{4,6},{6,8},{8,10},{10,12},{12,14},{14,0},{1,3},{3,5},... | collective-permute-start | bytes 786440 | tf_op jit(solution)/shard_map/ppermute | solution.py:185
  5.9 1.3 %collective-permute-start.2 = (bf16[2,2,4,16,512]{4,3,2,1,0:T(8,128)(2,1)}, bf16[2,2,4,16,512]{4,3,2,1,0:T(8,128)(2,1)S(1)}, u32[]{:S(2)}, u32[]{:S(2)}) collective-permute-start(bf16[2,2,4,16,512]{4,3,2,1,0:T(8,128)(2,1)} %get-tuple-element.22), channel_id=1, source_target_pairs={{0,3},{1,2},{2,5},{3,4},{4,7},{5,6},{6,9},{7,8},{8,11},{9,10},{10,... | collective-permute-start | bytes 786440 | tf_op jit(solution)/shard_map/ppermute | solution.py:195
  7.2 3.2 %collective-permute-start.1 = (bf16[2,2,4,16,512]{4,3,2,1,0:T(8,128)(2,1)S(1)}, bf16[2,2,4,16,512]{4,3,2,1,0:T(8,128)(2,1)S(1)}, u32[]{:S(2)}, u32[]{:S(2)}) collective-permute-start(bf16[2,2,4,16,512]{4,3,2,1,0:T(8,128)(2,1)S(1)} %get-tuple-element.21), channel_id=1, source_target_pairs={{2,0},{4,2},{6,4},{8,6},{10,8},{12,10},{14,12},{0,14},{3,1},{5,3},... | collective-permute-start | bytes 786440 | tf_op jit(solution)/shard_map/ppermute | solution.py:186
  10.4 0.1 collective-permute-start.4
  10.5 0.1 constant_dynamic-slice_fusion.2
  10.6 0.1 copy.23
  10.8 0.2 dynamic-slice_maximum_fusion.1
  11.0 0.1 copy.15
  11.0 0.7 reshape.50.refs_7_
  11.8 0.0 copy-done.9
  11.8 1.1 %copy.27 = bf16[16,4,8,512]{3,0,2,1:T(8,128)(2,1)} copy(bf16[16,4,8,512]{3,2,1,0:T(8,128)(2,1)S(1)} %copy-done.9) | data formatting | bytes 1048576 | tf_op args[1]
  13.0 11.1 %collective-permute-done.refs_0_ = bf16[2,2,4,16,512]{4,3,2,1,0:T(8,128)(2,1)S(1)} collective-permute-done((bf16[2,2,4,16,512]{4,3,2,1,0:T(8,128)(2,1)}, bf16[2,2,4,16,512]{4,3,2,1,0:T(8,128)(2,1)S(1)}, u32[]{:S(2)}, u32[]{:S(2)}) %collective-permute-start) | collective-permute-done | bytes 262176 | tf_op jit(solution)/shard_map/ppermute | solution.py:185
  24.1 3.2 %collective-permute-done.1.refs_2_ = bf16[2,2,4,16,512]{4,3,2,1,0:T(8,128)(2,1)S(1)} collective-permute-done((bf16[2,2,4,16,512]{4,3,2,1,0:T(8,128)(2,1)S(1)}, bf16[2,2,4,16,512]{4,3,2,1,0:T(8,128)(2,1)S(1)}, u32[]{:S(2)}, u32[]{:S(2)}) %collective-permute-start.1) | collective-permute-done | bytes 262176 | tf_op jit(solution)/shard_map/ppermute | solution.py:186
  27.3 1.9 %collective-permute-done.2.refs_3_ = bf16[2,2,4,16,512]{4,3,2,1,0:T(8,128)(2,1)S(1)} collective-permute-done((bf16[2,2,4,16,512]{4,3,2,1,0:T(8,128)(2,1)}, bf16[2,2,4,16,512]{4,3,2,1,0:T(8,128)(2,1)S(1)}, u32[]{:S(2)}, u32[]{:S(2)}) %collective-permute-start.2) | collective-permute-done | bytes 262176 | tf_op jit(solution)/shard_map/ppermute | solution.py:195
  29.2 3.1 %collective-permute-done.4.refs_5_ = bf16[2,2,4,16,512]{4,3,2,1,0:T(8,128)(2,1)S(1)} collective-permute-done((bf16[2,2,4,16,512]{4,3,2,1,0:T(8,128)(2,1)S(1)}, bf16[2,2,4,16,512]{4,3,2,1,0:T(8,128)(2,1)S(1)}, u32[]{:S(2)}, u32[]{:S(2)}) %collective-permute-start.4) | collective-permute-done | bytes 262176 | tf_op jit(solution)/shard_map/ppermute | solution.py:196
  32.3 0.7 copy-done.6
  33.0 0.2 copy-done.2
  33.2 5.7 %shard_map.76 = (bf16[1,8,16,512]{3,2,1,0:T(8,128)(2,1)}, f32[288,48]{1,0:T(8,128)}) custom-call(bf16[2,2,4,16,512]{4,3,2,1,0:T(8,128)(2,1)} %copy-done.3, bf16[4,2,4,16,512]{4,3,2,1,0:T(8,128)(2,1)} %bitcast.28, bf16[2,2,4,16,512]{4,3,2,1,0:T(8,128)(2,1)} %copy-done.5, bf16[2,2,4,16,512]{4,3,2,1,0:T(8,128)(2,1)} %copy-done.4, ...), custom_call_target="tpu_custom_call" | custom-call | tf_op jit(solution)/shard_map/pallas_call | solution.py:210
  38.9 0.1 collective-permute-start.5
  39.0 0.8 copy.17.u_ref
  39.7 11.0 %shard_map.77 = (bf16[3,8,16,512]{3,2,1,0:T(8,128)(2,1)}, f32[288,48]{1,0:T(8,128)}) custom-call(bf16[2,2,4,16,512]{4,3,2,1,0:T(8,128)(2,1)} %copy-done.3, bf16[4,2,4,16,512]{4,3,2,1,0:T(8,128)(2,1)} %bitcast.29, bf16[2,2,4,16,512]{4,3,2,1,0:T(8,128)(2,1)} %copy-done.5, bf16[2,2,4,16,512]{4,3,2,1,0:T(8,128)(2,1)} %copy-done.4, ...), custom_call_target="tpu_custom_call" | custom-call | tf_op jit(solution)/shard_map/pallas_call | solution.py:210
  50.7 1.0 %copy.18 = f32[288,48]{0,1:T(8,128)S(1)} copy(f32[288,48]{1,0:T(8,128)} %get-tuple-element.14) | data formatting | bytes 110592 | tf_op jit(solution)/shard_map/pallas_call | solution.py:210
  51.7 0.2 reshape.55
  51.9 0.6 rev.7
  52.5 0.2 dynamic-slice_maximum_fusion
  52.7 0.2 copy.20
  52.9 0.2 reshape.57
  53.1 0.6 copy-done.13
  53.7 0.1 copy-done.14
  53.8 4.8 %shard_map.78 = (f32[2,4,64,256]{3,2,1,0:T(8,128)}, f32[3,144,64]{2,1,0:T(8,128)}) custom-call(bf16[3,128,512]{2,1,0:T(8,128)(2,1)} %bitcast.39, bf16[1,128,512]{2,1,0:T(8,128)(2,1)} %bitcast.41, bf16[1,128,512]{2,1,0:T(8,128)(2,1)} %copy-done.14, bf16[2,4,32,256]{3,2,1,0:T(8,128)(2,1)} %bitcast.36, bf16[2,4,32,256]{3,2,1,0:T(8,128)(2,1)} %copy-done.13, ...), custom_call_target="tpu_custom_call" | custom-call | tf_op jit(solution)/shard_map/pallas_call | solution.py:246
  58.6 1.1 %reshape_reshape.3 = f32[27648]{0:T(1024)S(1)} reshape(f32[3,144,64]{2,1,0:T(8,128)} %get-tuple-element.13) | data formatting | bytes 221184 | tf_op jit(solution)/shard_map/reshape;reshape | solution.py:263
  59.7 1.7 %collective-permute-start.8 = (f32[41472]{0:T(1024)S(1)}, f32[41472]{0:T(1024)S(1)}, u32[]{:S(2)}, u32[]{:S(2)}) collective-permute-start(f32[41472]{0:T(1024)S(1)} %constant_dynamic-update-slice_fusion), channel_id=1, source_target_pairs={{0,2},{2,0},{4,6},{6,4},{8,10},{10,8},{12,14},{14,12},{1,3},{3,1},... | collective-permute-start | bytes 497672 | tf_op jit(solution)/shard_map/ppermute | solution.py:40
  61.5 0.1 collective-permute-start.7
  61.5 4.6 %collective-permute-done.8 = f32[41472]{0:T(1024)S(1)} collective-permute-done((f32[41472]{0:T(1024)S(1)}, f32[41472]{0:T(1024)S(1)}, u32[]{:S(2)}, u32[]{:S(2)}) %collective-permute-start.8) | collective-permute-done | bytes 165920 | tf_op jit(solution)/shard_map/ppermute | solution.py:40
  66.1 1.3 %collective-permute-start.9 = (f32[41472]{0:T(1024)S(1)}, f32[41472]{0:T(1024)S(1)}, u32[]{:S(2)}, u32[]{:S(2)}) collective-permute-start(f32[41472]{0:T(1024)S(1)} %add.50), channel_id=1, source_target_pairs={{0,4},{2,6},{4,0},{6,2},{8,12},{10,14},{12,8},{14,10},{1,5},{3,7},... | collective-permute-start | bytes 497672 | tf_op jit(solution)/shard_map/ppermute | solution.py:40
  67.4 4.3 %collective-permute-done.9 = f32[41472]{0:T(1024)S(1)} collective-permute-done((f32[41472]{0:T(1024)S(1)}, f32[41472]{0:T(1024)S(1)}, u32[]{:S(2)}, u32[]{:S(2)}) %collective-permute-start.9) | collective-permute-done | bytes 165920 | tf_op jit(solution)/shard_map/ppermute | solution.py:40
  71.7 2.2 %collective-permute-start.10 = (f32[41472]{0:T(1024)S(1)}, f32[41472]{0:T(1024)S(1)}, u32[]{:S(2)}, u32[]{:S(2)}) collective-permute-start(f32[41472]{0:T(1024)S(1)} %add.51), channel_id=1, source_target_pairs={{0,8},{2,10},{4,12},{6,14},{8,0},{10,2},{12,4},{14,6},{1,9},{3,11}... | collective-permute-start | bytes 497672 | tf_op jit(solution)/shard_map/ppermute | solution.py:40
  74.0 0.8 copy.21
  74.8 6.1 %collective-permute-done.10 = f32[41472]{0:T(1024)S(1)} collective-permute-done((f32[41472]{0:T(1024)S(1)}, f32[41472]{0:T(1024)S(1)}, u32[]{:S(2)}, u32[]{:S(2)}) %collective-permute-start.10) | collective-permute-done | bytes 165920 | tf_op jit(solution)/shard_map/ppermute | solution.py:40
  80.9 0.6 copy-done.7
  81.6 0.2 slice.28
  81.8 0.9 %copy.22 = f32[27,32,16]{1,2,0:T(8,128)} copy(f32[27,32,16]{2,1,0:T(8,128)S(1)} %slice.28) | data formatting | bytes 110592
  82.6 0.0 slice-done
  82.7 0.8 reshape.58
  (42 shorter events, 0.3 us)
Async XLA Ops:
  0.6 38.3 %copy-start = (bf16[27,32,64]{2,1,0:T(8,128)(2,1)S(1)}, bf16[27,32,64]{2,1,0:T(8,128)(2,1)}, u32[]{:S(2)}) copy-start(bf16[27,32,64]{2,1,0:T(8,128)(2,1)} %param.8) | copy-start | bytes 331780
  2.1 1.3 %copy-start.1 = (bf16[16,4,4,2,512]{4,0,2,3,1:T(8,128)(2,1)}, bf16[16,4,4,2,512]{4,0,2,3,1:T(8,128)(2,1)S(1)}, u32[]{:S(2)}) copy-start(bf16[16,4,4,2,512]{4,0,2,3,1:T(8,128)(2,1)S(1)} %copy.28) | copy-start | bytes 1572868
  2.1 8.4 %copy-start.11 = (bf16[27,32,32]{2,1,0:T(8,128)(2,1)S(1)}, bf16[27,32,32]{2,1,0:T(8,128)(2,1)}, u32[]{:S(2)}) copy-start(bf16[27,32,32]{2,1,0:T(8,128)(2,1)} %param.9) | copy-start | bytes 165892
  2.1 30.2 %collective-permute-start.3 = (bf16[4,2,4,16,512]{4,3,2,1,0:T(8,128)(2,1)S(1)}, bf16[4,2,4,16,512]{4,3,2,1,0:T(8,128)(2,1)S(1)}, u32[]{:S(2)}, u32[]{:S(2)}) collective-permute-start(bf16[4,2,4,16,512]{4,3,2,1,0:T(8,128)(2,1)S(1)} %bitcast.26), channel_id=1, source_target_pairs={{0,1},{1,0},{2,3},{3,2},{4,5},{5,4},{6,7},{7,6},{8,9},{9,8},{10,11... | collective-permute-start | bytes 1572872 | tf_op jit(solution)/shard_map/ppermute | solution.py:187
  3.3 20.7 %collective-permute-start = (bf16[2,2,4,16,512]{4,3,2,1,0:T(8,128)(2,1)}, bf16[2,2,4,16,512]{4,3,2,1,0:T(8,128)(2,1)S(1)}, u32[]{:S(2)}, u32[]{:S(2)}) collective-permute-start(bf16[2,2,4,16,512]{4,3,2,1,0:T(8,128)(2,1)} %get-tuple-element.22), channel_id=1, source_target_pairs={{0,2},{2,4},{4,6},{6,8},{8,10},{10,12},{12,14},{14,0},{1,3},{3,5},... | collective-permute-start | bytes 786440 | tf_op jit(solution)/shard_map/ppermute | solution.py:185
  5.9 23.3 %collective-permute-start.2 = (bf16[2,2,4,16,512]{4,3,2,1,0:T(8,128)(2,1)}, bf16[2,2,4,16,512]{4,3,2,1,0:T(8,128)(2,1)S(1)}, u32[]{:S(2)}, u32[]{:S(2)}) collective-permute-start(bf16[2,2,4,16,512]{4,3,2,1,0:T(8,128)(2,1)} %get-tuple-element.22), channel_id=1, source_target_pairs={{0,3},{1,2},{2,5},{3,4},{4,7},{5,6},{6,9},{7,8},{8,11},{9,10},{10,... | collective-permute-start | bytes 786440 | tf_op jit(solution)/shard_map/ppermute | solution.py:195
  7.2 20.1 %collective-permute-start.1 = (bf16[2,2,4,16,512]{4,3,2,1,0:T(8,128)(2,1)S(1)}, bf16[2,2,4,16,512]{4,3,2,1,0:T(8,128)(2,1)S(1)}, u32[]{:S(2)}, u32[]{:S(2)}) collective-permute-start(bf16[2,2,4,16,512]{4,3,2,1,0:T(8,128)(2,1)S(1)} %get-tuple-element.21), channel_id=1, source_target_pairs={{2,0},{4,2},{6,4},{8,6},{10,8},{12,10},{14,12},{0,14},{3,1},{5,3},... | collective-permute-start | bytes 786440 | tf_op jit(solution)/shard_map/ppermute | solution.py:186
  10.4 21.9 %collective-permute-start.4 = (bf16[2,2,4,16,512]{4,3,2,1,0:T(8,128)(2,1)S(1)}, bf16[2,2,4,16,512]{4,3,2,1,0:T(8,128)(2,1)S(1)}, u32[]{:S(2)}, u32[]{:S(2)}) collective-permute-start(bf16[2,2,4,16,512]{4,3,2,1,0:T(8,128)(2,1)S(1)} %get-tuple-element.21), channel_id=1, source_target_pairs={{2,1},{3,0},{4,3},{5,2},{6,5},{7,4},{8,7},{9,6},{10,9},{11,8},{12,... | collective-permute-start | bytes 786440 | tf_op jit(solution)/shard_map/ppermute | solution.py:196
  10.8 1.0 %copy-start.9 = (bf16[16,4,8,512]{3,2,1,0:T(8,128)(2,1)S(1)}, bf16[16,4,8,512]{3,2,1,0:T(8,128)(2,1)}, u32[]{:S(2)}) copy-start(bf16[16,4,8,512]{3,2,1,0:T(8,128)(2,1)} %param.6) | copy-start | bytes 1572868
  11.8 1.1 %copy-start.12 = (bf16[32,2,4,256]{3,2,1,0:T(4,128)(2,1)S(1)}, bf16[32,2,4,256]{3,2,1,0:T(4,128)(2,1)}, u32[]{:S(2)}) copy-start(bf16[32,2,4,256]{3,2,1,0:T(4,128)(2,1)} %param.5) | copy-start | bytes 393220
  13.0 25.9 %copy-start.10 = (bf16[32,2,4,256]{3,0,2,1:T(8,128)(2,1)}, bf16[32,2,4,256]{3,0,2,1:T(8,128)(2,1)S(1)}, u32[]{:S(2)}) copy-start(bf16[32,2,4,256]{3,0,2,1:T(8,128)(2,1)S(1)} %copy.29) | copy-start | bytes 393220
  24.1 8.2 %copy-start.3 = (bf16[2,2,4,16,512]{4,3,2,1,0:T(8,128)(2,1)}, bf16[2,2,4,16,512]{4,3,2,1,0:T(8,128)(2,1)S(1)}, u32[]{:S(2)}) copy-start(bf16[2,2,4,16,512]{4,3,2,1,0:T(8,128)(2,1)S(1)} %collective-permute-done.refs_0_) | copy-start | bytes 786436
  24.1 29.0 %collective-permute-start.6 = (bf16[2,4,32,256]{3,2,1,0:T(8,128)(2,1)S(1)}, bf16[2,4,32,256]{3,2,1,0:T(8,128)(2,1)S(1)}, u32[]{:S(2)}, u32[]{:S(2)}) collective-permute-start(bf16[2,4,32,256]{3,2,1,0:T(8,128)(2,1)S(1)} %bitcast.35), channel_id=1, source_target_pairs={{0,1},{1,0},{2,3},{3,2},{4,5},{5,4},{6,7},{7,6},{8,9},{9,8},{10,11... | collective-permute-start | bytes 393224 | tf_op jit(solution)/shard_map/ppermute | solution.py:237
  27.3 5.0 %copy-start.5 = (bf16[2,2,4,16,512]{4,3,2,1,0:T(8,128)(2,1)}, bf16[2,2,4,16,512]{4,3,2,1,0:T(8,128)(2,1)S(1)}, u32[]{:S(2)}) copy-start(bf16[2,2,4,16,512]{4,3,2,1,0:T(8,128)(2,1)S(1)} %collective-permute-done.1.refs_2_) | copy-start | bytes 786436
  29.2 3.1 %copy-start.4 = (bf16[2,2,4,16,512]{4,3,2,1,0:T(8,128)(2,1)}, bf16[2,2,4,16,512]{4,3,2,1,0:T(8,128)(2,1)S(1)}, u32[]{:S(2)}) copy-start(bf16[2,2,4,16,512]{4,3,2,1,0:T(8,128)(2,1)S(1)} %collective-permute-done.2.refs_3_) | copy-start | bytes 786436
  32.3 0.7 copy-start.6
  32.3 0.9 %copy-start.2 = (bf16[4,2,4,16,512]{4,3,2,1,0:T(8,128)(2,1)}, bf16[4,2,4,16,512]{4,3,2,1,0:T(8,128)(2,1)S(1)}, u32[]{:S(2)}) copy-start(bf16[4,2,4,16,512]{4,3,2,1,0:T(8,128)(2,1)S(1)} %collective-permute-done.3.refs_4_) | copy-start | bytes 1572868
  38.9 14.2 %collective-permute-start.5 = (bf16[1,128,512]{2,1,0:T(8,128)(2,1)}, bf16[1,128,512]{2,1,0:T(8,128)(2,1)S(1)}, u32[]{:S(2)}, u32[]{:S(2)}) collective-permute-start(bf16[1,128,512]{2,1,0:T(8,128)(2,1)} %bitcast.40), channel_id=1, source_target_pairs={{14,0},{0,2},{2,4},{4,6},{6,8},{8,10},{10,12},{12,14},{15,1},{1,3}... | collective-permute-start | bytes 393224 | tf_op jit(solution)/shard_map/ppermute | solution.py:30
  53.1 0.6 copy-start.13
  53.1 0.7 copy-start.14
  58.6 2.9 %copy-start.8 = (f32[2,4,64,256]{3,2,1,0:T(8,128)S(1)}, f32[2,4,64,256]{3,2,1,0:T(8,128)}, u32[]{:S(2)}) copy-start(f32[2,4,64,256]{3,2,1,0:T(8,128)} %get-tuple-element.12) | copy-start | bytes 1572868
  59.7 6.4 %collective-permute-start.8 = (f32[41472]{0:T(1024)S(1)}, f32[41472]{0:T(1024)S(1)}, u32[]{:S(2)}, u32[]{:S(2)}) collective-permute-start(f32[41472]{0:T(1024)S(1)} %constant_dynamic-update-slice_fusion), channel_id=1, source_target_pairs={{0,2},{2,0},{4,6},{6,4},{8,10},{10,8},{12,14},{14,12},{1,3},{3,1},... | collective-permute-start | bytes 497672 | tf_op jit(solution)/shard_map/ppermute | solution.py:40
  61.5 12.5 %collective-permute-start.7 = (f32[2,4,32,256]{3,2,1,0:T(8,128)S(1)}, f32[2,4,32,256]{3,2,1,0:T(8,128)S(1)}, u32[]{:S(2)}, u32[]{:S(2)}) collective-permute-start(f32[2,4,32,256]{3,2,1,0:T(8,128)S(1)} %constant_dynamic-slice_fusion), channel_id=1, source_target_pairs={{0,1},{1,0},{2,3},{3,2},{4,5},{5,4},{6,7},{7,6},{8,9},{9,8},{10,11... | collective-permute-start | bytes 786440 | tf_op jit(solution)/shard_map/ppermute | solution.py:260
  66.1 5.6 %collective-permute-start.9 = (f32[41472]{0:T(1024)S(1)}, f32[41472]{0:T(1024)S(1)}, u32[]{:S(2)}, u32[]{:S(2)}) collective-permute-start(f32[41472]{0:T(1024)S(1)} %add.50), channel_id=1, source_target_pairs={{0,4},{2,6},{4,0},{6,2},{8,12},{10,14},{12,8},{14,10},{1,5},{3,7},... | collective-permute-start | bytes 497672 | tf_op jit(solution)/shard_map/ppermute | solution.py:40
  71.7 9.2 %collective-permute-start.10 = (f32[41472]{0:T(1024)S(1)}, f32[41472]{0:T(1024)S(1)}, u32[]{:S(2)}, u32[]{:S(2)}) collective-permute-start(f32[41472]{0:T(1024)S(1)} %add.51), channel_id=1, source_target_pairs={{0,8},{2,10},{4,12},{6,14},{8,0},{10,2},{12,4},{14,6},{1,9},{3,11}... | collective-permute-start | bytes 497672 | tf_op jit(solution)/shard_map/ppermute | solution.py:40
  80.9 0.7 copy-start.7
  81.8 0.9 %slice-start = ((f32[41472]{0:T(1024)}), f32[27648]{0:T(1024)S(1)}, s32[]{:S(2)}) async-start(f32[41472]{0:T(1024)} %copy-done.7), calls=%async_computation | async-start | bytes 221184 | tf_op jit(solution)/shard_map/slice | solution.py:265

commit v14 on v12

--- a/solution.py
+++ b/solution.py
@@ -48,14 +48,15 @@
 
 def fine_kernel(z_lo, z_hi, scale, *refs):
     pieces = refs[:6]
-    if len(refs) == 13:
-        sp_ref, w_ref, start_ref, gp_ref, r_ref, g_ref, sems = refs[6:]
+    if len(refs) == 14:
+        sp_ref, w_ref, start_ref, gp_ref, r_ref, final_ref, g_ref, sems = refs[6:]
     else:
         sp_ref, w_ref, gp_ref, r_ref, g_ref, sems = refs[6:]
-        start_ref = None
+        start_ref = final_ref = None
     planes_z, planes_x, part_ch, cells_y = sp_ref.shape
     wide = g_ref.shape[4]
     low_count = pieces[0].shape[0]
+    core = lax.axis_index("ch")
     needed = sorted({z + 4 - 2 * dz for z in range(z_lo, z_hi) for dz in range(3)})
     edge = jnp.zeros(g_ref[:, :, :, 0].shape, g_ref.dtype)
     g_ref[:, :, :, 0] = edge
@@ -77,7 +78,7 @@
                         plane // 2,
                         parity,
                         pl.ds(1, planes_x // 2),
-                        pl.ds(half * part_ch, part_ch),
+                        pl.ds(pl.multiple_of(((half + core) % 2) * part_ch, part_ch), part_ch),
                     ],
                     sems.at[len(copies)],
                 )
@@ -114,8 +115,15 @@
         return carry
 
     lax.fori_loop(0, (z_hi - z_lo) * planes_x, body, 0)
-    if scale != 1.0:
-        r_ref[...] = r_ref[...] * scale
+    if final_ref is not None:
+        acc = r_ref[...] * scale
+        for dz in range(3):
+            for dx in range(3):
+                rows_at = (3 * (2 - dz) + (2 - dx)) * wide
+                for dy in range(3):
+                    final_ref[9 * dz + 3 * dx + dy] = acc[
+                        rows_at : rows_at + wide, dy * part_ch : (dy + 1) * part_ch
+                    ]
 
 
 def coarse_kernel(scale, gp_ref, last_ref, below_ref, own_ref, other_ref, u_ref, gc_ref, gu_ref, y_ref):
@@ -191,7 +199,6 @@
     pre_rows = jnp.transpose(saved_pre, (1, 2, 0, 3))
 
     refine_cols = lax.dynamic_slice_in_dim(refine_weight, channel_start, part_ch, 2)
-    refine_cols = jnp.roll(refine_cols, -channel_start, axis=1)
     refine_w = refine_cols.reshape(3, 3, 3, all_ch, part_ch)[::-1, ::-1]
     refine_w = jnp.transpose(refine_w, (2, 4, 0, 1, 3)).reshape(3 * part_ch, 9 * all_ch)
 
@@ -205,9 +212,10 @@
             out_shape=(
                 jax.ShapeDtypeStruct((z_hi - z_lo, planes_x, part_ch, cells_y), jnp.bfloat16),
                 jax.ShapeDtypeStruct((9 * all_ch, 3 * part_ch), jnp.float32),
-            ),
+            )
+            + ((jax.ShapeDtypeStruct((27, all_ch, part_ch), jnp.float32),) if start else ()),
             in_specs=[pl.BlockSpec(memory_space=pl.ANY)] * 6 + vmem_specs(2 + len(start)),
-            out_specs=tuple(vmem_specs(2)),
+            out_specs=tuple(vmem_specs(2 + len(start))),
             scratch_shapes=[
                 pltpu.VMEM(
                     (2, halo_z // 2, 2, planes_x // 2 + 2, all_ch, cells_y), jnp.bfloat16
@@ -219,12 +227,8 @@
     grad_last, refine_last = fine_rows(planes_z - 1, planes_z)
     last_rows = grad_last.reshape(1, planes_x * part_ch, cells_y)
     below_z = passed_along(last_rows, ("gz", "sec"), 1)
-    grad_main, refine_acc = fine_rows(0, planes_z - 1, refine_last)
+    grad_main, _, refine_terms = fine_rows(0, planes_z - 1, refine_last)
     grad_rows = grad_main.reshape(planes_z - 1, planes_x * part_ch, cells_y)
-    refine_terms = refine_acc.reshape(3, 3, all_ch, 3, part_ch)[::-1, ::-1]
-    refine_terms = jnp.transpose(refine_terms, (0, 1, 3, 2, 4)).reshape(27, all_ch, part_ch)
-    refine_terms = jnp.roll(refine_terms, channel_start, axis=1)
-
 
     coarse_own = jnp.transpose(coarse, (1, 2, 0, 3))
     coarse_other = lax.ppermute(coarse_own, "ch", swap)

time: 73.7 us -> 73.8 us (level)
  waiting for transfers between devices: 23.5 us -> 25.1 us
  local copies, waits for them, and re-layouts: 13 us -> 11.7 us
    pallas_call x1 -> x0, local copies, waits for them, and re-layouts: 1.02 us -> none  [fine_rows(): pl.pallas_call(functools.partial(fine_kernel, z_lo, z_hi, scale), out_sha...]
    ppermute x3, waiting for transfers between devices: 13.8 us -> 14.8 us  [summed_over_slabs(): block = block + lax.ppermute(block, axis, route)]
    reshape x1, local copies, waits for them, and re-layouts: 0.17 us -> 1.18 us  [local(): flat = jnp.concatenate([up_terms.reshape(-1), refine_terms.reshape(-1)])]
  transfers between devices with their start and end apart: 11 -> 11, of which waited for: 5 -> 5; matrix products, arithmetic and copies ran while one was open for 9% -> 7% of each run, Pallas kernels for 23% -> 23%
where the time goes in v14:
time: 73.8 us; the launch traced here: 73.3 us
  waiting for transfers between devices  25.1 us (34%)
  Pallas kernels  21.6 us (29%)
  starting transfers between devices  13.9 us (19%)
  local copies, waits for them, and re-layouts  11.7 us (16%)
  between operations  0.94 us (1%)
    pallas_call x2, Pallas kernels, fine_rows(): pl.pallas_call(functools.partial(fine_kernel, z_lo, z_hi, scale), out_sha...  16.8 us
    ppermute x3, waiting for transfers between devices, summed_over_slabs(): block = block + lax.ppermute(block, axis, route)  14.8 us
    ppermute x1, waiting for transfers between devices, local(): low = lax.ppermute(rows[planes_z - 2:], ('gz', 'sec'), forward)  8.07 us
    unnamed x37, local copies, waits for them, and re-layouts  6.63 us
    ppermute x3, starting transfers between devices, summed_over_slabs(): block = block + lax.ppermute(block, axis, route)  6.36 us
    pallas_call x1, Pallas kernels, local(): pl.pallas_call(functools.partial(coarse_kernel, float(coarse_total) ** (-...  4.8 us
    ppermute x1, starting transfers between devices, local(): high = lax.ppermute(rows[:2], ('gz', 'sec'), backward)  3.1 us
    ppermute x1, starting transfers between devices, local(): low = lax.ppermute(rows[planes_z - 2:], ('gz', 'sec'), forward)  2.99 us
  transfers between devices with their start and end apart: 11, of which 5 were waited for; matrix products, arithmetic and copies ran while one was open for 7% of the time, Pallas kernels for 23%

profile of v14, /device:TPU:0, one launch (start us, length us, event | category | flops | bytes accessed | tf_op | source)
XLA Modules:
  0.0 73.3 jit_solution(16243288723415587663)
XLA Ops:
  0.6 0.0 copy-start
  0.6 1.4 %copy.11 = bf16[16,4,8,512]{3,0,2,1:T(8,128)(2,1)S(1)} copy(bf16[16,4,8,512]{3,2,1,0:T(8,128)(2,1)} %param.7) | data formatting | bytes 1048576 | tf_op args[2]
  2.1 0.0 copy-start.12
  2.1 0.0 copy-start.11
  2.1 3.0 %collective-permute-start = (bf16[2,2,4,16,512]{4,3,2,1,0:T(8,128)(2,1)S(1)}, bf16[2,2,4,16,512]{4,3,2,1,0:T(8,128)(2,1)S(1)}, u32[]{:S(2)}, u32[]{:S(2)}) collective-permute-start(bf16[2,2,4,16,512]{4,3,2,1,0:T(8,128)(2,1)S(1)} %get-tuple-element.22), channel_id=1, source_target_pairs={{0,2},{2,4},{4,6},{6,8},{8,10},{10,12},{12,14},{14,0},{1,3},{3,5},... | collective-permute-start | bytes 786440 | tf_op jit(solution)/shard_map/ppermute | solution.py:193
  5.1 3.1 %collective-permute-start.1 = (bf16[2,2,4,16,512]{4,3,2,1,0:T(8,128)(2,1)S(1)}, bf16[2,2,4,16,512]{4,3,2,1,0:T(8,128)(2,1)S(1)}, u32[]{:S(2)}, u32[]{:S(2)}) collective-permute-start(bf16[2,2,4,16,512]{4,3,2,1,0:T(8,128)(2,1)S(1)} %get-tuple-element.21), channel_id=1, source_target_pairs={{2,0},{4,2},{6,4},{8,6},{10,8},{12,10},{14,12},{0,14},{3,1},{5,3},... | collective-permute-start | bytes 786440 | tf_op jit(solution)/shard_map/ppermute | solution.py:194
  8.2 8.1 %collective-permute-done.refs_0_ = bf16[2,2,4,16,512]{4,3,2,1,0:T(8,128)(2,1)S(1)} collective-permute-done((bf16[2,2,4,16,512]{4,3,2,1,0:T(8,128)(2,1)S(1)}, bf16[2,2,4,16,512]{4,3,2,1,0:T(8,128)(2,1)S(1)}, u32[]{:S(2)}, u32[]{:S(2)}) %collective-permute-start) | collective-permute-done | bytes 262176 | tf_op jit(solution)/shard_map/ppermute | solution.py:193
  16.3 0.0 collective-permute-start.2
  16.3 2.2 %collective-permute-done.1.refs_2_ = bf16[2,2,4,16,512]{4,3,2,1,0:T(8,128)(2,1)S(1)} collective-permute-done((bf16[2,2,4,16,512]{4,3,2,1,0:T(8,128)(2,1)S(1)}, bf16[2,2,4,16,512]{4,3,2,1,0:T(8,128)(2,1)S(1)}, u32[]{:S(2)}, u32[]{:S(2)}) %collective-permute-start.1) | collective-permute-done | bytes 262176 | tf_op jit(solution)/shard_map/ppermute | solution.py:194
  18.5 0.0 collective-permute-start.4
  18.6 0.6 collective-permute-start.6
  19.1 0.1 constant_dynamic-slice_fusion.2
  19.3 0.0 copy-start.9
  19.3 0.1 copy.20
  19.5 0.1 copy.15
  19.5 0.8 %reshape.44.refs_7_ = bf16[48,288]{1,0:T(8,128)(2,1)} reshape(bf16[3,16,3,3,32]{4,3,2,1,0:T(4,128)(2,1)S(1)} %copy.15) | data formatting | bytes 55296 | tf_op jit(solution)/shard_map/reshape | solution.py:203
  20.3 0.0 copy-done.9
  20.3 1.1 %copy.24 = bf16[16,4,8,512]{3,0,2,1:T(8,128)(2,1)} copy(bf16[16,4,8,512]{3,2,1,0:T(8,128)(2,1)S(1)} %copy-done.9) | data formatting | bytes 1048576 | tf_op args[1]
  21.5 0.0 collective-permute-done.2.refs_3_
  21.5 0.0 collective-permute-done.4.refs_5_
  21.5 0.7 copy-done.5
  22.2 0.1 copy-done.6
  22.3 0.2 copy-done.2
  22.4 5.7 %shard_map.76 = (bf16[1,8,16,512]{3,2,1,0:T(8,128)(2,1)}, f32[288,48]{1,0:T(8,128)}) custom-call(bf16[2,2,4,16,512]{4,3,2,1,0:T(8,128)(2,1)} %copy-done.3, bf16[4,2,4,16,512]{4,3,2,1,0:T(8,128)(2,1)} %bitcast.24, bf16[2,2,4,16,512]{4,3,2,1,0:T(8,128)(2,1)} %copy-done.4, bf16[2,2,4,16,512]{4,3,2,1,0:T(8,128)(2,1)} %copy-done.5, ...), custom_call_target="tpu_custom_call" | custom-call | tf_op jit(solution)/shard_map/pallas_call | solution.py:210
  28.1 0.8 %collective-permute-start.5 = (bf16[1,128,512]{2,1,0:T(8,128)(2,1)}, bf16[1,128,512]{2,1,0:T(8,128)(2,1)S(1)}, u32[]{:S(2)}, u32[]{:S(2)}) collective-permute-start(bf16[1,128,512]{2,1,0:T(8,128)(2,1)} %bitcast.34), channel_id=1, source_target_pairs={{14,0},{0,2},{2,4},{4,6},{6,8},{8,10},{10,12},{12,14},{15,1},{1,3}... | collective-permute-start | bytes 393224 | tf_op jit(solution)/shard_map/ppermute | solution.py:30
  28.9 0.8 %copy.17.u_ref = bf16[3,64,144]{2,1,0:T(8,128)(2,1)} copy(bf16[3,64,144]{1,2,0:T(8,128)(2,1)S(1)} %bitcast.31) | data formatting | bytes 110592 | tf_op jit(solution)/shard_map/reshape | solution.py:241
  29.6 11.1 %shard_map.77 = (bf16[3,8,16,512]{3,2,1,0:T(8,128)(2,1)}, f32[288,48]{1,0:T(8,128)}, f32[27,32,16]{2,1,0:T(8,128)}) custom-call(bf16[2,2,4,16,512]{4,3,2,1,0:T(8,128)(2,1)} %copy-done.3, bf16[4,2,4,16,512]{4,3,2,1,0:T(8,128)(2,1)} %bitcast.25, bf16[2,2,4,16,512]{4,3,2,1,0:T(8,128)(2,1)} %copy-done.4, bf16[2,2,4,16,512]{4,3,2,1,0:T(8,128)(2,1)} %copy-done.5, ...), custom_call_target="tpu_custom_call" | custom-call | tf_op jit(solution)/shard_map/pallas_call | solution.py:210
  40.8 1.2 %reshape.49 = f32[13824]{0:T(1024)S(1)} reshape(f32[27,32,16]{2,1,0:T(8,128)} %get-tuple-element.14) | data formatting | bytes 110592 | tf_op jit(solution)/shard_map/reshape | solution.py:260
  42.0 0.0 copy-start.14
  42.0 0.6 copy-done.13
  42.6 0.0 copy-done.14
  42.7 4.8 %shard_map.78 = (f32[2,4,64,256]{3,2,1,0:T(8,128)}, f32[3,144,64]{2,1,0:T(8,128)}) custom-call(bf16[3,128,512]{2,1,0:T(8,128)(2,1)} %bitcast.33, bf16[1,128,512]{2,1,0:T(8,128)(2,1)} %bitcast.35, bf16[1,128,512]{2,1,0:T(8,128)(2,1)} %copy-done.14, bf16[2,4,32,256]{3,2,1,0:T(8,128)(2,1)} %bitcast.30, bf16[2,4,32,256]{3,2,1,0:T(8,128)(2,1)} %copy-done.13, ...), custom_call_target="tpu_custom_call" | custom-call | tf_op jit(solution)/shard_map/pallas_call | solution.py:243
  47.5 1.1 %reshape_reshape.3 = f32[27648]{0:T(1024)S(1)} reshape(f32[3,144,64]{2,1,0:T(8,128)} %get-tuple-element.13) | data formatting | bytes 221184 | tf_op jit(solution)/shard_map/reshape;reshape | solution.py:260
  48.6 2.1 %collective-permute-start.8 = (f32[41472]{0:T(1024)S(1)}, f32[41472]{0:T(1024)S(1)}, u32[]{:S(2)}, u32[]{:S(2)}) collective-permute-start(f32[41472]{0:T(1024)S(1)} %constant_dynamic-update-slice_fusion), channel_id=1, source_target_pairs={{0,2},{2,0},{4,6},{6,4},{8,10},{10,8},{12,14},{14,12},{1,3},{3,1},... | collective-permute-start | bytes 497672 | tf_op jit(solution)/shard_map/ppermute | solution.py:40
  50.7 0.1 collective-permute-start.7
  50.8 4.5 %collective-permute-done.8 = f32[41472]{0:T(1024)S(1)} collective-permute-done((f32[41472]{0:T(1024)S(1)}, f32[41472]{0:T(1024)S(1)}, u32[]{:S(2)}, u32[]{:S(2)}) %collective-permute-start.8) | collective-permute-done | bytes 165920 | tf_op jit(solution)/shard_map/ppermute | solution.py:40
  55.3 1.6 %collective-permute-start.9 = (f32[41472]{0:T(1024)S(1)}, f32[41472]{0:T(1024)S(1)}, u32[]{:S(2)}, u32[]{:S(2)}) collective-permute-start(f32[41472]{0:T(1024)S(1)} %add.27), channel_id=1, source_target_pairs={{0,4},{2,6},{4,0},{6,2},{8,12},{10,14},{12,8},{14,10},{1,5},{3,7},... | collective-permute-start | bytes 497672 | tf_op jit(solution)/shard_map/ppermute | solution.py:40
  56.9 4.3 %collective-permute-done.9 = f32[41472]{0:T(1024)S(1)} collective-permute-done((f32[41472]{0:T(1024)S(1)}, f32[41472]{0:T(1024)S(1)}, u32[]{:S(2)}, u32[]{:S(2)}) %collective-permute-start.9) | collective-permute-done | bytes 165920 | tf_op jit(solution)/shard_map/ppermute | solution.py:40
  61.2 2.7 %collective-permute-start.10 = (f32[41472]{0:T(1024)S(1)}, f32[41472]{0:T(1024)S(1)}, u32[]{:S(2)}, u32[]{:S(2)}) collective-permute-start(f32[41472]{0:T(1024)S(1)} %add.28), channel_id=1, source_target_pairs={{0,8},{2,10},{4,12},{6,14},{8,0},{10,2},{12,4},{14,6},{1,9},{3,11}... | collective-permute-start | bytes 497672 | tf_op jit(solution)/shard_map/ppermute | solution.py:40
  63.9 0.8 %copy.18 = bf16[32,2,4,256]{3,2,1,0:T(4,128)(2,1)} copy(bf16[32,2,4,256]{3,0,2,1:T(8,128)(2,1)S(1)} %fusion) | data formatting | bytes 262144
  64.7 6.0 %collective-permute-done.10 = f32[41472]{0:T(1024)S(1)} collective-permute-done((f32[41472]{0:T(1024)S(1)}, f32[41472]{0:T(1024)S(1)}, u32[]{:S(2)}, u32[]{:S(2)}) %collective-permute-start.10) | collective-permute-done | bytes 165920 | tf_op jit(solution)/shard_map/ppermute | solution.py:40
  70.7 0.0 copy-start.7
  70.8 0.6 copy-done.7
  71.4 0.2 slice.26
  71.6 0.0 slice-start
  71.6 0.9 %copy.19 = f32[27,32,16]{1,2,0:T(8,128)} copy(f32[27,32,16]{2,1,0:T(8,128)S(1)} %slice.26) | data formatting | bytes 110592
  72.5 0.0 slice-done
  72.5 0.8 %reshape.50 = f32[27,16,64]{2,1,0:T(8,128)} reshape(f32[27648]{0:T(1024)S(1)} %slice-done) | data formatting | bytes 221184 | tf_op jit(solution)/shard_map/reshape | solution.py:262
  (35 shorter events, 0.3 us)
Async XLA Ops:
  0.6 28.2 %copy-start = (bf16[27,32,64]{2,1,0:T(8,128)(2,1)S(1)}, bf16[27,32,64]{2,1,0:T(8,128)(2,1)}, u32[]{:S(2)}) copy-start(bf16[27,32,64]{2,1,0:T(8,128)(2,1)} %param.8) | copy-start | bytes 331780
  2.1 6.2 %copy-start.1 = (bf16[16,4,4,2,512]{4,0,2,3,1:T(8,128)(2,1)}, bf16[16,4,4,2,512]{4,0,2,3,1:T(8,128)(2,1)S(1)}, u32[]{:S(2)}) copy-start(bf16[16,4,4,2,512]{4,0,2,3,1:T(8,128)(2,1)S(1)} %copy.25) | copy-start | bytes 1572868
  2.1 16.5 %copy-start.12 = (bf16[32,2,4,256]{3,2,1,0:T(4,128)(2,1)S(1)}, bf16[32,2,4,256]{3,2,1,0:T(4,128)(2,1)}, u32[]{:S(2)}) copy-start(bf16[32,2,4,256]{3,2,1,0:T(4,128)(2,1)} %param.5) | copy-start | bytes 393220
  2.1 17.0 %copy-start.11 = (bf16[27,32,32]{2,1,0:T(8,128)(2,1)S(1)}, bf16[27,32,32]{2,1,0:T(8,128)(2,1)}, u32[]{:S(2)}) copy-start(bf16[27,32,32]{2,1,0:T(8,128)(2,1)} %param.9) | copy-start | bytes 165892
  2.1 14.2 %collective-permute-start = (bf16[2,2,4,16,512]{4,3,2,1,0:T(8,128)(2,1)S(1)}, bf16[2,2,4,16,512]{4,3,2,1,0:T(8,128)(2,1)S(1)}, u32[]{:S(2)}, u32[]{:S(2)}) collective-permute-start(bf16[2,2,4,16,512]{4,3,2,1,0:T(8,128)(2,1)S(1)} %get-tuple-element.22), channel_id=1, source_target_pairs={{0,2},{2,4},{4,6},{6,8},{8,10},{10,12},{12,14},{14,0},{1,3},{3,5},... | collective-permute-start | bytes 786440 | tf_op jit(solution)/shard_map/ppermute | solution.py:193
  5.1 13.4 %collective-permute-start.1 = (bf16[2,2,4,16,512]{4,3,2,1,0:T(8,128)(2,1)S(1)}, bf16[2,2,4,16,512]{4,3,2,1,0:T(8,128)(2,1)S(1)}, u32[]{:S(2)}, u32[]{:S(2)}) collective-permute-start(bf16[2,2,4,16,512]{4,3,2,1,0:T(8,128)(2,1)S(1)} %get-tuple-element.21), channel_id=1, source_target_pairs={{2,0},{4,2},{6,4},{8,6},{10,8},{12,10},{14,12},{0,14},{3,1},{5,3},... | collective-permute-start | bytes 786440 | tf_op jit(solution)/shard_map/ppermute | solution.py:194
  8.2 13.2 %collective-permute-start.3 = (bf16[4,2,4,16,512]{4,3,2,1,0:T(8,128)(2,1)S(1)}, bf16[4,2,4,16,512]{4,3,2,1,0:T(8,128)(2,1)S(1)}, u32[]{:S(2)}, u32[]{:S(2)}) collective-permute-start(bf16[4,2,4,16,512]{4,3,2,1,0:T(8,128)(2,1)S(1)} %bitcast.23), channel_id=1, source_target_pairs={{0,1},{1,0},{2,3},{3,2},{4,5},{5,4},{6,7},{7,6},{8,9},{9,8},{10,11... | collective-permute-start | bytes 1572872 | tf_op jit(solution)/shard_map/ppermute | solution.py:195
  16.3 3.0 %copy-start.3 = (bf16[2,2,4,16,512]{4,3,2,1,0:T(8,128)(2,1)}, bf16[2,2,4,16,512]{4,3,2,1,0:T(8,128)(2,1)S(1)}, u32[]{:S(2)}) copy-start(bf16[2,2,4,16,512]{4,3,2,1,0:T(8,128)(2,1)S(1)} %collective-permute-done.refs_0_) | copy-start | bytes 786436
  16.3 5.1 %collective-permute-start.2 = (bf16[2,2,4,16,512]{4,3,2,1,0:T(8,128)(2,1)S(1)}, bf16[2,2,4,16,512]{4,3,2,1,0:T(8,128)(2,1)S(1)}, u32[]{:S(2)}, u32[]{:S(2)}) collective-permute-start(bf16[2,2,4,16,512]{4,3,2,1,0:T(8,128)(2,1)S(1)} %collective-permute-done.refs_0_), channel_id=1, source_target_pairs={{0,1},{1,0},{2,3},{3,2},{4,5},{5,4},{6,7},{7,6},{8,9},{9,8},{10,11... | collective-permute-start | bytes 786440 | tf_op jit(solution)/shard_map/ppermute | solution.py:196
  18.5 0.8 %copy-start.4 = (bf16[2,2,4,16,512]{4,3,2,1,0:T(8,128)(2,1)}, bf16[2,2,4,16,512]{4,3,2,1,0:T(8,128)(2,1)S(1)}, u32[]{:S(2)}) copy-start(bf16[2,2,4,16,512]{4,3,2,1,0:T(8,128)(2,1)S(1)} %collective-permute-done.1.refs_2_) | copy-start | bytes 786436
  18.5 2.9 %collective-permute-start.4 = (bf16[2,2,4,16,512]{4,3,2,1,0:T(8,128)(2,1)S(1)}, bf16[2,2,4,16,512]{4,3,2,1,0:T(8,128)(2,1)S(1)}, u32[]{:S(2)}, u32[]{:S(2)}) collective-permute-start(bf16[2,2,4,16,512]{4,3,2,1,0:T(8,128)(2,1)S(1)} %collective-permute-done.1.refs_2_), channel_id=1, source_target_pairs={{0,1},{1,0},{2,3},{3,2},{4,5},{5,4},{6,7},{7,6},{8,9},{9,8},{10,11... | collective-permute-start | bytes 786440 | tf_op jit(solution)/shard_map/ppermute | solution.py:197
  18.6 0.7 copy-start.10
  18.6 23.4 %collective-permute-start.6 = (bf16[2,4,32,256]{3,2,1,0:T(8,128)(2,1)S(1)}, bf16[2,4,32,256]{3,2,1,0:T(8,128)(2,1)S(1)}, u32[]{:S(2)}, u32[]{:S(2)}) collective-permute-start(bf16[2,4,32,256]{3,2,1,0:T(8,128)(2,1)S(1)} %bitcast.29), channel_id=1, source_target_pairs={{0,1},{1,0},{2,3},{3,2},{4,5},{5,4},{6,7},{7,6},{8,9},{9,8},{10,11... | collective-permute-start | bytes 393224 | tf_op jit(solution)/shard_map/ppermute | solution.py:234
  19.3 1.0 %copy-start.9 = (bf16[16,4,8,512]{3,2,1,0:T(8,128)(2,1)S(1)}, bf16[16,4,8,512]{3,2,1,0:T(8,128)(2,1)}, u32[]{:S(2)}) copy-start(bf16[16,4,8,512]{3,2,1,0:T(8,128)(2,1)} %param.6) | copy-start | bytes 1572868
  21.5 0.7 copy-start.5
  21.5 0.8 %copy-start.6 = (bf16[2,2,4,16,512]{4,3,2,1,0:T(8,128)(2,1)}, bf16[2,2,4,16,512]{4,3,2,1,0:T(8,128)(2,1)S(1)}, u32[]{:S(2)}) copy-start(bf16[2,2,4,16,512]{4,3,2,1,0:T(8,128)(2,1)S(1)} %collective-permute-done.4.refs_5_) | copy-start | bytes 786436
  21.5 1.0 %copy-start.2 = (bf16[4,2,4,16,512]{4,3,2,1,0:T(8,128)(2,1)}, bf16[4,2,4,16,512]{4,3,2,1,0:T(8,128)(2,1)S(1)}, u32[]{:S(2)}) copy-start(bf16[4,2,4,16,512]{4,3,2,1,0:T(8,128)(2,1)S(1)} %collective-permute-done.3.refs_4_) | copy-start | bytes 1572868
  28.1 13.9 %collective-permute-start.5 = (bf16[1,128,512]{2,1,0:T(8,128)(2,1)}, bf16[1,128,512]{2,1,0:T(8,128)(2,1)S(1)}, u32[]{:S(2)}, u32[]{:S(2)}) collective-permute-start(bf16[1,128,512]{2,1,0:T(8,128)(2,1)} %bitcast.34), channel_id=1, source_target_pairs={{14,0},{0,2},{2,4},{4,6},{6,8},{8,10},{10,12},{12,14},{15,1},{1,3}... | collective-permute-start | bytes 393224 | tf_op jit(solution)/shard_map/ppermute | solution.py:30
  42.0 0.7 copy-start.13
  42.0 0.7 copy-start.14
  47.5 3.2 %copy-start.8 = (f32[2,4,64,256]{3,2,1,0:T(8,128)S(1)}, f32[2,4,64,256]{3,2,1,0:T(8,128)}, u32[]{:S(2)}) copy-start(f32[2,4,64,256]{3,2,1,0:T(8,128)} %get-tuple-element.12) | copy-start | bytes 1572868
  48.6 6.7 %collective-permute-start.8 = (f32[41472]{0:T(1024)S(1)}, f32[41472]{0:T(1024)S(1)}, u32[]{:S(2)}, u32[]{:S(2)}) collective-permute-start(f32[41472]{0:T(1024)S(1)} %constant_dynamic-update-slice_fusion), channel_id=1, source_target_pairs={{0,2},{2,0},{4,6},{6,4},{8,10},{10,8},{12,14},{14,12},{1,3},{3,1},... | collective-permute-start | bytes 497672 | tf_op jit(solution)/shard_map/ppermute | solution.py:40
  50.7 13.2 %collective-permute-start.7 = (f32[2,4,32,256]{3,2,1,0:T(8,128)S(1)}, f32[2,4,32,256]{3,2,1,0:T(8,128)S(1)}, u32[]{:S(2)}, u32[]{:S(2)}) collective-permute-start(f32[2,4,32,256]{3,2,1,0:T(8,128)S(1)} %constant_dynamic-slice_fusion), channel_id=1, source_target_pairs={{0,1},{1,0},{2,3},{3,2},{4,5},{5,4},{6,7},{7,6},{8,9},{9,8},{10,11... | collective-permute-start | bytes 786440 | tf_op jit(solution)/shard_map/ppermute | solution.py:257
  55.3 5.9 %collective-permute-start.9 = (f32[41472]{0:T(1024)S(1)}, f32[41472]{0:T(1024)S(1)}, u32[]{:S(2)}, u32[]{:S(2)}) collective-permute-start(f32[41472]{0:T(1024)S(1)} %add.27), channel_id=1, source_target_pairs={{0,4},{2,6},{4,0},{6,2},{8,12},{10,14},{12,8},{14,10},{1,5},{3,7},... | collective-permute-start | bytes 497672 | tf_op jit(solution)/shard_map/ppermute | solution.py:40
  61.2 9.5 %collective-permute-start.10 = (f32[41472]{0:T(1024)S(1)}, f32[41472]{0:T(1024)S(1)}, u32[]{:S(2)}, u32[]{:S(2)}) collective-permute-start(f32[41472]{0:T(1024)S(1)} %add.28), channel_id=1, source_target_pairs={{0,8},{2,10},{4,12},{6,14},{8,0},{10,2},{12,4},{14,6},{1,9},{3,11}... | collective-permute-start | bytes 497672 | tf_op jit(solution)/shard_map/ppermute | solution.py:40
  70.7 0.7 copy-start.7
  71.6 0.9 %slice-start = ((f32[41472]{0:T(1024)}), f32[27648]{0:T(1024)S(1)}, s32[]{:S(2)}) async-start(f32[41472]{0:T(1024)} %copy-done.7), calls=%async_computation | async-start | bytes 221184 | tf_op jit(solution)/shard_map/slice | solution.py:262

commit v15 on v14

--- a/solution.py
+++ b/solution.py
@@ -190,8 +190,12 @@
     forward = [(i, (i + 1) % count) for i in range(count)]
     backward = [(target, source) for source, target in forward]
     swap = [(i, i ^ 1) for i in range(lax.axis_size("ch"))]
-    low = lax.ppermute(rows[planes_z - 2 :], ("gz", "sec"), forward)
-    high = lax.ppermute(rows[:2], ("gz", "sec"), backward)
+    def laid_out(block):
+        block = block.reshape(part_ch, block.shape[1], planes_x // 2, 2, cells_y)
+        return jnp.transpose(block, (1, 3, 2, 0, 4))
+
+    low = laid_out(lax.ppermute(out_grad[:, planes_z - 2 :], ("gz", "sec"), forward))
+    high = laid_out(lax.ppermute(out_grad[:, :2], ("gz", "sec"), backward))
     rows_other = lax.ppermute(rows, "ch", swap)
     low_other = lax.ppermute(low, "ch", swap)
     high_other = lax.ppermute(high, "ch", swap)

time: 73.8 us -> 73.3 us (level)
  waiting for transfers between devices: 25.1 us -> 23.7 us
  local copies, waits for them, and re-layouts: 11.7 us -> 12.9 us
    ppermute x3, waiting for transfers between devices: 14.8 us -> 13.6 us  [summed_over_slabs(): block = block + lax.ppermute(block, axis, route)]
    unnamed x37, local copies, waits for them, and re-layouts: 6.63 us -> 7.81 us
where the time goes in v15:
time: 73.3 us; the launch traced here: 72.8 us
  waiting for transfers between devices  23.7 us (32%)
  Pallas kernels  21.6 us (29%)
  starting transfers between devices  13.6 us (19%)
  local copies, waits for them, and re-layouts  12.9 us (18%)
  between operations  0.97 us (1%)
    pallas_call x2, Pallas kernels, fine_rows(): pl.pallas_call(functools.partial(fine_kernel, z_lo, z_hi, scale), out_sha...  16.8 us
    ppermute x3, waiting for transfers between devices, summed_over_slabs(): block = block + lax.ppermute(block, axis, route)  13.6 us
    ppermute x1, waiting for transfers between devices, local(): lax.ppermute(out_grad[:, planes_z - 2:], ('gz', 'sec'), forward)  7.95 us
    unnamed x37, local copies, waits for them, and re-layouts  7.81 us
    ppermute x3, starting transfers between devices, summed_over_slabs(): block = block + lax.ppermute(block, axis, route)  6.45 us
    pallas_call x1, Pallas kernels, local(): pl.pallas_call(functools.partial(coarse_kernel, float(coarse_total) ** (-...  4.8 us
    ppermute x1, starting transfers between devices, local(): high = laid_out(lax.ppermute(out_grad[:, :2], ('gz', 'sec'), backward))  3.1 us
    ppermute x1, starting transfers between devices, local(): lax.ppermute(out_grad[:, planes_z - 2:], ('gz', 'sec'), forward)  2.99 us
  transfers between devices with their start and end apart: 11, of which 5 were waited for; matrix products, arithmetic and copies ran while one was open for 7% of the time, Pallas kernels for 23%

profile of v15, /device:TPU:0, one launch (start us, length us, event | category | flops | bytes accessed | tf_op | source)
XLA Modules:
  0.0 72.8 jit_solution(3004979447173549203)
XLA Ops:
  0.6 0.0 copy-start
  0.6 1.4 %copy.11 = bf16[16,4,8,512]{3,0,2,1:T(8,128)(2,1)S(1)} copy(bf16[16,4,8,512]{3,2,1,0:T(8,128)(2,1)} %param.7) | data formatting | bytes 1048576 | tf_op args[2]
  2.1 3.0 %collective-permute-start = (bf16[16,2,8,512]{3,0,2,1:T(8,128)(2,1)S(1)}, bf16[16,2,8,512]{3,0,2,1:T(8,128)(2,1)S(1)}, u32[]{:S(2)}, u32[]{:S(2)}) collective-permute-start(bf16[16,2,8,512]{3,0,2,1:T(8,128)(2,1)S(1)} %get-tuple-element.22), channel_id=1, source_target_pairs={{0,2},{2,4},{4,6},{6,8},{8,10},{10,12},{12,14},{14,0},{1,3},{3,5},... | collective-permute-start | bytes 786440 | tf_op jit(solution)/shard_map/ppermute | solution.py:197
  5.1 3.1 %collective-permute-start.1 = (bf16[16,2,8,512]{3,0,2,1:T(8,128)(2,1)S(1)}, bf16[16,2,8,512]{3,0,2,1:T(8,128)(2,1)S(1)}, u32[]{:S(2)}, u32[]{:S(2)}) collective-permute-start(bf16[16,2,8,512]{3,0,2,1:T(8,128)(2,1)S(1)} %get-tuple-element.21), channel_id=1, source_target_pairs={{2,0},{4,2},{6,4},{8,6},{10,8},{12,10},{14,12},{0,14},{3,1},{5,3},... | collective-permute-start | bytes 786440 | tf_op jit(solution)/shard_map/ppermute | solution.py:198
  8.2 0.1 collective-permute-start.3
  8.3 8.0 %collective-permute-done = bf16[16,2,8,512]{3,0,2,1:T(8,128)(2,1)S(1)} collective-permute-done((bf16[16,2,8,512]{3,0,2,1:T(8,128)(2,1)S(1)}, bf16[16,2,8,512]{3,0,2,1:T(8,128)(2,1)S(1)}, u32[]{:S(2)}, u32[]{:S(2)}) %collective-permute-start) | collective-permute-done | bytes 262176 | tf_op jit(solution)/shard_map/ppermute | solution.py:197
  16.3 0.1 collective-permute-start.2
  16.4 2.1 %collective-permute-done.1 = bf16[16,2,8,512]{3,0,2,1:T(8,128)(2,1)S(1)} collective-permute-done((bf16[16,2,8,512]{3,0,2,1:T(8,128)(2,1)S(1)}, bf16[16,2,8,512]{3,0,2,1:T(8,128)(2,1)S(1)}, u32[]{:S(2)}, u32[]{:S(2)}) %collective-permute-start.1) | collective-permute-done | bytes 262176 | tf_op jit(solution)/shard_map/ppermute | solution.py:198
  18.5 0.0 copy-start.11
  18.5 0.1 collective-permute-start.4
  18.6 0.8 %copy-done.12 = bf16[32,2,4,256]{3,2,1,0:T(4,128)(2,1)S(1)} copy-done((bf16[32,2,4,256]{3,2,1,0:T(4,128)(2,1)S(1)}, bf16[32,2,4,256]{3,2,1,0:T(4,128)(2,1)}, u32[]{:S(2)}) %copy-start.12) | copy-done | bytes 131096
  19.4 0.1 collective-permute-start.6
  19.5 0.1 copy-done.11
  19.5 0.1 constant_dynamic-slice_fusion.2
  19.7 0.4 copy-done.10
  20.0 0.1 copy.24
  20.2 0.1 copy.19
  20.3 0.8 %reshape.52.refs_7_ = bf16[48,288]{1,0:T(8,128)(2,1)} reshape(bf16[3,16,3,3,32]{4,3,2,1,0:T(4,128)(2,1)S(1)} %copy.19) | data formatting | bytes 55296 | tf_op jit(solution)/shard_map/reshape | solution.py:207
  21.0 0.0 copy-done.9
  21.1 1.1 %copy.30 = bf16[16,4,8,512]{3,0,2,1:T(8,128)(2,1)} copy(bf16[16,4,8,512]{3,2,1,0:T(8,128)(2,1)S(1)} %copy-done.9) | data formatting | bytes 1048576 | tf_op args[1]
  22.2 0.7 copy-done.5
  22.9 0.1 copy-done.6
  23.0 0.2 copy-done.4
  23.2 5.7 %shard_map.76 = (bf16[1,8,16,512]{3,2,1,0:T(8,128)(2,1)}, f32[288,48]{1,0:T(8,128)}) custom-call(bf16[2,2,4,16,512]{4,3,2,1,0:T(8,128)(2,1)} %bitcast.37, bf16[4,2,4,16,512]{4,3,2,1,0:T(8,128)(2,1)} %bitcast.32, bf16[2,2,4,16,512]{4,3,2,1,0:T(8,128)(2,1)} %bitcast.40, bf16[2,2,4,16,512]{4,3,2,1,0:T(8,128)(2,1)} %copy-done.5, ...), custom_call_target="tpu_custom_call" | custom-call | tf_op jit(solution)/shard_map/pallas_call | solution.py:214
  28.8 0.7 collective-permute-start.5
  29.5 0.8 %copy.21.u_ref = bf16[3,64,144]{2,1,0:T(8,128)(2,1)} copy(bf16[3,64,144]{1,2,0:T(8,128)(2,1)S(1)} %bitcast.44) | data formatting | bytes 110592 | tf_op jit(solution)/shard_map/reshape | solution.py:245
  30.3 11.1 %shard_map.77 = (bf16[3,8,16,512]{3,2,1,0:T(8,128)(2,1)}, f32[288,48]{1,0:T(8,128)}, f32[27,32,16]{2,1,0:T(8,128)}) custom-call(bf16[2,2,4,16,512]{4,3,2,1,0:T(8,128)(2,1)} %bitcast.38, bf16[4,2,4,16,512]{4,3,2,1,0:T(8,128)(2,1)} %bitcast.33, bf16[2,2,4,16,512]{4,3,2,1,0:T(8,128)(2,1)} %bitcast.41, bf16[2,2,4,16,512]{4,3,2,1,0:T(8,128)(2,1)} %copy-done.5, ...), custom_call_target="tpu_custom_call" | custom-call | tf_op jit(solution)/shard_map/pallas_call | solution.py:214
  41.4 1.2 %reshape.57 = f32[13824]{0:T(1024)S(1)} reshape(f32[27,32,16]{2,1,0:T(8,128)} %get-tuple-element.14) | data formatting | bytes 110592 | tf_op jit(solution)/shard_map/reshape | solution.py:264
  42.6 0.0 copy-start.14
  42.6 0.6 copy-done.13
  43.3 0.0 copy-done.14
  43.3 4.8 %shard_map.78 = (f32[2,4,64,256]{3,2,1,0:T(8,128)}, f32[3,144,64]{2,1,0:T(8,128)}) custom-call(bf16[3,128,512]{2,1,0:T(8,128)(2,1)} %bitcast.46, bf16[1,128,512]{2,1,0:T(8,128)(2,1)} %bitcast.50, bf16[1,128,512]{2,1,0:T(8,128)(2,1)} %copy-done.14, bf16[2,4,32,256]{3,2,1,0:T(8,128)(2,1)} %bitcast.43, bf16[2,4,32,256]{3,2,1,0:T(8,128)(2,1)} %copy-done.13, ...), custom_call_target="tpu_custom_call" | custom-call | tf_op jit(solution)/shard_map/pallas_call | solution.py:247
  48.1 1.1 %reshape_reshape.3 = f32[27648]{0:T(1024)S(1)} reshape(f32[3,144,64]{2,1,0:T(8,128)} %get-tuple-element.13) | data formatting | bytes 221184 | tf_op jit(solution)/shard_map/reshape;reshape | solution.py:264
  49.2 2.1 %collective-permute-start.8 = (f32[41472]{0:T(1024)S(1)}, f32[41472]{0:T(1024)S(1)}, u32[]{:S(2)}, u32[]{:S(2)}) collective-permute-start(f32[41472]{0:T(1024)S(1)} %constant_dynamic-update-slice_fusion), channel_id=1, source_target_pairs={{0,2},{2,0},{4,6},{6,4},{8,10},{10,8},{12,14},{14,12},{1,3},{3,1},... | collective-permute-start | bytes 497672 | tf_op jit(solution)/shard_map/ppermute | solution.py:40
  51.4 0.1 collective-permute-start.7
  51.5 4.2 %collective-permute-done.8 = f32[41472]{0:T(1024)S(1)} collective-permute-done((f32[41472]{0:T(1024)S(1)}, f32[41472]{0:T(1024)S(1)}, u32[]{:S(2)}, u32[]{:S(2)}) %collective-permute-start.8) | collective-permute-done | bytes 165920 | tf_op jit(solution)/shard_map/ppermute | solution.py:40
  55.7 1.6 %collective-permute-start.9 = (f32[41472]{0:T(1024)S(1)}, f32[41472]{0:T(1024)S(1)}, u32[]{:S(2)}, u32[]{:S(2)}) collective-permute-start(f32[41472]{0:T(1024)S(1)} %add.27), channel_id=1, source_target_pairs={{0,4},{2,6},{4,0},{6,2},{8,12},{10,14},{12,8},{14,10},{1,5},{3,7},... | collective-permute-start | bytes 497672 | tf_op jit(solution)/shard_map/ppermute | solution.py:40
  57.3 3.9 %collective-permute-done.9 = f32[41472]{0:T(1024)S(1)} collective-permute-done((f32[41472]{0:T(1024)S(1)}, f32[41472]{0:T(1024)S(1)}, u32[]{:S(2)}, u32[]{:S(2)}) %collective-permute-start.9) | collective-permute-done | bytes 165920 | tf_op jit(solution)/shard_map/ppermute | solution.py:40
  61.2 2.7 %collective-permute-start.10 = (f32[41472]{0:T(1024)S(1)}, f32[41472]{0:T(1024)S(1)}, u32[]{:S(2)}, u32[]{:S(2)}) collective-permute-start(f32[41472]{0:T(1024)S(1)} %add.28), channel_id=1, source_target_pairs={{0,8},{2,10},{4,12},{6,14},{8,0},{10,2},{12,4},{14,6},{1,9},{3,11}... | collective-permute-start | bytes 497672 | tf_op jit(solution)/shard_map/ppermute | solution.py:40
  63.9 0.8 %copy.22 = bf16[32,2,4,256]{3,2,1,0:T(4,128)(2,1)} copy(bf16[32,2,4,256]{3,0,2,1:T(8,128)(2,1)S(1)} %fusion) | data formatting | bytes 262144
  64.6 5.6 %collective-permute-done.10 = f32[41472]{0:T(1024)S(1)} collective-permute-done((f32[41472]{0:T(1024)S(1)}, f32[41472]{0:T(1024)S(1)}, u32[]{:S(2)}, u32[]{:S(2)}) %collective-permute-start.10) | collective-permute-done | bytes 165920 | tf_op jit(solution)/shard_map/ppermute | solution.py:40
  70.3 0.0 copy-start.7
  70.3 0.6 copy-done.7
  71.0 0.2 slice.26
  71.1 0.0 slice-start
  71.1 0.9 %copy.23 = f32[27,32,16]{1,2,0:T(8,128)} copy(f32[27,32,16]{2,1,0:T(8,128)S(1)} %slice.26) | data formatting | bytes 110592
  72.0 0.0 slice-done
  72.0 0.8 %reshape.58 = f32[27,16,64]{2,1,0:T(8,128)} reshape(f32[27648]{0:T(1024)S(1)} %slice-done) | data formatting | bytes 221184 | tf_op jit(solution)/shard_map/reshape | solution.py:266
  (37 shorter events, 0.3 us)
Async XLA Ops:
  0.6 28.9 %copy-start = (bf16[27,32,64]{2,1,0:T(8,128)(2,1)S(1)}, bf16[27,32,64]{2,1,0:T(8,128)(2,1)}, u32[]{:S(2)}) copy-start(bf16[27,32,64]{2,1,0:T(8,128)(2,1)} %param.8) | copy-start | bytes 331780
  2.1 14.2 %collective-permute-start = (bf16[16,2,8,512]{3,0,2,1:T(8,128)(2,1)S(1)}, bf16[16,2,8,512]{3,0,2,1:T(8,128)(2,1)S(1)}, u32[]{:S(2)}, u32[]{:S(2)}) collective-permute-start(bf16[16,2,8,512]{3,0,2,1:T(8,128)(2,1)S(1)} %get-tuple-element.22), channel_id=1, source_target_pairs={{0,2},{2,4},{4,6},{6,8},{8,10},{10,12},{12,14},{14,0},{1,3},{3,5},... | collective-permute-start | bytes 786440 | tf_op jit(solution)/shard_map/ppermute | solution.py:197
  5.1 13.4 %collective-permute-start.1 = (bf16[16,2,8,512]{3,0,2,1:T(8,128)(2,1)S(1)}, bf16[16,2,8,512]{3,0,2,1:T(8,128)(2,1)S(1)}, u32[]{:S(2)}, u32[]{:S(2)}) collective-permute-start(bf16[16,2,8,512]{3,0,2,1:T(8,128)(2,1)S(1)} %get-tuple-element.21), channel_id=1, source_target_pairs={{2,0},{4,2},{6,4},{8,6},{10,8},{12,10},{14,12},{0,14},{3,1},{5,3},... | collective-permute-start | bytes 786440 | tf_op jit(solution)/shard_map/ppermute | solution.py:198
  8.2 10.3 %copy-start.1 = (bf16[16,4,4,2,512]{4,0,2,3,1:T(8,128)(2,1)}, bf16[16,4,4,2,512]{4,0,2,3,1:T(8,128)(2,1)S(1)}, u32[]{:S(2)}) copy-start(bf16[16,4,4,2,512]{4,0,2,3,1:T(8,128)(2,1)S(1)} %copy.31) | copy-start | bytes 1572868
  8.2 14.0 %collective-permute-start.3 = (bf16[4,2,4,16,512]{4,3,2,1,0:T(8,128)(2,1)S(1)}, bf16[4,2,4,16,512]{4,3,2,1,0:T(8,128)(2,1)S(1)}, u32[]{:S(2)}, u32[]{:S(2)}) collective-permute-start(bf16[4,2,4,16,512]{4,3,2,1,0:T(8,128)(2,1)S(1)} %bitcast.31), channel_id=1, source_target_pairs={{0,1},{1,0},{2,3},{3,2},{4,5},{5,4},{6,7},{7,6},{8,9},{9,8},{10,11... | collective-permute-start | bytes 1572872 | tf_op jit(solution)/shard_map/ppermute | solution.py:199
  16.3 2.2 %copy-start.2 = (bf16[16,2,4,2,512]{4,0,2,3,1:T(8,128)(2,1)}, bf16[16,2,4,2,512]{4,0,2,3,1:T(8,128)(2,1)S(1)}, u32[]{:S(2)}) copy-start(bf16[16,2,4,2,512]{4,0,2,3,1:T(8,128)(2,1)S(1)} %copy.33) | copy-start | bytes 786436
  16.3 5.9 %collective-permute-start.2 = (bf16[2,2,4,16,512]{4,3,2,1,0:T(8,128)(2,1)S(1)}, bf16[2,2,4,16,512]{4,3,2,1,0:T(8,128)(2,1)S(1)}, u32[]{:S(2)}, u32[]{:S(2)}) collective-permute-start(bf16[2,2,4,16,512]{4,3,2,1,0:T(8,128)(2,1)S(1)} %bitcast.36), channel_id=1, source_target_pairs={{0,1},{1,0},{2,3},{3,2},{4,5},{5,4},{6,7},{7,6},{8,9},{9,8},{10,11... | collective-permute-start | bytes 786440 | tf_op jit(solution)/shard_map/ppermute | solution.py:200
  18.4 0.9 %copy-start.12 = (bf16[32,2,4,256]{3,2,1,0:T(4,128)(2,1)S(1)}, bf16[32,2,4,256]{3,2,1,0:T(4,128)(2,1)}, u32[]{:S(2)}) copy-start(bf16[32,2,4,256]{3,2,1,0:T(4,128)(2,1)} %param.5) | copy-start | bytes 393220
  18.5 1.2 %copy-start.3 = (bf16[16,2,4,2,512]{4,0,2,3,1:T(8,128)(2,1)}, bf16[16,2,4,2,512]{4,0,2,3,1:T(8,128)(2,1)S(1)}, u32[]{:S(2)}) copy-start(bf16[16,2,4,2,512]{4,0,2,3,1:T(8,128)(2,1)S(1)} %copy.32) | copy-start | bytes 786436
  18.5 1.1 %copy-start.11 = (bf16[27,32,32]{2,1,0:T(8,128)(2,1)S(1)}, bf16[27,32,32]{2,1,0:T(8,128)(2,1)}, u32[]{:S(2)}) copy-start(bf16[27,32,32]{2,1,0:T(8,128)(2,1)} %param.9) | copy-start | bytes 165892
  18.5 3.7 %collective-permute-start.4 = (bf16[2,2,4,16,512]{4,3,2,1,0:T(8,128)(2,1)S(1)}, bf16[2,2,4,16,512]{4,3,2,1,0:T(8,128)(2,1)S(1)}, u32[]{:S(2)}, u32[]{:S(2)}) collective-permute-start(bf16[2,2,4,16,512]{4,3,2,1,0:T(8,128)(2,1)S(1)} %bitcast.39), channel_id=1, source_target_pairs={{0,1},{1,0},{2,3},{3,2},{4,5},{5,4},{6,7},{7,6},{8,9},{9,8},{10,11... | collective-permute-start | bytes 786440 | tf_op jit(solution)/shard_map/ppermute | solution.py:201
  19.4 0.7 copy-start.10
  19.4 23.2 %collective-permute-start.6 = (bf16[2,4,32,256]{3,2,1,0:T(8,128)(2,1)S(1)}, bf16[2,4,32,256]{3,2,1,0:T(8,128)(2,1)S(1)}, u32[]{:S(2)}, u32[]{:S(2)}) collective-permute-start(bf16[2,4,32,256]{3,2,1,0:T(8,128)(2,1)S(1)} %bitcast.42), channel_id=1, source_target_pairs={{0,1},{1,0},{2,3},{3,2},{4,5},{5,4},{6,7},{7,6},{8,9},{9,8},{10,11... | collective-permute-start | bytes 393224 | tf_op jit(solution)/shard_map/ppermute | solution.py:238
  20.0 1.0 %copy-start.9 = (bf16[16,4,8,512]{3,2,1,0:T(8,128)(2,1)S(1)}, bf16[16,4,8,512]{3,2,1,0:T(8,128)(2,1)}, u32[]{:S(2)}) copy-start(bf16[16,4,8,512]{3,2,1,0:T(8,128)(2,1)} %param.6) | copy-start | bytes 1572868
  22.2 0.7 copy-start.5
  22.2 0.8 %copy-start.6 = (bf16[2,2,4,16,512]{4,3,2,1,0:T(8,128)(2,1)}, bf16[2,2,4,16,512]{4,3,2,1,0:T(8,128)(2,1)S(1)}, u32[]{:S(2)}) copy-start(bf16[2,2,4,16,512]{4,3,2,1,0:T(8,128)(2,1)S(1)} %collective-permute-done.4.refs_5_) | copy-start | bytes 786436
  22.2 1.0 %copy-start.4 = (bf16[4,2,4,16,512]{4,3,2,1,0:T(8,128)(2,1)}, bf16[4,2,4,16,512]{4,3,2,1,0:T(8,128)(2,1)S(1)}, u32[]{:S(2)}) copy-start(bf16[4,2,4,16,512]{4,3,2,1,0:T(8,128)(2,1)S(1)} %collective-permute-done.3.refs_4_) | copy-start | bytes 1572868
  28.8 13.8 %collective-permute-start.5 = (bf16[1,128,512]{2,1,0:T(8,128)(2,1)}, bf16[1,128,512]{2,1,0:T(8,128)(2,1)S(1)}, u32[]{:S(2)}, u32[]{:S(2)}) collective-permute-start(bf16[1,128,512]{2,1,0:T(8,128)(2,1)} %bitcast.49), channel_id=1, source_target_pairs={{14,0},{0,2},{2,4},{4,6},{6,8},{8,10},{10,12},{12,14},{15,1},{1,3}... | collective-permute-start | bytes 393224 | tf_op jit(solution)/shard_map/ppermute | solution.py:30
  42.6 0.7 copy-start.13
  42.6 0.7 copy-start.14
  48.1 3.3 %copy-start.8 = (f32[2,4,64,256]{3,2,1,0:T(8,128)S(1)}, f32[2,4,64,256]{3,2,1,0:T(8,128)}, u32[]{:S(2)}) copy-start(f32[2,4,64,256]{3,2,1,0:T(8,128)} %get-tuple-element.12) | copy-start | bytes 1572868
  49.2 6.4 %collective-permute-start.8 = (f32[41472]{0:T(1024)S(1)}, f32[41472]{0:T(1024)S(1)}, u32[]{:S(2)}, u32[]{:S(2)}) collective-permute-start(f32[41472]{0:T(1024)S(1)} %constant_dynamic-update-slice_fusion), channel_id=1, source_target_pairs={{0,2},{2,0},{4,6},{6,4},{8,10},{10,8},{12,14},{14,12},{1,3},{3,1},... | collective-permute-start | bytes 497672 | tf_op jit(solution)/shard_map/ppermute | solution.py:40
  51.4 12.4 %collective-permute-start.7 = (f32[2,4,32,256]{3,2,1,0:T(8,128)S(1)}, f32[2,4,32,256]{3,2,1,0:T(8,128)S(1)}, u32[]{:S(2)}, u32[]{:S(2)}) collective-permute-start(f32[2,4,32,256]{3,2,1,0:T(8,128)S(1)} %constant_dynamic-slice_fusion), channel_id=1, source_target_pairs={{0,1},{1,0},{2,3},{3,2},{4,5},{5,4},{6,7},{7,6},{8,9},{9,8},{10,11... | collective-permute-start | bytes 786440 | tf_op jit(solution)/shard_map/ppermute | solution.py:261
  55.7 5.5 %collective-permute-start.9 = (f32[41472]{0:T(1024)S(1)}, f32[41472]{0:T(1024)S(1)}, u32[]{:S(2)}, u32[]{:S(2)}) collective-permute-start(f32[41472]{0:T(1024)S(1)} %add.27), channel_id=1, source_target_pairs={{0,4},{2,6},{4,0},{6,2},{8,12},{10,14},{12,8},{14,10},{1,5},{3,7},... | collective-permute-start | bytes 497672 | tf_op jit(solution)/shard_map/ppermute | solution.py:40
  61.2 9.1 %collective-permute-start.10 = (f32[41472]{0:T(1024)S(1)}, f32[41472]{0:T(1024)S(1)}, u32[]{:S(2)}, u32[]{:S(2)}) collective-permute-start(f32[41472]{0:T(1024)S(1)} %add.28), channel_id=1, source_target_pairs={{0,8},{2,10},{4,12},{6,14},{8,0},{10,2},{12,4},{14,6},{1,9},{3,11}... | collective-permute-start | bytes 497672 | tf_op jit(solution)/shard_map/ppermute | solution.py:40
  70.3 0.7 copy-start.7
  71.1 0.9 %slice-start = ((f32[41472]{0:T(1024)}), f32[27648]{0:T(1024)S(1)}, s32[]{:S(2)}) async-start(f32[41472]{0:T(1024)} %copy-done.7), calls=%async_computation | async-start | bytes 221184 | tf_op jit(solution)/shard_map/slice | solution.py:266

commit v16 on v15

--- a/solution.py
+++ b/solution.py
@@ -47,15 +47,15 @@
 
 
 def fine_kernel(z_lo, z_hi, scale, *refs):
-    pieces = refs[:6]
-    if len(refs) == 14:
-        sp_ref, w_ref, start_ref, gp_ref, r_ref, final_ref, g_ref, sems = refs[6:]
+    pieces = refs[:4]
+    if len(refs) == 12:
+        sp_ref, w_ref, start_ref, gp_ref, r_ref, final_ref, g_ref, sems = refs[4:]
     else:
-        sp_ref, w_ref, gp_ref, r_ref, g_ref, sems = refs[6:]
+        sp_ref, w_ref, gp_ref, r_ref, g_ref, sems = refs[4:]
         start_ref = final_ref = None
     planes_z, planes_x, part_ch, cells_y = sp_ref.shape
     wide = g_ref.shape[4]
-    low_count = pieces[0].shape[0]
+    low_count = pieces[0].shape[0] // 2
     core = lax.axis_index("ch")
     needed = sorted({z + 4 - 2 * dz for z in range(z_lo, z_hi) for dz in range(3)})
     edge = jnp.zeros(g_ref[:, :, :, 0].shape, g_ref.dtype)
@@ -68,11 +68,11 @@
         elif plane < low_count + planes_z:
             part, at = 1, plane - low_count
         else:
-            part, at = 2, plane - low_count - planes_z
+            part, at = 0, plane - planes_z
         for half in range(2):
             for parity in range(2):
                 copy = pltpu.make_async_copy(
-                    pieces[3 * half + part].at[at, parity],
+                    pieces[2 * half + part].at[at, parity],
                     g_ref.at[
                         plane % 2,
                         plane // 2,
@@ -194,12 +194,12 @@
         block = block.reshape(part_ch, block.shape[1], planes_x // 2, 2, cells_y)
         return jnp.transpose(block, (1, 3, 2, 0, 4))
 
-    low = laid_out(lax.ppermute(out_grad[:, planes_z - 2 :], ("gz", "sec"), forward))
-    high = laid_out(lax.ppermute(out_grad[:, :2], ("gz", "sec"), backward))
+    low_raw = lax.ppermute(out_grad[:, planes_z - 2 :], ("gz", "sec"), forward)
+    high_raw = lax.ppermute(out_grad[:, :2], ("gz", "sec"), backward)
+    halos = laid_out(jnp.concatenate([low_raw, high_raw], axis=1))
     rows_other = lax.ppermute(rows, "ch", swap)
-    low_other = lax.ppermute(low, "ch", swap)
-    high_other = lax.ppermute(high, "ch", swap)
-    halo_z = low.shape[0] + planes_z + high.shape[0]
+    halos_other = lax.ppermute(halos, "ch", swap)
+    halo_z = halos.shape[0] + planes_z
     pre_rows = jnp.transpose(saved_pre, (1, 2, 0, 3))
 
     refine_cols = lax.dynamic_slice_in_dim(refine_weight, channel_start, part_ch, 2)
@@ -218,7 +218,7 @@
                 jax.ShapeDtypeStruct((9 * all_ch, 3 * part_ch), jnp.float32),
             )
             + ((jax.ShapeDtypeStruct((27, all_ch, part_ch), jnp.float32),) if start else ()),
-            in_specs=[pl.BlockSpec(memory_space=pl.ANY)] * 6 + vmem_specs(2 + len(start)),
+            in_specs=[pl.BlockSpec(memory_space=pl.ANY)] * 4 + vmem_specs(2 + len(start)),
             out_specs=tuple(vmem_specs(2 + len(start))),
             scratch_shapes=[
                 pltpu.VMEM(
@@ -226,7 +226,7 @@
                 ),
                 pltpu.SemaphoreType.DMA((4 * halo_z,)),
             ],
-        )(low, rows, high, low_other, rows_other, high_other, pre_rows, refine_w, *start)
+        )(halos, rows, halos_other, rows_other, pre_rows, refine_w, *start)
 
     grad_last, refine_last = fine_rows(planes_z - 1, planes_z)
     last_rows = grad_last.reshape(1, planes_x * part_ch, cells_y)

time: 73.3 us -> 73.4 us (level)
    ppermute x4 -> x3, waiting for transfers between devices: 10 us -> 10.2 us  [the longest x1 7.95 us: local(): low_raw = lax.ppermute(out_grad[:, planes_z - 2:], ('gz', 'sec'), forward)]
    ppermute x4 -> x3, starting transfers between devices: 6.24 us -> 6.17 us  [the longest x1 3.1 us: local(): high_raw = lax.ppermute(out_grad[:, :2], ('gz', 'sec'), backward)]
    unnamed x37 -> x33, local copies, waits for them, and re-layouts: 7.81 us -> 7.82 us
  transfers between devices with their start and end apart: 11 -> 10, of which waited for: 5 -> 5; matrix products, arithmetic and copies ran while one was open for 7% -> 7% of each run, Pallas kernels for 23% -> 23%
where the time goes in v16:
time: 73.4 us; the launch traced here: 72.9 us
  waiting for transfers between devices  23.9 us (33%)
  Pallas kernels  21.6 us (29%)
  starting transfers between devices  13.5 us (18%)
  local copies, waits for them, and re-layouts  12.9 us (18%)
  between operations  0.94 us (1%)
    pallas_call x2, Pallas kernels, fine_rows(): pl.pallas_call(functools.partial(fine_kernel, z_lo, z_hi, scale), out_sha...  16.8 us
    ppermute x3, waiting for transfers between devices, summed_over_slabs(): block = block + lax.ppermute(block, axis, route)  13.7 us
    ppermute x1, waiting for transfers between devices, local(): low_raw = lax.ppermute(out_grad[:, planes_z - 2:], ('gz', 'sec'), forward)  7.95 us
    unnamed x33, local copies, waits for them, and re-layouts  7.82 us
    ppermute x3, starting transfers between devices, summed_over_slabs(): block = block + lax.ppermute(block, axis, route)  6.8 us
    pallas_call x1, Pallas kernels, local(): pl.pallas_call(functools.partial(coarse_kernel, float(coarse_total) ** (-...  4.8 us
    ppermute x1, starting transfers between devices, local(): high_raw = lax.ppermute(out_grad[:, :2], ('gz', 'sec'), backward)  3.1 us
    ppermute x1, starting transfers between devices, local(): low_raw = lax.ppermute(out_grad[:, planes_z - 2:], ('gz', 'sec'), forward)  2.99 us
  transfers between devices with their start and end apart: 10, of which 5 were waited for; matrix products, arithmetic and copies ran while one was open for 7% of the time, Pallas kernels for 23%

profile of v16, /device:TPU:0, one launch (start us, length us, event | category | flops | bytes accessed | tf_op | source)
XLA Modules:
  0.0 72.9 jit_solution(5206132538394674823)
XLA Ops:
  0.6 0.0 copy-start
  0.6 1.4 %copy.11 = bf16[16,4,8,512]{3,0,2,1:T(8,128)(2,1)S(1)} copy(bf16[16,4,8,512]{3,2,1,0:T(8,128)(2,1)} %param.7) | data formatting | bytes 1048576 | tf_op args[2]
  2.1 3.0 %collective-permute-start = (bf16[16,2,8,512]{3,0,2,1:T(8,128)(2,1)S(1)}, bf16[16,2,8,512]{3,0,2,1:T(8,128)(2,1)S(1)}, u32[]{:S(2)}, u32[]{:S(2)}) collective-permute-start(bf16[16,2,8,512]{3,0,2,1:T(8,128)(2,1)S(1)} %get-tuple-element.21), channel_id=1, source_target_pairs={{0,2},{2,4},{4,6},{6,8},{8,10},{10,12},{12,14},{14,0},{1,3},{3,5},... | collective-permute-start | bytes 786440 | tf_op jit(solution)/shard_map/ppermute | solution.py:197
  5.1 3.1 %collective-permute-start.1 = (bf16[16,2,8,512]{3,0,2,1:T(8,128)(2,1)S(1)}, bf16[16,2,8,512]{3,0,2,1:T(8,128)(2,1)S(1)}, u32[]{:S(2)}, u32[]{:S(2)}) collective-permute-start(bf16[16,2,8,512]{3,0,2,1:T(8,128)(2,1)S(1)} %get-tuple-element.22), channel_id=1, source_target_pairs={{2,0},{4,2},{6,4},{8,6},{10,8},{12,10},{14,12},{0,14},{3,1},{5,3},... | collective-permute-start | bytes 786440 | tf_op jit(solution)/shard_map/ppermute | solution.py:198
  8.2 0.1 collective-permute-start.3
  8.3 8.0 %collective-permute-done = bf16[16,2,8,512]{3,0,2,1:T(8,128)(2,1)S(1)} collective-permute-done((bf16[16,2,8,512]{3,0,2,1:T(8,128)(2,1)S(1)}, bf16[16,2,8,512]{3,0,2,1:T(8,128)(2,1)S(1)}, u32[]{:S(2)}, u32[]{:S(2)}) %collective-permute-start) | collective-permute-done | bytes 262176 | tf_op jit(solution)/shard_map/ppermute | solution.py:197
  16.2 2.2 %collective-permute-done.1 = bf16[16,2,8,512]{3,0,2,1:T(8,128)(2,1)S(1)} collective-permute-done((bf16[16,2,8,512]{3,0,2,1:T(8,128)(2,1)S(1)}, bf16[16,2,8,512]{3,0,2,1:T(8,128)(2,1)S(1)}, u32[]{:S(2)}, u32[]{:S(2)}) %collective-permute-start.1) | collective-permute-done | bytes 262176 | tf_op jit(solution)/shard_map/ppermute | solution.py:198
  18.5 0.0 copy-start.10
  18.6 0.0 copy-start.9
  18.6 0.1 collective-permute-start.2
  18.7 0.8 %copy-done.10 = bf16[32,2,4,256]{3,2,1,0:T(4,128)(2,1)S(1)} copy-done((bf16[32,2,4,256]{3,2,1,0:T(4,128)(2,1)S(1)}, bf16[32,2,4,256]{3,2,1,0:T(4,128)(2,1)}, u32[]{:S(2)}) %copy-start.10) | copy-done | bytes 131096
  19.4 0.1 collective-permute-start.5
  19.5 0.2 copy-done.9
  19.7 0.1 constant_dynamic-slice_fusion.2
  19.8 0.2 copy-done.8
  20.1 0.1 copy.23
  20.2 0.1 copy.18
  20.3 0.7 %reshape.48.refs_5_ = bf16[48,288]{1,0:T(8,128)(2,1)} reshape(bf16[3,16,3,3,32]{4,3,2,1,0:T(4,128)(2,1)S(1)} %copy.18) | data formatting | bytes 55296 | tf_op jit(solution)/shard_map/reshape | solution.py:207
  21.1 0.1 copy-done.7
  21.1 1.1 %copy.28 = bf16[16,4,8,512]{3,0,2,1:T(8,128)(2,1)} copy(bf16[16,4,8,512]{3,2,1,0:T(8,128)(2,1)S(1)} %copy-done.7) | data formatting | bytes 1048576 | tf_op args[1]
  22.2 0.0 collective-permute-done.2.refs_2_
  22.2 0.8 %copy-done.3 = bf16[4,2,4,16,512]{4,3,2,1,0:T(8,128)(2,1)} copy-done((bf16[4,2,4,16,512]{4,3,2,1,0:T(8,128)(2,1)}, bf16[4,2,4,16,512]{4,3,2,1,0:T(8,128)(2,1)S(1)}, u32[]{:S(2)}) %copy-start.3) | copy-done | bytes 524312
  23.0 0.2 copy-done.4
  23.2 5.7 %shard_map.76 = (bf16[1,8,16,512]{3,2,1,0:T(8,128)(2,1)}, f32[288,48]{1,0:T(8,128)}) custom-call(bf16[4,2,4,16,512]{4,3,2,1,0:T(8,128)(2,1)} %bitcast.31, bf16[4,2,4,16,512]{4,3,2,1,0:T(8,128)(2,1)} %bitcast.28, bf16[4,2,4,16,512]{4,3,2,1,0:T(8,128)(2,1)} %copy-done.4, bf16[4,2,4,16,512]{4,3,2,1,0:T(8,128)(2,1)} %copy-done.3, ...), custom_call_target="tpu_custom_call" | custom-call | tf_op jit(solution)/shard_map/pallas_call | solution.py:214
  28.9 0.3 collective-permute-start.4
  29.2 0.8 %copy.20.u_ref = bf16[3,64,144]{2,1,0:T(8,128)(2,1)} copy(bf16[3,64,144]{1,2,0:T(8,128)(2,1)S(1)} %bitcast.38) | data formatting | bytes 110592 | tf_op jit(solution)/shard_map/reshape | solution.py:245
  30.0 11.1 %shard_map.77 = (bf16[3,8,16,512]{3,2,1,0:T(8,128)(2,1)}, f32[288,48]{1,0:T(8,128)}, f32[27,32,16]{2,1,0:T(8,128)}) custom-call(bf16[4,2,4,16,512]{4,3,2,1,0:T(8,128)(2,1)} %bitcast.32, bf16[4,2,4,16,512]{4,3,2,1,0:T(8,128)(2,1)} %bitcast.29, bf16[4,2,4,16,512]{4,3,2,1,0:T(8,128)(2,1)} %copy-done.4, bf16[4,2,4,16,512]{4,3,2,1,0:T(8,128)(2,1)} %copy-done.3, ...), custom_call_target="tpu_custom_call" | custom-call | tf_op jit(solution)/shard_map/pallas_call | solution.py:214
  41.1 1.2 %reshape.53 = f32[13824]{0:T(1024)S(1)} reshape(f32[27,32,16]{2,1,0:T(8,128)} %get-tuple-element.14) | data formatting | bytes 110592 | tf_op jit(solution)/shard_map/reshape | solution.py:264
  42.3 0.0 copy-start.12
  42.3 0.6 copy-done.11
  43.0 0.0 copy-done.12
  43.0 4.8 %shard_map.78 = (f32[2,4,64,256]{3,2,1,0:T(8,128)}, f32[3,144,64]{2,1,0:T(8,128)}) custom-call(bf16[3,128,512]{2,1,0:T(8,128)(2,1)} %bitcast.40, bf16[1,128,512]{2,1,0:T(8,128)(2,1)} %bitcast.42, bf16[1,128,512]{2,1,0:T(8,128)(2,1)} %copy-done.12, bf16[2,4,32,256]{3,2,1,0:T(8,128)(2,1)} %bitcast.37, bf16[2,4,32,256]{3,2,1,0:T(8,128)(2,1)} %copy-done.11, ...), custom_call_target="tpu_custom_call" | custom-call | tf_op jit(solution)/shard_map/pallas_call | solution.py:247
  47.8 1.1 %reshape_reshape.3 = f32[27648]{0:T(1024)S(1)} reshape(f32[3,144,64]{2,1,0:T(8,128)} %get-tuple-element.13) | data formatting | bytes 221184 | tf_op jit(solution)/shard_map/reshape;reshape | solution.py:264
  48.9 2.5 %collective-permute-start.7 = (f32[41472]{0:T(1024)S(1)}, f32[41472]{0:T(1024)S(1)}, u32[]{:S(2)}, u32[]{:S(2)}) collective-permute-start(f32[41472]{0:T(1024)S(1)} %constant_dynamic-update-slice_fusion), channel_id=1, source_target_pairs={{0,2},{2,0},{4,6},{6,4},{8,10},{10,8},{12,14},{14,12},{1,3},{3,1},... | collective-permute-start | bytes 497672 | tf_op jit(solution)/shard_map/ppermute | solution.py:40
  51.4 0.1 collective-permute-start.6
  51.5 4.2 %collective-permute-done.7 = f32[41472]{0:T(1024)S(1)} collective-permute-done((f32[41472]{0:T(1024)S(1)}, f32[41472]{0:T(1024)S(1)}, u32[]{:S(2)}, u32[]{:S(2)}) %collective-permute-start.7) | collective-permute-done | bytes 165920 | tf_op jit(solution)/shard_map/ppermute | solution.py:40
  55.7 1.6 %collective-permute-start.8 = (f32[41472]{0:T(1024)S(1)}, f32[41472]{0:T(1024)S(1)}, u32[]{:S(2)}, u32[]{:S(2)}) collective-permute-start(f32[41472]{0:T(1024)S(1)} %add.27), channel_id=1, source_target_pairs={{0,4},{2,6},{4,0},{6,2},{8,12},{10,14},{12,8},{14,10},{1,5},{3,7},... | collective-permute-start | bytes 497672 | tf_op jit(solution)/shard_map/ppermute | solution.py:40
  57.4 3.9 %collective-permute-done.8 = f32[41472]{0:T(1024)S(1)} collective-permute-done((f32[41472]{0:T(1024)S(1)}, f32[41472]{0:T(1024)S(1)}, u32[]{:S(2)}, u32[]{:S(2)}) %collective-permute-start.8) | collective-permute-done | bytes 165920 | tf_op jit(solution)/shard_map/ppermute | solution.py:40
  61.3 2.7 %collective-permute-start.9 = (f32[41472]{0:T(1024)S(1)}, f32[41472]{0:T(1024)S(1)}, u32[]{:S(2)}, u32[]{:S(2)}) collective-permute-start(f32[41472]{0:T(1024)S(1)} %add.28), channel_id=1, source_target_pairs={{0,8},{2,10},{4,12},{6,14},{8,0},{10,2},{12,4},{14,6},{1,9},{3,11}... | collective-permute-start | bytes 497672 | tf_op jit(solution)/shard_map/ppermute | solution.py:40
  64.0 0.8 %copy.21 = bf16[32,2,4,256]{3,2,1,0:T(4,128)(2,1)} copy(bf16[32,2,4,256]{3,0,2,1:T(8,128)(2,1)S(1)} %fusion) | data formatting | bytes 262144
  64.7 5.6 %collective-permute-done.9 = f32[41472]{0:T(1024)S(1)} collective-permute-done((f32[41472]{0:T(1024)S(1)}, f32[41472]{0:T(1024)S(1)}, u32[]{:S(2)}, u32[]{:S(2)}) %collective-permute-start.9) | collective-permute-done | bytes 165920 | tf_op jit(solution)/shard_map/ppermute | solution.py:40
  70.4 0.0 copy-start.5
  70.4 0.6 copy-done.5
  71.1 0.2 slice.26
  71.2 0.0 slice-start
  71.2 0.9 %copy.22 = f32[27,32,16]{1,2,0:T(8,128)} copy(f32[27,32,16]{2,1,0:T(8,128)S(1)} %slice.26) | data formatting | bytes 110592
  72.1 0.0 slice-done
  72.1 0.8 %reshape.54 = f32[27,16,64]{2,1,0:T(8,128)} reshape(f32[27648]{0:T(1024)S(1)} %slice-done) | data formatting | bytes 221184 | tf_op jit(solution)/shard_map/reshape | solution.py:266
  (31 shorter events, 0.4 us)
Async XLA Ops:
  0.6 28.6 %copy-start = (bf16[27,32,64]{2,1,0:T(8,128)(2,1)S(1)}, bf16[27,32,64]{2,1,0:T(8,128)(2,1)}, u32[]{:S(2)}) copy-start(bf16[27,32,64]{2,1,0:T(8,128)(2,1)} %param.8) | copy-start | bytes 331780
  2.1 14.2 %collective-permute-start = (bf16[16,2,8,512]{3,0,2,1:T(8,128)(2,1)S(1)}, bf16[16,2,8,512]{3,0,2,1:T(8,128)(2,1)S(1)}, u32[]{:S(2)}, u32[]{:S(2)}) collective-permute-start(bf16[16,2,8,512]{3,0,2,1:T(8,128)(2,1)S(1)} %get-tuple-element.21), channel_id=1, source_target_pairs={{0,2},{2,4},{4,6},{6,8},{8,10},{10,12},{12,14},{14,0},{1,3},{3,5},... | collective-permute-start | bytes 786440 | tf_op jit(solution)/shard_map/ppermute | solution.py:197
  5.1 13.4 %collective-permute-start.1 = (bf16[16,2,8,512]{3,0,2,1:T(8,128)(2,1)S(1)}, bf16[16,2,8,512]{3,0,2,1:T(8,128)(2,1)S(1)}, u32[]{:S(2)}, u32[]{:S(2)}) collective-permute-start(bf16[16,2,8,512]{3,0,2,1:T(8,128)(2,1)S(1)} %get-tuple-element.22), channel_id=1, source_target_pairs={{2,0},{4,2},{6,4},{8,6},{10,8},{12,10},{14,12},{0,14},{3,1},{5,3},... | collective-permute-start | bytes 786440 | tf_op jit(solution)/shard_map/ppermute | solution.py:198
  8.2 10.3 %copy-start.1 = (bf16[16,4,4,2,512]{4,0,2,3,1:T(8,128)(2,1)}, bf16[16,4,4,2,512]{4,0,2,3,1:T(8,128)(2,1)S(1)}, u32[]{:S(2)}) copy-start(bf16[16,4,4,2,512]{4,0,2,3,1:T(8,128)(2,1)S(1)} %copy.29) | copy-start | bytes 1572868
  8.2 14.0 %collective-permute-start.3 = (bf16[4,2,4,16,512]{4,3,2,1,0:T(8,128)(2,1)S(1)}, bf16[4,2,4,16,512]{4,3,2,1,0:T(8,128)(2,1)S(1)}, u32[]{:S(2)}, u32[]{:S(2)}) collective-permute-start(bf16[4,2,4,16,512]{4,3,2,1,0:T(8,128)(2,1)S(1)} %bitcast.27), channel_id=1, source_target_pairs={{0,1},{1,0},{2,3},{3,2},{4,5},{5,4},{6,7},{7,6},{8,9},{9,8},{10,11... | collective-permute-start | bytes 1572872 | tf_op jit(solution)/shard_map/ppermute | solution.py:200
  18.5 0.9 %copy-start.10 = (bf16[32,2,4,256]{3,2,1,0:T(4,128)(2,1)S(1)}, bf16[32,2,4,256]{3,2,1,0:T(4,128)(2,1)}, u32[]{:S(2)}) copy-start(bf16[32,2,4,256]{3,2,1,0:T(4,128)(2,1)} %param.5) | copy-start | bytes 393220
  18.6 1.7 %copy-start.2 = (bf16[16,4,4,2,512]{4,0,2,3,1:T(8,128)(2,1)}, bf16[16,4,4,2,512]{4,0,2,3,1:T(8,128)(2,1)S(1)}, u32[]{:S(2)}) copy-start(bf16[16,4,4,2,512]{4,0,2,3,1:T(8,128)(2,1)S(1)} %copy.30) | copy-start | bytes 1572868
  18.6 1.1 %copy-start.9 = (bf16[27,32,32]{2,1,0:T(8,128)(2,1)S(1)}, bf16[27,32,32]{2,1,0:T(8,128)(2,1)}, u32[]{:S(2)}) copy-start(bf16[27,32,32]{2,1,0:T(8,128)(2,1)} %param.9) | copy-start | bytes 165892
  18.6 3.6 %collective-permute-start.2 = (bf16[4,2,4,16,512]{4,3,2,1,0:T(8,128)(2,1)S(1)}, bf16[4,2,4,16,512]{4,3,2,1,0:T(8,128)(2,1)S(1)}, u32[]{:S(2)}, u32[]{:S(2)}) collective-permute-start(bf16[4,2,4,16,512]{4,3,2,1,0:T(8,128)(2,1)S(1)} %bitcast.30), channel_id=1, source_target_pairs={{0,1},{1,0},{2,3},{3,2},{4,5},{5,4},{6,7},{7,6},{8,9},{9,8},{10,11... | collective-permute-start | bytes 1572872 | tf_op jit(solution)/shard_map/ppermute | solution.py:201
  19.4 0.6 copy-start.8
  19.4 22.8 %collective-permute-start.5 = (bf16[2,4,32,256]{3,2,1,0:T(8,128)(2,1)S(1)}, bf16[2,4,32,256]{3,2,1,0:T(8,128)(2,1)S(1)}, u32[]{:S(2)}, u32[]{:S(2)}) collective-permute-start(bf16[2,4,32,256]{3,2,1,0:T(8,128)(2,1)S(1)} %bitcast.36), channel_id=1, source_target_pairs={{0,1},{1,0},{2,3},{3,2},{4,5},{5,4},{6,7},{7,6},{8,9},{9,8},{10,11... | collective-permute-start | bytes 393224 | tf_op jit(solution)/shard_map/ppermute | solution.py:238
  20.1 1.0 %copy-start.7 = (bf16[16,4,8,512]{3,2,1,0:T(8,128)(2,1)S(1)}, bf16[16,4,8,512]{3,2,1,0:T(8,128)(2,1)}, u32[]{:S(2)}) copy-start(bf16[16,4,8,512]{3,2,1,0:T(8,128)(2,1)} %param.6) | copy-start | bytes 1572868
  22.2 0.8 %copy-start.3 = (bf16[4,2,4,16,512]{4,3,2,1,0:T(8,128)(2,1)}, bf16[4,2,4,16,512]{4,3,2,1,0:T(8,128)(2,1)S(1)}, u32[]{:S(2)}) copy-start(bf16[4,2,4,16,512]{4,3,2,1,0:T(8,128)(2,1)S(1)} %collective-permute-done.3.refs_3_) | copy-start | bytes 1572868
  22.2 1.0 %copy-start.4 = (bf16[4,2,4,16,512]{4,3,2,1,0:T(8,128)(2,1)}, bf16[4,2,4,16,512]{4,3,2,1,0:T(8,128)(2,1)S(1)}, u32[]{:S(2)}) copy-start(bf16[4,2,4,16,512]{4,3,2,1,0:T(8,128)(2,1)S(1)} %collective-permute-done.2.refs_2_) | copy-start | bytes 1572868
  28.9 13.4 %collective-permute-start.4 = (bf16[1,128,512]{2,1,0:T(8,128)(2,1)}, bf16[1,128,512]{2,1,0:T(8,128)(2,1)S(1)}, u32[]{:S(2)}, u32[]{:S(2)}) collective-permute-start(bf16[1,128,512]{2,1,0:T(8,128)(2,1)} %bitcast.41), channel_id=1, source_target_pairs={{14,0},{0,2},{2,4},{4,6},{6,8},{8,10},{10,12},{12,14},{15,1},{1,3}... | collective-permute-start | bytes 393224 | tf_op jit(solution)/shard_map/ppermute | solution.py:30
  42.3 0.7 copy-start.11
  42.3 0.7 copy-start.12
  47.8 3.6 %copy-start.6 = (f32[2,4,64,256]{3,2,1,0:T(8,128)S(1)}, f32[2,4,64,256]{3,2,1,0:T(8,128)}, u32[]{:S(2)}) copy-start(f32[2,4,64,256]{3,2,1,0:T(8,128)} %get-tuple-element.12) | copy-start | bytes 1572868
  48.9 6.8 %collective-permute-start.7 = (f32[41472]{0:T(1024)S(1)}, f32[41472]{0:T(1024)S(1)}, u32[]{:S(2)}, u32[]{:S(2)}) collective-permute-start(f32[41472]{0:T(1024)S(1)} %constant_dynamic-update-slice_fusion), channel_id=1, source_target_pairs={{0,2},{2,0},{4,6},{6,4},{8,10},{10,8},{12,14},{14,12},{1,3},{3,1},... | collective-permute-start | bytes 497672 | tf_op jit(solution)/shard_map/ppermute | solution.py:40
  51.4 12.5 %collective-permute-start.6 = (f32[2,4,32,256]{3,2,1,0:T(8,128)S(1)}, f32[2,4,32,256]{3,2,1,0:T(8,128)S(1)}, u32[]{:S(2)}, u32[]{:S(2)}) collective-permute-start(f32[2,4,32,256]{3,2,1,0:T(8,128)S(1)} %constant_dynamic-slice_fusion), channel_id=1, source_target_pairs={{0,1},{1,0},{2,3},{3,2},{4,5},{5,4},{6,7},{7,6},{8,9},{9,8},{10,11... | collective-permute-start | bytes 786440 | tf_op jit(solution)/shard_map/ppermute | solution.py:261
  55.7 5.5 %collective-permute-start.8 = (f32[41472]{0:T(1024)S(1)}, f32[41472]{0:T(1024)S(1)}, u32[]{:S(2)}, u32[]{:S(2)}) collective-permute-start(f32[41472]{0:T(1024)S(1)} %add.27), channel_id=1, source_target_pairs={{0,4},{2,6},{4,0},{6,2},{8,12},{10,14},{12,8},{14,10},{1,5},{3,7},... | collective-permute-start | bytes 497672 | tf_op jit(solution)/shard_map/ppermute | solution.py:40
  61.3 9.1 %collective-permute-start.9 = (f32[41472]{0:T(1024)S(1)}, f32[41472]{0:T(1024)S(1)}, u32[]{:S(2)}, u32[]{:S(2)}) collective-permute-start(f32[41472]{0:T(1024)S(1)} %add.28), channel_id=1, source_target_pairs={{0,8},{2,10},{4,12},{6,14},{8,0},{10,2},{12,4},{14,6},{1,9},{3,11}... | collective-permute-start | bytes 497672 | tf_op jit(solution)/shard_map/ppermute | solution.py:40
  70.4 0.7 copy-start.5
  71.2 0.9 %slice-start = ((f32[41472]{0:T(1024)}), f32[27648]{0:T(1024)S(1)}, s32[]{:S(2)}) async-start(f32[41472]{0:T(1024)} %copy-done.5), calls=%async_computation | async-start | bytes 221184 | tf_op jit(solution)/shard_map/slice | solution.py:266

commit v17 on v16

--- a/solution.py
+++ b/solution.py
@@ -40,6 +40,28 @@
         block = block + lax.ppermute(block, axis, route)
         step *= 2
     return block
+
+
+def summed_into(block, axis, shapes):
+    count = lax.axis_size(axis)
+    if count & (count - 1) or count < 2:
+        block = summed_over_slabs(block, axis)
+        other = jnp.zeros_like(block)
+    else:
+        step = 1
+        while step < count // 2:
+            route = [(i, i ^ step) for i in range(count)]
+            block = block + lax.ppermute(block, axis, route)
+            step *= 2
+        other = lax.ppermute(block, axis, [(i, i ^ step) for i in range(count)])
+    parts, at = [], 0
+    for shape in shapes:
+        size = 1
+        for extent in shape:
+            size *= extent
+        parts.append(block[at : at + size].reshape(shape) + other[at : at + size].reshape(shape))
+        at += size
+    return parts
 
 
 def vmem_specs(count):
@@ -262,9 +284,7 @@
     coarse_summed = lax.dynamic_slice_in_dim(coarse_acc, coarse_start, own_k, 2) + received
     grad_coarse = jnp.transpose(coarse_summed, (2, 0, 1, 3)).astype(jnp.bfloat16)
     flat = jnp.concatenate([up_terms.reshape(-1), refine_terms.reshape(-1)])
-    flat = summed_over_slabs(flat, ("gz", "sec"))
-    grad_up = flat[: up_terms.size].reshape(up_terms.shape)
-    grad_refine = flat[up_terms.size :].reshape(refine_terms.shape)
+    grad_up, grad_refine = summed_into(flat, ("gz", "sec"), (up_terms.shape, refine_terms.shape))
     return (grad_coarse, grad_up, grad_refine)
 
 

time: 73.4 us -> 72.7 us (level)
    add x0 -> x2, local copies, waits for them, and re-layouts: none -> 0.96 us  [summed_into(): block[at:at + size].reshape(shape) + other[at:at + size].reshape(shape)]
    reshape x1 -> x0, local copies, waits for them, and re-layouts: 0.79 us -> none  [local(): grad_up = flat[:up_terms.size].reshape(up_terms.shape)]
    unnamed x33 -> x31, local copies, waits for them, and re-layouts: 7.82 us -> 7.18 us
where the time goes in v17:
time: 72.7 us; the launch traced here: 72.2 us
  waiting for transfers between devices  23.8 us (33%)
  Pallas kernels  21.6 us (30%)
  starting transfers between devices  13.5 us (19%)
  local copies, waits for them, and re-layouts  12.2 us (17%)
  between operations  0.91 us (1%)
    pallas_call x2, Pallas kernels, fine_rows(): pl.pallas_call(functools.partial(fine_kernel, z_lo, z_hi, scale), out_sha...  16.8 us
    ppermute x2, waiting for transfers between devices, summed_into(): block = block + lax.ppermute(block, axis, route)  8 us
    ppermute x1, waiting for transfers between devices, local(): low_raw = lax.ppermute(out_grad[:, planes_z - 2:], ('gz', 'sec'), forward)  7.95 us
    unnamed x31, local copies, waits for them, and re-layouts  7.18 us
    ppermute x1, waiting for transfers between devices, summed_into(): other = lax.ppermute(block, axis, [(i, i ^ step) for i in range(count)])  5.6 us
    pallas_call x1, Pallas kernels, local(): pl.pallas_call(functools.partial(coarse_kernel, float(coarse_total) ** (-...  4.8 us
    ppermute x2, starting transfers between devices, summed_into(): block = block + lax.ppermute(block, axis, route)  4.15 us
    ppermute x1, starting transfers between devices, local(): high_raw = lax.ppermute(out_grad[:, :2], ('gz', 'sec'), backward)  3.1 us
  transfers between devices with their start and end apart: 10, of which 5 were waited for; matrix products, arithmetic and copies ran while one was open for 7% of the time, Pallas kernels for 23%

profile of v17, /device:TPU:0, one launch (start us, length us, event | category | flops | bytes accessed | tf_op | source)
XLA Modules:
  0.0 72.2 jit_solution(15278886080154575934)
XLA Ops:
  0.6 0.0 copy-start
  0.6 1.4 %copy.11 = bf16[16,4,8,512]{3,0,2,1:T(8,128)(2,1)S(1)} copy(bf16[16,4,8,512]{3,2,1,0:T(8,128)(2,1)} %param.7) | data formatting | bytes 1048576 | tf_op args[2]
  2.1 3.0 %collective-permute-start = (bf16[16,2,8,512]{3,0,2,1:T(8,128)(2,1)S(1)}, bf16[16,2,8,512]{3,0,2,1:T(8,128)(2,1)S(1)}, u32[]{:S(2)}, u32[]{:S(2)}) collective-permute-start(bf16[16,2,8,512]{3,0,2,1:T(8,128)(2,1)S(1)} %get-tuple-element.21), channel_id=1, source_target_pairs={{0,2},{2,4},{4,6},{6,8},{8,10},{10,12},{12,14},{14,0},{1,3},{3,5},... | collective-permute-start | bytes 786440 | tf_op jit(solution)/shard_map/ppermute | solution.py:219
  5.1 3.1 %collective-permute-start.1 = (bf16[16,2,8,512]{3,0,2,1:T(8,128)(2,1)S(1)}, bf16[16,2,8,512]{3,0,2,1:T(8,128)(2,1)S(1)}, u32[]{:S(2)}, u32[]{:S(2)}) collective-permute-start(bf16[16,2,8,512]{3,0,2,1:T(8,128)(2,1)S(1)} %get-tuple-element.22), channel_id=1, source_target_pairs={{2,0},{4,2},{6,4},{8,6},{10,8},{12,10},{14,12},{0,14},{3,1},{5,3},... | collective-permute-start | bytes 786440 | tf_op jit(solution)/shard_map/ppermute | solution.py:220
  8.2 0.1 collective-permute-start.3
  8.3 8.0 %collective-permute-done = bf16[16,2,8,512]{3,0,2,1:T(8,128)(2,1)S(1)} collective-permute-done((bf16[16,2,8,512]{3,0,2,1:T(8,128)(2,1)S(1)}, bf16[16,2,8,512]{3,0,2,1:T(8,128)(2,1)S(1)}, u32[]{:S(2)}, u32[]{:S(2)}) %collective-permute-start) | collective-permute-done | bytes 262176 | tf_op jit(solution)/shard_map/ppermute | solution.py:219
  16.2 2.2 %collective-permute-done.1 = bf16[16,2,8,512]{3,0,2,1:T(8,128)(2,1)S(1)} collective-permute-done((bf16[16,2,8,512]{3,0,2,1:T(8,128)(2,1)S(1)}, bf16[16,2,8,512]{3,0,2,1:T(8,128)(2,1)S(1)}, u32[]{:S(2)}, u32[]{:S(2)}) %collective-permute-start.1) | collective-permute-done | bytes 262176 | tf_op jit(solution)/shard_map/ppermute | solution.py:220
  18.5 0.0 copy-start.9
  18.6 0.0 copy-start.8
  18.6 0.1 collective-permute-start.2
  18.7 0.8 %copy-done.9 = bf16[32,2,4,256]{3,2,1,0:T(4,128)(2,1)S(1)} copy-done((bf16[32,2,4,256]{3,2,1,0:T(4,128)(2,1)S(1)}, bf16[32,2,4,256]{3,2,1,0:T(4,128)(2,1)}, u32[]{:S(2)}) %copy-start.9) | copy-done | bytes 131096
  19.4 0.1 collective-permute-start.5
  19.5 0.2 copy-done.8
  19.7 0.1 constant_dynamic-slice_fusion.2
  19.8 0.2 copy-done.7
  20.1 0.1 copy.23
  20.3 0.1 copy.18
  20.3 0.7 %reshape.58.refs_5_ = bf16[48,288]{1,0:T(8,128)(2,1)} reshape(bf16[3,16,3,3,32]{4,3,2,1,0:T(4,128)(2,1)S(1)} %copy.18) | data formatting | bytes 55296 | tf_op jit(solution)/shard_map/reshape | solution.py:229
  21.1 0.1 copy-done.6
  21.1 1.1 %copy.28 = bf16[16,4,8,512]{3,0,2,1:T(8,128)(2,1)} copy(bf16[16,4,8,512]{3,2,1,0:T(8,128)(2,1)S(1)} %copy-done.6) | data formatting | bytes 1048576 | tf_op args[1]
  22.2 0.0 collective-permute-done.3.refs_3_
  22.2 0.0 collective-permute-done.2.refs_2_
  22.2 0.8 %copy-done.3 = bf16[4,2,4,16,512]{4,3,2,1,0:T(8,128)(2,1)} copy-done((bf16[4,2,4,16,512]{4,3,2,1,0:T(8,128)(2,1)}, bf16[4,2,4,16,512]{4,3,2,1,0:T(8,128)(2,1)S(1)}, u32[]{:S(2)}) %copy-start.3) | copy-done | bytes 524312
  23.0 0.2 copy-done.4
  23.2 5.7 %shard_map.76 = (bf16[1,8,16,512]{3,2,1,0:T(8,128)(2,1)}, f32[288,48]{1,0:T(8,128)}) custom-call(bf16[4,2,4,16,512]{4,3,2,1,0:T(8,128)(2,1)} %bitcast.31, bf16[4,2,4,16,512]{4,3,2,1,0:T(8,128)(2,1)} %bitcast.28, bf16[4,2,4,16,512]{4,3,2,1,0:T(8,128)(2,1)} %copy-done.4, bf16[4,2,4,16,512]{4,3,2,1,0:T(8,128)(2,1)} %copy-done.3, ...), custom_call_target="tpu_custom_call" | custom-call | tf_op jit(solution)/shard_map/pallas_call | solution.py:236
  28.9 0.3 collective-permute-start.4
  29.2 0.8 %copy.20.u_ref = bf16[3,64,144]{2,1,0:T(8,128)(2,1)} copy(bf16[3,64,144]{1,2,0:T(8,128)(2,1)S(1)} %bitcast.38) | data formatting | bytes 110592 | tf_op jit(solution)/shard_map/reshape | solution.py:267
  30.0 11.1 %shard_map.77 = (bf16[3,8,16,512]{3,2,1,0:T(8,128)(2,1)}, f32[288,48]{1,0:T(8,128)}, f32[27,32,16]{2,1,0:T(8,128)}) custom-call(bf16[4,2,4,16,512]{4,3,2,1,0:T(8,128)(2,1)} %bitcast.32, bf16[4,2,4,16,512]{4,3,2,1,0:T(8,128)(2,1)} %bitcast.29, bf16[4,2,4,16,512]{4,3,2,1,0:T(8,128)(2,1)} %copy-done.4, bf16[4,2,4,16,512]{4,3,2,1,0:T(8,128)(2,1)} %copy-done.3, ...), custom_call_target="tpu_custom_call" | custom-call | tf_op jit(solution)/shard_map/pallas_call | solution.py:236
  41.1 1.2 %reshape.63 = f32[13824]{0:T(1024)S(1)} reshape(f32[27,32,16]{2,1,0:T(8,128)} %get-tuple-element.14) | data formatting | bytes 110592 | tf_op jit(solution)/shard_map/reshape | solution.py:286
  42.3 0.0 collective-permute-done.5.other_ref
  42.3 0.0 collective-permute-done.4.below_ref
  42.3 0.0 copy-start.11
  42.4 0.6 copy-done.10
  43.0 0.0 copy-done.11
  43.0 4.8 %shard_map.78 = (f32[2,4,64,256]{3,2,1,0:T(8,128)}, f32[3,144,64]{2,1,0:T(8,128)}) custom-call(bf16[3,128,512]{2,1,0:T(8,128)(2,1)} %bitcast.40, bf16[1,128,512]{2,1,0:T(8,128)(2,1)} %bitcast.42, bf16[1,128,512]{2,1,0:T(8,128)(2,1)} %copy-done.11, bf16[2,4,32,256]{3,2,1,0:T(8,128)(2,1)} %bitcast.37, bf16[2,4,32,256]{3,2,1,0:T(8,128)(2,1)} %copy-done.10, ...), custom_call_target="tpu_custom_call" | custom-call | tf_op jit(solution)/shard_map/pallas_call | solution.py:269
  47.8 1.1 %reshape_reshape.3 = f32[27648]{0:T(1024)S(1)} reshape(f32[3,144,64]{2,1,0:T(8,128)} %get-tuple-element.13) | data formatting | bytes 221184 | tf_op jit(solution)/shard_map/reshape;reshape | solution.py:286
  48.9 2.5 %collective-permute-start.7 = (f32[41472]{0:T(1024)S(1)}, f32[41472]{0:T(1024)S(1)}, u32[]{:S(2)}, u32[]{:S(2)}) collective-permute-start(f32[41472]{0:T(1024)S(1)} %constant_dynamic-update-slice_fusion), channel_id=1, source_target_pairs={{0,2},{2,0},{4,6},{6,4},{8,10},{10,8},{12,14},{14,12},{1,3},{3,1},... | collective-permute-start | bytes 497672 | tf_op jit(solution)/shard_map/ppermute | solution.py:54
  51.5 0.1 collective-permute-start.6
  51.6 4.2 %collective-permute-done.7 = f32[41472]{0:T(1024)S(1)} collective-permute-done((f32[41472]{0:T(1024)S(1)}, f32[41472]{0:T(1024)S(1)}, u32[]{:S(2)}, u32[]{:S(2)}) %collective-permute-start.7) | collective-permute-done | bytes 165920 | tf_op jit(solution)/shard_map/ppermute | solution.py:54
  55.7 1.7 %collective-permute-start.8 = (f32[41472]{0:T(1024)S(1)}, f32[41472]{0:T(1024)S(1)}, u32[]{:S(2)}, u32[]{:S(2)}) collective-permute-start(f32[41472]{0:T(1024)S(1)} %add.36), channel_id=1, source_target_pairs={{0,4},{2,6},{4,0},{6,2},{8,12},{10,14},{12,8},{14,10},{1,5},{3,7},... | collective-permute-start | bytes 497672 | tf_op jit(solution)/shard_map/ppermute | solution.py:54
  57.4 3.8 %collective-permute-done.8 = f32[41472]{0:T(1024)S(1)} collective-permute-done((f32[41472]{0:T(1024)S(1)}, f32[41472]{0:T(1024)S(1)}, u32[]{:S(2)}, u32[]{:S(2)}) %collective-permute-start.8) | collective-permute-done | bytes 165920 | tf_op jit(solution)/shard_map/ppermute | solution.py:54
  61.3 2.7 %collective-permute-start.9 = (f32[41472]{0:T(1024)S(1)}, f32[41472]{0:T(1024)S(1)}, u32[]{:S(2)}, u32[]{:S(2)}) collective-permute-start(f32[41472]{0:T(1024)S(1)} %add.37), channel_id=1, source_target_pairs={{0,8},{2,10},{4,12},{6,14},{8,0},{10,2},{12,4},{14,6},{1,9},{3,11}... | collective-permute-start | bytes 497672 | tf_op jit(solution)/shard_map/ppermute | solution.py:56
  63.9 0.0 collective-permute-done.6
  64.0 0.8 %copy.21 = bf16[32,2,4,256]{3,2,1,0:T(4,128)(2,1)} copy(bf16[32,2,4,256]{3,0,2,1:T(8,128)(2,1)S(1)} %fusion) | data formatting | bytes 262144
  64.7 5.6 %collective-permute-done.9 = f32[41472]{0:T(1024)S(1)} collective-permute-done((f32[41472]{0:T(1024)S(1)}, f32[41472]{0:T(1024)S(1)}, u32[]{:S(2)}, u32[]{:S(2)}) %collective-permute-start.9) | collective-permute-done | bytes 165920 | tf_op jit(solution)/shard_map/ppermute | solution.py:56
  70.3 0.2 add.41
  70.5 0.9 %copy.22 = f32[27,32,16]{1,2,0:T(8,128)} copy(f32[27,32,16]{2,1,0:T(8,128)S(1)} %add.41) | data formatting | bytes 110592
  71.4 0.8 %add.39 = f32[27,16,64]{2,1,0:T(8,128)} reshape(f32[27648]{0:T(1024)S(1)} %slice_add_fusion) | data formatting | bytes 221184 | tf_op jit(solution)/shard_map/add | solution.py:62
  (27 shorter events, 0.4 us)
Async XLA Ops:
  0.6 28.6 %copy-start = (bf16[27,32,64]{2,1,0:T(8,128)(2,1)S(1)}, bf16[27,32,64]{2,1,0:T(8,128)(2,1)}, u32[]{:S(2)}) copy-start(bf16[27,32,64]{2,1,0:T(8,128)(2,1)} %param.8) | copy-start | bytes 331780
  2.1 14.2 %collective-permute-start = (bf16[16,2,8,512]{3,0,2,1:T(8,128)(2,1)S(1)}, bf16[16,2,8,512]{3,0,2,1:T(8,128)(2,1)S(1)}, u32[]{:S(2)}, u32[]{:S(2)}) collective-permute-start(bf16[16,2,8,512]{3,0,2,1:T(8,128)(2,1)S(1)} %get-tuple-element.21), channel_id=1, source_target_pairs={{0,2},{2,4},{4,6},{6,8},{8,10},{10,12},{12,14},{14,0},{1,3},{3,5},... | collective-permute-start | bytes 786440 | tf_op jit(solution)/shard_map/ppermute | solution.py:219
  5.1 13.4 %collective-permute-start.1 = (bf16[16,2,8,512]{3,0,2,1:T(8,128)(2,1)S(1)}, bf16[16,2,8,512]{3,0,2,1:T(8,128)(2,1)S(1)}, u32[]{:S(2)}, u32[]{:S(2)}) collective-permute-start(bf16[16,2,8,512]{3,0,2,1:T(8,128)(2,1)S(1)} %get-tuple-element.22), channel_id=1, source_target_pairs={{2,0},{4,2},{6,4},{8,6},{10,8},{12,10},{14,12},{0,14},{3,1},{5,3},... | collective-permute-start | bytes 786440 | tf_op jit(solution)/shard_map/ppermute | solution.py:220
  8.2 10.3 %copy-start.1 = (bf16[16,4,4,2,512]{4,0,2,3,1:T(8,128)(2,1)}, bf16[16,4,4,2,512]{4,0,2,3,1:T(8,128)(2,1)S(1)}, u32[]{:S(2)}) copy-start(bf16[16,4,4,2,512]{4,0,2,3,1:T(8,128)(2,1)S(1)} %copy.29) | copy-start | bytes 1572868
  8.2 14.0 %collective-permute-start.3 = (bf16[4,2,4,16,512]{4,3,2,1,0:T(8,128)(2,1)S(1)}, bf16[4,2,4,16,512]{4,3,2,1,0:T(8,128)(2,1)S(1)}, u32[]{:S(2)}, u32[]{:S(2)}) collective-permute-start(bf16[4,2,4,16,512]{4,3,2,1,0:T(8,128)(2,1)S(1)} %bitcast.27), channel_id=1, source_target_pairs={{0,1},{1,0},{2,3},{3,2},{4,5},{5,4},{6,7},{7,6},{8,9},{9,8},{10,11... | collective-permute-start | bytes 1572872 | tf_op jit(solution)/shard_map/ppermute | solution.py:222
  18.5 0.9 %copy-start.9 = (bf16[32,2,4,256]{3,2,1,0:T(4,128)(2,1)S(1)}, bf16[32,2,4,256]{3,2,1,0:T(4,128)(2,1)}, u32[]{:S(2)}) copy-start(bf16[32,2,4,256]{3,2,1,0:T(4,128)(2,1)} %param.5) | copy-start | bytes 393220
  18.6 1.7 %copy-start.2 = (bf16[16,4,4,2,512]{4,0,2,3,1:T(8,128)(2,1)}, bf16[16,4,4,2,512]{4,0,2,3,1:T(8,128)(2,1)S(1)}, u32[]{:S(2)}) copy-start(bf16[16,4,4,2,512]{4,0,2,3,1:T(8,128)(2,1)S(1)} %copy.30) | copy-start | bytes 1572868
  18.6 1.1 %copy-start.8 = (bf16[27,32,32]{2,1,0:T(8,128)(2,1)S(1)}, bf16[27,32,32]{2,1,0:T(8,128)(2,1)}, u32[]{:S(2)}) copy-start(bf16[27,32,32]{2,1,0:T(8,128)(2,1)} %param.9) | copy-start | bytes 165892
  18.6 3.6 %collective-permute-start.2 = (bf16[4,2,4,16,512]{4,3,2,1,0:T(8,128)(2,1)S(1)}, bf16[4,2,4,16,512]{4,3,2,1,0:T(8,128)(2,1)S(1)}, u32[]{:S(2)}, u32[]{:S(2)}) collective-permute-start(bf16[4,2,4,16,512]{4,3,2,1,0:T(8,128)(2,1)S(1)} %bitcast.30), channel_id=1, source_target_pairs={{0,1},{1,0},{2,3},{3,2},{4,5},{5,4},{6,7},{7,6},{8,9},{9,8},{10,11... | collective-permute-start | bytes 1572872 | tf_op jit(solution)/shard_map/ppermute | solution.py:223
  19.4 0.6 copy-start.7
  19.4 22.9 %collective-permute-start.5 = (bf16[2,4,32,256]{3,2,1,0:T(8,128)(2,1)S(1)}, bf16[2,4,32,256]{3,2,1,0:T(8,128)(2,1)S(1)}, u32[]{:S(2)}, u32[]{:S(2)}) collective-permute-start(bf16[2,4,32,256]{3,2,1,0:T(8,128)(2,1)S(1)} %bitcast.36), channel_id=1, source_target_pairs={{0,1},{1,0},{2,3},{3,2},{4,5},{5,4},{6,7},{7,6},{8,9},{9,8},{10,11... | collective-permute-start | bytes 393224 | tf_op jit(solution)/shard_map/ppermute | solution.py:260
  20.1 1.0 %copy-start.6 = (bf16[16,4,8,512]{3,2,1,0:T(8,128)(2,1)S(1)}, bf16[16,4,8,512]{3,2,1,0:T(8,128)(2,1)}, u32[]{:S(2)}) copy-start(bf16[16,4,8,512]{3,2,1,0:T(8,128)(2,1)} %param.6) | copy-start | bytes 1572868
  22.2 0.8 %copy-start.3 = (bf16[4,2,4,16,512]{4,3,2,1,0:T(8,128)(2,1)}, bf16[4,2,4,16,512]{4,3,2,1,0:T(8,128)(2,1)S(1)}, u32[]{:S(2)}) copy-start(bf16[4,2,4,16,512]{4,3,2,1,0:T(8,128)(2,1)S(1)} %collective-permute-done.3.refs_3_) | copy-start | bytes 1572868
  22.2 1.0 %copy-start.4 = (bf16[4,2,4,16,512]{4,3,2,1,0:T(8,128)(2,1)}, bf16[4,2,4,16,512]{4,3,2,1,0:T(8,128)(2,1)S(1)}, u32[]{:S(2)}) copy-start(bf16[4,2,4,16,512]{4,3,2,1,0:T(8,128)(2,1)S(1)} %collective-permute-done.2.refs_2_) | copy-start | bytes 1572868
  28.9 13.5 %collective-permute-start.4 = (bf16[1,128,512]{2,1,0:T(8,128)(2,1)}, bf16[1,128,512]{2,1,0:T(8,128)(2,1)S(1)}, u32[]{:S(2)}, u32[]{:S(2)}) collective-permute-start(bf16[1,128,512]{2,1,0:T(8,128)(2,1)} %bitcast.41), channel_id=1, source_target_pairs={{14,0},{0,2},{2,4},{4,6},{6,8},{8,10},{10,12},{12,14},{15,1},{1,3}... | collective-permute-start | bytes 393224 | tf_op jit(solution)/shard_map/ppermute | solution.py:30
  42.3 0.7 copy-start.10
  42.3 0.7 copy-start.11
  47.8 3.6 %copy-start.5 = (f32[2,4,64,256]{3,2,1,0:T(8,128)S(1)}, f32[2,4,64,256]{3,2,1,0:T(8,128)}, u32[]{:S(2)}) copy-start(f32[2,4,64,256]{3,2,1,0:T(8,128)} %get-tuple-element.12) | copy-start | bytes 1572868
  48.9 6.8 %collective-permute-start.7 = (f32[41472]{0:T(1024)S(1)}, f32[41472]{0:T(1024)S(1)}, u32[]{:S(2)}, u32[]{:S(2)}) collective-permute-start(f32[41472]{0:T(1024)S(1)} %constant_dynamic-update-slice_fusion), channel_id=1, source_target_pairs={{0,2},{2,0},{4,6},{6,4},{8,10},{10,8},{12,14},{14,12},{1,3},{3,1},... | collective-permute-start | bytes 497672 | tf_op jit(solution)/shard_map/ppermute | solution.py:54
  51.5 12.5 %collective-permute-start.6 = (f32[2,4,32,256]{3,2,1,0:T(8,128)S(1)}, f32[2,4,32,256]{3,2,1,0:T(8,128)S(1)}, u32[]{:S(2)}, u32[]{:S(2)}) collective-permute-start(f32[2,4,32,256]{3,2,1,0:T(8,128)S(1)} %constant_dynamic-slice_fusion), channel_id=1, source_target_pairs={{0,1},{1,0},{2,3},{3,2},{4,5},{5,4},{6,7},{7,6},{8,9},{9,8},{10,11... | collective-permute-start | bytes 786440 | tf_op jit(solution)/shard_map/ppermute | solution.py:283
  55.7 5.5 %collective-permute-start.8 = (f32[41472]{0:T(1024)S(1)}, f32[41472]{0:T(1024)S(1)}, u32[]{:S(2)}, u32[]{:S(2)}) collective-permute-start(f32[41472]{0:T(1024)S(1)} %add.36), channel_id=1, source_target_pairs={{0,4},{2,6},{4,0},{6,2},{8,12},{10,14},{12,8},{14,10},{1,5},{3,7},... | collective-permute-start | bytes 497672 | tf_op jit(solution)/shard_map/ppermute | solution.py:54
  61.3 9.1 %collective-permute-start.9 = (f32[41472]{0:T(1024)S(1)}, f32[41472]{0:T(1024)S(1)}, u32[]{:S(2)}, u32[]{:S(2)}) collective-permute-start(f32[41472]{0:T(1024)S(1)} %add.37), channel_id=1, source_target_pairs={{0,8},{2,10},{4,12},{6,14},{8,0},{10,2},{12,4},{14,6},{1,9},{3,11}... | collective-permute-start | bytes 497672 | tf_op jit(solution)/shard_map/ppermute | solution.py:56

commit v18 on v17

--- a/solution.py
+++ b/solution.py
@@ -48,11 +48,11 @@
         block = summed_over_slabs(block, axis)
         other = jnp.zeros_like(block)
     else:
-        step = 1
-        while step < count // 2:
+        step = count // 2
+        while step > 1:
             route = [(i, i ^ step) for i in range(count)]
             block = block + lax.ppermute(block, axis, route)
-            step *= 2
+            step //= 2
         other = lax.ppermute(block, axis, [(i, i ^ step) for i in range(count)])
     parts, at = [], 0
     for shape in shapes:

time: 72.7 us -> 73.2 us (level)
  waiting for transfers between devices: 23.8 us -> 25.2 us
  starting transfers between devices: 13.5 us -> 12.5 us
    ppermute x2, waiting for transfers between devices: 8 us -> 12.5 us  [summed_into(): block = block + lax.ppermute(block, axis, route)]
    ppermute x1, waiting for transfers between devices: 5.6 us -> 2.54 us  [summed_into(): other = lax.ppermute(block, axis, [(i, i ^ step) for i in range(count)])]
    ppermute x2, starting transfers between devices: 4.15 us -> 3.37 us  [summed_into(): block = block + lax.ppermute(block, axis, route)]
where the time goes in v18:
time: 73.2 us; the launch traced here: 72.7 us
  waiting for transfers between devices  25.2 us (34%)
  Pallas kernels  21.6 us (30%)
  starting transfers between devices  12.5 us (17%)
  local copies, waits for them, and re-layouts  12.2 us (17%)
  between operations  0.91 us (1%)
    pallas_call x2, Pallas kernels, fine_rows(): pl.pallas_call(functools.partial(fine_kernel, z_lo, z_hi, scale), out_sha...  16.8 us
    ppermute x2, waiting for transfers between devices, summed_into(): block = block + lax.ppermute(block, axis, route)  12.5 us
    ppermute x1, waiting for transfers between devices, local(): low_raw = lax.ppermute(out_grad[:, planes_z - 2:], ('gz', 'sec'), forward)  7.95 us
    unnamed x31, local copies, waits for them, and re-layouts  7.18 us
    pallas_call x1, Pallas kernels, local(): pl.pallas_call(functools.partial(coarse_kernel, float(coarse_total) ** (-...  4.8 us
    ppermute x2, starting transfers between devices, summed_into(): block = block + lax.ppermute(block, axis, route)  3.37 us
    ppermute x1, starting transfers between devices, local(): high_raw = lax.ppermute(out_grad[:, :2], ('gz', 'sec'), backward)  3.1 us
    ppermute x1, starting transfers between devices, local(): low_raw = lax.ppermute(out_grad[:, planes_z - 2:], ('gz', 'sec'), forward)  2.99 us
  transfers between devices with their start and end apart: 10, of which 5 were waited for; matrix products, arithmetic and copies ran while one was open for 7% of the time, Pallas kernels for 23%

profile of v18, /device:TPU:0, one launch (start us, length us, event | category | flops | bytes accessed | tf_op | source)
XLA Modules:
  0.0 72.7 jit_solution(8847993709744650675)
XLA Ops:
  0.6 0.0 copy-start
  0.6 1.4 %copy.11 = bf16[16,4,8,512]{3,0,2,1:T(8,128)(2,1)S(1)} copy(bf16[16,4,8,512]{3,2,1,0:T(8,128)(2,1)} %param.7) | data formatting | bytes 1048576 | tf_op args[2]
  2.1 3.0 %collective-permute-start = (bf16[16,2,8,512]{3,0,2,1:T(8,128)(2,1)S(1)}, bf16[16,2,8,512]{3,0,2,1:T(8,128)(2,1)S(1)}, u32[]{:S(2)}, u32[]{:S(2)}) collective-permute-start(bf16[16,2,8,512]{3,0,2,1:T(8,128)(2,1)S(1)} %get-tuple-element.21), channel_id=1, source_target_pairs={{0,2},{2,4},{4,6},{6,8},{8,10},{10,12},{12,14},{14,0},{1,3},{3,5},... | collective-permute-start | bytes 786440 | tf_op jit(solution)/shard_map/ppermute | solution.py:219
  5.1 3.1 %collective-permute-start.1 = (bf16[16,2,8,512]{3,0,2,1:T(8,128)(2,1)S(1)}, bf16[16,2,8,512]{3,0,2,1:T(8,128)(2,1)S(1)}, u32[]{:S(2)}, u32[]{:S(2)}) collective-permute-start(bf16[16,2,8,512]{3,0,2,1:T(8,128)(2,1)S(1)} %get-tuple-element.22), channel_id=1, source_target_pairs={{2,0},{4,2},{6,4},{8,6},{10,8},{12,10},{14,12},{0,14},{3,1},{5,3},... | collective-permute-start | bytes 786440 | tf_op jit(solution)/shard_map/ppermute | solution.py:220
  8.2 0.1 collective-permute-start.3
  8.3 8.0 %collective-permute-done = bf16[16,2,8,512]{3,0,2,1:T(8,128)(2,1)S(1)} collective-permute-done((bf16[16,2,8,512]{3,0,2,1:T(8,128)(2,1)S(1)}, bf16[16,2,8,512]{3,0,2,1:T(8,128)(2,1)S(1)}, u32[]{:S(2)}, u32[]{:S(2)}) %collective-permute-start) | collective-permute-done | bytes 262176 | tf_op jit(solution)/shard_map/ppermute | solution.py:219
  16.2 2.2 %collective-permute-done.1 = bf16[16,2,8,512]{3,0,2,1:T(8,128)(2,1)S(1)} collective-permute-done((bf16[16,2,8,512]{3,0,2,1:T(8,128)(2,1)S(1)}, bf16[16,2,8,512]{3,0,2,1:T(8,128)(2,1)S(1)}, u32[]{:S(2)}, u32[]{:S(2)}) %collective-permute-start.1) | collective-permute-done | bytes 262176 | tf_op jit(solution)/shard_map/ppermute | solution.py:220
  18.5 0.0 copy-start.9
  18.6 0.0 copy-start.8
  18.6 0.1 collective-permute-start.2
  18.7 0.8 %copy-done.9 = bf16[32,2,4,256]{3,2,1,0:T(4,128)(2,1)S(1)} copy-done((bf16[32,2,4,256]{3,2,1,0:T(4,128)(2,1)S(1)}, bf16[32,2,4,256]{3,2,1,0:T(4,128)(2,1)}, u32[]{:S(2)}) %copy-start.9) | copy-done | bytes 131096
  19.4 0.1 collective-permute-start.5
  19.5 0.2 copy-done.8
  19.7 0.1 constant_dynamic-slice_fusion.2
  19.8 0.2 copy-done.7
  20.1 0.1 copy.23
  20.3 0.1 copy.18
  20.3 0.7 %reshape.58.refs_5_ = bf16[48,288]{1,0:T(8,128)(2,1)} reshape(bf16[3,16,3,3,32]{4,3,2,1,0:T(4,128)(2,1)S(1)} %copy.18) | data formatting | bytes 55296 | tf_op jit(solution)/shard_map/reshape | solution.py:229
  21.1 0.1 copy-done.6
  21.1 1.1 %copy.28 = bf16[16,4,8,512]{3,0,2,1:T(8,128)(2,1)} copy(bf16[16,4,8,512]{3,2,1,0:T(8,128)(2,1)S(1)} %copy-done.6) | data formatting | bytes 1048576 | tf_op args[1]
  22.2 0.0 collective-permute-done.3.refs_3_
  22.2 0.0 collective-permute-done.2.refs_2_
  22.2 0.8 %copy-done.3 = bf16[4,2,4,16,512]{4,3,2,1,0:T(8,128)(2,1)} copy-done((bf16[4,2,4,16,512]{4,3,2,1,0:T(8,128)(2,1)}, bf16[4,2,4,16,512]{4,3,2,1,0:T(8,128)(2,1)S(1)}, u32[]{:S(2)}) %copy-start.3) | copy-done | bytes 524312
  23.0 0.2 copy-done.4
  23.2 5.7 %shard_map.76 = (bf16[1,8,16,512]{3,2,1,0:T(8,128)(2,1)}, f32[288,48]{1,0:T(8,128)}) custom-call(bf16[4,2,4,16,512]{4,3,2,1,0:T(8,128)(2,1)} %bitcast.31, bf16[4,2,4,16,512]{4,3,2,1,0:T(8,128)(2,1)} %bitcast.28, bf16[4,2,4,16,512]{4,3,2,1,0:T(8,128)(2,1)} %copy-done.4, bf16[4,2,4,16,512]{4,3,2,1,0:T(8,128)(2,1)} %copy-done.3, ...), custom_call_target="tpu_custom_call" | custom-call | tf_op jit(solution)/shard_map/pallas_call | solution.py:236
  28.9 0.3 collective-permute-start.4
  29.2 0.8 %copy.20.u_ref = bf16[3,64,144]{2,1,0:T(8,128)(2,1)} copy(bf16[3,64,144]{1,2,0:T(8,128)(2,1)S(1)} %bitcast.38) | data formatting | bytes 110592 | tf_op jit(solution)/shard_map/reshape | solution.py:267
  30.0 11.1 %shard_map.77 = (bf16[3,8,16,512]{3,2,1,0:T(8,128)(2,1)}, f32[288,48]{1,0:T(8,128)}, f32[27,32,16]{2,1,0:T(8,128)}) custom-call(bf16[4,2,4,16,512]{4,3,2,1,0:T(8,128)(2,1)} %bitcast.32, bf16[4,2,4,16,512]{4,3,2,1,0:T(8,128)(2,1)} %bitcast.29, bf16[4,2,4,16,512]{4,3,2,1,0:T(8,128)(2,1)} %copy-done.4, bf16[4,2,4,16,512]{4,3,2,1,0:T(8,128)(2,1)} %copy-done.3, ...), custom_call_target="tpu_custom_call" | custom-call | tf_op jit(solution)/shard_map/pallas_call | solution.py:236
  41.1 1.2 %reshape.63 = f32[13824]{0:T(1024)S(1)} reshape(f32[27,32,16]{2,1,0:T(8,128)} %get-tuple-element.14) | data formatting | bytes 110592 | tf_op jit(solution)/shard_map/reshape | solution.py:286
  42.3 0.0 collective-permute-done.5.other_ref
  42.3 0.0 collective-permute-done.4.below_ref
  42.3 0.0 copy-start.11
  42.4 0.6 copy-done.10
  43.0 0.0 copy-done.11
  43.0 4.8 %shard_map.78 = (f32[2,4,64,256]{3,2,1,0:T(8,128)}, f32[3,144,64]{2,1,0:T(8,128)}) custom-call(bf16[3,128,512]{2,1,0:T(8,128)(2,1)} %bitcast.40, bf16[1,128,512]{2,1,0:T(8,128)(2,1)} %bitcast.42, bf16[1,128,512]{2,1,0:T(8,128)(2,1)} %copy-done.11, bf16[2,4,32,256]{3,2,1,0:T(8,128)(2,1)} %bitcast.37, bf16[2,4,32,256]{3,2,1,0:T(8,128)(2,1)} %copy-done.10, ...), custom_call_target="tpu_custom_call" | custom-call | tf_op jit(solution)/shard_map/pallas_call | solution.py:269
  47.8 1.1 %reshape_reshape.3 = f32[27648]{0:T(1024)S(1)} reshape(f32[3,144,64]{2,1,0:T(8,128)} %get-tuple-element.13) | data formatting | bytes 221184 | tf_op jit(solution)/shard_map/reshape;reshape | solution.py:286
  48.9 2.7 %collective-permute-start.7 = (f32[41472]{0:T(1024)S(1)}, f32[41472]{0:T(1024)S(1)}, u32[]{:S(2)}, u32[]{:S(2)}) collective-permute-start(f32[41472]{0:T(1024)S(1)} %constant_dynamic-update-slice_fusion), channel_id=1, source_target_pairs={{0,8},{2,10},{4,12},{6,14},{8,0},{10,2},{12,4},{14,6},{1,9},{3,11}... | collective-permute-start | bytes 497672 | tf_op jit(solution)/shard_map/ppermute | solution.py:54
  51.6 0.1 collective-permute-start.6
  51.7 7.8 %collective-permute-done.7 = f32[41472]{0:T(1024)S(1)} collective-permute-done((f32[41472]{0:T(1024)S(1)}, f32[41472]{0:T(1024)S(1)}, u32[]{:S(2)}, u32[]{:S(2)}) %collective-permute-start.7) | collective-permute-done | bytes 165920 | tf_op jit(solution)/shard_map/ppermute | solution.py:54
  59.6 0.7 collective-permute-start.8
  60.3 4.7 %collective-permute-done.8 = f32[41472]{0:T(1024)S(1)} collective-permute-done((f32[41472]{0:T(1024)S(1)}, f32[41472]{0:T(1024)S(1)}, u32[]{:S(2)}, u32[]{:S(2)}) %collective-permute-start.8) | collective-permute-done | bytes 165920 | tf_op jit(solution)/shard_map/ppermute | solution.py:54
  65.0 2.5 %collective-permute-start.9 = (f32[41472]{0:T(1024)S(1)}, f32[41472]{0:T(1024)S(1)}, u32[]{:S(2)}, u32[]{:S(2)}) collective-permute-start(f32[41472]{0:T(1024)S(1)} %add.37), channel_id=1, source_target_pairs={{0,2},{2,0},{4,6},{6,4},{8,10},{10,8},{12,14},{14,12},{1,3},{3,1},... | collective-permute-start | bytes 497672 | tf_op jit(solution)/shard_map/ppermute | solution.py:56
  67.5 0.0 collective-permute-done.6
  67.5 0.8 %copy.21 = bf16[32,2,4,256]{3,2,1,0:T(4,128)(2,1)} copy(bf16[32,2,4,256]{3,0,2,1:T(8,128)(2,1)S(1)} %fusion) | data formatting | bytes 262144
  68.3 2.5 %collective-permute-done.9 = f32[41472]{0:T(1024)S(1)} collective-permute-done((f32[41472]{0:T(1024)S(1)}, f32[41472]{0:T(1024)S(1)}, u32[]{:S(2)}, u32[]{:S(2)}) %collective-permute-start.9) | collective-permute-done | bytes 165920 | tf_op jit(solution)/shard_map/ppermute | solution.py:56
  70.8 0.2 add.41
  71.0 0.9 %copy.22 = f32[27,32,16]{1,2,0:T(8,128)} copy(f32[27,32,16]{2,1,0:T(8,128)S(1)} %add.41) | data formatting | bytes 110592
  71.9 0.8 %add.39 = f32[27,16,64]{2,1,0:T(8,128)} reshape(f32[27648]{0:T(1024)S(1)} %slice_add_fusion) | data formatting | bytes 221184 | tf_op jit(solution)/shard_map/add | solution.py:62
  (27 shorter events, 0.4 us)
Async XLA Ops:
  0.6 28.6 %copy-start = (bf16[27,32,64]{2,1,0:T(8,128)(2,1)S(1)}, bf16[27,32,64]{2,1,0:T(8,128)(2,1)}, u32[]{:S(2)}) copy-start(bf16[27,32,64]{2,1,0:T(8,128)(2,1)} %param.8) | copy-start | bytes 331780
  2.1 14.2 %collective-permute-start = (bf16[16,2,8,512]{3,0,2,1:T(8,128)(2,1)S(1)}, bf16[16,2,8,512]{3,0,2,1:T(8,128)(2,1)S(1)}, u32[]{:S(2)}, u32[]{:S(2)}) collective-permute-start(bf16[16,2,8,512]{3,0,2,1:T(8,128)(2,1)S(1)} %get-tuple-element.21), channel_id=1, source_target_pairs={{0,2},{2,4},{4,6},{6,8},{8,10},{10,12},{12,14},{14,0},{1,3},{3,5},... | collective-permute-start | bytes 786440 | tf_op jit(solution)/shard_map/ppermute | solution.py:219
  5.1 13.4 %collective-permute-start.1 = (bf16[16,2,8,512]{3,0,2,1:T(8,128)(2,1)S(1)}, bf16[16,2,8,512]{3,0,2,1:T(8,128)(2,1)S(1)}, u32[]{:S(2)}, u32[]{:S(2)}) collective-permute-start(bf16[16,2,8,512]{3,0,2,1:T(8,128)(2,1)S(1)} %get-tuple-element.22), channel_id=1, source_target_pairs={{2,0},{4,2},{6,4},{8,6},{10,8},{12,10},{14,12},{0,14},{3,1},{5,3},... | collective-permute-start | bytes 786440 | tf_op jit(solution)/shard_map/ppermute | solution.py:220
  8.2 10.3 %copy-start.1 = (bf16[16,4,4,2,512]{4,0,2,3,1:T(8,128)(2,1)}, bf16[16,4,4,2,512]{4,0,2,3,1:T(8,128)(2,1)S(1)}, u32[]{:S(2)}) copy-start(bf16[16,4,4,2,512]{4,0,2,3,1:T(8,128)(2,1)S(1)} %copy.29) | copy-start | bytes 1572868
  8.2 14.0 %collective-permute-start.3 = (bf16[4,2,4,16,512]{4,3,2,1,0:T(8,128)(2,1)S(1)}, bf16[4,2,4,16,512]{4,3,2,1,0:T(8,128)(2,1)S(1)}, u32[]{:S(2)}, u32[]{:S(2)}) collective-permute-start(bf16[4,2,4,16,512]{4,3,2,1,0:T(8,128)(2,1)S(1)} %bitcast.27), channel_id=1, source_target_pairs={{0,1},{1,0},{2,3},{3,2},{4,5},{5,4},{6,7},{7,6},{8,9},{9,8},{10,11... | collective-permute-start | bytes 1572872 | tf_op jit(solution)/shard_map/ppermute | solution.py:222
  18.5 0.9 %copy-start.9 = (bf16[32,2,4,256]{3,2,1,0:T(4,128)(2,1)S(1)}, bf16[32,2,4,256]{3,2,1,0:T(4,128)(2,1)}, u32[]{:S(2)}) copy-start(bf16[32,2,4,256]{3,2,1,0:T(4,128)(2,1)} %param.5) | copy-start | bytes 393220
  18.6 1.7 %copy-start.2 = (bf16[16,4,4,2,512]{4,0,2,3,1:T(8,128)(2,1)}, bf16[16,4,4,2,512]{4,0,2,3,1:T(8,128)(2,1)S(1)}, u32[]{:S(2)}) copy-start(bf16[16,4,4,2,512]{4,0,2,3,1:T(8,128)(2,1)S(1)} %copy.30) | copy-start | bytes 1572868
  18.6 1.1 %copy-start.8 = (bf16[27,32,32]{2,1,0:T(8,128)(2,1)S(1)}, bf16[27,32,32]{2,1,0:T(8,128)(2,1)}, u32[]{:S(2)}) copy-start(bf16[27,32,32]{2,1,0:T(8,128)(2,1)} %param.9) | copy-start | bytes 165892
  18.6 3.6 %collective-permute-start.2 = (bf16[4,2,4,16,512]{4,3,2,1,0:T(8,128)(2,1)S(1)}, bf16[4,2,4,16,512]{4,3,2,1,0:T(8,128)(2,1)S(1)}, u32[]{:S(2)}, u32[]{:S(2)}) collective-permute-start(bf16[4,2,4,16,512]{4,3,2,1,0:T(8,128)(2,1)S(1)} %bitcast.30), channel_id=1, source_target_pairs={{0,1},{1,0},{2,3},{3,2},{4,5},{5,4},{6,7},{7,6},{8,9},{9,8},{10,11... | collective-permute-start | bytes 1572872 | tf_op jit(solution)/shard_map/ppermute | solution.py:223
  19.4 0.6 copy-start.7
  19.4 22.9 %collective-permute-start.5 = (bf16[2,4,32,256]{3,2,1,0:T(8,128)(2,1)S(1)}, bf16[2,4,32,256]{3,2,1,0:T(8,128)(2,1)S(1)}, u32[]{:S(2)}, u32[]{:S(2)}) collective-permute-start(bf16[2,4,32,256]{3,2,1,0:T(8,128)(2,1)S(1)} %bitcast.36), channel_id=1, source_target_pairs={{0,1},{1,0},{2,3},{3,2},{4,5},{5,4},{6,7},{7,6},{8,9},{9,8},{10,11... | collective-permute-start | bytes 393224 | tf_op jit(solution)/shard_map/ppermute | solution.py:260
  20.1 1.0 %copy-start.6 = (bf16[16,4,8,512]{3,2,1,0:T(8,128)(2,1)S(1)}, bf16[16,4,8,512]{3,2,1,0:T(8,128)(2,1)}, u32[]{:S(2)}) copy-start(bf16[16,4,8,512]{3,2,1,0:T(8,128)(2,1)} %param.6) | copy-start | bytes 1572868
  22.2 0.8 %copy-start.3 = (bf16[4,2,4,16,512]{4,3,2,1,0:T(8,128)(2,1)}, bf16[4,2,4,16,512]{4,3,2,1,0:T(8,128)(2,1)S(1)}, u32[]{:S(2)}) copy-start(bf16[4,2,4,16,512]{4,3,2,1,0:T(8,128)(2,1)S(1)} %collective-permute-done.3.refs_3_) | copy-start | bytes 1572868
  22.2 1.0 %copy-start.4 = (bf16[4,2,4,16,512]{4,3,2,1,0:T(8,128)(2,1)}, bf16[4,2,4,16,512]{4,3,2,1,0:T(8,128)(2,1)S(1)}, u32[]{:S(2)}) copy-start(bf16[4,2,4,16,512]{4,3,2,1,0:T(8,128)(2,1)S(1)} %collective-permute-done.2.refs_2_) | copy-start | bytes 1572868
  28.9 13.5 %collective-permute-start.4 = (bf16[1,128,512]{2,1,0:T(8,128)(2,1)}, bf16[1,128,512]{2,1,0:T(8,128)(2,1)S(1)}, u32[]{:S(2)}, u32[]{:S(2)}) collective-permute-start(bf16[1,128,512]{2,1,0:T(8,128)(2,1)} %bitcast.41), channel_id=1, source_target_pairs={{14,0},{0,2},{2,4},{4,6},{6,8},{8,10},{10,12},{12,14},{15,1},{1,3}... | collective-permute-start | bytes 393224 | tf_op jit(solution)/shard_map/ppermute | solution.py:30
  42.3 0.7 copy-start.10
  42.3 0.7 copy-start.11
  47.8 3.8 %copy-start.5 = (f32[2,4,64,256]{3,2,1,0:T(8,128)S(1)}, f32[2,4,64,256]{3,2,1,0:T(8,128)}, u32[]{:S(2)}) copy-start(f32[2,4,64,256]{3,2,1,0:T(8,128)} %get-tuple-element.12) | copy-start | bytes 1572868
  48.9 10.6 %collective-permute-start.7 = (f32[41472]{0:T(1024)S(1)}, f32[41472]{0:T(1024)S(1)}, u32[]{:S(2)}, u32[]{:S(2)}) collective-permute-start(f32[41472]{0:T(1024)S(1)} %constant_dynamic-update-slice_fusion), channel_id=1, source_target_pairs={{0,8},{2,10},{4,12},{6,14},{8,0},{10,2},{12,4},{14,6},{1,9},{3,11}... | collective-permute-start | bytes 497672 | tf_op jit(solution)/shard_map/ppermute | solution.py:54
  51.6 15.9 %collective-permute-start.6 = (f32[2,4,32,256]{3,2,1,0:T(8,128)S(1)}, f32[2,4,32,256]{3,2,1,0:T(8,128)S(1)}, u32[]{:S(2)}, u32[]{:S(2)}) collective-permute-start(f32[2,4,32,256]{3,2,1,0:T(8,128)S(1)} %constant_dynamic-slice_fusion), channel_id=1, source_target_pairs={{0,1},{1,0},{2,3},{3,2},{4,5},{5,4},{6,7},{7,6},{8,9},{9,8},{10,11... | collective-permute-start | bytes 786440 | tf_op jit(solution)/shard_map/ppermute | solution.py:283
  59.6 5.4 %collective-permute-start.8 = (f32[41472]{0:T(1024)S(1)}, f32[41472]{0:T(1024)S(1)}, u32[]{:S(2)}, u32[]{:S(2)}) collective-permute-start(f32[41472]{0:T(1024)S(1)} %add.36), channel_id=1, source_target_pairs={{0,4},{2,6},{4,0},{6,2},{8,12},{10,14},{12,8},{14,10},{1,5},{3,7},... | collective-permute-start | bytes 497672 | tf_op jit(solution)/shard_map/ppermute | solution.py:54
  65.0 5.8 %collective-permute-start.9 = (f32[41472]{0:T(1024)S(1)}, f32[41472]{0:T(1024)S(1)}, u32[]{:S(2)}, u32[]{:S(2)}) collective-permute-start(f32[41472]{0:T(1024)S(1)} %add.37), channel_id=1, source_target_pairs={{0,2},{2,0},{4,6},{6,4},{8,10},{10,8},{12,14},{14,12},{1,3},{3,1},... | collective-permute-start | bytes 497672 | tf_op jit(solution)/shard_map/ppermute | solution.py:56

commit v19 on v17

--- a/solution.py
+++ b/solution.py
@@ -118,10 +118,10 @@
         x = step % planes_x
         pre_act = sp_ref[z, x].astype(jnp.float32)
         slopes = jnp.where(pre_act > 0, 1.0, leak_slope).astype(jnp.float32)
-        hidden = (pre_act * slopes).astype(jnp.bfloat16).astype(jnp.float32)
+        hidden = (pre_act * slopes).astype(jnp.bfloat16)
         rolled = jnp.concatenate(
             [pltpu.roll(hidden, 2, 1), hidden, pltpu.roll(hidden, cells_y - 2, 1)], axis=0
-        ).astype(jnp.bfloat16)
+        )
         block = g_ref[z % 2, pl.ds(z // 2, 3), x % 2, pl.ds(x // 2, 3)]
         block = block.reshape(9 * wide, cells_y)
         total = jnp.dot(w_ref[...], block, preferred_element_type=jnp.float32)

time: 72.7 us -> 72.4 us (level)
  no operation moved by 1% of the time
where the time goes in v19:
time: 72.4 us; the launch traced here: 71.9 us
  waiting for transfers between devices  23.8 us (33%)
  Pallas kernels  21.3 us (29%)
  starting transfers between devices  13.5 us (19%)
  local copies, waits for them, and re-layouts  12.2 us (17%)
  between operations  0.91 us (1%)
    pallas_call x2, Pallas kernels, fine_rows(): pl.pallas_call(functools.partial(fine_kernel, z_lo, z_hi, scale), out_sha...  16.5 us
    ppermute x2, waiting for transfers between devices, summed_into(): block = block + lax.ppermute(block, axis, route)  8.02 us
    ppermute x1, waiting for transfers between devices, local(): low_raw = lax.ppermute(out_grad[:, planes_z - 2:], ('gz', 'sec'), forward)  7.95 us
    unnamed x31, local copies, waits for them, and re-layouts  7.18 us
    ppermute x1, waiting for transfers between devices, summed_into(): other = lax.ppermute(block, axis, [(i, i ^ step) for i in range(count)])  5.61 us
    pallas_call x1, Pallas kernels, local(): pl.pallas_call(functools.partial(coarse_kernel, float(coarse_total) ** (-...  4.8 us
    ppermute x2, starting transfers between devices, summed_into(): block = block + lax.ppermute(block, axis, route)  4.15 us
    ppermute x1, starting transfers between devices, local(): high_raw = lax.ppermute(out_grad[:, :2], ('gz', 'sec'), backward)  3.1 us
  transfers between devices with their start and end apart: 10, of which 5 were waited for; matrix products, arithmetic and copies ran while one was open for 7% of the time, Pallas kernels for 23%

profile of v19, /device:TPU:0, one launch (start us, length us, event | category | flops | bytes accessed | tf_op | source)
XLA Modules:
  0.0 71.9 jit_solution(3987203645162181415)
XLA Ops:
  0.6 0.0 copy-start
  0.6 1.4 %copy.11 = bf16[16,4,8,512]{3,0,2,1:T(8,128)(2,1)S(1)} copy(bf16[16,4,8,512]{3,2,1,0:T(8,128)(2,1)} %param.7) | data formatting | bytes 1048576 | tf_op args[2]
  2.1 3.0 %collective-permute-start = (bf16[16,2,8,512]{3,0,2,1:T(8,128)(2,1)S(1)}, bf16[16,2,8,512]{3,0,2,1:T(8,128)(2,1)S(1)}, u32[]{:S(2)}, u32[]{:S(2)}) collective-permute-start(bf16[16,2,8,512]{3,0,2,1:T(8,128)(2,1)S(1)} %get-tuple-element.21), channel_id=1, source_target_pairs={{0,2},{2,4},{4,6},{6,8},{8,10},{10,12},{12,14},{14,0},{1,3},{3,5},... | collective-permute-start | bytes 786440 | tf_op jit(solution)/shard_map/ppermute | solution.py:219
  5.1 3.1 %collective-permute-start.1 = (bf16[16,2,8,512]{3,0,2,1:T(8,128)(2,1)S(1)}, bf16[16,2,8,512]{3,0,2,1:T(8,128)(2,1)S(1)}, u32[]{:S(2)}, u32[]{:S(2)}) collective-permute-start(bf16[16,2,8,512]{3,0,2,1:T(8,128)(2,1)S(1)} %get-tuple-element.22), channel_id=1, source_target_pairs={{2,0},{4,2},{6,4},{8,6},{10,8},{12,10},{14,12},{0,14},{3,1},{5,3},... | collective-permute-start | bytes 786440 | tf_op jit(solution)/shard_map/ppermute | solution.py:220
  8.2 0.1 collective-permute-start.3
  8.3 8.0 %collective-permute-done = bf16[16,2,8,512]{3,0,2,1:T(8,128)(2,1)S(1)} collective-permute-done((bf16[16,2,8,512]{3,0,2,1:T(8,128)(2,1)S(1)}, bf16[16,2,8,512]{3,0,2,1:T(8,128)(2,1)S(1)}, u32[]{:S(2)}, u32[]{:S(2)}) %collective-permute-start) | collective-permute-done | bytes 262176 | tf_op jit(solution)/shard_map/ppermute | solution.py:219
  16.2 2.2 %collective-permute-done.1 = bf16[16,2,8,512]{3,0,2,1:T(8,128)(2,1)S(1)} collective-permute-done((bf16[16,2,8,512]{3,0,2,1:T(8,128)(2,1)S(1)}, bf16[16,2,8,512]{3,0,2,1:T(8,128)(2,1)S(1)}, u32[]{:S(2)}, u32[]{:S(2)}) %collective-permute-start.1) | collective-permute-done | bytes 262176 | tf_op jit(solution)/shard_map/ppermute | solution.py:220
  18.5 0.0 copy-start.9
  18.6 0.0 copy-start.8
  18.6 0.1 collective-permute-start.2
  18.7 0.8 %copy-done.9 = bf16[32,2,4,256]{3,2,1,0:T(4,128)(2,1)S(1)} copy-done((bf16[32,2,4,256]{3,2,1,0:T(4,128)(2,1)S(1)}, bf16[32,2,4,256]{3,2,1,0:T(4,128)(2,1)}, u32[]{:S(2)}) %copy-start.9) | copy-done | bytes 131096
  19.4 0.1 collective-permute-start.5
  19.5 0.2 copy-done.8
  19.7 0.1 constant_dynamic-slice_fusion.2
  19.8 0.2 copy-done.7
  20.1 0.1 copy.23
  20.3 0.1 copy.18
  20.3 0.7 %reshape.58.refs_5_ = bf16[48,288]{1,0:T(8,128)(2,1)} reshape(bf16[3,16,3,3,32]{4,3,2,1,0:T(4,128)(2,1)S(1)} %copy.18) | data formatting | bytes 55296 | tf_op jit(solution)/shard_map/reshape | solution.py:229
  21.1 0.1 copy-done.6
  21.1 1.1 %copy.28 = bf16[16,4,8,512]{3,0,2,1:T(8,128)(2,1)} copy(bf16[16,4,8,512]{3,2,1,0:T(8,128)(2,1)S(1)} %copy-done.6) | data formatting | bytes 1048576 | tf_op args[1]
  22.2 0.0 collective-permute-done.3.refs_3_
  22.2 0.0 collective-permute-done.2.refs_2_
  22.2 0.8 %copy-done.3 = bf16[4,2,4,16,512]{4,3,2,1,0:T(8,128)(2,1)} copy-done((bf16[4,2,4,16,512]{4,3,2,1,0:T(8,128)(2,1)}, bf16[4,2,4,16,512]{4,3,2,1,0:T(8,128)(2,1)S(1)}, u32[]{:S(2)}) %copy-start.3) | copy-done | bytes 524312
  23.0 0.2 copy-done.4
  23.2 5.6 %shard_map.76 = (bf16[1,8,16,512]{3,2,1,0:T(8,128)(2,1)}, f32[288,48]{1,0:T(8,128)}) custom-call(bf16[4,2,4,16,512]{4,3,2,1,0:T(8,128)(2,1)} %bitcast.31, bf16[4,2,4,16,512]{4,3,2,1,0:T(8,128)(2,1)} %bitcast.28, bf16[4,2,4,16,512]{4,3,2,1,0:T(8,128)(2,1)} %copy-done.4, bf16[4,2,4,16,512]{4,3,2,1,0:T(8,128)(2,1)} %copy-done.3, ...), custom_call_target="tpu_custom_call" | custom-call | tf_op jit(solution)/shard_map/pallas_call | solution.py:236
  28.8 0.3 collective-permute-start.4
  29.2 0.8 %copy.20.u_ref = bf16[3,64,144]{2,1,0:T(8,128)(2,1)} copy(bf16[3,64,144]{1,2,0:T(8,128)(2,1)S(1)} %bitcast.38) | data formatting | bytes 110592 | tf_op jit(solution)/shard_map/reshape | solution.py:267
  29.9 10.9 %shard_map.77 = (bf16[3,8,16,512]{3,2,1,0:T(8,128)(2,1)}, f32[288,48]{1,0:T(8,128)}, f32[27,32,16]{2,1,0:T(8,128)}) custom-call(bf16[4,2,4,16,512]{4,3,2,1,0:T(8,128)(2,1)} %bitcast.32, bf16[4,2,4,16,512]{4,3,2,1,0:T(8,128)(2,1)} %bitcast.29, bf16[4,2,4,16,512]{4,3,2,1,0:T(8,128)(2,1)} %copy-done.4, bf16[4,2,4,16,512]{4,3,2,1,0:T(8,128)(2,1)} %copy-done.3, ...), custom_call_target="tpu_custom_call" | custom-call | tf_op jit(solution)/shard_map/pallas_call | solution.py:236
  40.9 1.2 %reshape.63 = f32[13824]{0:T(1024)S(1)} reshape(f32[27,32,16]{2,1,0:T(8,128)} %get-tuple-element.14) | data formatting | bytes 110592 | tf_op jit(solution)/shard_map/reshape | solution.py:286
  42.0 0.0 collective-permute-done.5.other_ref
  42.1 0.0 collective-permute-done.4.below_ref
  42.1 0.0 copy-start.11
  42.1 0.6 copy-done.10
  42.7 0.0 copy-done.11
  42.8 4.8 %shard_map.78 = (f32[2,4,64,256]{3,2,1,0:T(8,128)}, f32[3,144,64]{2,1,0:T(8,128)}) custom-call(bf16[3,128,512]{2,1,0:T(8,128)(2,1)} %bitcast.40, bf16[1,128,512]{2,1,0:T(8,128)(2,1)} %bitcast.42, bf16[1,128,512]{2,1,0:T(8,128)(2,1)} %copy-done.11, bf16[2,4,32,256]{3,2,1,0:T(8,128)(2,1)} %bitcast.37, bf16[2,4,32,256]{3,2,1,0:T(8,128)(2,1)} %copy-done.10, ...), custom_call_target="tpu_custom_call" | custom-call | tf_op jit(solution)/shard_map/pallas_call | solution.py:269
  47.6 1.1 %reshape_reshape.3 = f32[27648]{0:T(1024)S(1)} reshape(f32[3,144,64]{2,1,0:T(8,128)} %get-tuple-element.13) | data formatting | bytes 221184 | tf_op jit(solution)/shard_map/reshape;reshape | solution.py:286
  48.7 2.5 %collective-permute-start.7 = (f32[41472]{0:T(1024)S(1)}, f32[41472]{0:T(1024)S(1)}, u32[]{:S(2)}, u32[]{:S(2)}) collective-permute-start(f32[41472]{0:T(1024)S(1)} %constant_dynamic-update-slice_fusion), channel_id=1, source_target_pairs={{0,2},{2,0},{4,6},{6,4},{8,10},{10,8},{12,14},{14,12},{1,3},{3,1},... | collective-permute-start | bytes 497672 | tf_op jit(solution)/shard_map/ppermute | solution.py:54
  51.2 0.1 collective-permute-start.6
  51.3 4.2 %collective-permute-done.7 = f32[41472]{0:T(1024)S(1)} collective-permute-done((f32[41472]{0:T(1024)S(1)}, f32[41472]{0:T(1024)S(1)}, u32[]{:S(2)}, u32[]{:S(2)}) %collective-permute-start.7) | collective-permute-done | bytes 165920 | tf_op jit(solution)/shard_map/ppermute | solution.py:54
  55.5 1.6 %collective-permute-start.8 = (f32[41472]{0:T(1024)S(1)}, f32[41472]{0:T(1024)S(1)}, u32[]{:S(2)}, u32[]{:S(2)}) collective-permute-start(f32[41472]{0:T(1024)S(1)} %add.36), channel_id=1, source_target_pairs={{0,4},{2,6},{4,0},{6,2},{8,12},{10,14},{12,8},{14,10},{1,5},{3,7},... | collective-permute-start | bytes 497672 | tf_op jit(solution)/shard_map/ppermute | solution.py:54
  57.1 3.9 %collective-permute-done.8 = f32[41472]{0:T(1024)S(1)} collective-permute-done((f32[41472]{0:T(1024)S(1)}, f32[41472]{0:T(1024)S(1)}, u32[]{:S(2)}, u32[]{:S(2)}) %collective-permute-start.8) | collective-permute-done | bytes 165920 | tf_op jit(solution)/shard_map/ppermute | solution.py:54
  61.0 2.7 %collective-permute-start.9 = (f32[41472]{0:T(1024)S(1)}, f32[41472]{0:T(1024)S(1)}, u32[]{:S(2)}, u32[]{:S(2)}) collective-permute-start(f32[41472]{0:T(1024)S(1)} %add.37), channel_id=1, source_target_pairs={{0,8},{2,10},{4,12},{6,14},{8,0},{10,2},{12,4},{14,6},{1,9},{3,11}... | collective-permute-start | bytes 497672 | tf_op jit(solution)/shard_map/ppermute | solution.py:56
  63.7 0.0 collective-permute-done.6
  63.7 0.8 %copy.21 = bf16[32,2,4,256]{3,2,1,0:T(4,128)(2,1)} copy(bf16[32,2,4,256]{3,0,2,1:T(8,128)(2,1)S(1)} %fusion) | data formatting | bytes 262144
  64.5 5.6 %collective-permute-done.9 = f32[41472]{0:T(1024)S(1)} collective-permute-done((f32[41472]{0:T(1024)S(1)}, f32[41472]{0:T(1024)S(1)}, u32[]{:S(2)}, u32[]{:S(2)}) %collective-permute-start.9) | collective-permute-done | bytes 165920 | tf_op jit(solution)/shard_map/ppermute | solution.py:56
  70.1 0.2 add.41
  70.3 0.9 %copy.22 = f32[27,32,16]{1,2,0:T(8,128)} copy(f32[27,32,16]{2,1,0:T(8,128)S(1)} %add.41) | data formatting | bytes 110592
  71.2 0.8 %add.39 = f32[27,16,64]{2,1,0:T(8,128)} reshape(f32[27648]{0:T(1024)S(1)} %slice_add_fusion) | data formatting | bytes 221184 | tf_op jit(solution)/shard_map/add | solution.py:62
  (27 shorter events, 0.4 us)
Async XLA Ops:
  0.6 28.5 %copy-start = (bf16[27,32,64]{2,1,0:T(8,128)(2,1)S(1)}, bf16[27,32,64]{2,1,0:T(8,128)(2,1)}, u32[]{:S(2)}) copy-start(bf16[27,32,64]{2,1,0:T(8,128)(2,1)} %param.8) | copy-start | bytes 331780
  2.1 14.2 %collective-permute-start = (bf16[16,2,8,512]{3,0,2,1:T(8,128)(2,1)S(1)}, bf16[16,2,8,512]{3,0,2,1:T(8,128)(2,1)S(1)}, u32[]{:S(2)}, u32[]{:S(2)}) collective-permute-start(bf16[16,2,8,512]{3,0,2,1:T(8,128)(2,1)S(1)} %get-tuple-element.21), channel_id=1, source_target_pairs={{0,2},{2,4},{4,6},{6,8},{8,10},{10,12},{12,14},{14,0},{1,3},{3,5},... | collective-permute-start | bytes 786440 | tf_op jit(solution)/shard_map/ppermute | solution.py:219
  5.1 13.4 %collective-permute-start.1 = (bf16[16,2,8,512]{3,0,2,1:T(8,128)(2,1)S(1)}, bf16[16,2,8,512]{3,0,2,1:T(8,128)(2,1)S(1)}, u32[]{:S(2)}, u32[]{:S(2)}) collective-permute-start(bf16[16,2,8,512]{3,0,2,1:T(8,128)(2,1)S(1)} %get-tuple-element.22), channel_id=1, source_target_pairs={{2,0},{4,2},{6,4},{8,6},{10,8},{12,10},{14,12},{0,14},{3,1},{5,3},... | collective-permute-start | bytes 786440 | tf_op jit(solution)/shard_map/ppermute | solution.py:220
  8.2 10.3 %copy-start.1 = (bf16[16,4,4,2,512]{4,0,2,3,1:T(8,128)(2,1)}, bf16[16,4,4,2,512]{4,0,2,3,1:T(8,128)(2,1)S(1)}, u32[]{:S(2)}) copy-start(bf16[16,4,4,2,512]{4,0,2,3,1:T(8,128)(2,1)S(1)} %copy.29) | copy-start | bytes 1572868
  8.2 14.0 %collective-permute-start.3 = (bf16[4,2,4,16,512]{4,3,2,1,0:T(8,128)(2,1)S(1)}, bf16[4,2,4,16,512]{4,3,2,1,0:T(8,128)(2,1)S(1)}, u32[]{:S(2)}, u32[]{:S(2)}) collective-permute-start(bf16[4,2,4,16,512]{4,3,2,1,0:T(8,128)(2,1)S(1)} %bitcast.27), channel_id=1, source_target_pairs={{0,1},{1,0},{2,3},{3,2},{4,5},{5,4},{6,7},{7,6},{8,9},{9,8},{10,11... | collective-permute-start | bytes 1572872 | tf_op jit(solution)/shard_map/ppermute | solution.py:222
  18.5 0.9 %copy-start.9 = (bf16[32,2,4,256]{3,2,1,0:T(4,128)(2,1)S(1)}, bf16[32,2,4,256]{3,2,1,0:T(4,128)(2,1)}, u32[]{:S(2)}) copy-start(bf16[32,2,4,256]{3,2,1,0:T(4,128)(2,1)} %param.5) | copy-start | bytes 393220
  18.6 1.7 %copy-start.2 = (bf16[16,4,4,2,512]{4,0,2,3,1:T(8,128)(2,1)}, bf16[16,4,4,2,512]{4,0,2,3,1:T(8,128)(2,1)S(1)}, u32[]{:S(2)}) copy-start(bf16[16,4,4,2,512]{4,0,2,3,1:T(8,128)(2,1)S(1)} %copy.30) | copy-start | bytes 1572868
  18.6 1.1 %copy-start.8 = (bf16[27,32,32]{2,1,0:T(8,128)(2,1)S(1)}, bf16[27,32,32]{2,1,0:T(8,128)(2,1)}, u32[]{:S(2)}) copy-start(bf16[27,32,32]{2,1,0:T(8,128)(2,1)} %param.9) | copy-start | bytes 165892
  18.6 3.6 %collective-permute-start.2 = (bf16[4,2,4,16,512]{4,3,2,1,0:T(8,128)(2,1)S(1)}, bf16[4,2,4,16,512]{4,3,2,1,0:T(8,128)(2,1)S(1)}, u32[]{:S(2)}, u32[]{:S(2)}) collective-permute-start(bf16[4,2,4,16,512]{4,3,2,1,0:T(8,128)(2,1)S(1)} %bitcast.30), channel_id=1, source_target_pairs={{0,1},{1,0},{2,3},{3,2},{4,5},{5,4},{6,7},{7,6},{8,9},{9,8},{10,11... | collective-permute-start | bytes 1572872 | tf_op jit(solution)/shard_map/ppermute | solution.py:223
  19.4 0.6 copy-start.7
  19.4 22.6 %collective-permute-start.5 = (bf16[2,4,32,256]{3,2,1,0:T(8,128)(2,1)S(1)}, bf16[2,4,32,256]{3,2,1,0:T(8,128)(2,1)S(1)}, u32[]{:S(2)}, u32[]{:S(2)}) collective-permute-start(bf16[2,4,32,256]{3,2,1,0:T(8,128)(2,1)S(1)} %bitcast.36), channel_id=1, source_target_pairs={{0,1},{1,0},{2,3},{3,2},{4,5},{5,4},{6,7},{7,6},{8,9},{9,8},{10,11... | collective-permute-start | bytes 393224 | tf_op jit(solution)/shard_map/ppermute | solution.py:260
  20.1 1.0 %copy-start.6 = (bf16[16,4,8,512]{3,2,1,0:T(8,128)(2,1)S(1)}, bf16[16,4,8,512]{3,2,1,0:T(8,128)(2,1)}, u32[]{:S(2)}) copy-start(bf16[16,4,8,512]{3,2,1,0:T(8,128)(2,1)} %param.6) | copy-start | bytes 1572868
  22.2 0.8 %copy-start.3 = (bf16[4,2,4,16,512]{4,3,2,1,0:T(8,128)(2,1)}, bf16[4,2,4,16,512]{4,3,2,1,0:T(8,128)(2,1)S(1)}, u32[]{:S(2)}) copy-start(bf16[4,2,4,16,512]{4,3,2,1,0:T(8,128)(2,1)S(1)} %collective-permute-done.3.refs_3_) | copy-start | bytes 1572868
  22.2 1.0 %copy-start.4 = (bf16[4,2,4,16,512]{4,3,2,1,0:T(8,128)(2,1)}, bf16[4,2,4,16,512]{4,3,2,1,0:T(8,128)(2,1)S(1)}, u32[]{:S(2)}) copy-start(bf16[4,2,4,16,512]{4,3,2,1,0:T(8,128)(2,1)S(1)} %collective-permute-done.2.refs_2_) | copy-start | bytes 1572868
  28.8 13.3 %collective-permute-start.4 = (bf16[1,128,512]{2,1,0:T(8,128)(2,1)}, bf16[1,128,512]{2,1,0:T(8,128)(2,1)S(1)}, u32[]{:S(2)}, u32[]{:S(2)}) collective-permute-start(bf16[1,128,512]{2,1,0:T(8,128)(2,1)} %bitcast.41), channel_id=1, source_target_pairs={{14,0},{0,2},{2,4},{4,6},{6,8},{8,10},{10,12},{12,14},{15,1},{1,3}... | collective-permute-start | bytes 393224 | tf_op jit(solution)/shard_map/ppermute | solution.py:30
  42.1 0.7 copy-start.10
  42.1 0.7 copy-start.11
  47.6 3.6 %copy-start.5 = (f32[2,4,64,256]{3,2,1,0:T(8,128)S(1)}, f32[2,4,64,256]{3,2,1,0:T(8,128)}, u32[]{:S(2)}) copy-start(f32[2,4,64,256]{3,2,1,0:T(8,128)} %get-tuple-element.12) | copy-start | bytes 1572868
  48.7 6.8 %collective-permute-start.7 = (f32[41472]{0:T(1024)S(1)}, f32[41472]{0:T(1024)S(1)}, u32[]{:S(2)}, u32[]{:S(2)}) collective-permute-start(f32[41472]{0:T(1024)S(1)} %constant_dynamic-update-slice_fusion), channel_id=1, source_target_pairs={{0,2},{2,0},{4,6},{6,4},{8,10},{10,8},{12,14},{14,12},{1,3},{3,1},... | collective-permute-start | bytes 497672 | tf_op jit(solution)/shard_map/ppermute | solution.py:54
  51.2 12.5 %collective-permute-start.6 = (f32[2,4,32,256]{3,2,1,0:T(8,128)S(1)}, f32[2,4,32,256]{3,2,1,0:T(8,128)S(1)}, u32[]{:S(2)}, u32[]{:S(2)}) collective-permute-start(f32[2,4,32,256]{3,2,1,0:T(8,128)S(1)} %constant_dynamic-slice_fusion), channel_id=1, source_target_pairs={{0,1},{1,0},{2,3},{3,2},{4,5},{5,4},{6,7},{7,6},{8,9},{9,8},{10,11... | collective-permute-start | bytes 786440 | tf_op jit(solution)/shard_map/ppermute | solution.py:283
  55.5 5.5 %collective-permute-start.8 = (f32[41472]{0:T(1024)S(1)}, f32[41472]{0:T(1024)S(1)}, u32[]{:S(2)}, u32[]{:S(2)}) collective-permute-start(f32[41472]{0:T(1024)S(1)} %add.36), channel_id=1, source_target_pairs={{0,4},{2,6},{4,0},{6,2},{8,12},{10,14},{12,8},{14,10},{1,5},{3,7},... | collective-permute-start | bytes 497672 | tf_op jit(solution)/shard_map/ppermute | solution.py:54
  61.0 9.1 %collective-permute-start.9 = (f32[41472]{0:T(1024)S(1)}, f32[41472]{0:T(1024)S(1)}, u32[]{:S(2)}, u32[]{:S(2)}) collective-permute-start(f32[41472]{0:T(1024)S(1)} %add.37), channel_id=1, source_target_pairs={{0,8},{2,10},{4,12},{6,14},{8,0},{10,2},{12,4},{14,6},{1,9},{3,11}... | collective-permute-start | bytes 497672 | tf_op jit(solution)/shard_map/ppermute | solution.py:56

commit v20 on v17

--- a/solution.py
+++ b/solution.py
@@ -84,6 +84,7 @@
     g_ref[:, :, :, 0] = edge
     g_ref[:, :, :, planes_x // 2 + 1] = edge
     copies = []
+    by_plane = {}
     for plane in needed:
         if plane < low_count:
             part, at = 0, plane
@@ -106,12 +107,11 @@
                 )
                 copy.start()
                 copies.append(copy)
+                by_plane.setdefault(plane, []).append(copy)
     if start_ref is None:
         r_ref[...] = jnp.zeros(r_ref.shape, r_ref.dtype)
     else:
         r_ref[...] = start_ref[...]
-    for copy in copies:
-        copy.wait()
 
     def body(step, carry):
         z = z_lo + step // planes_x
@@ -136,7 +136,11 @@
         gp_ref[z - z_lo, x] = (grad_hidden * slopes).astype(gp_ref.dtype)
         return carry
 
-    lax.fori_loop(0, (z_hi - z_lo) * planes_x, body, 0)
+    for z in range(z_lo, z_hi):
+        for plane in sorted({z + 4 - 2 * dz for dz in range(3)}):
+            for copy in by_plane.pop(plane, []):
+                copy.wait()
+        lax.fori_loop((z - z_lo) * planes_x, (z - z_lo + 1) * planes_x, body, 0)
     if final_ref is not None:
         acc = r_ref[...] * scale
         for dz in range(3):

time: 72.7 us -> 72.6 us (level)
  no operation moved by 1% of the time
where the time goes in v20:
time: 72.6 us; the launch traced here: 72.1 us
  waiting for transfers between devices  23.8 us (33%)
  Pallas kernels  21.4 us (29%)
  starting transfers between devices  13.5 us (19%)
  local copies, waits for them, and re-layouts  12.2 us (17%)
  between operations  0.91 us (1%)
    pallas_call x2, Pallas kernels, fine_rows(): pl.pallas_call(functools.partial(fine_kernel, z_lo, z_hi, scale), out_sha...  16.6 us
    ppermute x2, waiting for transfers between devices, summed_into(): block = block + lax.ppermute(block, axis, route)  8.02 us
    ppermute x1, waiting for transfers between devices, local(): low_raw = lax.ppermute(out_grad[:, planes_z - 2:], ('gz', 'sec'), forward)  7.95 us
    unnamed x31, local copies, waits for them, and re-layouts  7.18 us
    ppermute x1, waiting for transfers between devices, summed_into(): other = lax.ppermute(block, axis, [(i, i ^ step) for i in range(count)])  5.61 us
    pallas_call x1, Pallas kernels, local(): pl.pallas_call(functools.partial(coarse_kernel, float(coarse_total) ** (-...  4.79 us
    ppermute x2, starting transfers between devices, summed_into(): block = block + lax.ppermute(block, axis, route)  4.15 us
    ppermute x1, starting transfers between devices, local(): high_raw = lax.ppermute(out_grad[:, :2], ('gz', 'sec'), backward)  3.1 us
  transfers between devices with their start and end apart: 10, of which 5 were waited for; matrix products, arithmetic and copies ran while one was open for 7% of the time, Pallas kernels for 23%

profile of v20, /device:TPU:0, one launch (start us, length us, event | category | flops | bytes accessed | tf_op | source)
XLA Modules:
  0.0 72.1 jit_solution(5841457967330983223)
XLA Ops:
  0.6 0.0 copy-start
  0.6 1.4 %copy.11 = bf16[16,4,8,512]{3,0,2,1:T(8,128)(2,1)S(1)} copy(bf16[16,4,8,512]{3,2,1,0:T(8,128)(2,1)} %param.7) | data formatting | bytes 1048576 | tf_op args[2]
  2.1 3.0 %collective-permute-start = (bf16[16,2,8,512]{3,0,2,1:T(8,128)(2,1)S(1)}, bf16[16,2,8,512]{3,0,2,1:T(8,128)(2,1)S(1)}, u32[]{:S(2)}, u32[]{:S(2)}) collective-permute-start(bf16[16,2,8,512]{3,0,2,1:T(8,128)(2,1)S(1)} %get-tuple-element.21), channel_id=1, source_target_pairs={{0,2},{2,4},{4,6},{6,8},{8,10},{10,12},{12,14},{14,0},{1,3},{3,5},... | collective-permute-start | bytes 786440 | tf_op jit(solution)/shard_map/ppermute | solution.py:223
  5.1 3.1 %collective-permute-start.1 = (bf16[16,2,8,512]{3,0,2,1:T(8,128)(2,1)S(1)}, bf16[16,2,8,512]{3,0,2,1:T(8,128)(2,1)S(1)}, u32[]{:S(2)}, u32[]{:S(2)}) collective-permute-start(bf16[16,2,8,512]{3,0,2,1:T(8,128)(2,1)S(1)} %get-tuple-element.22), channel_id=1, source_target_pairs={{2,0},{4,2},{6,4},{8,6},{10,8},{12,10},{14,12},{0,14},{3,1},{5,3},... | collective-permute-start | bytes 786440 | tf_op jit(solution)/shard_map/ppermute | solution.py:224
  8.2 0.1 collective-permute-start.3
  8.3 8.0 %collective-permute-done = bf16[16,2,8,512]{3,0,2,1:T(8,128)(2,1)S(1)} collective-permute-done((bf16[16,2,8,512]{3,0,2,1:T(8,128)(2,1)S(1)}, bf16[16,2,8,512]{3,0,2,1:T(8,128)(2,1)S(1)}, u32[]{:S(2)}, u32[]{:S(2)}) %collective-permute-start) | collective-permute-done | bytes 262176 | tf_op jit(solution)/shard_map/ppermute | solution.py:223
  16.2 2.2 %collective-permute-done.1 = bf16[16,2,8,512]{3,0,2,1:T(8,128)(2,1)S(1)} collective-permute-done((bf16[16,2,8,512]{3,0,2,1:T(8,128)(2,1)S(1)}, bf16[16,2,8,512]{3,0,2,1:T(8,128)(2,1)S(1)}, u32[]{:S(2)}, u32[]{:S(2)}) %collective-permute-start.1) | collective-permute-done | bytes 262176 | tf_op jit(solution)/shard_map/ppermute | solution.py:224
  18.5 0.0 copy-start.9
  18.6 0.0 copy-start.8
  18.6 0.1 collective-permute-start.2
  18.7 0.8 %copy-done.9 = bf16[32,2,4,256]{3,2,1,0:T(4,128)(2,1)S(1)} copy-done((bf16[32,2,4,256]{3,2,1,0:T(4,128)(2,1)S(1)}, bf16[32,2,4,256]{3,2,1,0:T(4,128)(2,1)}, u32[]{:S(2)}) %copy-start.9) | copy-done | bytes 131096
  19.4 0.1 collective-permute-start.5
  19.5 0.2 copy-done.8
  19.7 0.1 constant_dynamic-slice_fusion.2
  19.8 0.2 copy-done.7
  20.1 0.1 copy.23
  20.3 0.1 copy.18
  20.3 0.7 %reshape.58.refs_5_ = bf16[48,288]{1,0:T(8,128)(2,1)} reshape(bf16[3,16,3,3,32]{4,3,2,1,0:T(4,128)(2,1)S(1)} %copy.18) | data formatting | bytes 55296 | tf_op jit(solution)/shard_map/reshape | solution.py:233
  21.1 0.1 copy-done.6
  21.1 1.1 %copy.28 = bf16[16,4,8,512]{3,0,2,1:T(8,128)(2,1)} copy(bf16[16,4,8,512]{3,2,1,0:T(8,128)(2,1)S(1)} %copy-done.6) | data formatting | bytes 1048576 | tf_op args[1]
  22.2 0.0 collective-permute-done.3.refs_3_
  22.2 0.0 collective-permute-done.2.refs_2_
  22.2 0.8 %copy-done.3 = bf16[4,2,4,16,512]{4,3,2,1,0:T(8,128)(2,1)} copy-done((bf16[4,2,4,16,512]{4,3,2,1,0:T(8,128)(2,1)}, bf16[4,2,4,16,512]{4,3,2,1,0:T(8,128)(2,1)S(1)}, u32[]{:S(2)}) %copy-start.3) | copy-done | bytes 524312
  23.0 0.2 copy-done.4
  23.2 5.7 %shard_map.76 = (bf16[1,8,16,512]{3,2,1,0:T(8,128)(2,1)}, f32[288,48]{1,0:T(8,128)}) custom-call(bf16[4,2,4,16,512]{4,3,2,1,0:T(8,128)(2,1)} %bitcast.31, bf16[4,2,4,16,512]{4,3,2,1,0:T(8,128)(2,1)} %bitcast.28, bf16[4,2,4,16,512]{4,3,2,1,0:T(8,128)(2,1)} %copy-done.4, bf16[4,2,4,16,512]{4,3,2,1,0:T(8,128)(2,1)} %copy-done.3, ...), custom_call_target="tpu_custom_call" | custom-call | tf_op jit(solution)/shard_map/pallas_call | solution.py:240
  28.9 0.3 collective-permute-start.4
  29.2 0.8 %copy.20.u_ref = bf16[3,64,144]{2,1,0:T(8,128)(2,1)} copy(bf16[3,64,144]{1,2,0:T(8,128)(2,1)S(1)} %bitcast.38) | data formatting | bytes 110592 | tf_op jit(solution)/shard_map/reshape | solution.py:271
  30.0 11.0 %shard_map.77 = (bf16[3,8,16,512]{3,2,1,0:T(8,128)(2,1)}, f32[288,48]{1,0:T(8,128)}, f32[27,32,16]{2,1,0:T(8,128)}) custom-call(bf16[4,2,4,16,512]{4,3,2,1,0:T(8,128)(2,1)} %bitcast.32, bf16[4,2,4,16,512]{4,3,2,1,0:T(8,128)(2,1)} %bitcast.29, bf16[4,2,4,16,512]{4,3,2,1,0:T(8,128)(2,1)} %copy-done.4, bf16[4,2,4,16,512]{4,3,2,1,0:T(8,128)(2,1)} %copy-done.3, ...), custom_call_target="tpu_custom_call" | custom-call | tf_op jit(solution)/shard_map/pallas_call | solution.py:240
  41.0 1.2 %reshape.63 = f32[13824]{0:T(1024)S(1)} reshape(f32[27,32,16]{2,1,0:T(8,128)} %get-tuple-element.14) | data formatting | bytes 110592 | tf_op jit(solution)/shard_map/reshape | solution.py:290
  42.2 0.0 collective-permute-done.5.other_ref
  42.2 0.0 collective-permute-done.4.below_ref
  42.2 0.0 copy-start.11
  42.2 0.6 copy-done.10
  42.8 0.0 copy-done.11
  42.9 4.8 %shard_map.78 = (f32[2,4,64,256]{3,2,1,0:T(8,128)}, f32[3,144,64]{2,1,0:T(8,128)}) custom-call(bf16[3,128,512]{2,1,0:T(8,128)(2,1)} %bitcast.40, bf16[1,128,512]{2,1,0:T(8,128)(2,1)} %bitcast.42, bf16[1,128,512]{2,1,0:T(8,128)(2,1)} %copy-done.11, bf16[2,4,32,256]{3,2,1,0:T(8,128)(2,1)} %bitcast.37, bf16[2,4,32,256]{3,2,1,0:T(8,128)(2,1)} %copy-done.10, ...), custom_call_target="tpu_custom_call" | custom-call | tf_op jit(solution)/shard_map/pallas_call | solution.py:273
  47.7 1.1 %reshape_reshape.3 = f32[27648]{0:T(1024)S(1)} reshape(f32[3,144,64]{2,1,0:T(8,128)} %get-tuple-element.13) | data formatting | bytes 221184 | tf_op jit(solution)/shard_map/reshape;reshape | solution.py:290
  48.8 2.5 %collective-permute-start.7 = (f32[41472]{0:T(1024)S(1)}, f32[41472]{0:T(1024)S(1)}, u32[]{:S(2)}, u32[]{:S(2)}) collective-permute-start(f32[41472]{0:T(1024)S(1)} %constant_dynamic-update-slice_fusion), channel_id=1, source_target_pairs={{0,2},{2,0},{4,6},{6,4},{8,10},{10,8},{12,14},{14,12},{1,3},{3,1},... | collective-permute-start | bytes 497672 | tf_op jit(solution)/shard_map/ppermute | solution.py:54
  51.3 0.1 collective-permute-start.6
  51.4 4.2 %collective-permute-done.7 = f32[41472]{0:T(1024)S(1)} collective-permute-done((f32[41472]{0:T(1024)S(1)}, f32[41472]{0:T(1024)S(1)}, u32[]{:S(2)}, u32[]{:S(2)}) %collective-permute-start.7) | collective-permute-done | bytes 165920 | tf_op jit(solution)/shard_map/ppermute | solution.py:54
  55.6 1.6 %collective-permute-start.8 = (f32[41472]{0:T(1024)S(1)}, f32[41472]{0:T(1024)S(1)}, u32[]{:S(2)}, u32[]{:S(2)}) collective-permute-start(f32[41472]{0:T(1024)S(1)} %add.36), channel_id=1, source_target_pairs={{0,4},{2,6},{4,0},{6,2},{8,12},{10,14},{12,8},{14,10},{1,5},{3,7},... | collective-permute-start | bytes 497672 | tf_op jit(solution)/shard_map/ppermute | solution.py:54
  57.2 3.9 %collective-permute-done.8 = f32[41472]{0:T(1024)S(1)} collective-permute-done((f32[41472]{0:T(1024)S(1)}, f32[41472]{0:T(1024)S(1)}, u32[]{:S(2)}, u32[]{:S(2)}) %collective-permute-start.8) | collective-permute-done | bytes 165920 | tf_op jit(solution)/shard_map/ppermute | solution.py:54
  61.1 2.7 %collective-permute-start.9 = (f32[41472]{0:T(1024)S(1)}, f32[41472]{0:T(1024)S(1)}, u32[]{:S(2)}, u32[]{:S(2)}) collective-permute-start(f32[41472]{0:T(1024)S(1)} %add.37), channel_id=1, source_target_pairs={{0,8},{2,10},{4,12},{6,14},{8,0},{10,2},{12,4},{14,6},{1,9},{3,11}... | collective-permute-start | bytes 497672 | tf_op jit(solution)/shard_map/ppermute | solution.py:56
  63.8 0.0 collective-permute-done.6
  63.8 0.8 %copy.21 = bf16[32,2,4,256]{3,2,1,0:T(4,128)(2,1)} copy(bf16[32,2,4,256]{3,0,2,1:T(8,128)(2,1)S(1)} %fusion) | data formatting | bytes 262144
  64.6 5.6 %collective-permute-done.9 = f32[41472]{0:T(1024)S(1)} collective-permute-done((f32[41472]{0:T(1024)S(1)}, f32[41472]{0:T(1024)S(1)}, u32[]{:S(2)}, u32[]{:S(2)}) %collective-permute-start.9) | collective-permute-done | bytes 165920 | tf_op jit(solution)/shard_map/ppermute | solution.py:56
  70.2 0.2 add.41
  70.4 0.9 %copy.22 = f32[27,32,16]{1,2,0:T(8,128)} copy(f32[27,32,16]{2,1,0:T(8,128)S(1)} %add.41) | data formatting | bytes 110592
  71.3 0.8 %add.39 = f32[27,16,64]{2,1,0:T(8,128)} reshape(f32[27648]{0:T(1024)S(1)} %slice_add_fusion) | data formatting | bytes 221184 | tf_op jit(solution)/shard_map/add | solution.py:62
  (27 shorter events, 0.4 us)
Async XLA Ops:
  0.6 28.6 %copy-start = (bf16[27,32,64]{2,1,0:T(8,128)(2,1)S(1)}, bf16[27,32,64]{2,1,0:T(8,128)(2,1)}, u32[]{:S(2)}) copy-start(bf16[27,32,64]{2,1,0:T(8,128)(2,1)} %param.8) | copy-start | bytes 331780
  2.1 14.2 %collective-permute-start = (bf16[16,2,8,512]{3,0,2,1:T(8,128)(2,1)S(1)}, bf16[16,2,8,512]{3,0,2,1:T(8,128)(2,1)S(1)}, u32[]{:S(2)}, u32[]{:S(2)}) collective-permute-start(bf16[16,2,8,512]{3,0,2,1:T(8,128)(2,1)S(1)} %get-tuple-element.21), channel_id=1, source_target_pairs={{0,2},{2,4},{4,6},{6,8},{8,10},{10,12},{12,14},{14,0},{1,3},{3,5},... | collective-permute-start | bytes 786440 | tf_op jit(solution)/shard_map/ppermute | solution.py:223
  5.1 13.4 %collective-permute-start.1 = (bf16[16,2,8,512]{3,0,2,1:T(8,128)(2,1)S(1)}, bf16[16,2,8,512]{3,0,2,1:T(8,128)(2,1)S(1)}, u32[]{:S(2)}, u32[]{:S(2)}) collective-permute-start(bf16[16,2,8,512]{3,0,2,1:T(8,128)(2,1)S(1)} %get-tuple-element.22), channel_id=1, source_target_pairs={{2,0},{4,2},{6,4},{8,6},{10,8},{12,10},{14,12},{0,14},{3,1},{5,3},... | collective-permute-start | bytes 786440 | tf_op jit(solution)/shard_map/ppermute | solution.py:224
  8.2 10.3 %copy-start.1 = (bf16[16,4,4,2,512]{4,0,2,3,1:T(8,128)(2,1)}, bf16[16,4,4,2,512]{4,0,2,3,1:T(8,128)(2,1)S(1)}, u32[]{:S(2)}) copy-start(bf16[16,4,4,2,512]{4,0,2,3,1:T(8,128)(2,1)S(1)} %copy.29) | copy-start | bytes 1572868
  8.2 14.0 %collective-permute-start.3 = (bf16[4,2,4,16,512]{4,3,2,1,0:T(8,128)(2,1)S(1)}, bf16[4,2,4,16,512]{4,3,2,1,0:T(8,128)(2,1)S(1)}, u32[]{:S(2)}, u32[]{:S(2)}) collective-permute-start(bf16[4,2,4,16,512]{4,3,2,1,0:T(8,128)(2,1)S(1)} %bitcast.27), channel_id=1, source_target_pairs={{0,1},{1,0},{2,3},{3,2},{4,5},{5,4},{6,7},{7,6},{8,9},{9,8},{10,11... | collective-permute-start | bytes 1572872 | tf_op jit(solution)/shard_map/ppermute | solution.py:226
  18.5 0.9 %copy-start.9 = (bf16[32,2,4,256]{3,2,1,0:T(4,128)(2,1)S(1)}, bf16[32,2,4,256]{3,2,1,0:T(4,128)(2,1)}, u32[]{:S(2)}) copy-start(bf16[32,2,4,256]{3,2,1,0:T(4,128)(2,1)} %param.5) | copy-start | bytes 393220
  18.6 1.7 %copy-start.2 = (bf16[16,4,4,2,512]{4,0,2,3,1:T(8,128)(2,1)}, bf16[16,4,4,2,512]{4,0,2,3,1:T(8,128)(2,1)S(1)}, u32[]{:S(2)}) copy-start(bf16[16,4,4,2,512]{4,0,2,3,1:T(8,128)(2,1)S(1)} %copy.30) | copy-start | bytes 1572868
  18.6 1.1 %copy-start.8 = (bf16[27,32,32]{2,1,0:T(8,128)(2,1)S(1)}, bf16[27,32,32]{2,1,0:T(8,128)(2,1)}, u32[]{:S(2)}) copy-start(bf16[27,32,32]{2,1,0:T(8,128)(2,1)} %param.9) | copy-start | bytes 165892
  18.6 3.6 %collective-permute-start.2 = (bf16[4,2,4,16,512]{4,3,2,1,0:T(8,128)(2,1)S(1)}, bf16[4,2,4,16,512]{4,3,2,1,0:T(8,128)(2,1)S(1)}, u32[]{:S(2)}, u32[]{:S(2)}) collective-permute-start(bf16[4,2,4,16,512]{4,3,2,1,0:T(8,128)(2,1)S(1)} %bitcast.30), channel_id=1, source_target_pairs={{0,1},{1,0},{2,3},{3,2},{4,5},{5,4},{6,7},{7,6},{8,9},{9,8},{10,11... | collective-permute-start | bytes 1572872 | tf_op jit(solution)/shard_map/ppermute | solution.py:227
  19.4 0.6 copy-start.7
  19.4 22.7 %collective-permute-start.5 = (bf16[2,4,32,256]{3,2,1,0:T(8,128)(2,1)S(1)}, bf16[2,4,32,256]{3,2,1,0:T(8,128)(2,1)S(1)}, u32[]{:S(2)}, u32[]{:S(2)}) collective-permute-start(bf16[2,4,32,256]{3,2,1,0:T(8,128)(2,1)S(1)} %bitcast.36), channel_id=1, source_target_pairs={{0,1},{1,0},{2,3},{3,2},{4,5},{5,4},{6,7},{7,6},{8,9},{9,8},{10,11... | collective-permute-start | bytes 393224 | tf_op jit(solution)/shard_map/ppermute | solution.py:264
  20.1 1.0 %copy-start.6 = (bf16[16,4,8,512]{3,2,1,0:T(8,128)(2,1)S(1)}, bf16[16,4,8,512]{3,2,1,0:T(8,128)(2,1)}, u32[]{:S(2)}) copy-start(bf16[16,4,8,512]{3,2,1,0:T(8,128)(2,1)} %param.6) | copy-start | bytes 1572868
  22.2 0.8 %copy-start.3 = (bf16[4,2,4,16,512]{4,3,2,1,0:T(8,128)(2,1)}, bf16[4,2,4,16,512]{4,3,2,1,0:T(8,128)(2,1)S(1)}, u32[]{:S(2)}) copy-start(bf16[4,2,4,16,512]{4,3,2,1,0:T(8,128)(2,1)S(1)} %collective-permute-done.3.refs_3_) | copy-start | bytes 1572868
  22.2 1.0 %copy-start.4 = (bf16[4,2,4,16,512]{4,3,2,1,0:T(8,128)(2,1)}, bf16[4,2,4,16,512]{4,3,2,1,0:T(8,128)(2,1)S(1)}, u32[]{:S(2)}) copy-start(bf16[4,2,4,16,512]{4,3,2,1,0:T(8,128)(2,1)S(1)} %collective-permute-done.2.refs_2_) | copy-start | bytes 1572868
  28.9 13.3 %collective-permute-start.4 = (bf16[1,128,512]{2,1,0:T(8,128)(2,1)}, bf16[1,128,512]{2,1,0:T(8,128)(2,1)S(1)}, u32[]{:S(2)}, u32[]{:S(2)}) collective-permute-start(bf16[1,128,512]{2,1,0:T(8,128)(2,1)} %bitcast.41), channel_id=1, source_target_pairs={{14,0},{0,2},{2,4},{4,6},{6,8},{8,10},{10,12},{12,14},{15,1},{1,3}... | collective-permute-start | bytes 393224 | tf_op jit(solution)/shard_map/ppermute | solution.py:30
  42.2 0.7 copy-start.10
  42.2 0.7 copy-start.11
  47.7 3.6 %copy-start.5 = (f32[2,4,64,256]{3,2,1,0:T(8,128)S(1)}, f32[2,4,64,256]{3,2,1,0:T(8,128)}, u32[]{:S(2)}) copy-start(f32[2,4,64,256]{3,2,1,0:T(8,128)} %get-tuple-element.12) | copy-start | bytes 1572868
  48.8 6.8 %collective-permute-start.7 = (f32[41472]{0:T(1024)S(1)}, f32[41472]{0:T(1024)S(1)}, u32[]{:S(2)}, u32[]{:S(2)}) collective-permute-start(f32[41472]{0:T(1024)S(1)} %constant_dynamic-update-slice_fusion), channel_id=1, source_target_pairs={{0,2},{2,0},{4,6},{6,4},{8,10},{10,8},{12,14},{14,12},{1,3},{3,1},... | collective-permute-start | bytes 497672 | tf_op jit(solution)/shard_map/ppermute | solution.py:54
  51.3 12.5 %collective-permute-start.6 = (f32[2,4,32,256]{3,2,1,0:T(8,128)S(1)}, f32[2,4,32,256]{3,2,1,0:T(8,128)S(1)}, u32[]{:S(2)}, u32[]{:S(2)}) collective-permute-start(f32[2,4,32,256]{3,2,1,0:T(8,128)S(1)} %constant_dynamic-slice_fusion), channel_id=1, source_target_pairs={{0,1},{1,0},{2,3},{3,2},{4,5},{5,4},{6,7},{7,6},{8,9},{9,8},{10,11... | collective-permute-start | bytes 786440 | tf_op jit(solution)/shard_map/ppermute | solution.py:287
  55.6 5.5 %collective-permute-start.8 = (f32[41472]{0:T(1024)S(1)}, f32[41472]{0:T(1024)S(1)}, u32[]{:S(2)}, u32[]{:S(2)}) collective-permute-start(f32[41472]{0:T(1024)S(1)} %add.36), channel_id=1, source_target_pairs={{0,4},{2,6},{4,0},{6,2},{8,12},{10,14},{12,8},{14,10},{1,5},{3,7},... | collective-permute-start | bytes 497672 | tf_op jit(solution)/shard_map/ppermute | solution.py:54
  61.1 9.1 %collective-permute-start.9 = (f32[41472]{0:T(1024)S(1)}, f32[41472]{0:T(1024)S(1)}, u32[]{:S(2)}, u32[]{:S(2)}) collective-permute-start(f32[41472]{0:T(1024)S(1)} %add.37), channel_id=1, source_target_pairs={{0,8},{2,10},{4,12},{6,14},{8,0},{10,2},{12,4},{14,6},{1,9},{3,11}... | collective-permute-start | bytes 497672 | tf_op jit(solution)/shard_map/ppermute | solution.py:56
